TPU v7x, 128 devices: a whole 4x4x4 slice. The times are simulated.
128 devices in a mesh: pos: 8 (over y, core), stream: 16 (over z, x).
Axes of the slice: x: 4, y: 4, z: 4, core: 2. Of those that a mesh axis runs over, the one named last changes fastest.
Arguments:
- tokens_in: bfloat16 [16, 4096, 8192], P('stream', 'pos'), may hold values from -6 to 6
- proj_in: bfloat16 [16, 4096, 256], P('stream', 'pos'), may hold values from -1.75 to 1.75
- step_raw: bfloat16 [16, 4096, 128], P('stream', 'pos')
- decay_log: float32 [128], replicated, may hold values from -0.7 to 0.7
- head_skip_weight: float32 [128], replicated, may hold values from 0.5 to 1.5
- row_counts: int32 [8, 16, 16], replicated, may hold values from 16 to 48, as said below
Outputs:
- layer_out: bfloat16 [16, 4096, 8192], P('stream', 'pos')
Inputs may be any that keep to these rules, and one draw needn't show every extreme that they name: For each p, every row and every column of row_counts[p] sums to 512; all rows and columns of row_counts[p] hold the same list of values in some order, and the list splits into pairs whose sum is twice the list's mean; each row_counts[p] holds the value 48.
All inputs are finite; a program needn't handle non-finite values.
Results may differ from a plain program's by a relative error of at most 0.0037.
Values may be sent and summed in bfloat16 or wider, within the bound.
No kernel may reach another device: no remote copies, remote signals or barrier semaphores. Data moves between devices by JAX's collectives and lax.ppermute only.
A program may use at most 256 MiB of HBM per device.

v0:
```python
import jax
import jax.numpy as jnp
from jax import lax
from jax.experimental import pallas as pl
from jax.experimental.pallas import tpu as pltpu
from jax.sharding import PartitionSpec as P

GROUP = 8
TILE = 128
CHUNK_GROUPS = (4, 4, 4, 4)
EXTRA = 16


def lane_pick(low, high):
    lane_low = lax.broadcasted_iota(jnp.int32, (1, 128), 1) < 64
    return jnp.where(lane_low, low, high)


def carried_kernel(bt_ref, facg_ref, decay_ref, tok_ref, out_ref):
    pairs = out_ref.shape[0]
    state_size = bt_ref.shape[0]
    for q in range(pairs):
        x = tok_ref[:, 128 * q : 128 * (q + 1)].astype(jnp.float32)
        factor = lane_pick(facg_ref[0, :, 2 * q : 2 * q + 1], facg_ref[0, :, 2 * q + 1 : 2 * q + 2])
        scaled = (factor * x).astype(jnp.bfloat16)
        out_ref[q, 0:state_size, :] = jnp.dot(
            bt_ref[...], scaled, preferred_element_type=jnp.float32
        ).astype(out_ref.dtype)
        rows = lax.broadcasted_iota(jnp.int32, (EXTRA, 128), 0)
        decay = decay_ref[:, 128 * q : 128 * (q + 1)]
        high = decay.astype(out_ref.dtype)
        low = (decay - high.astype(jnp.float32)).astype(out_ref.dtype)
        extra = jnp.where(rows == 0, high, jnp.where(rows == 1, low, jnp.zeros_like(high)))
        out_ref[q, state_size : state_size + EXTRA, :] = extra


def local_kernel(scores_ref, cumg_ref, cumt_ref, stept_ref, tok_ref, skip_ref, out_ref):
    length = scores_ref.shape[0]
    heads = cumt_ref.shape[0]
    for q in range(heads // 2):
        x = tok_ref[:, 128 * q : 128 * (q + 1)]
        skip = skip_ref[:, 128 * q : 128 * (q + 1)]
        for i in range(length // TILE):
            r0 = i * TILE
            width = (i + 1) * TILE
            rows = lax.broadcasted_iota(jnp.int32, (TILE, width), 0) + r0
            cols = lax.broadcasted_iota(jnp.int32, (TILE, width), 1)
            causal = rows >= cols
            sc = scores_ref[r0 : r0 + TILE, 0:width]
            parts = []
            for j in range(2):
                h = 2 * q + j
                ct = cumg_ref[0, r0 : r0 + TILE, h : h + 1]
                cs = cumt_ref[h : h + 1, 0:width]
                st = stept_ref[h : h + 1, 0:width]
                w = jnp.where(causal, jnp.exp(ct - cs), 0.0)
                wb = ((sc * w) * st).astype(jnp.bfloat16)
                parts.append(jnp.dot(wb, x[0:width], preferred_element_type=jnp.float32))
            xt = x[r0 : r0 + TILE].astype(jnp.float32)
            total = lane_pick(parts[0], parts[1]) + skip * xt
            out_ref[r0 : r0 + TILE, 128 * q : 128 * (q + 1)] = total


def combine_kernel(place_ref, *refs):
    if len(refs) == 6:
        refs = refs[1:]
    part_ref, gath_ref, cumg_ref, c_ref, out_ref = refs
    here = place_ref[0]
    peers = gath_ref.shape[0]
    pairs = gath_ref.shape[1]
    state_size = c_ref.shape[1]
    for q in range(pairs):
        run = jnp.ones((1, 128), jnp.float32)
        state = jnp.zeros((state_size, 128), jnp.float32)
        for k in range(peers - 1, -1, -1):
            if k + 1 < peers:
                pair = gath_ref[k + 1, q, state_size : state_size + 2, :].astype(jnp.float32)
                later = pair[0:1] + pair[1:2]
                run = jnp.where(k + 1 < here, run * later, 1.0)
            weight = jnp.where(k < here, run, 0.0)
            state = state + weight * gath_ref[k, q, 0:state_size, :].astype(jnp.float32)
        readable = state.astype(jnp.bfloat16)
        inherited = jnp.dot(c_ref[...], readable, preferred_element_type=jnp.float32)
        decay = lane_pick(
            jnp.exp(cumg_ref[0, :, 2 * q : 2 * q + 1]), jnp.exp(cumg_ref[0, :, 2 * q + 1 : 2 * q + 2])
        )
        total = part_ref[:, 128 * q : 128 * (q + 1)] + decay * inherited
        out_ref[:, 128 * q : 128 * (q + 1)] = total.astype(out_ref.dtype)


def arbitrary():
    return pltpu.CompilerParams(dimension_semantics=("arbitrary",))


def carried_call(bt, fac_grouped, decay_lanes, tokens, first):
    length, width = tokens.shape
    groups = width // (GROUP * 64)
    state_size = bt.shape[0]
    return pl.pallas_call(
        carried_kernel,
        grid=(groups,),
        in_specs=[
            pl.BlockSpec(bt.shape, lambda g: (0, 0)),
            pl.BlockSpec((1, length, GROUP), lambda g: (g + first, 0, 0)),
            pl.BlockSpec((1, GROUP * 64), lambda g: (0, g + first)),
            pl.BlockSpec((length, GROUP * 64), lambda g: (0, g)),
        ],
        out_specs=pl.BlockSpec((GROUP // 2, state_size + EXTRA, 128), lambda g: (g, 0, 0)),
        out_shape=jax.ShapeDtypeStruct((width // 128, state_size + EXTRA, 128), jnp.bfloat16),
        compiler_params=arbitrary(),
    )(bt, fac_grouped, decay_lanes, tokens)


def local_call(scores, cum_grouped, cum_t, step_t, tokens, skip_lanes, first):
    length, width = tokens.shape
    groups = width // (GROUP * 64)
    return pl.pallas_call(
        local_kernel,
        grid=(groups,),
        in_specs=[
            pl.BlockSpec((length, length), lambda g: (0, 0)),
            pl.BlockSpec((1, length, GROUP), lambda g: (g + first, 0, 0)),
            pl.BlockSpec((GROUP, length), lambda g: (g + first, 0)),
            pl.BlockSpec((GROUP, length), lambda g: (g + first, 0)),
            pl.BlockSpec((length, GROUP * 64), lambda g: (0, g)),
            pl.BlockSpec((1, GROUP * 64), lambda g: (0, g + first)),
        ],
        out_specs=pl.BlockSpec((length, GROUP * 64), lambda g: (0, g)),
        out_shape=jax.ShapeDtypeStruct((length, width), jnp.float32),
        compiler_params=arbitrary(),
    )(scores, cum_grouped, cum_t, step_t, tokens, skip_lanes)


def combine_call(buffer, place, partial, gathered, cum_grouped, readout, first, total_width):
    length, width = partial.shape
    groups = width // (GROUP * 64)
    state_rows = gathered.shape[2]
    in_specs = [
        pl.BlockSpec((length, GROUP * 64), lambda g: (0, g)),
        pl.BlockSpec((gathered.shape[0], GROUP // 2, state_rows, 128), lambda g: (0, g, 0, 0)),
        pl.BlockSpec((1, length, GROUP), lambda g: (g + first, 0, 0)),
        pl.BlockSpec(readout.shape, lambda g: (0, 0)),
    ]
    operands = [partial, gathered, cum_grouped, readout]
    aliases = {}
    if buffer is not None:
        in_specs = [pl.BlockSpec(memory_space=pl.ANY)] + in_specs
        operands = [buffer] + operands
        aliases = {1: 0}
    return pl.pallas_call(
        combine_kernel,
        grid=(groups,),
        in_specs=[pl.BlockSpec(memory_space=pltpu.SMEM)] + in_specs,
        out_specs=pl.BlockSpec((length, GROUP * 64), lambda g: (0, g + first)),
        out_shape=jax.ShapeDtypeStruct((length, total_width), jnp.bfloat16),
        input_output_aliases=aliases,
        compiler_params=arbitrary(),
    )(place, *operands)


def send_rows(rows, pick_rows, stream_count, capacity):
    width = rows.shape[1]
    return jnp.take(rows, pick_rows, axis=0, mode="clip").reshape(stream_count, capacity, width)


def receive_rows(arrived, flat_rows):
    width = arrived.shape[2]
    return jnp.take(arrived.reshape(-1, width), flat_rows, axis=0, mode="clip")


def deliver(rows, pick_rows, flat_rows, stream_count, capacity):
    send = send_rows(rows, pick_rows, stream_count, capacity)
    arrived = lax.all_to_all(send, "stream", split_axis=0, concat_axis=0, tiled=True)
    return receive_rows(arrived, flat_rows)


def on_device(tokens_in, proj_in, step_raw, decay_log, head_skip_weight, row_counts):
    stream_count = lax.axis_size("stream")
    stream_index = lax.axis_index("stream")
    place_index = lax.axis_index("pos")
    tokens = tokens_in[0]
    local_rows, inner = tokens.shape
    head_count = step_raw.shape[2]
    head_size = inner // head_count
    state_size = proj_in.shape[2] // 2
    capacity = 3 * local_rows // (2 * stream_count)

    place_counts = lax.dynamic_index_in_dim(row_counts, place_index, 0, keepdims=False)
    send_counts = lax.dynamic_index_in_dim(place_counts, stream_index, 0, keepdims=False)
    recv_counts = lax.dynamic_index_in_dim(place_counts, stream_index, 1, keepdims=False)
    send_start = jnp.cumsum(send_counts) - send_counts
    slot_range = jnp.arange(capacity, dtype=jnp.int32)
    pick_rows = jnp.clip(send_start[:, None] + slot_range[None, :], 0, local_rows - 1).reshape(-1)
    recv_end = jnp.cumsum(recv_counts)
    recv_start = recv_end - recv_counts
    positions = jnp.arange(local_rows, dtype=jnp.int32)
    source = jnp.sum((recv_end[:, None] <= positions[None, :]).astype(jnp.int32), axis=0)
    source = jnp.clip(source, 0, stream_count - 1)
    source_start = jnp.take(recv_start, source)
    flat_rows = source * capacity + positions - source_start

    small = jnp.concatenate([proj_in[0], step_raw[0]], axis=1)
    ordered_small = deliver(small, pick_rows, flat_rows, stream_count, capacity)
    ordered_proj = ordered_small[:, : 2 * state_size]
    ordered_steps = ordered_small[:, 2 * state_size :]

    inputs = ordered_proj[:, :state_size]
    readout = ordered_proj[:, state_size:]
    decay_rates = -jnp.exp(decay_log)
    steps = jax.nn.softplus(ordered_steps.astype(jnp.float32))
    cum = jnp.cumsum(steps * decay_rates[None, :], axis=0)
    ending = cum[-1]
    factor = jnp.exp(ending[None, :] - cum) * steps
    groups = head_count // GROUP

    def grouped(a):
        return a.reshape(local_rows, groups, GROUP).transpose(1, 0, 2)

    cum_grouped = grouped(cum)
    fac_grouped = grouped(factor)
    cum_t = cum.T
    step_t = steps.T
    decay_lanes = jnp.repeat(jnp.exp(ending), head_size).reshape(1, -1)
    skip_lanes = jnp.repeat(head_skip_weight, head_size).reshape(1, -1)
    scores = jnp.dot(readout, inputs.T, preferred_element_type=jnp.float32)
    bt = inputs.T
    place = place_index.astype(jnp.int32).reshape(1)

    sizes = CHUNK_GROUPS
    firsts = [sum(sizes[:c]) for c in range(len(sizes))]
    group_width = GROUP * head_size
    sends = [
        send_rows(tokens[:, f * group_width : (f + n) * group_width], pick_rows, stream_count, capacity)
        for f, n in zip(firsts, sizes)
    ]
    partials = []
    gathers = []
    result = None
    done = 0
    for c in range(len(sizes)):
        arrived = lax.all_to_all(sends[c], "stream", split_axis=0, concat_axis=0, tiled=True)
        tied = {"arrived": arrived}
        if c + 1 < len(sizes):
            tied["send"] = sends[c + 1]
        if c >= 1:
            tied["partial"] = partials[c - 1]
        if c >= 2:
            result = combine_call(
                result, place, partials[done], gathers[done], cum_grouped, readout,
                firsts[done], inner,
            )
            done += 1
            tied["result"] = result
        tied = lax.optimization_barrier(tied)
        arrived = tied["arrived"]
        if c + 1 < len(sizes):
            sends[c + 1] = tied["send"]
        if c >= 2:
            result = tied["result"]
        chunk_tokens = receive_rows(arrived, flat_rows)
        carried = carried_call(bt, fac_grouped, decay_lanes, chunk_tokens, firsts[c])
        gathers.append(lax.all_gather(carried, "pos"))
        partials.append(
            local_call(scores, cum_grouped, cum_t, step_t, chunk_tokens, skip_lanes, firsts[c])
        )
    while done < len(sizes):
        result = combine_call(
            result, place, partials[done], gathers[done], cum_grouped, readout, firsts[done], inner
        )
        done += 1
    return result[None]


def solution(mesh):
    in_specs = (
        P("stream", "pos", None),
        P("stream", "pos", None),
        P("stream", "pos", None),
        P(),
        P(),
        P(),
    )
    out_specs = P("stream", "pos", None)
    return jax.shard_map(
        on_device, mesh=mesh, in_specs=in_specs, out_specs=out_specs, check_vma=False
    )
```

profile of v0, /device:TPU:1, one launch (start us, length us, event | category | flops | bytes accessed | tf_op | source)
XLA Modules:
  0.0 341.8 jit_solution(15550050063814848964)
XLA Ops:
  6.5 0.7 fusion.6
  7.5 0.7 bitcast_subtract_fusion
  8.3 1.1 pad_maximum_fusion
  9.4 3.2 gather_fusion.2
  12.6 8.4 %all-to-all-start.2 = ((bf16[16,48,384]{2,1,0:T(8,128)(2,1)}), bf16[16,48,384]{2,1,0:T(8,128)(2,1)S(1)}, u32[]{:S(2)}, u32[]{:S(2)}) async-start(bf16[16,48,384]{2,1,0:T(8,128)(2,1)} %bitcast.8), calls=%async_computation.2 | async-start | bytes 1179648 | tf_op jit(solution)/shard_map/all_to_all | solution.py:173
  21.1 0.9 dynamic-slice_reduce_fusion
  22.1 5.8 %fusion.12 = (bf16[512,2048]{1,0:T(8,128)(2,1)S(1)}, bf16[512,2048]{1,0:T(8,128)(2,1)}, bf16[512,2048]{1,0:T(8,128)(2,1)}, bf16[512,2048]{1,0:T(8,128)(2,1)}) fusion(bf16[512,8192]{1,0:T(8,128)(2,1)} %bitcast.100), kind=kLoop, calls=%fused_computation.61 | loop fusion | bytes 16777216 | tf_op jit(solution)/shard_map/slice | solution.py:233
  27.9 8.9 %gather_fusion.1 = bf16[768,2048]{1,0:T(8,128)(2,1)} fusion(bf16[512,2048]{1,0:T(8,128)(2,1)} %get-tuple-element.36, s32[1024]{0:T(1024)S(1)} %pad_clamp_fusion.1), kind=kCustom, calls=%fused_computation.1 | custom fusion | bytes 6294528 | tf_op jit(solution)/shard_map/jit(_take)/gather | solution.py:163
  36.8 8.9 %gather_fusion = bf16[768,2048]{1,0:T(8,128)(2,1)} fusion(bf16[512,2048]{1,0:T(8,128)(2,1)} %get-tuple-element.37, s32[1024]{0:T(1024)S(1)} %pad_clamp_fusion.1), kind=kCustom, calls=%fused_computation | custom fusion | bytes 6294528 | tf_op jit(solution)/shard_map/jit(_take)/gather | solution.py:163
  45.9 6.7 %all-to-all-start = ((bf16[16,48,2048]{2,1,0:T(8,128)(2,1)}), bf16[16,48,2048]{2,1,0:T(8,128)(2,1)}, u32[]{:S(2)}, u32[]{:S(2)}) async-start(bf16[16,48,2048]{2,1,0:T(8,128)(2,1)} %bitcast.91), calls=%async_computation | async-start | bytes 6291456 | tf_op jit(solution)/shard_map/all_to_all | solution.py:241
  53.2 0.7 fusion.14
  53.9 4.2 %compare_select_fusion.2 = (s32[512,1]{0,1:T(1,128)S(1)}, s32[512,1]{0,1:T(1,128)S(1)}) fusion(s32[]{:T(128)} %bitcast.21, s32[]{:T(128)} %bitcast.22, s32[]{:T(128)} %bitcast.23, s32[]{:T(128)} %bitcast.24, s32[]{:T(128)} %bitcast.25, s32[]{:T(128)} %bitcast.27, s32[]{:T(128)} %bitcast.26, s32[512,1]{0,1:T(1,128)S(1)} %bitcast.115), kind=kLoop, calls=%fused_computation.37 | loop fusion | flops 7680 | bytes 6172 | tf_op jit(solution)/shard_map/jit(_take)/gather | solution.py:199
  58.2 5.6 %select_select_fusion = s32[512]{0:T(512)S(1)} fusion(pred[512]{0:T(512)(128)(4,1)S(1)} %get-tuple-element.30, pred[512]{0:T(512)(128)(4,1)S(1)} %get-tuple-element.29, pred[512]{0:T(512)(128)(4,1)S(1)} %get-tuple-element.31, pred[512]{0:T(512)(128)(4,1)S(1)} %get-tuple-element.28, pred[512]{0:T(512)(128)(4,1)S(1)} %get-tuple-element.27, ...), kind=kLoop, calls=%fused_computation.50 | loop fusion | flops 4608 | bytes 8740 | tf_op jit(solution)/shard_map/jit(_take)/gather | solution.py:199
  63.8 1.9 gather_fusion.3
  65.7 0.8 fusion.13
  67.7 0.9 multiply_bitcast_fusion
  68.5 2.6 copy.39
  71.2 0.7 reshape_reshape.7.decay_ref
  71.9 1.7 copy.40
  73.6 24.1 %all-to-all-done = bf16[16,48,2048]{2,1,0:T(8,128)(2,1)} async-done(((bf16[16,48,2048]{2,1,0:T(8,128)(2,1)}), bf16[16,48,2048]{2,1,0:T(8,128)(2,1)}, u32[]{:S(2)}, u32[]{:S(2)}) %all-to-all-start) | async-done | bytes 3145760 | tf_op jit(solution)/shard_map/all_to_all | solution.py:241
  97.7 7.5 %gather_fusion.4 = bf16[512,2048]{1,0:T(8,128)(2,1)} fusion(bf16[768,2048]{1,0:T(8,128)(2,1)} %bitcast.37, s32[1024]{0:T(1024)S(1)} %pad_clamp_fusion), kind=kCustom, calls=%fused_computation.4 | custom fusion | bytes 4196352 | tf_op jit(solution)/shard_map/jit(_take)/gather | solution.py:168
  105.2 5.6 %shard_map.66 = bf16[16,144,128]{2,1,0:T(8,128)(2,1)} custom-call(bf16[128,512]{1,0:T(8,128)(2,1)} %bitcast.105, f32[16,512,8]{2,1,0:T(8,128)} %bitcast.85, f32[1,8192]{1,0:T(1,128)} %reshape_reshape.7.decay_ref, bf16[512,2048]{1,0:T(8,128)(2,1)} %gather_fusion.4), custom_call_target="tpu_custom_call" | custom-call | tf_op jit(solution)/shard_map/pallas_call | solution.py:99
  110.9 4.5 %all-to-all-start.1 = ((bf16[16,48,2048]{2,1,0:T(8,128)(2,1)}), bf16[16,48,2048]{2,1,0:T(8,128)(2,1)}, u32[]{:S(2)}, u32[]{:S(2)}) async-start(bf16[16,48,2048]{2,1,0:T(8,128)(2,1)} %bitcast.90), calls=%async_computation.1 | async-start | bytes 6291456 | tf_op jit(solution)/shard_map/all_to_all | solution.py:241
  115.7 0.7 reshape_reshape.6.skip_ref
  116.4 9.0 %gather_fusion.5 = bf16[768,2048]{1,0:T(8,128)(2,1)} fusion(bf16[512,2048]{1,0:T(8,128)(2,1)} %get-tuple-element.35, s32[1024]{0:T(1024)S(1)} %pad_clamp_fusion.1), kind=kCustom, calls=%fused_computation.5 | custom fusion | bytes 6294528 | tf_op jit(solution)/shard_map/jit(_take)/gather | solution.py:163
  125.4 2.7 copy.38
  128.1 1.3 fusion.7.scores_ref
  129.4 9.4 %shard_map.64.refs_0_ = f32[512,2048]{1,0:T(8,128)} custom-call(f32[512,512]{1,0:T(8,128)} %fusion.7.scores_ref, f32[16,512,8]{2,1,0:T(8,128)} %bitcast.77, f32[128,512]{1,0:T(8,128)} %bitcast.96, f32[128,512]{1,0:T(8,128)} %get-tuple-element.45.stept_ref, bf16[512,2048]{1,0:T(8,128)(2,1)} %gather_fusion.4, f32[1,8192]{1,0:T(1,128)} %reshape_reshape.6.skip_ref), custom_call_target="tpu_custom_call" | custom-call | tf_op jit(solution)/shard_map/pallas_call | solution.py:117
  138.8 18.5 %all-to-all-done.1 = bf16[16,48,2048]{2,1,0:T(8,128)(2,1)} async-done(((bf16[16,48,2048]{2,1,0:T(8,128)(2,1)}), bf16[16,48,2048]{2,1,0:T(8,128)(2,1)}, u32[]{:S(2)}, u32[]{:S(2)}) %all-to-all-start.1) | async-done | bytes 3145760 | tf_op jit(solution)/shard_map/all_to_all | solution.py:241
  157.3 7.5 %gather_fusion.6 = bf16[512,2048]{1,0:T(8,128)(2,1)} fusion(bf16[768,2048]{1,0:T(8,128)(2,1)} %bitcast.39, s32[1024]{0:T(1024)S(1)} %pad_clamp_fusion), kind=kCustom, calls=%fused_computation.6 | custom fusion | bytes 4196352 | tf_op jit(solution)/shard_map/jit(_take)/gather | solution.py:168
  164.8 5.6 %shard_map.69 = bf16[16,144,128]{2,1,0:T(8,128)(2,1)} custom-call(bf16[128,512]{1,0:T(8,128)(2,1)} %bitcast.106, f32[16,512,8]{2,1,0:T(8,128)} %bitcast.86, f32[1,8192]{1,0:T(1,128)} %reshape_reshape.7.decay_ref, bf16[512,2048]{1,0:T(8,128)(2,1)} %gather_fusion.6), custom_call_target="tpu_custom_call" | custom-call | tf_op jit(solution)/shard_map/pallas_call | solution.py:99
  170.5 5.6 %all-to-all-start.3 = ((bf16[16,48,2048]{2,1,0:T(8,128)(2,1)}), bf16[16,48,2048]{2,1,0:T(8,128)(2,1)}, u32[]{:S(2)}, u32[]{:S(2)}) async-start(bf16[16,48,2048]{2,1,0:T(8,128)(2,1)} %bitcast.93), calls=%async_computation.3 | async-start | bytes 6291456 | tf_op jit(solution)/shard_map/all_to_all | solution.py:241
  176.4 4.2 %gather_fusion.7 = bf16[768,2048]{1,0:T(8,128)(2,1)} fusion(bf16[512,2048]{1,0:T(8,128)(2,1)S(1)} %get-tuple-element.34, s32[1024]{0:T(1024)S(1)} %pad_clamp_fusion.1), kind=kCustom, calls=%fused_computation.7 | custom fusion | bytes 6294528 | tf_op jit(solution)/shard_map/jit(_take)/gather | solution.py:163
  180.6 9.7 %shard_map.65.refs_1_ = f32[512,2048]{1,0:T(8,128)} custom-call(f32[512,512]{1,0:T(8,128)} %fusion.7.scores_ref, f32[16,512,8]{2,1,0:T(8,128)} %bitcast.78, f32[128,512]{1,0:T(8,128)} %bitcast.97, f32[128,512]{1,0:T(8,128)} %get-tuple-element.45.stept_ref, bf16[512,2048]{1,0:T(8,128)(2,1)} %gather_fusion.6, f32[1,8192]{1,0:T(1,128)} %reshape_reshape.6.skip_ref), custom_call_target="tpu_custom_call" | custom-call | tf_op jit(solution)/shard_map/pallas_call | solution.py:117
  190.3 6.9 %shard_map.67.refs_0_ = bf16[512,8192]{1,0:T(8,128)(2,1)} custom-call(s32[1]{0:T(128)} %bitcast.place_ref, f32[512,2048]{1,0:T(8,128)} %shard_map.64.refs_0_, bf16[8,16,144,128]{3,2,1,0:T(8,128)(2,1)} %bitcast.101, f32[16,512,8]{2,1,0:T(8,128)} %bitcast.79, bf16[512,128]{1,0:T(8,128)(2,1)} %get-tuple-element.38.refs_3_.refs_4_), custom_call_target="tpu_custom_call" | custom-call | tf_op jit(solution)/shard_map/pallas_call | solution.py:150
  197.1 20.9 %all-to-all-done.3 = bf16[16,48,2048]{2,1,0:T(8,128)(2,1)} async-done(((bf16[16,48,2048]{2,1,0:T(8,128)(2,1)}), bf16[16,48,2048]{2,1,0:T(8,128)(2,1)}, u32[]{:S(2)}, u32[]{:S(2)}) %all-to-all-start.3) | async-done | bytes 3145760 | tf_op jit(solution)/shard_map/all_to_all | solution.py:241
  218.1 7.6 %gather_fusion.8 = bf16[512,2048]{1,0:T(8,128)(2,1)} fusion(bf16[768,2048]{1,0:T(8,128)(2,1)} %bitcast.45, s32[1024]{0:T(1024)S(1)} %pad_clamp_fusion), kind=kCustom, calls=%fused_computation.8 | custom fusion | bytes 4196352 | tf_op jit(solution)/shard_map/jit(_take)/gather | solution.py:168
  225.6 5.6 %shard_map.71 = bf16[16,144,128]{2,1,0:T(8,128)(2,1)} custom-call(bf16[128,512]{1,0:T(8,128)(2,1)} %bitcast.107, f32[16,512,8]{2,1,0:T(8,128)} %bitcast.87, f32[1,8192]{1,0:T(1,128)} %reshape_reshape.7.decay_ref, bf16[512,2048]{1,0:T(8,128)(2,1)} %gather_fusion.8), custom_call_target="tpu_custom_call" | custom-call | tf_op jit(solution)/shard_map/pallas_call | solution.py:99
  231.3 5.7 %all-to-all-start.4 = ((bf16[16,48,2048]{2,1,0:T(8,128)(2,1)}), bf16[16,48,2048]{2,1,0:T(8,128)(2,1)}, u32[]{:S(2)}, u32[]{:S(2)}) async-start(bf16[16,48,2048]{2,1,0:T(8,128)(2,1)} %bitcast.92), calls=%async_computation.4 | async-start | bytes 6291456 | tf_op jit(solution)/shard_map/all_to_all | solution.py:241
  237.3 9.4 %shard_map.68.refs_1_ = f32[512,2048]{1,0:T(8,128)} custom-call(f32[512,512]{1,0:T(8,128)} %fusion.7.scores_ref, f32[16,512,8]{2,1,0:T(8,128)} %bitcast.80, f32[128,512]{1,0:T(8,128)} %bitcast.98, f32[128,512]{1,0:T(8,128)} %get-tuple-element.45.stept_ref, bf16[512,2048]{1,0:T(8,128)(2,1)} %gather_fusion.8, f32[1,8192]{1,0:T(1,128)} %reshape_reshape.6.skip_ref), custom_call_target="tpu_custom_call" | custom-call | tf_op jit(solution)/shard_map/pallas_call | solution.py:117
  246.7 6.8 %shard_map.70.refs_0_ = bf16[512,8192]{1,0:T(8,128)(2,1)} custom-call(s32[1]{0:T(128)} %bitcast.place_ref, bf16[512,8192]{1,0:T(8,128)(2,1)} %shard_map.67.refs_0_, f32[512,2048]{1,0:T(8,128)} %shard_map.65.refs_1_, bf16[8,16,144,128]{3,2,1,0:T(8,128)(2,1)} %bitcast.102, f32[16,512,8]{2,1,0:T(8,128)} %bitcast.81, ...), custom_call_target="tpu_custom_call", output_to_operand_aliasing={{}: (1, {})} | custom-call | tf_op jit(solution)/shard_map/pallas_call | solution.py:150
  253.4 25.6 %all-to-all-done.4 = bf16[16,48,2048]{2,1,0:T(8,128)(2,1)} async-done(((bf16[16,48,2048]{2,1,0:T(8,128)(2,1)}), bf16[16,48,2048]{2,1,0:T(8,128)(2,1)}, u32[]{:S(2)}, u32[]{:S(2)}) %all-to-all-start.4) | async-done | bytes 3145760 | tf_op jit(solution)/shard_map/all_to_all | solution.py:241
  279.0 7.6 %gather_fusion.9 = bf16[512,2048]{1,0:T(8,128)(2,1)} fusion(bf16[768,2048]{1,0:T(8,128)(2,1)} %bitcast.48, s32[1024]{0:T(1024)S(1)} %pad_clamp_fusion), kind=kCustom, calls=%fused_computation.9 | custom fusion | bytes 4196352 | tf_op jit(solution)/shard_map/jit(_take)/gather | solution.py:168
  286.6 5.6 %shard_map.74 = bf16[16,144,128]{2,1,0:T(8,128)(2,1)} custom-call(bf16[128,512]{1,0:T(8,128)(2,1)} %bitcast.108, f32[16,512,8]{2,1,0:T(8,128)} %bitcast.88, f32[1,8192]{1,0:T(1,128)} %reshape_reshape.7.decay_ref, bf16[512,2048]{1,0:T(8,128)(2,1)} %gather_fusion.9), custom_call_target="tpu_custom_call" | custom-call | tf_op jit(solution)/shard_map/pallas_call | solution.py:99
  292.2 9.4 %shard_map.73.refs_1_ = f32[512,2048]{1,0:T(8,128)} custom-call(f32[512,512]{1,0:T(8,128)} %fusion.7.scores_ref, f32[16,512,8]{2,1,0:T(8,128)} %bitcast.82, f32[128,512]{1,0:T(8,128)} %bitcast.99, f32[128,512]{1,0:T(8,128)} %get-tuple-element.45.stept_ref, bf16[512,2048]{1,0:T(8,128)(2,1)} %gather_fusion.9, f32[1,8192]{1,0:T(1,128)} %reshape_reshape.6.skip_ref), custom_call_target="tpu_custom_call" | custom-call | tf_op jit(solution)/shard_map/pallas_call | solution.py:117
  301.7 7.0 %shard_map.72.refs_0_ = bf16[512,8192]{1,0:T(8,128)(2,1)} custom-call(s32[1]{0:T(128)} %bitcast.place_ref, bf16[512,8192]{1,0:T(8,128)(2,1)} %shard_map.70.refs_0_, f32[512,2048]{1,0:T(8,128)} %shard_map.68.refs_1_, bf16[8,16,144,128]{3,2,1,0:T(8,128)(2,1)} %bitcast.103, f32[16,512,8]{2,1,0:T(8,128)} %bitcast.83, ...), custom_call_target="tpu_custom_call", output_to_operand_aliasing={{}: (1, {})} | custom-call | tf_op jit(solution)/shard_map/pallas_call | solution.py:150
  308.7 19.6 %all-gather.15.cloned.1.call-done = bf16[128,144,128]{2,1,0:T(8,128)(2,1)} async-done(((bf16[16,144,128]{2,1,0:T(8,128)(2,1)}), bf16[128,144,128]{2,1,0:T(8,128)(2,1)}) %all-gather.15.cloned.1.call-update) | async-done | bytes 4718608 | tf_op jit(solution)/shard_map/all_gather | solution.py:262
  328.3 6.7 %shard_map.75 = bf16[512,8192]{1,0:T(8,128)(2,1)} custom-call(s32[1]{0:T(128)} %bitcast.place_ref, bf16[512,8192]{1,0:T(8,128)(2,1)} %shard_map.72.refs_0_, f32[512,2048]{1,0:T(8,128)} %shard_map.73.refs_1_, bf16[8,16,144,128]{3,2,1,0:T(8,128)(2,1)} %bitcast.104, f32[16,512,8]{2,1,0:T(8,128)} %bitcast.84, ...), custom_call_target="tpu_custom_call", output_to_operand_aliasing={{}: (1, {})} | custom-call | tf_op jit(solution)/shard_map/pallas_call | solution.py:150
  (49 shorter events, 3.4 us)
Async XLA Ops:
  12.6 33.2 %all-to-all-start.2 = ((bf16[16,48,384]{2,1,0:T(8,128)(2,1)}), bf16[16,48,384]{2,1,0:T(8,128)(2,1)S(1)}, u32[]{:S(2)}, u32[]{:S(2)}) async-start(bf16[16,48,384]{2,1,0:T(8,128)(2,1)} %bitcast.8), calls=%async_computation.2 | async-start | bytes 1179648 | tf_op jit(solution)/shard_map/all_to_all | solution.py:173
  45.9 17.9 %copy-start.2 = (f32[128]{0:T(128)S(1)}, f32[128]{0:T(128)}, u32[]{:S(2)}) copy-start(f32[128]{0:T(128)} %param.9) | copy-start | bytes 1540
  45.9 51.8 %all-to-all-start = ((bf16[16,48,2048]{2,1,0:T(8,128)(2,1)}), bf16[16,48,2048]{2,1,0:T(8,128)(2,1)}, u32[]{:S(2)}, u32[]{:S(2)}) async-start(bf16[16,48,2048]{2,1,0:T(8,128)(2,1)} %bitcast.91), calls=%async_computation | async-start | bytes 6291456 | tf_op jit(solution)/shard_map/all_to_all | solution.py:241
  52.6 137.7 %all-gather.9.cloned.1.call-start = ((), (), s32[]{:S(2)}) async-start(), calls=%async_computation.5 | async-start | bytes 5308416 | tf_op jit(solution)/shard_map/all_gather | solution.py:262
  67.5 57.9 %copy-start = (f32[16,8,4,128]{3,1,2,0:T(8,128)}, f32[16,8,4,128]{3,1,2,0:T(8,128)S(1)}, u32[]{:S(2)}) copy-start(f32[16,8,4,128]{3,1,2,0:T(8,128)S(1)} %copy.50) | copy-start | bytes 786436
  110.9 4.7 %copy-start.1 = (f32[128]{0:T(128)S(1)}, f32[128]{0:T(128)}, u32[]{:S(2)}) copy-start(f32[128]{0:T(128)} %param.10) | copy-start | bytes 1540
  110.9 46.4 %all-to-all-start.1 = ((bf16[16,48,2048]{2,1,0:T(8,128)(2,1)}), bf16[16,48,2048]{2,1,0:T(8,128)(2,1)}, u32[]{:S(2)}, u32[]{:S(2)}) async-start(bf16[16,48,2048]{2,1,0:T(8,128)(2,1)} %bitcast.90), calls=%async_computation.1 | async-start | bytes 6291456 | tf_op jit(solution)/shard_map/all_to_all | solution.py:241
  115.4 131.3 %all-gather.11.cloned.1.call-start = ((), (), s32[]{:S(2)}) async-start(), calls=%async_computation.6 | async-start | bytes 5308416 | tf_op jit(solution)/shard_map/all_gather | solution.py:262
  170.5 47.6 %all-to-all-start.3 = ((bf16[16,48,2048]{2,1,0:T(8,128)(2,1)}), bf16[16,48,2048]{2,1,0:T(8,128)(2,1)}, u32[]{:S(2)}, u32[]{:S(2)}) async-start(bf16[16,48,2048]{2,1,0:T(8,128)(2,1)} %bitcast.93), calls=%async_computation.3 | async-start | bytes 6291456 | tf_op jit(solution)/shard_map/all_to_all | solution.py:241
  176.1 125.6 %all-gather.13.cloned.1.call-start = ((), (), s32[]{:S(2)}) async-start(), calls=%async_computation.7 | async-start | bytes 5308416 | tf_op jit(solution)/shard_map/all_gather | solution.py:262
  231.3 47.7 %all-to-all-start.4 = ((bf16[16,48,2048]{2,1,0:T(8,128)(2,1)}), bf16[16,48,2048]{2,1,0:T(8,128)(2,1)}, u32[]{:S(2)}, u32[]{:S(2)}) async-start(bf16[16,48,2048]{2,1,0:T(8,128)(2,1)} %bitcast.92), calls=%async_computation.4 | async-start | bytes 6291456 | tf_op jit(solution)/shard_map/all_to_all | solution.py:241
  237.0 91.3 %all-gather.15.cloned.1.call-start = ((), (), s32[]{:S(2)}) async-start(), calls=%async_computation.8 | async-start | bytes 5308416 | tf_op jit(solution)/shard_map/all_gather | solution.py:262
Sparse Core Ops, SparseCore 0:
  111.0 34.2 all-gather.8
  170.6 35.9 all-gather.10
  231.4 36.0 all-gather.12
  292.3 35.9 all-gather.14
where the time goes:
time: 348 us; the launch traced here: 342 us
  waiting for transfers between devices  109 us (31%)
  Pallas kernels  87.8 us (25%)
  local copies, waits for them, and re-layouts  84.7 us (24%)
  starting transfers between devices  32.2 us (9%)
  between operations  13.6 us (4%)
  other arithmetic  13.3 us (4%)
    all_to_all x4, waiting for transfers between devices, on_device(): lax.all_to_all(sends[c], 'stream', split_axis=0, concat_axis=0, tiled=True)  89.1 us
    pallas_call x4, Pallas kernels, local_call(): pl.pallas_call(local_kernel, grid=(groups,), in_specs=[pl.BlockSpec((leng...  38 us
    gather x5, local copies, waits for them, and re-layouts, send_rows(): jnp.take(rows, pick_rows, axis=0, mode='clip')  34.3 us
    gather x5, local copies, waits for them, and re-layouts, receive_rows(): return jnp.take(arrived.reshape(-1, width), flat_rows, axis=0, mode='clip')  32.1 us
    pallas_call x4, Pallas kernels, combine_call(): pl.pallas_call(combine_kernel, grid=(groups,), in_specs=[pl.BlockSpec(mem...  27.3 us
    pallas_call x4, Pallas kernels, carried_call(): pl.pallas_call(carried_kernel, grid=(groups,), in_specs=[pl.BlockSpec(bt....  22.5 us
    all_to_all x4, starting transfers between devices, on_device(): lax.all_to_all(sends[c], 'stream', split_axis=0, concat_axis=0, tiled=True)  22.5 us
    all_gather x4, waiting for transfers between devices, on_device(): gathers.append(lax.all_gather(carried, 'pos'))  19.6 us
  transfers between devices with their start and end apart: 9, of which 5 were waited for; matrix products, arithmetic and copies ran while one was open for 25% of the time, Pallas kernels for 22%

commit v1 on v0

--- a/solution.py
+++ b/solution.py
@@ -16,13 +16,11 @@
     return jnp.where(lane_low, low, high)
 
 
-def carried_kernel(bt_ref, facg_ref, decay_ref, tok_ref, out_ref):
+def carried_kernel(bt_ref, decay_ref, scaled_ref, out_ref):
     pairs = out_ref.shape[0]
     state_size = bt_ref.shape[0]
     for q in range(pairs):
-        x = tok_ref[:, 128 * q : 128 * (q + 1)].astype(jnp.float32)
-        factor = lane_pick(facg_ref[0, :, 2 * q : 2 * q + 1], facg_ref[0, :, 2 * q + 1 : 2 * q + 2])
-        scaled = (factor * x).astype(jnp.bfloat16)
+        scaled = scaled_ref[:, 128 * q : 128 * (q + 1)]
         out_ref[q, 0:state_size, :] = jnp.dot(
             bt_ref[...], scaled, preferred_element_type=jnp.float32
         ).astype(out_ref.dtype)
@@ -92,8 +90,8 @@
     return pltpu.CompilerParams(dimension_semantics=("arbitrary",))
 
 
-def carried_call(bt, fac_grouped, decay_lanes, tokens, first):
-    length, width = tokens.shape
+def carried_call(bt, decay_lanes, scaled, first):
+    length, width = scaled.shape
     groups = width // (GROUP * 64)
     state_size = bt.shape[0]
     return pl.pallas_call(
@@ -101,14 +99,13 @@
         grid=(groups,),
         in_specs=[
             pl.BlockSpec(bt.shape, lambda g: (0, 0)),
-            pl.BlockSpec((1, length, GROUP), lambda g: (g + first, 0, 0)),
             pl.BlockSpec((1, GROUP * 64), lambda g: (0, g + first)),
             pl.BlockSpec((length, GROUP * 64), lambda g: (0, g)),
         ],
         out_specs=pl.BlockSpec((GROUP // 2, state_size + EXTRA, 128), lambda g: (g, 0, 0)),
         out_shape=jax.ShapeDtypeStruct((width // 128, state_size + EXTRA, 128), jnp.bfloat16),
         compiler_params=arbitrary(),
-    )(bt, fac_grouped, decay_lanes, tokens)
+    )(bt, decay_lanes, scaled)
 
 
 def local_call(scores, cum_grouped, cum_t, step_t, tokens, skip_lanes, first):
@@ -160,12 +157,16 @@
 
 def send_rows(rows, pick_rows, stream_count, capacity):
     width = rows.shape[1]
-    return jnp.take(rows, pick_rows, axis=0, mode="clip").reshape(stream_count, capacity, width)
+    picked = jnp.take(rows, pick_rows, axis=0, mode="clip", indices_are_sorted=True)
+    return picked.reshape(stream_count, capacity, width)
 
 
 def receive_rows(arrived, flat_rows):
     width = arrived.shape[2]
-    return jnp.take(arrived.reshape(-1, width), flat_rows, axis=0, mode="clip")
+    return jnp.take(
+        arrived.reshape(-1, width), flat_rows, axis=0, mode="clip",
+        unique_indices=True, indices_are_sorted=True,
+    )
 
 
 def deliver(rows, pick_rows, flat_rows, stream_count, capacity):
@@ -217,7 +218,6 @@
         return a.reshape(local_rows, groups, GROUP).transpose(1, 0, 2)
 
     cum_grouped = grouped(cum)
-    fac_grouped = grouped(factor)
     cum_t = cum.T
     step_t = steps.T
     decay_lanes = jnp.repeat(jnp.exp(ending), head_size).reshape(1, -1)
@@ -258,7 +258,13 @@
         if c >= 2:
             result = tied["result"]
         chunk_tokens = receive_rows(arrived, flat_rows)
-        carried = carried_call(bt, fac_grouped, decay_lanes, chunk_tokens, firsts[c])
+        heads_here = sizes[c] * GROUP
+        chunk_factor = factor[:, firsts[c] * GROUP : firsts[c] * GROUP + heads_here]
+        scaled = (
+            chunk_factor[:, :, None] * chunk_tokens.reshape(local_rows, heads_here, head_size)
+        ).astype(jnp.bfloat16)
+        scaled = scaled.reshape(local_rows, heads_here * head_size)
+        carried = carried_call(bt, decay_lanes, scaled, firsts[c])
         gathers.append(lax.all_gather(carried, "pos"))
         partials.append(
             local_call(scores, cum_grouped, cum_t, step_t, chunk_tokens, skip_lanes, firsts[c])

time: 348 us -> 361 us (1.037)
  waiting for transfers between devices: 109 us -> 79.4 us
  local copies, waits for them, and re-layouts: 84.7 us -> 113 us
  other arithmetic: 13.3 us -> 33.4 us
  Pallas kernels: 87.8 us -> 81.2 us
    mul x0 -> x8, local copies, waits for them, and re-layouts: none -> 32 us  [on_device(): chunk_factor[:, :, None]]
    all_to_all x4, waiting for transfers between devices: 89.1 us -> 59.7 us  [on_device(): lax.all_to_all(sends[c], 'stream', split_axis=0, concat_axis=0, tiled=True)]
    convert_element_type x0 -> x4, other arithmetic: none -> 19.8 us  [on_device(): scaled = (chunk_factor[:, :, None] * chunk_tokens.reshape(local_rows, hea...]
    pallas_call x4, Pallas kernels: 22.5 us -> 16.1 us  [carried_call(): pl.pallas_call(carried_kernel, grid=(groups,), in_specs=[pl.BlockSpec(bt....]
  transfers between devices with their start and end apart: 9 -> 9, of which waited for: 5 -> 5; matrix products, arithmetic and copies ran while one was open for 25% -> 36% of each run, Pallas kernels for 22% -> 20%
where the time goes in v1:
time: 361 us; the launch traced here: 354 us
  local copies, waits for them, and re-layouts  113 us (31%)
  Pallas kernels  81.2 us (22%)
  waiting for transfers between devices  79.4 us (22%)
  other arithmetic  33.4 us (9%)
  starting transfers between devices  32.2 us (9%)
  between operations  13.7 us (4%)
    all_to_all x4, waiting for transfers between devices, on_device(): lax.all_to_all(sends[c], 'stream', split_axis=0, concat_axis=0, tiled=True)  59.7 us
    pallas_call x4, Pallas kernels, local_call(): pl.pallas_call(local_kernel, grid=(groups,), in_specs=[pl.BlockSpec((leng...  37.7 us
    gather x5, local copies, waits for them, and re-layouts, send_rows(): jnp.take(rows, pick_rows, axis=0, mode='clip', indices_are_sorted=True)  34.4 us
    mul x8, local copies, waits for them, and re-layouts, on_device(): chunk_factor[:, :, None]  32 us
    gather x5, local copies, waits for them, and re-layouts, receive_rows(): jnp.take(arrived.reshape(-1, width), flat_rows, axis=0, mode='clip', uniq...  30.4 us
    pallas_call x4, Pallas kernels, combine_call(): pl.pallas_call(combine_kernel, grid=(groups,), in_specs=[pl.BlockSpec(mem...  27.3 us
    all_to_all x4, starting transfers between devices, on_device(): lax.all_to_all(sends[c], 'stream', split_axis=0, concat_axis=0, tiled=True)  22.5 us
    convert_element_type x4, other arithmetic, on_device(): scaled = (chunk_factor[:, :, None] * chunk_tokens.reshape(local_rows, hea...  19.8 us
  transfers between devices with their start and end apart: 9, of which 5 were waited for; matrix products, arithmetic and copies ran while one was open for 36% of the time, Pallas kernels for 20%

profile of v1, /device:TPU:1, one launch (start us, length us, event | category | flops | bytes accessed | tf_op | source)
XLA Modules:
  0.0 353.7 jit_solution(3851556134501748067)
XLA Ops:
  9.4 3.2 gather_fusion.2
  12.6 8.4 %all-to-all-start.2 = ((bf16[16,48,384]{2,1,0:T(8,128)(2,1)}), bf16[16,48,384]{2,1,0:T(8,128)(2,1)S(1)}, u32[]{:S(2)}, u32[]{:S(2)}) async-start(bf16[16,48,384]{2,1,0:T(8,128)(2,1)} %bitcast.8), calls=%async_computation.2 | async-start | bytes 1179648 | tf_op jit(solution)/shard_map/all_to_all | solution.py:174
  21.1 5.7 %fusion.12 = (bf16[512,2048]{1,0:T(8,128)(2,1)S(1)}, bf16[512,2048]{1,0:T(8,128)(2,1)}, bf16[512,2048]{1,0:T(8,128)(2,1)}, bf16[512,2048]{1,0:T(8,128)(2,1)}) fusion(bf16[512,8192]{1,0:T(8,128)(2,1)} %bitcast.101), kind=kLoop, calls=%fused_computation.65 | loop fusion | bytes 16777216 | tf_op jit(solution)/shard_map/slice | solution.py:233
  27.9 9.0 %gather_fusion.1 = bf16[768,2048]{1,0:T(8,128)(2,1)} fusion(bf16[512,2048]{1,0:T(8,128)(2,1)} %get-tuple-element.36, s32[1024]{0:T(1024)S(1)} %pad_clamp_fusion.1), kind=kCustom, calls=%fused_computation.1 | custom fusion | bytes 6294528 | tf_op jit(solution)/shard_map/jit(_take)/gather | solution.py:160
  36.8 9.0 %gather_fusion = bf16[768,2048]{1,0:T(8,128)(2,1)} fusion(bf16[512,2048]{1,0:T(8,128)(2,1)} %get-tuple-element.37, s32[1024]{0:T(1024)S(1)} %pad_clamp_fusion.1), kind=kCustom, calls=%fused_computation | custom fusion | bytes 6294528 | tf_op jit(solution)/shard_map/jit(_take)/gather | solution.py:160
  45.9 6.7 %all-to-all-start = ((bf16[16,48,2048]{2,1,0:T(8,128)(2,1)}), bf16[16,48,2048]{2,1,0:T(8,128)(2,1)}, u32[]{:S(2)}, u32[]{:S(2)}) async-start(bf16[16,48,2048]{2,1,0:T(8,128)(2,1)} %bitcast.92), calls=%async_computation | async-start | bytes 6291456 | tf_op jit(solution)/shard_map/all_to_all | solution.py:241
  53.9 4.4 %compare_select_fusion.2 = (s32[512,1]{0,1:T(1,128)S(1)}, s32[512,1]{0,1:T(1,128)S(1)}) fusion(s32[]{:T(128)} %bitcast.21, s32[]{:T(128)} %bitcast.22, s32[]{:T(128)} %bitcast.23, s32[]{:T(128)} %bitcast.24, s32[]{:T(128)} %bitcast.25, s32[]{:T(128)} %bitcast.27, s32[]{:T(128)} %bitcast.26, s32[512,1]{0,1:T(1,128)S(1)} %bitcast.116), kind=kLoop, calls=%fused_computation.41 | loop fusion | flops 7680 | bytes 6172 | tf_op jit(solution)/shard_map/jit(_take)/gather | solution.py:200
  58.4 5.6 %select_select_fusion = s32[512]{0:T(512)S(1)} fusion(pred[512]{0:T(512)(128)(4,1)S(1)} %get-tuple-element.30, pred[512]{0:T(512)(128)(4,1)S(1)} %get-tuple-element.29, pred[512]{0:T(512)(128)(4,1)S(1)} %get-tuple-element.31, pred[512]{0:T(512)(128)(4,1)S(1)} %get-tuple-element.28, pred[512]{0:T(512)(128)(4,1)S(1)} %get-tuple-element.27, ...), kind=kLoop, calls=%fused_computation.54 | loop fusion | flops 4608 | bytes 8740 | tf_op jit(solution)/shard_map/jit(_take)/gather | solution.py:200
  64.0 1.9 gather_fusion.3
  71.3 2.5 mul.73
  73.8 5.4 %copy.49 = f32[512,2048]{1,0:T(8,128)} copy(f32[512,2048]{0,1:T(8,128)} %bitcast.87) | data formatting | bytes 8388608 | tf_op jit(solution)/shard_map/mul | solution.py:264
  79.2 18.6 %all-to-all-done = bf16[16,48,2048]{2,1,0:T(8,128)(2,1)} async-done(((bf16[16,48,2048]{2,1,0:T(8,128)(2,1)}), bf16[16,48,2048]{2,1,0:T(8,128)(2,1)}, u32[]{:S(2)}, u32[]{:S(2)}) %all-to-all-start) | async-done | bytes 3145760 | tf_op jit(solution)/shard_map/all_to_all | solution.py:241
  97.8 7.5 %gather_fusion.4 = bf16[512,2048]{1,0:T(8,128)(2,1)} fusion(bf16[768,2048]{1,0:T(8,128)(2,1)} %bitcast.37, s32[1024]{0:T(1024)S(1)} %pad_clamp_fusion), kind=kCustom, calls=%fused_computation.4 | custom fusion | bytes 4196352 | tf_op jit(solution)/shard_map/jit(_take)/gather | solution.py:166
  105.3 4.9 %multiply_convert_fusion.3.scaled_ref = bf16[512,2048]{1,0:T(8,128)(2,1)} fusion(f32[512,2048]{1,0:T(8,128)} %copy.49, bf16[512,2048]{1,0:T(8,128)(2,1)} %gather_fusion.4), kind=kLoop, calls=%fused_computation.13 | loop fusion | flops 3145728 | bytes 8388608 | tf_op jit(solution)/shard_map/convert_element_type | solution.py:265
  110.2 4.0 %shard_map.66 = bf16[16,144,128]{2,1,0:T(8,128)(2,1)} custom-call(bf16[128,512]{1,0:T(8,128)(2,1)} %bitcast.106, f32[1,8192]{1,0:T(1,128)} %reshape_reshape.7.decay_ref, bf16[512,2048]{1,0:T(8,128)(2,1)} %multiply_convert_fusion.3.scaled_ref), custom_call_target="tpu_custom_call" | custom-call | tf_op jit(solution)/shard_map/pallas_call | solution.py:97
  114.2 4.5 %all-to-all-start.1 = ((bf16[16,48,2048]{2,1,0:T(8,128)(2,1)}), bf16[16,48,2048]{2,1,0:T(8,128)(2,1)}, u32[]{:S(2)}, u32[]{:S(2)}) async-start(bf16[16,48,2048]{2,1,0:T(8,128)(2,1)} %bitcast.91), calls=%async_computation.1 | async-start | bytes 6291456 | tf_op jit(solution)/shard_map/all_to_all | solution.py:241
  119.8 9.0 %gather_fusion.5 = bf16[768,2048]{1,0:T(8,128)(2,1)} fusion(bf16[512,2048]{1,0:T(8,128)(2,1)} %get-tuple-element.35, s32[1024]{0:T(1024)S(1)} %pad_clamp_fusion.1), kind=kCustom, calls=%fused_computation.5 | custom fusion | bytes 6294528 | tf_op jit(solution)/shard_map/jit(_take)/gather | solution.py:160
  128.7 2.7 copy.48
  131.5 2.5 mul.76
  134.0 5.6 %copy.50 = f32[512,2048]{1,0:T(8,128)} copy(f32[512,2048]{0,1:T(8,128)} %bitcast.88) | data formatting | bytes 8388608 | tf_op jit(solution)/shard_map/mul | solution.py:264
  140.8 9.4 %shard_map.64.refs_0_ = f32[512,2048]{1,0:T(8,128)} custom-call(f32[512,512]{1,0:T(8,128)} %fusion.7.scores_ref, f32[16,512,8]{2,1,0:T(8,128)} %bitcast.78, f32[128,512]{1,0:T(8,128)} %bitcast.97, f32[128,512]{1,0:T(8,128)} %get-tuple-element.49.stept_ref, bf16[512,2048]{1,0:T(8,128)(2,1)} %gather_fusion.4, f32[1,8192]{1,0:T(1,128)} %reshape_reshape.6.skip_ref), custom_call_target="tpu_custom_call" | custom-call | tf_op jit(solution)/shard_map/pallas_call | solution.py:114
  150.3 10.4 %all-to-all-done.1 = bf16[16,48,2048]{2,1,0:T(8,128)(2,1)} async-done(((bf16[16,48,2048]{2,1,0:T(8,128)(2,1)}), bf16[16,48,2048]{2,1,0:T(8,128)(2,1)}, u32[]{:S(2)}, u32[]{:S(2)}) %all-to-all-start.1) | async-done | bytes 3145760 | tf_op jit(solution)/shard_map/all_to_all | solution.py:241
  160.6 7.6 %gather_fusion.6 = bf16[512,2048]{1,0:T(8,128)(2,1)} fusion(bf16[768,2048]{1,0:T(8,128)(2,1)} %bitcast.39, s32[1024]{0:T(1024)S(1)} %pad_clamp_fusion), kind=kCustom, calls=%fused_computation.6 | custom fusion | bytes 4196352 | tf_op jit(solution)/shard_map/jit(_take)/gather | solution.py:166
  168.2 4.9 %multiply_convert_fusion.2.scaled_ref = bf16[512,2048]{1,0:T(8,128)(2,1)} fusion(f32[512,2048]{1,0:T(8,128)} %copy.50, bf16[512,2048]{1,0:T(8,128)(2,1)} %gather_fusion.6), kind=kLoop, calls=%fused_computation.12 | loop fusion | flops 3145728 | bytes 8388608 | tf_op jit(solution)/shard_map/convert_element_type | solution.py:265
  173.1 4.0 %shard_map.69 = bf16[16,144,128]{2,1,0:T(8,128)(2,1)} custom-call(bf16[128,512]{1,0:T(8,128)(2,1)} %bitcast.107, f32[1,8192]{1,0:T(1,128)} %reshape_reshape.7.decay_ref, bf16[512,2048]{1,0:T(8,128)(2,1)} %multiply_convert_fusion.2.scaled_ref), custom_call_target="tpu_custom_call" | custom-call | tf_op jit(solution)/shard_map/pallas_call | solution.py:97
  177.2 5.6 %all-to-all-start.3 = ((bf16[16,48,2048]{2,1,0:T(8,128)(2,1)}), bf16[16,48,2048]{2,1,0:T(8,128)(2,1)}, u32[]{:S(2)}, u32[]{:S(2)}) async-start(bf16[16,48,2048]{2,1,0:T(8,128)(2,1)} %bitcast.94), calls=%async_computation.3 | async-start | bytes 6291456 | tf_op jit(solution)/shard_map/all_to_all | solution.py:241
  183.1 4.2 %gather_fusion.7 = bf16[768,2048]{1,0:T(8,128)(2,1)} fusion(bf16[512,2048]{1,0:T(8,128)(2,1)S(1)} %get-tuple-element.34, s32[1024]{0:T(1024)S(1)} %pad_clamp_fusion.1), kind=kCustom, calls=%fused_computation.7 | custom fusion | bytes 6294528 | tf_op jit(solution)/shard_map/jit(_take)/gather | solution.py:160
  187.3 2.5 mul.79
  189.8 5.4 %copy.51 = f32[512,2048]{1,0:T(8,128)} copy(f32[512,2048]{0,1:T(8,128)} %bitcast.89) | data formatting | bytes 8388608 | tf_op jit(solution)/shard_map/mul | solution.py:264
  195.3 9.5 %shard_map.65.refs_1_ = f32[512,2048]{1,0:T(8,128)} custom-call(f32[512,512]{1,0:T(8,128)} %fusion.7.scores_ref, f32[16,512,8]{2,1,0:T(8,128)} %bitcast.79, f32[128,512]{1,0:T(8,128)} %bitcast.98, f32[128,512]{1,0:T(8,128)} %get-tuple-element.49.stept_ref, bf16[512,2048]{1,0:T(8,128)(2,1)} %gather_fusion.6, f32[1,8192]{1,0:T(1,128)} %reshape_reshape.6.skip_ref), custom_call_target="tpu_custom_call" | custom-call | tf_op jit(solution)/shard_map/pallas_call | solution.py:114
  204.8 6.8 %shard_map.67.refs_0_ = bf16[512,8192]{1,0:T(8,128)(2,1)} custom-call(s32[1]{0:T(128)} %bitcast.place_ref, f32[512,2048]{1,0:T(8,128)} %shard_map.64.refs_0_, bf16[8,16,144,128]{3,2,1,0:T(8,128)(2,1)} %bitcast.102, f32[16,512,8]{2,1,0:T(8,128)} %bitcast.80, bf16[512,128]{1,0:T(8,128)(2,1)} %get-tuple-element.38.refs_3_.refs_4_), custom_call_target="tpu_custom_call" | custom-call | tf_op jit(solution)/shard_map/pallas_call | solution.py:147
  211.6 13.2 %all-to-all-done.3 = bf16[16,48,2048]{2,1,0:T(8,128)(2,1)} async-done(((bf16[16,48,2048]{2,1,0:T(8,128)(2,1)}), bf16[16,48,2048]{2,1,0:T(8,128)(2,1)}, u32[]{:S(2)}, u32[]{:S(2)}) %all-to-all-start.3) | async-done | bytes 3145760 | tf_op jit(solution)/shard_map/all_to_all | solution.py:241
  224.8 6.7 %gather_fusion.8 = bf16[512,2048]{1,0:T(8,128)(2,1)S(1)} fusion(bf16[768,2048]{1,0:T(8,128)(2,1)} %bitcast.44, s32[1024]{0:T(1024)S(1)} %pad_clamp_fusion), kind=kCustom, calls=%fused_computation.8 | custom fusion | bytes 4196352 | tf_op jit(solution)/shard_map/jit(_take)/gather | solution.py:166
  231.5 5.0 %multiply_convert_fusion.1.scaled_ref = bf16[512,2048]{1,0:T(8,128)(2,1)} fusion(f32[512,2048]{1,0:T(8,128)} %copy.51, bf16[512,2048]{1,0:T(8,128)(2,1)S(1)} %gather_fusion.8), kind=kLoop, calls=%fused_computation.11 | loop fusion | flops 3145728 | bytes 8388608 | tf_op jit(solution)/shard_map/convert_element_type | solution.py:265
  236.5 4.0 %shard_map.71 = bf16[16,144,128]{2,1,0:T(8,128)(2,1)} custom-call(bf16[128,512]{1,0:T(8,128)(2,1)} %bitcast.108, f32[1,8192]{1,0:T(1,128)} %reshape_reshape.7.decay_ref, bf16[512,2048]{1,0:T(8,128)(2,1)} %multiply_convert_fusion.1.scaled_ref), custom_call_target="tpu_custom_call" | custom-call | tf_op jit(solution)/shard_map/pallas_call | solution.py:97
  240.6 5.7 %all-to-all-start.4 = ((bf16[16,48,2048]{2,1,0:T(8,128)(2,1)}), bf16[16,48,2048]{2,1,0:T(8,128)(2,1)}, u32[]{:S(2)}, u32[]{:S(2)}) async-start(bf16[16,48,2048]{2,1,0:T(8,128)(2,1)} %bitcast.93), calls=%async_computation.4 | async-start | bytes 6291456 | tf_op jit(solution)/shard_map/all_to_all | solution.py:241
  246.5 2.5 mul.82
  249.0 5.5 %copy.52 = f32[512,2048]{1,0:T(8,128)} copy(f32[512,2048]{0,1:T(8,128)} %bitcast.90) | data formatting | bytes 8388608 | tf_op jit(solution)/shard_map/mul | solution.py:264
  254.5 9.4 %shard_map.68.refs_1_ = f32[512,2048]{1,0:T(8,128)} custom-call(f32[512,512]{1,0:T(8,128)} %fusion.7.scores_ref, f32[16,512,8]{2,1,0:T(8,128)} %bitcast.81, f32[128,512]{1,0:T(8,128)} %bitcast.99, f32[128,512]{1,0:T(8,128)} %get-tuple-element.49.stept_ref, bf16[512,2048]{1,0:T(8,128)(2,1)} %copy-done, f32[1,8192]{1,0:T(1,128)} %reshape_reshape.6.skip_ref), custom_call_target="tpu_custom_call" | custom-call | tf_op jit(solution)/shard_map/pallas_call | solution.py:114
  264.0 6.8 %shard_map.70.refs_0_ = bf16[512,8192]{1,0:T(8,128)(2,1)} custom-call(s32[1]{0:T(128)} %bitcast.place_ref, bf16[512,8192]{1,0:T(8,128)(2,1)} %shard_map.67.refs_0_, f32[512,2048]{1,0:T(8,128)} %shard_map.65.refs_1_, bf16[8,16,144,128]{3,2,1,0:T(8,128)(2,1)} %bitcast.103, f32[16,512,8]{2,1,0:T(8,128)} %bitcast.82, ...), custom_call_target="tpu_custom_call", output_to_operand_aliasing={{}: (1, {})} | custom-call | tf_op jit(solution)/shard_map/pallas_call | solution.py:147
  270.8 17.5 %all-to-all-done.4 = bf16[16,48,2048]{2,1,0:T(8,128)(2,1)} async-done(((bf16[16,48,2048]{2,1,0:T(8,128)(2,1)}), bf16[16,48,2048]{2,1,0:T(8,128)(2,1)}, u32[]{:S(2)}, u32[]{:S(2)}) %all-to-all-start.4) | async-done | bytes 3145760 | tf_op jit(solution)/shard_map/all_to_all | solution.py:241
  288.3 6.7 %gather_fusion.9 = bf16[512,2048]{1,0:T(8,128)(2,1)S(1)} fusion(bf16[768,2048]{1,0:T(8,128)(2,1)} %bitcast.49, s32[1024]{0:T(1024)S(1)} %pad_clamp_fusion), kind=kCustom, calls=%fused_computation.9 | custom fusion | bytes 4196352 | tf_op jit(solution)/shard_map/jit(_take)/gather | solution.py:166
  295.0 5.0 %multiply_convert_fusion.scaled_ref = bf16[512,2048]{1,0:T(8,128)(2,1)} fusion(f32[512,2048]{1,0:T(8,128)} %copy.52, bf16[512,2048]{1,0:T(8,128)(2,1)S(1)} %gather_fusion.9), kind=kLoop, calls=%fused_computation.10 | loop fusion | flops 3145728 | bytes 8388608 | tf_op jit(solution)/shard_map/convert_element_type | solution.py:265
  300.0 4.0 %shard_map.74 = bf16[16,144,128]{2,1,0:T(8,128)(2,1)} custom-call(bf16[128,512]{1,0:T(8,128)(2,1)} %bitcast.109, f32[1,8192]{1,0:T(1,128)} %reshape_reshape.7.decay_ref, bf16[512,2048]{1,0:T(8,128)(2,1)} %multiply_convert_fusion.scaled_ref), custom_call_target="tpu_custom_call" | custom-call | tf_op jit(solution)/shard_map/pallas_call | solution.py:97
  304.1 9.4 %shard_map.73.refs_1_ = f32[512,2048]{1,0:T(8,128)} custom-call(f32[512,512]{1,0:T(8,128)} %fusion.7.scores_ref, f32[16,512,8]{2,1,0:T(8,128)} %bitcast.83, f32[128,512]{1,0:T(8,128)} %bitcast.100, f32[128,512]{1,0:T(8,128)} %get-tuple-element.49.stept_ref, bf16[512,2048]{1,0:T(8,128)(2,1)} %copy-done.1, f32[1,8192]{1,0:T(1,128)} %reshape_reshape.6.skip_ref), custom_call_target="tpu_custom_call" | custom-call | tf_op jit(solution)/shard_map/pallas_call | solution.py:114
  313.5 7.0 %shard_map.72.refs_0_ = bf16[512,8192]{1,0:T(8,128)(2,1)} custom-call(s32[1]{0:T(128)} %bitcast.place_ref, bf16[512,8192]{1,0:T(8,128)(2,1)} %shard_map.70.refs_0_, f32[512,2048]{1,0:T(8,128)} %shard_map.68.refs_1_, bf16[8,16,144,128]{3,2,1,0:T(8,128)(2,1)} %bitcast.104, f32[16,512,8]{2,1,0:T(8,128)} %bitcast.84, ...), custom_call_target="tpu_custom_call", output_to_operand_aliasing={{}: (1, {})} | custom-call | tf_op jit(solution)/shard_map/pallas_call | solution.py:147
  320.5 19.7 %all-gather.15.cloned.1.call-done = bf16[128,144,128]{2,1,0:T(8,128)(2,1)} async-done(((bf16[16,144,128]{2,1,0:T(8,128)(2,1)}), bf16[128,144,128]{2,1,0:T(8,128)(2,1)}) %all-gather.15.cloned.1.call-update) | async-done | bytes 4718608 | tf_op jit(solution)/shard_map/all_gather | solution.py:268
  340.2 6.7 %shard_map.75 = bf16[512,8192]{1,0:T(8,128)(2,1)} custom-call(s32[1]{0:T(128)} %bitcast.place_ref, bf16[512,8192]{1,0:T(8,128)(2,1)} %shard_map.72.refs_0_, f32[512,2048]{1,0:T(8,128)} %shard_map.73.refs_1_, bf16[8,16,144,128]{3,2,1,0:T(8,128)(2,1)} %bitcast.105, f32[16,512,8]{2,1,0:T(8,128)} %bitcast.85, ...), custom_call_target="tpu_custom_call", output_to_operand_aliasing={{}: (1, {})} | custom-call | tf_op jit(solution)/shard_map/pallas_call | solution.py:147
  (65 shorter events, 13.5 us)
Async XLA Ops:
  12.6 33.3 %all-to-all-start.2 = ((bf16[16,48,384]{2,1,0:T(8,128)(2,1)}), bf16[16,48,384]{2,1,0:T(8,128)(2,1)S(1)}, u32[]{:S(2)}, u32[]{:S(2)}) async-start(bf16[16,48,384]{2,1,0:T(8,128)(2,1)} %bitcast.8), calls=%async_computation.2 | async-start | bytes 1179648 | tf_op jit(solution)/shard_map/all_to_all | solution.py:174
  45.9 18.1 %copy-start.4 = (f32[128]{0:T(128)S(1)}, f32[128]{0:T(128)}, u32[]{:S(2)}) copy-start(f32[128]{0:T(128)} %param.9) | copy-start | bytes 1540
  45.9 51.8 %all-to-all-start = ((bf16[16,48,2048]{2,1,0:T(8,128)(2,1)}), bf16[16,48,2048]{2,1,0:T(8,128)(2,1)}, u32[]{:S(2)}, u32[]{:S(2)}) async-start(bf16[16,48,2048]{2,1,0:T(8,128)(2,1)} %bitcast.92), calls=%async_computation | async-start | bytes 6291456 | tf_op jit(solution)/shard_map/all_to_all | solution.py:241
  52.6 152.1 %all-gather.9.cloned.1.call-start = ((), (), s32[]{:S(2)}) async-start(), calls=%async_computation.5 | async-start | bytes 5308416 | tf_op jit(solution)/shard_map/all_gather | solution.py:268
  67.7 61.0 %copy-start.2 = (f32[16,8,4,128]{3,1,2,0:T(8,128)}, f32[16,8,4,128]{3,1,2,0:T(8,128)S(1)}, u32[]{:S(2)}) copy-start(f32[16,8,4,128]{3,1,2,0:T(8,128)S(1)} %copy.63) | copy-start | bytes 786436
  114.2 4.7 %copy-start.3 = (f32[128]{0:T(128)S(1)}, f32[128]{0:T(128)}, u32[]{:S(2)}) copy-start(f32[128]{0:T(128)} %param.10) | copy-start | bytes 1540
  114.2 46.4 %all-to-all-start.1 = ((bf16[16,48,2048]{2,1,0:T(8,128)(2,1)}), bf16[16,48,2048]{2,1,0:T(8,128)(2,1)}, u32[]{:S(2)}, u32[]{:S(2)}) async-start(bf16[16,48,2048]{2,1,0:T(8,128)(2,1)} %bitcast.91), calls=%async_computation.1 | async-start | bytes 6291456 | tf_op jit(solution)/shard_map/all_to_all | solution.py:241
  118.7 145.2 %all-gather.11.cloned.1.call-start = ((), (), s32[]{:S(2)}) async-start(), calls=%async_computation.6 | async-start | bytes 5308416 | tf_op jit(solution)/shard_map/all_gather | solution.py:268
  177.2 47.6 %all-to-all-start.3 = ((bf16[16,48,2048]{2,1,0:T(8,128)(2,1)}), bf16[16,48,2048]{2,1,0:T(8,128)(2,1)}, u32[]{:S(2)}, u32[]{:S(2)}) async-start(bf16[16,48,2048]{2,1,0:T(8,128)(2,1)} %bitcast.94), calls=%async_computation.3 | async-start | bytes 6291456 | tf_op jit(solution)/shard_map/all_to_all | solution.py:241
  182.8 130.7 %all-gather.13.cloned.1.call-start = ((), (), s32[]{:S(2)}) async-start(), calls=%async_computation.7 | async-start | bytes 5308416 | tf_op jit(solution)/shard_map/all_gather | solution.py:268
  231.5 5.0 %copy-start = (bf16[512,2048]{1,0:T(8,128)(2,1)}, bf16[512,2048]{1,0:T(8,128)(2,1)S(1)}, u32[]{:S(2)}) copy-start(bf16[512,2048]{1,0:T(8,128)(2,1)S(1)} %gather_fusion.8) | copy-start | bytes 6291460
  240.6 47.7 %all-to-all-start.4 = ((bf16[16,48,2048]{2,1,0:T(8,128)(2,1)}), bf16[16,48,2048]{2,1,0:T(8,128)(2,1)}, u32[]{:S(2)}, u32[]{:S(2)}) async-start(bf16[16,48,2048]{2,1,0:T(8,128)(2,1)} %bitcast.93), calls=%async_computation.4 | async-start | bytes 6291456 | tf_op jit(solution)/shard_map/all_to_all | solution.py:241
  246.2 93.9 %all-gather.15.cloned.1.call-start = ((), (), s32[]{:S(2)}) async-start(), calls=%async_computation.8 | async-start | bytes 5308416 | tf_op jit(solution)/shard_map/all_gather | solution.py:268
  295.0 5.0 %copy-start.1 = (bf16[512,2048]{1,0:T(8,128)(2,1)}, bf16[512,2048]{1,0:T(8,128)(2,1)S(1)}, u32[]{:S(2)}) copy-start(bf16[512,2048]{1,0:T(8,128)(2,1)S(1)} %gather_fusion.9) | copy-start | bytes 6291460
Sparse Core Ops, SparseCore 0:
  114.4 34.2 all-gather.8
  177.3 35.9 all-gather.10
  240.7 36.0 all-gather.12
  304.2 35.9 all-gather.14

commit v2 on v0

--- a/solution.py
+++ b/solution.py
@@ -158,9 +158,10 @@
     )(place, *operands)
 
 
-def send_rows(rows, pick_rows, stream_count, capacity):
-    width = rows.shape[1]
-    return jnp.take(rows, pick_rows, axis=0, mode="clip").reshape(stream_count, capacity, width)
+def send_rows(rows, windows, stream_count, capacity):
+    return jnp.stack(
+        [lax.dynamic_slice_in_dim(rows, windows[d], capacity, 0) for d in range(stream_count)]
+    )
 
 
 def receive_rows(arrived, flat_rows):
@@ -168,8 +169,8 @@
     return jnp.take(arrived.reshape(-1, width), flat_rows, axis=0, mode="clip")
 
 
-def deliver(rows, pick_rows, flat_rows, stream_count, capacity):
-    send = send_rows(rows, pick_rows, stream_count, capacity)
+def deliver(rows, windows, flat_rows, stream_count, capacity):
+    send = send_rows(rows, windows, stream_count, capacity)
     arrived = lax.all_to_all(send, "stream", split_axis=0, concat_axis=0, tiled=True)
     return receive_rows(arrived, flat_rows)
 
@@ -189,18 +190,20 @@
     send_counts = lax.dynamic_index_in_dim(place_counts, stream_index, 0, keepdims=False)
     recv_counts = lax.dynamic_index_in_dim(place_counts, stream_index, 1, keepdims=False)
     send_start = jnp.cumsum(send_counts) - send_counts
-    slot_range = jnp.arange(capacity, dtype=jnp.int32)
-    pick_rows = jnp.clip(send_start[:, None] + slot_range[None, :], 0, local_rows - 1).reshape(-1)
+    windows = jnp.minimum(send_start, local_rows - capacity)
     recv_end = jnp.cumsum(recv_counts)
     recv_start = recv_end - recv_counts
+    earlier_streams = jnp.arange(stream_count, dtype=jnp.int32) < stream_index
+    their_start = jnp.sum(jnp.where(earlier_streams[None, :], place_counts, 0), axis=1)
+    their_offset = their_start - jnp.minimum(their_start, local_rows - capacity)
     positions = jnp.arange(local_rows, dtype=jnp.int32)
     source = jnp.sum((recv_end[:, None] <= positions[None, :]).astype(jnp.int32), axis=0)
     source = jnp.clip(source, 0, stream_count - 1)
-    source_start = jnp.take(recv_start, source)
+    source_start = jnp.take(recv_start - their_offset, source)
     flat_rows = source * capacity + positions - source_start
 
     small = jnp.concatenate([proj_in[0], step_raw[0]], axis=1)
-    ordered_small = deliver(small, pick_rows, flat_rows, stream_count, capacity)
+    ordered_small = deliver(small, windows, flat_rows, stream_count, capacity)
     ordered_proj = ordered_small[:, : 2 * state_size]
     ordered_steps = ordered_small[:, 2 * state_size :]
 
@@ -230,7 +233,7 @@
     firsts = [sum(sizes[:c]) for c in range(len(sizes))]
     group_width = GROUP * head_size
     sends = [
-        send_rows(tokens[:, f * group_width : (f + n) * group_width], pick_rows, stream_count, capacity)
+        send_rows(tokens[:, f * group_width : (f + n) * group_width], windows, stream_count, capacity)
         for f, n in zip(firsts, sizes)
     ]
     partials = []

time: 348 us -> 385 us (1.11)
  between operations: 13.6 us -> 43.3 us
  waiting for transfers between devices: 109 us -> 81.3 us
  other arithmetic: 13.3 us -> 34.1 us
  local copies, waits for them, and re-layouts: 84.7 us -> 104 us
    unnamed x10 -> x88, local copies, waits for them, and re-layouts: 1.81 us -> 57.6 us
    gather x6 -> x1, local copies, waits for them, and re-layouts: 35 us -> 0.7 us  [on_device(): source_start = jnp.take(recv_start - their_offset, source)]
    all_to_all x4, waiting for transfers between devices: 89.1 us -> 61.6 us  [on_device(): lax.all_to_all(sends[c], 'stream', split_axis=0, concat_axis=0, tiled=True)]
    gather x5, local copies, waits for them, and re-layouts: 32.1 us -> 16.1 us  [receive_rows(): return jnp.take(arrived.reshape(-1, width), flat_rows, axis=0, mode='clip')]
    unnamed x0 -> x15, other arithmetic: none -> 14.7 us
    another operation x7 -> x11, local copies, waits for them, and re-layouts: 1.19 us -> 12.8 us  [the longest x4 6.63 us: send_rows(): jnp.stack([lax.dynamic_slice_in_dim(rows, windows[d], capacity, 0) for d...]
    gather x4 -> x3, other arithmetic: 9.84 us -> 10.2 us  [on_device(): source_start = jnp.take(recv_start - their_offset, source)]
  transfers between devices with their start and end apart: 9 -> 9, of which waited for: 5 -> 5; matrix products, arithmetic and copies ran while one was open for 25% -> 31% of each run, Pallas kernels for 22% -> 20%
where the time goes in v2:
time: 385 us; the launch traced here: 382 us
  local copies, waits for them, and re-layouts  104 us (27%)
  Pallas kernels  87.8 us (23%)
  waiting for transfers between devices  81.3 us (21%)
  between operations  43.3 us (11%)
  other arithmetic  34.1 us (9%)
  starting transfers between devices  28.8 us (7%)
    all_to_all x4, waiting for transfers between devices, on_device(): lax.all_to_all(sends[c], 'stream', split_axis=0, concat_axis=0, tiled=True)  61.6 us
    unnamed x88, local copies, waits for them, and re-layouts  57.6 us
    pallas_call x4, Pallas kernels, local_call(): pl.pallas_call(local_kernel, grid=(groups,), in_specs=[pl.BlockSpec((leng...  37.8 us
    pallas_call x4, Pallas kernels, combine_call(): pl.pallas_call(combine_kernel, grid=(groups,), in_specs=[pl.BlockSpec(mem...  27.3 us
    pallas_call x4, Pallas kernels, carried_call(): pl.pallas_call(carried_kernel, grid=(groups,), in_specs=[pl.BlockSpec(bt....  22.7 us
    all_to_all x4, starting transfers between devices, on_device(): lax.all_to_all(sends[c], 'stream', split_axis=0, concat_axis=0, tiled=True)  19.8 us
    all_gather x4, waiting for transfers between devices, on_device(): gathers.append(lax.all_gather(carried, 'pos'))  19.6 us
    gather x5, local copies, waits for them, and re-layouts, receive_rows(): return jnp.take(arrived.reshape(-1, width), flat_rows, axis=0, mode='clip')  16.1 us
  transfers between devices with their start and end apart: 9, of which 5 were waited for; matrix products, arithmetic and copies ran while one was open for 31% of the time, Pallas kernels for 20%

profile of v2, /device:TPU:1, one launch (start us, length us, event | category | flops | bytes accessed | tf_op | source)
XLA Modules:
  0.0 381.9 jit_solution(12198729056103847858)
XLA Ops:
  54.1 8.4 %all-to-all-start.2 = ((bf16[16,48,384]{2,1,0:T(8,128)(2,1)}), bf16[16,48,384]{2,1,0:T(8,128)(2,1)S(1)}, u32[]{:S(2)}, u32[]{:S(2)}) async-start(bf16[16,48,384]{2,1,0:T(8,128)(2,1)} %constant_dynamic-update-slice_fusion), calls=%async_computation.2 | async-start | bytes 1179648 | tf_op jit(solution)/shard_map/all_to_all | solution.py:174
  63.5 5.4 %fusion.35 = (bf16[512,2048]{1,0:T(8,128)(2,1)}, bf16[512,2048]{1,0:T(8,128)(2,1)}, bf16[512,2048]{1,0:T(8,128)(2,1)S(1)}, bf16[512,2048]{1,0:T(8,128)(2,1)S(1)}) fusion(bf16[512,8192]{1,0:T(8,128)(2,1)} %bitcast.311), kind=kLoop, calls=%fused_computation.190 | loop fusion | bytes 16777216 | tf_op jit(solution)/shard_map/slice | solution.py:236
  81.0 1.8 bitcast_dynamic-update-slice_fusion.34
  87.6 6.7 %all-to-all-start = ((bf16[16,48,2048]{2,1,0:T(8,128)(2,1)}), bf16[16,48,2048]{2,1,0:T(8,128)(2,1)S(1)}, u32[]{:S(2)}, u32[]{:S(2)}) async-start(bf16[16,48,2048]{2,1,0:T(8,128)(2,1)} %bitcast_dynamic-update-slice_fusion.48), calls=%async_computation | async-start | bytes 6291456 | tf_op jit(solution)/shard_map/all_to_all | solution.py:244
  94.4 4.3 %compare_select_fusion.2 = (s32[512,1]{0,1:T(1,128)S(1)}, s32[512,1]{0,1:T(1,128)S(1)}) fusion(s32[]{:T(128)} %bitcast.83, s32[]{:T(128)} %bitcast.84, s32[]{:T(128)} %bitcast.85, s32[]{:T(128)} %bitcast.86, s32[]{:T(128)} %bitcast.87, s32[]{:T(128)} %bitcast.89, s32[]{:T(128)} %bitcast.88, s32[512,1]{0,1:T(1,128)S(1)} %bitcast.324), kind=kLoop, calls=%fused_computation.164 | loop fusion | flops 7680 | bytes 6172 | tf_op jit(solution)/shard_map/jit(_take)/gather | solution.py:202
  98.7 5.8 %select_select_fusion = s32[512]{0:T(512)S(1)} fusion(pred[512]{0:T(512)(128)(4,1)S(1)} %get-tuple-element.30, pred[512]{0:T(512)(128)(4,1)S(1)} %get-tuple-element.29, pred[512]{0:T(512)(128)(4,1)S(1)} %get-tuple-element.31, pred[512]{0:T(512)(128)(4,1)S(1)} %get-tuple-element.28, pred[512]{0:T(512)(128)(4,1)S(1)} %get-tuple-element.27, ...), kind=kLoop, calls=%fused_computation.176 | loop fusion | flops 4608 | bytes 8740 | tf_op jit(solution)/shard_map/jit(_take)/gather | solution.py:202
  104.6 1.7 bitcast_dynamic-update-slice_fusion.33
  108.0 2.9 gather_fusion
  113.4 1.8 multiply_bitcast_fusion.1
  115.2 1.8 reshape.156
  117.0 1.8 copy.36
  120.6 1.7 broadcast_add_fusion
  122.3 1.8 copy.37
  125.3 2.0 multiply_bitcast_fusion
  127.3 3.6 copy.39
  133.9 5.5 %all-to-all-done = bf16[16,48,2048]{2,1,0:T(8,128)(2,1)S(1)} async-done(((bf16[16,48,2048]{2,1,0:T(8,128)(2,1)}), bf16[16,48,2048]{2,1,0:T(8,128)(2,1)S(1)}, u32[]{:S(2)}, u32[]{:S(2)}) %all-to-all-start) | async-done | bytes 3145760 | tf_op jit(solution)/shard_map/all_to_all | solution.py:244
  139.4 3.3 gather_fusion.1
  142.7 5.8 %shard_map.66 = bf16[16,144,128]{2,1,0:T(8,128)(2,1)} custom-call(bf16[128,512]{1,0:T(8,128)(2,1)} %bitcast.316, f32[16,512,8]{2,1,0:T(8,128)} %bitcast.268, f32[1,8192]{1,0:T(1,128)} %reshape_reshape.7.decay_ref, bf16[512,2048]{1,0:T(8,128)(2,1)} %gather_fusion.1), custom_call_target="tpu_custom_call" | custom-call | tf_op jit(solution)/shard_map/pallas_call | solution.py:99
  158.8 1.7 bitcast_dynamic-update-slice_fusion.15
  163.8 1.7 bitcast_dynamic-update-slice_fusion.12
  165.5 3.7 all-to-all-start.1
  169.5 1.7 bitcast_dynamic-update-slice_fusion.11
  176.2 1.7 bitcast_dynamic-update-slice_fusion.7
  179.5 1.7 bitcast_dynamic-update-slice_fusion.5
  181.2 1.7 bitcast_dynamic-update-slice_fusion.4
  184.6 1.9 bitcast_dynamic-update-slice_fusion.2
  189.8 2.6 copy.38
  192.3 2.3 fusion.30.scores_ref
  194.6 9.4 %shard_map.64.refs_0_ = f32[512,2048]{1,0:T(8,128)} custom-call(f32[512,512]{1,0:T(8,128)} %fusion.30.scores_ref, f32[16,512,8]{2,1,0:T(8,128)} %bitcast.256, f32[128,512]{1,0:T(8,128)} %bitcast.307, f32[128,512]{1,0:T(8,128)} %get-tuple-element.45.stept_ref, bf16[512,2048]{1,0:T(8,128)(2,1)} %gather_fusion.1, f32[1,8192]{1,0:T(1,128)} %reshape_reshape.6.skip_ref), custom_call_target="tpu_custom_call" | custom-call | tf_op jit(solution)/shard_map/pallas_call | solution.py:117
  204.0 7.5 %all-to-all-done.1 = bf16[16,48,2048]{2,1,0:T(8,128)(2,1)S(1)} async-done(((bf16[16,48,2048]{2,1,0:T(8,128)(2,1)}), bf16[16,48,2048]{2,1,0:T(8,128)(2,1)S(1)}, u32[]{:S(2)}, u32[]{:S(2)}) %all-to-all-start.1) | async-done | bytes 3145760 | tf_op jit(solution)/shard_map/all_to_all | solution.py:244
  211.4 3.3 gather_fusion.2
  214.7 5.6 %shard_map.69 = bf16[16,144,128]{2,1,0:T(8,128)(2,1)} custom-call(bf16[128,512]{1,0:T(8,128)(2,1)} %bitcast.317, f32[16,512,8]{2,1,0:T(8,128)} %bitcast.269, f32[1,8192]{1,0:T(1,128)} %reshape_reshape.7.decay_ref, bf16[512,2048]{1,0:T(8,128)(2,1)} %gather_fusion.2), custom_call_target="tpu_custom_call" | custom-call | tf_op jit(solution)/shard_map/pallas_call | solution.py:99
  220.4 5.4 %all-to-all-start.3 = ((bf16[16,48,2048]{2,1,0:T(8,128)(2,1)}), bf16[16,48,2048]{2,1,0:T(8,128)(2,1)S(1)}, u32[]{:S(2)}, u32[]{:S(2)}) async-start(bf16[16,48,2048]{2,1,0:T(8,128)(2,1)} %bitcast_dynamic-update-slice_fusion.16), calls=%async_computation.3 | async-start | bytes 6291456 | tf_op jit(solution)/shard_map/all_to_all | solution.py:244
  229.2 9.6 %shard_map.65.refs_1_ = f32[512,2048]{1,0:T(8,128)} custom-call(f32[512,512]{1,0:T(8,128)} %fusion.30.scores_ref, f32[16,512,8]{2,1,0:T(8,128)} %bitcast.257, f32[128,512]{1,0:T(8,128)} %bitcast.308, f32[128,512]{1,0:T(8,128)} %get-tuple-element.45.stept_ref, bf16[512,2048]{1,0:T(8,128)(2,1)} %gather_fusion.2, f32[1,8192]{1,0:T(1,128)} %reshape_reshape.6.skip_ref), custom_call_target="tpu_custom_call" | custom-call | tf_op jit(solution)/shard_map/pallas_call | solution.py:117
  238.8 6.8 %shard_map.67.refs_0_ = bf16[512,8192]{1,0:T(8,128)(2,1)} custom-call(s32[1]{0:T(128)} %bitcast.place_ref, f32[512,2048]{1,0:T(8,128)} %shard_map.64.refs_0_, bf16[8,16,144,128]{3,2,1,0:T(8,128)(2,1)} %bitcast.312, f32[16,512,8]{2,1,0:T(8,128)} %bitcast.258, bf16[512,128]{1,0:T(8,128)(2,1)} %get-tuple-element.38.refs_3_.refs_4_), custom_call_target="tpu_custom_call" | custom-call | tf_op jit(solution)/shard_map/pallas_call | solution.py:150
  245.6 23.9 %all-to-all-done.3 = bf16[16,48,2048]{2,1,0:T(8,128)(2,1)S(1)} async-done(((bf16[16,48,2048]{2,1,0:T(8,128)(2,1)}), bf16[16,48,2048]{2,1,0:T(8,128)(2,1)S(1)}, u32[]{:S(2)}, u32[]{:S(2)}) %all-to-all-start.3) | async-done | bytes 3145760 | tf_op jit(solution)/shard_map/all_to_all | solution.py:244
  269.6 3.3 gather_fusion.3
  272.8 5.6 %shard_map.71 = bf16[16,144,128]{2,1,0:T(8,128)(2,1)} custom-call(bf16[128,512]{1,0:T(8,128)(2,1)} %bitcast.318, f32[16,512,8]{2,1,0:T(8,128)} %bitcast.270, f32[1,8192]{1,0:T(1,128)} %reshape_reshape.7.decay_ref, bf16[512,2048]{1,0:T(8,128)(2,1)} %gather_fusion.3), custom_call_target="tpu_custom_call" | custom-call | tf_op jit(solution)/shard_map/pallas_call | solution.py:99
  278.5 4.1 %all-to-all-start.4 = ((bf16[16,48,2048]{2,1,0:T(8,128)(2,1)}), bf16[16,48,2048]{2,1,0:T(8,128)(2,1)S(1)}, u32[]{:S(2)}, u32[]{:S(2)}) async-start(bf16[16,48,2048]{2,1,0:T(8,128)(2,1)} %bitcast_dynamic-update-slice_fusion), calls=%async_computation.4 | async-start | bytes 6291456 | tf_op jit(solution)/shard_map/all_to_all | solution.py:244
  282.8 9.4 %shard_map.68.refs_1_ = f32[512,2048]{1,0:T(8,128)} custom-call(f32[512,512]{1,0:T(8,128)} %fusion.30.scores_ref, f32[16,512,8]{2,1,0:T(8,128)} %bitcast.259, f32[128,512]{1,0:T(8,128)} %bitcast.309, f32[128,512]{1,0:T(8,128)} %get-tuple-element.45.stept_ref, bf16[512,2048]{1,0:T(8,128)(2,1)} %gather_fusion.3, f32[1,8192]{1,0:T(1,128)} %reshape_reshape.6.skip_ref), custom_call_target="tpu_custom_call" | custom-call | tf_op jit(solution)/shard_map/pallas_call | solution.py:117
  292.2 6.8 %shard_map.70.refs_0_ = bf16[512,8192]{1,0:T(8,128)(2,1)} custom-call(s32[1]{0:T(128)} %bitcast.place_ref, bf16[512,8192]{1,0:T(8,128)(2,1)} %shard_map.67.refs_0_, f32[512,2048]{1,0:T(8,128)} %shard_map.65.refs_1_, bf16[8,16,144,128]{3,2,1,0:T(8,128)(2,1)} %bitcast.313, f32[16,512,8]{2,1,0:T(8,128)} %bitcast.260, ...), custom_call_target="tpu_custom_call", output_to_operand_aliasing={{}: (1, {})} | custom-call | tf_op jit(solution)/shard_map/pallas_call | solution.py:150
  299.0 24.7 %all-to-all-done.4 = bf16[16,48,2048]{2,1,0:T(8,128)(2,1)S(1)} async-done(((bf16[16,48,2048]{2,1,0:T(8,128)(2,1)}), bf16[16,48,2048]{2,1,0:T(8,128)(2,1)S(1)}, u32[]{:S(2)}, u32[]{:S(2)}) %all-to-all-start.4) | async-done | bytes 3145760 | tf_op jit(solution)/shard_map/all_to_all | solution.py:244
  323.7 3.3 gather_fusion.4
  327.0 5.6 %shard_map.74 = bf16[16,144,128]{2,1,0:T(8,128)(2,1)} custom-call(bf16[128,512]{1,0:T(8,128)(2,1)} %bitcast.319, f32[16,512,8]{2,1,0:T(8,128)} %bitcast.271, f32[1,8192]{1,0:T(1,128)} %reshape_reshape.7.decay_ref, bf16[512,2048]{1,0:T(8,128)(2,1)} %gather_fusion.4), custom_call_target="tpu_custom_call" | custom-call | tf_op jit(solution)/shard_map/pallas_call | solution.py:99
  332.7 9.4 %shard_map.73.refs_1_ = f32[512,2048]{1,0:T(8,128)} custom-call(f32[512,512]{1,0:T(8,128)} %fusion.30.scores_ref, f32[16,512,8]{2,1,0:T(8,128)} %bitcast.261, f32[128,512]{1,0:T(8,128)} %bitcast.310, f32[128,512]{1,0:T(8,128)} %get-tuple-element.45.stept_ref, bf16[512,2048]{1,0:T(8,128)(2,1)} %gather_fusion.4, f32[1,8192]{1,0:T(1,128)} %reshape_reshape.6.skip_ref), custom_call_target="tpu_custom_call" | custom-call | tf_op jit(solution)/shard_map/pallas_call | solution.py:117
  342.1 7.0 %shard_map.72.refs_0_ = bf16[512,8192]{1,0:T(8,128)(2,1)} custom-call(s32[1]{0:T(128)} %bitcast.place_ref, bf16[512,8192]{1,0:T(8,128)(2,1)} %shard_map.70.refs_0_, f32[512,2048]{1,0:T(8,128)} %shard_map.68.refs_1_, bf16[8,16,144,128]{3,2,1,0:T(8,128)(2,1)} %bitcast.314, f32[16,512,8]{2,1,0:T(8,128)} %bitcast.262, ...), custom_call_target="tpu_custom_call", output_to_operand_aliasing={{}: (1, {})} | custom-call | tf_op jit(solution)/shard_map/pallas_call | solution.py:150
  349.1 19.6 %all-gather.15.cloned.1.call-done = bf16[128,144,128]{2,1,0:T(8,128)(2,1)} async-done(((bf16[16,144,128]{2,1,0:T(8,128)(2,1)}), bf16[128,144,128]{2,1,0:T(8,128)(2,1)}) %all-gather.15.cloned.1.call-update) | async-done | bytes 4718608 | tf_op jit(solution)/shard_map/all_gather | solution.py:265
  368.7 6.7 %shard_map.75 = bf16[512,8192]{1,0:T(8,128)(2,1)} custom-call(s32[1]{0:T(128)} %bitcast.place_ref, bf16[512,8192]{1,0:T(8,128)(2,1)} %shard_map.72.refs_0_, f32[512,2048]{1,0:T(8,128)} %shard_map.73.refs_1_, bf16[8,16,144,128]{3,2,1,0:T(8,128)(2,1)} %bitcast.315, f32[16,512,8]{2,1,0:T(8,128)} %bitcast.263, ...), custom_call_target="tpu_custom_call", output_to_operand_aliasing={{}: (1, {})} | custom-call | tf_op jit(solution)/shard_map/pallas_call | solution.py:150
  (141 shorter events, 75.0 us)
Async XLA Ops:
  6.5 42.0 %copy-start = (bf16[1,512,256]{2,1,0:T(8,128)(2,1)S(1)}, bf16[1,512,256]{2,1,0:T(8,128)(2,1)}, u32[]{:S(2)}) copy-start(bf16[1,512,256]{2,1,0:T(8,128)(2,1)} %param.7) | copy-start | bytes 786436
  6.5 42.0 %copy-start.1 = (bf16[1,512,128]{2,1,0:T(8,128)(2,1)S(1)}, bf16[1,512,128]{2,1,0:T(8,128)(2,1)}, u32[]{:S(2)}) copy-start(bf16[1,512,128]{2,1,0:T(8,128)(2,1)} %param.8) | copy-start | bytes 393220
  54.1 32.7 %all-to-all-start.2 = ((bf16[16,48,384]{2,1,0:T(8,128)(2,1)}), bf16[16,48,384]{2,1,0:T(8,128)(2,1)S(1)}, u32[]{:S(2)}, u32[]{:S(2)}) async-start(bf16[16,48,384]{2,1,0:T(8,128)(2,1)} %constant_dynamic-update-slice_fusion), calls=%async_computation.2 | async-start | bytes 1179648 | tf_op jit(solution)/shard_map/all_to_all | solution.py:174
  68.8 3.8 copy-start.5
  68.8 12.1 %copy-start.4 = (bf16[512,2048]{1,0:T(8,128)(2,1)}, bf16[512,2048]{1,0:T(8,128)(2,1)S(1)}, u32[]{:S(2)}) copy-start(bf16[512,2048]{1,0:T(8,128)(2,1)S(1)} %get-tuple-element.36) | copy-start | bytes 6291460
  69.7 3.6 copy-start.7
  86.8 17.8 %copy-start.12 = (f32[128]{0:T(128)S(1)}, f32[128]{0:T(128)}, u32[]{:S(2)}) copy-start(f32[128]{0:T(128)} %param.9) | copy-start | bytes 1540
  86.8 0.8 copy-start.2
  87.6 51.7 %all-to-all-start = ((bf16[16,48,2048]{2,1,0:T(8,128)(2,1)}), bf16[16,48,2048]{2,1,0:T(8,128)(2,1)S(1)}, u32[]{:S(2)}, u32[]{:S(2)}) async-start(bf16[16,48,2048]{2,1,0:T(8,128)(2,1)} %bitcast_dynamic-update-slice_fusion.48), calls=%async_computation | async-start | bytes 6291456 | tf_op jit(solution)/shard_map/all_to_all | solution.py:244
  94.3 144.5 %all-gather.9.cloned.1.call-start = ((), (), s32[]{:S(2)}) async-start(), calls=%async_computation.5 | async-start | bytes 5308416 | tf_op jit(solution)/shard_map/all_gather | solution.py:265
  110.9 13.2 %copy-start.8 = (bf16[512,384]{1,0:T(8,128)(2,1)}, bf16[512,384]{1,0:T(8,128)(2,1)S(1)}, u32[]{:S(2)}) copy-start(bf16[512,384]{1,0:T(8,128)(2,1)S(1)} %gather_fusion) | copy-start | bytes 1179652
  119.8 0.7 copy-start.9
  124.1 9.0 %copy-start.10 = (bf16[512,128]{1,0:T(8,128)(2,1)S(1)}, bf16[512,128]{1,0:T(8,128)(2,1)}, u32[]{:S(2)}) copy-start(bf16[512,128]{1,0:T(8,128)(2,1)} %get-tuple-element.39) | copy-start | bytes 393220
  125.1 64.7 %copy-start.6 = (f32[16,8,4,128]{3,1,2,0:T(8,128)}, f32[16,8,4,128]{3,1,2,0:T(8,128)S(1)}, u32[]{:S(2)}) copy-start(f32[16,8,4,128]{3,1,2,0:T(8,128)S(1)} %copy.50) | copy-start | bytes 786436
  142.7 5.8 %copy-start.11 = (f32[128]{0:T(128)S(1)}, f32[128]{0:T(128)}, u32[]{:S(2)}) copy-start(f32[128]{0:T(128)} %param.10) | copy-start | bytes 1540
  142.7 6.6 %copy-start.3 = (bf16[512,2048]{1,0:T(8,128)(2,1)S(1)}, bf16[512,2048]{1,0:T(8,128)(2,1)}, u32[]{:S(2)}) copy-start(bf16[512,2048]{1,0:T(8,128)(2,1)} %get-tuple-element.35) | copy-start | bytes 6291460
  165.5 45.9 %all-to-all-start.1 = ((bf16[16,48,2048]{2,1,0:T(8,128)(2,1)}), bf16[16,48,2048]{2,1,0:T(8,128)(2,1)S(1)}, u32[]{:S(2)}, u32[]{:S(2)}) async-start(bf16[16,48,2048]{2,1,0:T(8,128)(2,1)} %bitcast_dynamic-update-slice_fusion.32), calls=%async_computation.1 | async-start | bytes 6291456 | tf_op jit(solution)/shard_map/all_to_all | solution.py:244
  169.3 123.0 %all-gather.11.cloned.1.call-start = ((), (), s32[]{:S(2)}) async-start(), calls=%async_computation.6 | async-start | bytes 5308416 | tf_op jit(solution)/shard_map/all_gather | solution.py:265
  220.4 49.2 %all-to-all-start.3 = ((bf16[16,48,2048]{2,1,0:T(8,128)(2,1)}), bf16[16,48,2048]{2,1,0:T(8,128)(2,1)S(1)}, u32[]{:S(2)}, u32[]{:S(2)}) async-start(bf16[16,48,2048]{2,1,0:T(8,128)(2,1)} %bitcast_dynamic-update-slice_fusion.16), calls=%async_computation.3 | async-start | bytes 6291456 | tf_op jit(solution)/shard_map/all_to_all | solution.py:244
  225.8 116.3 %all-gather.13.cloned.1.call-start = ((), (), s32[]{:S(2)}) async-start(), calls=%async_computation.7 | async-start | bytes 5308416 | tf_op jit(solution)/shard_map/all_gather | solution.py:265
  278.5 45.2 %all-to-all-start.4 = ((bf16[16,48,2048]{2,1,0:T(8,128)(2,1)}), bf16[16,48,2048]{2,1,0:T(8,128)(2,1)S(1)}, u32[]{:S(2)}, u32[]{:S(2)}) async-start(bf16[16,48,2048]{2,1,0:T(8,128)(2,1)} %bitcast_dynamic-update-slice_fusion), calls=%async_computation.4 | async-start | bytes 6291456 | tf_op jit(solution)/shard_map/all_to_all | solution.py:244
  282.6 86.1 %all-gather.15.cloned.1.call-start = ((), (), s32[]{:S(2)}) async-start(), calls=%async_computation.8 | async-start | bytes 5308416 | tf_op jit(solution)/shard_map/all_gather | solution.py:265
Sparse Core Ops, SparseCore 0:
  148.6 34.2 all-gather.8
  220.5 35.6 all-gather.10
  278.6 34.7 all-gather.12
  332.8 35.8 all-gather.14

commit v3 on v0

--- a/solution.py
+++ b/solution.py
@@ -7,7 +7,7 @@
 
 GROUP = 8
 TILE = 128
-CHUNK_GROUPS = (4, 4, 4, 4)
+CHUNK_GROUPS = (4, 4, 4, 3, 1)
 EXTRA = 16
 
 

time: 348 us -> 348 us (level)
  waiting for transfers between devices: 109 us -> 97.1 us
  Pallas kernels: 87.8 us -> 94.5 us
  starting transfers between devices: 32.2 us -> 38 us
    all_to_all x4 -> x5, waiting for transfers between devices: 89.1 us -> 77.5 us  [on_device(): lax.all_to_all(sends[c], 'stream', split_axis=0, concat_axis=0, tiled=True)]
    all_to_all x4 -> x5, starting transfers between devices: 22.5 us -> 28.2 us  [on_device(): lax.all_to_all(sends[c], 'stream', split_axis=0, concat_axis=0, tiled=True)]
    pallas_call x4 -> x5, Pallas kernels: 38 us -> 40.7 us  [local_call(): pl.pallas_call(local_kernel, grid=(groups,), in_specs=[pl.BlockSpec((leng...]
    slice x1 -> x3, local copies, waits for them, and re-layouts: 5.76 us -> 8.33 us  [on_device(): tokens[:, f * group_width:(f + n) * group_width]]
    pallas_call x4 -> x5, Pallas kernels: 27.3 us -> 29.5 us  [combine_call(): pl.pallas_call(combine_kernel, grid=(groups,), in_specs=[pl.BlockSpec(mem...]
    gather x5 -> x6, local copies, waits for them, and re-layouts: 32.1 us -> 30.1 us  [receive_rows(): return jnp.take(arrived.reshape(-1, width), flat_rows, axis=0, mode='clip')]
    pallas_call x4 -> x5, Pallas kernels: 22.5 us -> 24.3 us  [carried_call(): pl.pallas_call(carried_kernel, grid=(groups,), in_specs=[pl.BlockSpec(bt....]
    gather x5 -> x6, local copies, waits for them, and re-layouts: 34.3 us -> 32.6 us  [send_rows(): jnp.take(rows, pick_rows, axis=0, mode='clip')]
  transfers between devices with their start and end apart: 9 -> 11, of which waited for: 5 -> 6; matrix products, arithmetic and copies ran while one was open for 25% -> 25% of each run, Pallas kernels for 22% -> 25%
where the time goes in v3:
time: 348 us; the launch traced here: 341 us
  waiting for transfers between devices  97.1 us (28%)
  Pallas kernels  94.5 us (27%)
  local copies, waits for them, and re-layouts  83.6 us (24%)
  starting transfers between devices  38 us (11%)
  between operations  13.7 us (4%)
  other arithmetic  13.4 us (4%)
    all_to_all x5, waiting for transfers between devices, on_device(): lax.all_to_all(sends[c], 'stream', split_axis=0, concat_axis=0, tiled=True)  77.5 us
    pallas_call x5, Pallas kernels, local_call(): pl.pallas_call(local_kernel, grid=(groups,), in_specs=[pl.BlockSpec((leng...  40.7 us
    gather x6, local copies, waits for them, and re-layouts, send_rows(): jnp.take(rows, pick_rows, axis=0, mode='clip')  32.6 us
    gather x6, local copies, waits for them, and re-layouts, receive_rows(): return jnp.take(arrived.reshape(-1, width), flat_rows, axis=0, mode='clip')  30.1 us
    pallas_call x5, Pallas kernels, combine_call(): pl.pallas_call(combine_kernel, grid=(groups,), in_specs=[pl.BlockSpec(mem...  29.5 us
    all_to_all x5, starting transfers between devices, on_device(): lax.all_to_all(sends[c], 'stream', split_axis=0, concat_axis=0, tiled=True)  28.2 us
    pallas_call x5, Pallas kernels, carried_call(): pl.pallas_call(carried_kernel, grid=(groups,), in_specs=[pl.BlockSpec(bt....  24.3 us
    all_gather x5, waiting for transfers between devices, on_device(): gathers.append(lax.all_gather(carried, 'pos'))  19.5 us
  transfers between devices with their start and end apart: 11, of which 6 were waited for; matrix products, arithmetic and copies ran while one was open for 25% of the time, Pallas kernels for 25%

profile of v3, /device:TPU:1, one launch (start us, length us, event | category | flops | bytes accessed | tf_op | source)
XLA Modules:
  0.0 341.4 jit_solution(17068381034845944235)
XLA Ops:
  8.3 1.1 pad_maximum_fusion
  9.4 3.3 gather_fusion.2
  12.7 8.4 %all-to-all-start.2 = ((bf16[16,48,384]{2,1,0:T(8,128)(2,1)}), bf16[16,48,384]{2,1,0:T(8,128)(2,1)S(1)}, u32[]{:S(2)}, u32[]{:S(2)}) async-start(bf16[16,48,384]{2,1,0:T(8,128)(2,1)} %bitcast.8), calls=%async_computation.2 | async-start | bytes 1179648 | tf_op jit(solution)/shard_map/all_to_all | solution.py:173
  21.1 5.7 %fusion.12 = (bf16[512,2048]{1,0:T(8,128)(2,1)S(1)}, bf16[512,2048]{1,0:T(8,128)(2,1)}, bf16[512,2048]{1,0:T(8,128)(2,1)}) fusion(bf16[512,8192]{1,0:T(8,128)(2,1)} %bitcast.108), kind=kLoop, calls=%fused_computation.63 | loop fusion | bytes 12582912 | tf_op jit(solution)/shard_map/slice | solution.py:233
  26.8 8.9 %gather_fusion = bf16[768,2048]{1,0:T(8,128)(2,1)} fusion(bf16[512,2048]{1,0:T(8,128)(2,1)} %get-tuple-element.42, s32[1024]{0:T(1024)S(1)} %pad_clamp_fusion.1), kind=kCustom, calls=%fused_computation | custom fusion | bytes 6294528 | tf_op jit(solution)/shard_map/jit(_take)/gather | solution.py:163
  35.8 9.0 %gather_fusion.1 = bf16[768,2048]{1,0:T(8,128)(2,1)} fusion(bf16[512,2048]{1,0:T(8,128)(2,1)} %get-tuple-element.41, s32[1024]{0:T(1024)S(1)} %pad_clamp_fusion.1), kind=kCustom, calls=%fused_computation.1 | custom fusion | bytes 6294528 | tf_op jit(solution)/shard_map/jit(_take)/gather | solution.py:163
  45.9 6.7 %all-to-all-start = ((bf16[16,48,2048]{2,1,0:T(8,128)(2,1)}), bf16[16,48,2048]{2,1,0:T(8,128)(2,1)}, u32[]{:S(2)}, u32[]{:S(2)}) async-start(bf16[16,48,2048]{2,1,0:T(8,128)(2,1)} %bitcast.106), calls=%async_computation | async-start | bytes 6291456 | tf_op jit(solution)/shard_map/all_to_all | solution.py:241
  53.9 4.2 %compare_select_fusion.2 = (s32[512,1]{0,1:T(1,128)S(1)}, s32[512,1]{0,1:T(1,128)S(1)}) fusion(s32[]{:T(128)} %bitcast.21, s32[]{:T(128)} %bitcast.22, s32[]{:T(128)} %bitcast.23, s32[]{:T(128)} %bitcast.24, s32[]{:T(128)} %bitcast.25, s32[]{:T(128)} %bitcast.27, s32[]{:T(128)} %bitcast.26, s32[512,1]{0,1:T(1,128)S(1)} %bitcast.127), kind=kLoop, calls=%fused_computation.39 | loop fusion | flops 7680 | bytes 6172 | tf_op jit(solution)/shard_map/jit(_take)/gather | solution.py:199
  58.2 5.6 %select_select_fusion = s32[512]{0:T(512)S(1)} fusion(pred[512]{0:T(512)(128)(4,1)S(1)} %get-tuple-element.36, pred[512]{0:T(512)(128)(4,1)S(1)} %get-tuple-element.35, pred[512]{0:T(512)(128)(4,1)S(1)} %get-tuple-element.37, pred[512]{0:T(512)(128)(4,1)S(1)} %get-tuple-element.34, pred[512]{0:T(512)(128)(4,1)S(1)} %get-tuple-element.33, ...), kind=kLoop, calls=%fused_computation.52 | loop fusion | flops 4608 | bytes 8740 | tf_op jit(solution)/shard_map/jit(_take)/gather | solution.py:199
  63.8 1.9 gather_fusion.3
  67.5 1.8 copy.41
  70.3 2.6 copy.40
  73.7 24.0 %all-to-all-done = bf16[16,48,2048]{2,1,0:T(8,128)(2,1)} async-done(((bf16[16,48,2048]{2,1,0:T(8,128)(2,1)}), bf16[16,48,2048]{2,1,0:T(8,128)(2,1)}, u32[]{:S(2)}, u32[]{:S(2)}) %all-to-all-start) | async-done | bytes 3145760 | tf_op jit(solution)/shard_map/all_to_all | solution.py:241
  97.7 7.5 %gather_fusion.4 = bf16[512,2048]{1,0:T(8,128)(2,1)} fusion(bf16[768,2048]{1,0:T(8,128)(2,1)} %bitcast.37, s32[1024]{0:T(1024)S(1)} %pad_clamp_fusion), kind=kCustom, calls=%fused_computation.4 | custom fusion | bytes 4196352 | tf_op jit(solution)/shard_map/jit(_take)/gather | solution.py:168
  105.2 5.6 %shard_map.66 = bf16[16,144,128]{2,1,0:T(8,128)(2,1)} custom-call(bf16[128,512]{1,0:T(8,128)(2,1)} %bitcast.111, f32[16,512,8]{2,1,0:T(8,128)} %bitcast.90, f32[1,8192]{1,0:T(1,128)} %reshape_reshape.7.decay_ref, bf16[512,2048]{1,0:T(8,128)(2,1)} %gather_fusion.4), custom_call_target="tpu_custom_call" | custom-call | tf_op jit(solution)/shard_map/pallas_call | solution.py:99
  110.9 4.5 %all-to-all-start.1 = ((bf16[16,48,2048]{2,1,0:T(8,128)(2,1)}), bf16[16,48,2048]{2,1,0:T(8,128)(2,1)}, u32[]{:S(2)}, u32[]{:S(2)}) async-start(bf16[16,48,2048]{2,1,0:T(8,128)(2,1)} %bitcast.105), calls=%async_computation.1 | async-start | bytes 6291456 | tf_op jit(solution)/shard_map/all_to_all | solution.py:241
  116.4 4.2 %gather_fusion.5 = bf16[768,2048]{1,0:T(8,128)(2,1)} fusion(bf16[512,2048]{1,0:T(8,128)(2,1)S(1)} %get-tuple-element.40, s32[1024]{0:T(1024)S(1)} %pad_clamp_fusion.1), kind=kCustom, calls=%fused_computation.5 | custom fusion | bytes 6294528 | tf_op jit(solution)/shard_map/jit(_take)/gather | solution.py:163
  120.6 2.7 copy.39
  123.4 1.3 fusion.7.scores_ref
  124.6 9.4 %shard_map.64.refs_0_ = f32[512,2048]{1,0:T(8,128)} custom-call(f32[512,512]{1,0:T(8,128)} %fusion.7.scores_ref, f32[16,512,8]{2,1,0:T(8,128)} %bitcast.80, f32[128,512]{1,0:T(8,128)} %bitcast.100, f32[128,512]{1,0:T(8,128)} %get-tuple-element.50.stept_ref, bf16[512,2048]{1,0:T(8,128)(2,1)} %gather_fusion.4, f32[1,8192]{1,0:T(1,128)} %reshape_reshape.6.skip_ref), custom_call_target="tpu_custom_call" | custom-call | tf_op jit(solution)/shard_map/pallas_call | solution.py:117
  134.1 23.2 %all-to-all-done.1 = bf16[16,48,2048]{2,1,0:T(8,128)(2,1)} async-done(((bf16[16,48,2048]{2,1,0:T(8,128)(2,1)}), bf16[16,48,2048]{2,1,0:T(8,128)(2,1)}, u32[]{:S(2)}, u32[]{:S(2)}) %all-to-all-start.1) | async-done | bytes 3145760 | tf_op jit(solution)/shard_map/all_to_all | solution.py:241
  157.3 7.5 %gather_fusion.6 = bf16[512,2048]{1,0:T(8,128)(2,1)} fusion(bf16[768,2048]{1,0:T(8,128)(2,1)} %bitcast.39, s32[1024]{0:T(1024)S(1)} %pad_clamp_fusion), kind=kCustom, calls=%fused_computation.6 | custom fusion | bytes 4196352 | tf_op jit(solution)/shard_map/jit(_take)/gather | solution.py:168
  164.8 5.6 %shard_map.69 = bf16[16,144,128]{2,1,0:T(8,128)(2,1)} custom-call(bf16[128,512]{1,0:T(8,128)(2,1)} %bitcast.112, f32[16,512,8]{2,1,0:T(8,128)} %bitcast.91, f32[1,8192]{1,0:T(1,128)} %reshape_reshape.7.decay_ref, bf16[512,2048]{1,0:T(8,128)(2,1)} %gather_fusion.6), custom_call_target="tpu_custom_call" | custom-call | tf_op jit(solution)/shard_map/pallas_call | solution.py:99
  170.5 5.6 %all-to-all-start.3 = ((bf16[16,48,2048]{2,1,0:T(8,128)(2,1)}), bf16[16,48,2048]{2,1,0:T(8,128)(2,1)}, u32[]{:S(2)}, u32[]{:S(2)}) async-start(bf16[16,48,2048]{2,1,0:T(8,128)(2,1)} %bitcast.38), calls=%async_computation.3 | async-start | bytes 6291456 | tf_op jit(solution)/shard_map/all_to_all | solution.py:241
  176.4 1.5 slice.96
  177.9 3.9 %gather_fusion.7 = bf16[768,1536]{1,0:T(8,128)(2,1)} fusion(bf16[512,1536]{1,0:T(8,128)(2,1)S(1)} %slice.96, s32[1024]{0:T(1024)S(1)} %pad_clamp_fusion.1), kind=kCustom, calls=%fused_computation.7 | custom fusion | bytes 4721664 | tf_op jit(solution)/shard_map/jit(_take)/gather | solution.py:163
  181.7 9.8 %shard_map.65.refs_1_ = f32[512,2048]{1,0:T(8,128)} custom-call(f32[512,512]{1,0:T(8,128)} %fusion.7.scores_ref, f32[16,512,8]{2,1,0:T(8,128)} %bitcast.81, f32[128,512]{1,0:T(8,128)} %bitcast.101, f32[128,512]{1,0:T(8,128)} %get-tuple-element.50.stept_ref, bf16[512,2048]{1,0:T(8,128)(2,1)} %gather_fusion.6, f32[1,8192]{1,0:T(1,128)} %reshape_reshape.6.skip_ref), custom_call_target="tpu_custom_call" | custom-call | tf_op jit(solution)/shard_map/pallas_call | solution.py:117
  191.5 6.8 %shard_map.67.refs_0_ = bf16[512,8192]{1,0:T(8,128)(2,1)} custom-call(s32[1]{0:T(128)} %bitcast.place_ref, f32[512,2048]{1,0:T(8,128)} %shard_map.64.refs_0_, bf16[8,16,144,128]{3,2,1,0:T(8,128)(2,1)} %bitcast.117, f32[16,512,8]{2,1,0:T(8,128)} %bitcast.82, bf16[512,128]{1,0:T(8,128)(2,1)} %get-tuple-element.43.refs_3_.refs_4_), custom_call_target="tpu_custom_call" | custom-call | tf_op jit(solution)/shard_map/pallas_call | solution.py:150
  198.3 19.7 %all-to-all-done.3 = bf16[16,48,2048]{2,1,0:T(8,128)(2,1)} async-done(((bf16[16,48,2048]{2,1,0:T(8,128)(2,1)}), bf16[16,48,2048]{2,1,0:T(8,128)(2,1)}, u32[]{:S(2)}, u32[]{:S(2)}) %all-to-all-start.3) | async-done | bytes 3145760 | tf_op jit(solution)/shard_map/all_to_all | solution.py:241
  218.0 7.5 %gather_fusion.8 = bf16[512,2048]{1,0:T(8,128)(2,1)} fusion(bf16[768,2048]{1,0:T(8,128)(2,1)} %bitcast.45, s32[1024]{0:T(1024)S(1)} %pad_clamp_fusion), kind=kCustom, calls=%fused_computation.8 | custom fusion | bytes 4196352 | tf_op jit(solution)/shard_map/jit(_take)/gather | solution.py:168
  225.5 5.6 %shard_map.72 = bf16[16,144,128]{2,1,0:T(8,128)(2,1)} custom-call(bf16[128,512]{1,0:T(8,128)(2,1)} %bitcast.113, f32[16,512,8]{2,1,0:T(8,128)} %bitcast.92, f32[1,8192]{1,0:T(1,128)} %reshape_reshape.7.decay_ref, bf16[512,2048]{1,0:T(8,128)(2,1)} %gather_fusion.8), custom_call_target="tpu_custom_call" | custom-call | tf_op jit(solution)/shard_map/pallas_call | solution.py:99
  231.2 5.6 %all-to-all-start.4 = ((bf16[16,48,1536]{2,1,0:T(8,128)(2,1)}), bf16[16,48,1536]{2,1,0:T(8,128)(2,1)S(1)}, u32[]{:S(2)}, u32[]{:S(2)}) async-start(bf16[16,48,1536]{2,1,0:T(8,128)(2,1)} %bitcast.107), calls=%async_computation.4 | async-start | bytes 4718592 | tf_op jit(solution)/shard_map/all_to_all | solution.py:241
  236.9 1.1 slice.97
  238.0 3.3 gather_fusion.9
  241.3 9.7 %shard_map.68.refs_1_ = f32[512,2048]{1,0:T(8,128)} custom-call(f32[512,512]{1,0:T(8,128)} %fusion.7.scores_ref, f32[16,512,8]{2,1,0:T(8,128)} %bitcast.83, f32[128,512]{1,0:T(8,128)} %bitcast.102, f32[128,512]{1,0:T(8,128)} %get-tuple-element.50.stept_ref, bf16[512,2048]{1,0:T(8,128)(2,1)} %gather_fusion.8, f32[1,8192]{1,0:T(1,128)} %reshape_reshape.6.skip_ref), custom_call_target="tpu_custom_call" | custom-call | tf_op jit(solution)/shard_map/pallas_call | solution.py:117
  251.0 6.9 %shard_map.70.refs_0_ = bf16[512,8192]{1,0:T(8,128)(2,1)} custom-call(s32[1]{0:T(128)} %bitcast.place_ref, bf16[512,8192]{1,0:T(8,128)(2,1)} %shard_map.67.refs_0_, f32[512,2048]{1,0:T(8,128)} %shard_map.65.refs_1_, bf16[8,16,144,128]{3,2,1,0:T(8,128)(2,1)} %bitcast.116, f32[16,512,8]{2,1,0:T(8,128)} %bitcast.84, ...), custom_call_target="tpu_custom_call", output_to_operand_aliasing={{}: (1, {})} | custom-call | tf_op jit(solution)/shard_map/pallas_call | solution.py:150
  257.8 10.6 %all-to-all-done.4 = bf16[16,48,1536]{2,1,0:T(8,128)(2,1)S(1)} async-done(((bf16[16,48,1536]{2,1,0:T(8,128)(2,1)}), bf16[16,48,1536]{2,1,0:T(8,128)(2,1)S(1)}, u32[]{:S(2)}, u32[]{:S(2)}) %all-to-all-start.4) | async-done | bytes 2359328 | tf_op jit(solution)/shard_map/all_to_all | solution.py:241
  268.4 2.9 gather_fusion.10
  271.3 4.7 %shard_map.74 = bf16[12,144,128]{2,1,0:T(8,128)(2,1)} custom-call(bf16[128,512]{1,0:T(8,128)(2,1)} %bitcast.114, f32[16,512,8]{2,1,0:T(8,128)} %bitcast.93, f32[1,8192]{1,0:T(1,128)} %reshape_reshape.7.decay_ref, bf16[512,1536]{1,0:T(8,128)(2,1)} %gather_fusion.10), custom_call_target="tpu_custom_call" | custom-call | tf_op jit(solution)/shard_map/pallas_call | solution.py:99
  276.1 5.7 %all-to-all-start.5 = ((bf16[16,48,512]{2,1,0:T(8,128)(2,1)}), bf16[16,48,512]{2,1,0:T(8,128)(2,1)S(1)}, u32[]{:S(2)}, u32[]{:S(2)}) async-start(bf16[16,48,512]{2,1,0:T(8,128)(2,1)} %bitcast.47), calls=%async_computation.5 | async-start | bytes 1572864 | tf_op jit(solution)/shard_map/all_to_all | solution.py:241
  282.1 7.7 %shard_map.71.refs_1_ = f32[512,1536]{1,0:T(8,128)} custom-call(f32[512,512]{1,0:T(8,128)} %fusion.7.scores_ref, f32[16,512,8]{2,1,0:T(8,128)} %bitcast.85, f32[128,512]{1,0:T(8,128)} %bitcast.103, f32[128,512]{1,0:T(8,128)} %get-tuple-element.50.stept_ref, bf16[512,1536]{1,0:T(8,128)(2,1)} %gather_fusion.10, f32[1,8192]{1,0:T(1,128)} %reshape_reshape.6.skip_ref), custom_call_target="tpu_custom_call" | custom-call | tf_op jit(solution)/shard_map/pallas_call | solution.py:117
  289.8 6.8 %shard_map.73.refs_0_ = bf16[512,8192]{1,0:T(8,128)(2,1)} custom-call(s32[1]{0:T(128)} %bitcast.place_ref, bf16[512,8192]{1,0:T(8,128)(2,1)} %shard_map.70.refs_0_, f32[512,2048]{1,0:T(8,128)} %shard_map.68.refs_1_, bf16[8,16,144,128]{3,2,1,0:T(8,128)(2,1)} %bitcast.118, f32[16,512,8]{2,1,0:T(8,128)} %bitcast.86, ...), custom_call_target="tpu_custom_call", output_to_operand_aliasing={{}: (1, {})} | custom-call | tf_op jit(solution)/shard_map/pallas_call | solution.py:150
  296.6 2.6 gather_fusion.11
  299.2 2.7 shard_map.77
  302.0 4.2 %shard_map.76.refs_1_ = f32[512,512]{1,0:T(8,128)} custom-call(f32[512,512]{1,0:T(8,128)} %fusion.7.scores_ref, f32[16,512,8]{2,1,0:T(8,128)} %bitcast.87, f32[128,512]{1,0:T(8,128)} %bitcast.104, f32[128,512]{1,0:T(8,128)} %get-tuple-element.50.stept_ref, bf16[512,512]{1,0:T(8,128)(2,1)} %gather_fusion.11, f32[1,8192]{1,0:T(1,128)} %reshape_reshape.6.skip_ref), custom_call_target="tpu_custom_call" | custom-call | tf_op jit(solution)/shard_map/pallas_call | solution.py:117
  306.4 5.9 %shard_map.75.refs_0_ = bf16[512,8192]{1,0:T(8,128)(2,1)} custom-call(s32[1]{0:T(128)} %bitcast.place_ref, bf16[512,8192]{1,0:T(8,128)(2,1)} %shard_map.73.refs_0_, f32[512,1536]{1,0:T(8,128)} %shard_map.71.refs_1_, bf16[8,12,144,128]{3,2,1,0:T(8,128)(2,1)} %bitcast.119, f32[16,512,8]{2,1,0:T(8,128)} %bitcast.88, ...), custom_call_target="tpu_custom_call", output_to_operand_aliasing={{}: (1, {})} | custom-call | tf_op jit(solution)/shard_map/pallas_call | solution.py:150
  312.3 19.2 %all-gather.19.cloned.1.call-done = bf16[32,144,128]{2,1,0:T(8,128)(2,1)} async-done(((bf16[4,144,128]{2,1,0:T(8,128)(2,1)}), bf16[32,144,128]{2,1,0:T(8,128)(2,1)}) %all-gather.19.cloned.1.call-update) | async-done | bytes 1179664 | tf_op jit(solution)/shard_map/all_gather | solution.py:262
  331.5 3.1 shard_map.78
  (61 shorter events, 9.8 us)
Async XLA Ops:
  12.7 33.2 %all-to-all-start.2 = ((bf16[16,48,384]{2,1,0:T(8,128)(2,1)}), bf16[16,48,384]{2,1,0:T(8,128)(2,1)S(1)}, u32[]{:S(2)}, u32[]{:S(2)}) async-start(bf16[16,48,384]{2,1,0:T(8,128)(2,1)} %bitcast.8), calls=%async_computation.2 | async-start | bytes 1179648 | tf_op jit(solution)/shard_map/all_to_all | solution.py:173
  45.9 17.9 %copy-start.2 = (f32[128]{0:T(128)S(1)}, f32[128]{0:T(128)}, u32[]{:S(2)}) copy-start(f32[128]{0:T(128)} %param.9) | copy-start | bytes 1540
  45.9 51.8 %all-to-all-start = ((bf16[16,48,2048]{2,1,0:T(8,128)(2,1)}), bf16[16,48,2048]{2,1,0:T(8,128)(2,1)}, u32[]{:S(2)}, u32[]{:S(2)}) async-start(bf16[16,48,2048]{2,1,0:T(8,128)(2,1)} %bitcast.106), calls=%async_computation | async-start | bytes 6291456 | tf_op jit(solution)/shard_map/all_to_all | solution.py:241
  52.6 138.9 %all-gather.11.cloned.1.call-start = ((), (), s32[]{:S(2)}) async-start(), calls=%async_computation.6 | async-start | bytes 5308416 | tf_op jit(solution)/shard_map/all_gather | solution.py:262
  67.5 53.2 %copy-start = (f32[16,8,4,128]{3,1,2,0:T(8,128)}, f32[16,8,4,128]{3,1,2,0:T(8,128)S(1)}, u32[]{:S(2)}) copy-start(f32[16,8,4,128]{3,1,2,0:T(8,128)S(1)} %copy.51) | copy-start | bytes 786436
  110.9 4.7 %copy-start.1 = (f32[128]{0:T(128)S(1)}, f32[128]{0:T(128)}, u32[]{:S(2)}) copy-start(f32[128]{0:T(128)} %param.10) | copy-start | bytes 1540
  110.9 46.4 %all-to-all-start.1 = ((bf16[16,48,2048]{2,1,0:T(8,128)(2,1)}), bf16[16,48,2048]{2,1,0:T(8,128)(2,1)}, u32[]{:S(2)}, u32[]{:S(2)}) async-start(bf16[16,48,2048]{2,1,0:T(8,128)(2,1)} %bitcast.105), calls=%async_computation.1 | async-start | bytes 6291456 | tf_op jit(solution)/shard_map/all_to_all | solution.py:241
  115.4 135.6 %all-gather.13.cloned.1.call-start = ((), (), s32[]{:S(2)}) async-start(), calls=%async_computation.7 | async-start | bytes 5308416 | tf_op jit(solution)/shard_map/all_gather | solution.py:262
  170.5 47.5 %all-to-all-start.3 = ((bf16[16,48,2048]{2,1,0:T(8,128)(2,1)}), bf16[16,48,2048]{2,1,0:T(8,128)(2,1)}, u32[]{:S(2)}, u32[]{:S(2)}) async-start(bf16[16,48,2048]{2,1,0:T(8,128)(2,1)} %bitcast.38), calls=%async_computation.3 | async-start | bytes 6291456 | tf_op jit(solution)/shard_map/all_to_all | solution.py:241
  176.1 113.7 %all-gather.15.cloned.1.call-start = ((), (), s32[]{:S(2)}) async-start(), calls=%async_computation.8 | async-start | bytes 5308416 | tf_op jit(solution)/shard_map/all_gather | solution.py:262
  231.2 37.2 %all-to-all-start.4 = ((bf16[16,48,1536]{2,1,0:T(8,128)(2,1)}), bf16[16,48,1536]{2,1,0:T(8,128)(2,1)S(1)}, u32[]{:S(2)}, u32[]{:S(2)}) async-start(bf16[16,48,1536]{2,1,0:T(8,128)(2,1)} %bitcast.107), calls=%async_computation.4 | async-start | bytes 4718592 | tf_op jit(solution)/shard_map/all_to_all | solution.py:241
  236.8 69.6 %all-gather.17.cloned.1.call-start = ((), (), s32[]{:S(2)}) async-start(), calls=%async_computation.9 | async-start | bytes 3981312 | tf_op jit(solution)/shard_map/all_gather | solution.py:262
  276.1 20.5 %all-to-all-start.5 = ((bf16[16,48,512]{2,1,0:T(8,128)(2,1)}), bf16[16,48,512]{2,1,0:T(8,128)(2,1)S(1)}, u32[]{:S(2)}, u32[]{:S(2)}) async-start(bf16[16,48,512]{2,1,0:T(8,128)(2,1)} %bitcast.47), calls=%async_computation.5 | async-start | bytes 1572864 | tf_op jit(solution)/shard_map/all_to_all | solution.py:241
  281.8 49.7 %all-gather.19.cloned.1.call-start = ((), (), s32[]{:S(2)}) async-start(), calls=%async_computation.10 | async-start | bytes 1327104 | tf_op jit(solution)/shard_map/all_gather | solution.py:262
Sparse Core Ops, SparseCore 0:
  111.0 34.2 all-gather.10
  170.6 35.9 all-gather.12
  231.3 36.0 all-gather.14
  276.2 30.1 all-gather.16
  307.9 23.5 all-gather.18

commit v4 on v3

--- a/solution.py
+++ b/solution.py
@@ -69,10 +69,17 @@
     peers = gath_ref.shape[0]
     pairs = gath_ref.shape[1]
     state_size = c_ref.shape[1]
+    relative = peers < lax.axis_size("pos")
     for q in range(pairs):
         run = jnp.ones((1, 128), jnp.float32)
         state = jnp.zeros((state_size, 128), jnp.float32)
-        for k in range(peers - 1, -1, -1):
+        if relative:
+            for j in range(peers):
+                if j > 0:
+                    pair = gath_ref[j - 1, q, state_size : state_size + 2, :].astype(jnp.float32)
+                    run = run * (pair[0:1] + pair[1:2])
+                state = state + run * gath_ref[j, q, 0:state_size, :].astype(jnp.float32)
+        for k in range(peers - 1, -1, -1) if not relative else ():
             if k + 1 < peers:
                 pair = gath_ref[k + 1, q, state_size : state_size + 2, :].astype(jnp.float32)
                 later = pair[0:1] + pair[1:2]
@@ -172,6 +179,15 @@
     send = send_rows(rows, pick_rows, stream_count, capacity)
     arrived = lax.all_to_all(send, "stream", split_axis=0, concat_axis=0, tiled=True)
     return receive_rows(arrived, flat_rows)
+
+
+def earlier_blocks(carried):
+    peers = lax.axis_size("pos")
+    moved = [
+        lax.ppermute(carried, "pos", [(i, i + shift) for i in range(peers - shift)])
+        for shift in range(1, peers)
+    ]
+    return jnp.stack(moved)
 
 
 def on_device(tokens_in, proj_in, step_raw, decay_log, head_skip_weight, row_counts):
@@ -259,7 +275,10 @@
             result = tied["result"]
         chunk_tokens = receive_rows(arrived, flat_rows)
         carried = carried_call(bt, fac_grouped, decay_lanes, chunk_tokens, firsts[c])
-        gathers.append(lax.all_gather(carried, "pos"))
+        if c + 1 < len(sizes):
+            gathers.append(lax.all_gather(carried, "pos"))
+        else:
+            gathers.append(earlier_blocks(carried))
         partials.append(
             local_call(scores, cum_grouped, cum_t, step_t, chunk_tokens, skip_lanes, firsts[c])
         )

time: 348 us -> 356 us (1.023)
  starting transfers between devices: 38 us -> 55 us
  waiting for transfers between devices: 97.1 us -> 83.4 us
  local copies, waits for them, and re-layouts: 83.6 us -> 87.3 us
    all_gather x5 -> x4, waiting for transfers between devices: 19.5 us -> 0.03 us  [on_device(): gathers.append(lax.all_gather(carried, 'pos'))]
    ppermute x0 -> x7, starting transfers between devices: none -> 16 us  [earlier_blocks(): lax.ppermute(carried, 'pos', [(i, i + shift) for i in range(peers - shift)])]
    ppermute x0 -> x7, waiting for transfers between devices: none -> 7.39 us  [earlier_blocks(): lax.ppermute(carried, 'pos', [(i, i + shift) for i in range(peers - shift)])]
  transfers between devices with their start and end apart: 11 -> 17, of which waited for: 6 -> 7; matrix products, arithmetic and copies ran while one was open for 25% -> 25% of each run, Pallas kernels for 25% -> 23%
where the time goes in v4:
time: 356 us; the launch traced here: 349 us
  Pallas kernels  94.8 us (27%)
  local copies, waits for them, and re-layouts  87.3 us (25%)
  waiting for transfers between devices  83.4 us (23%)
  starting transfers between devices  55 us (15%)
  between operations  13.8 us (4%)
  other arithmetic  13.4 us (4%)
    all_to_all x5, waiting for transfers between devices, on_device(): lax.all_to_all(sends[c], 'stream', split_axis=0, concat_axis=0, tiled=True)  75.9 us
    pallas_call x5, Pallas kernels, local_call(): pl.pallas_call(local_kernel, grid=(groups,), in_specs=[pl.BlockSpec((leng...  40.7 us
    gather x6, local copies, waits for them, and re-layouts, receive_rows(): return jnp.take(arrived.reshape(-1, width), flat_rows, axis=0, mode='clip')  33.5 us
    gather x6, local copies, waits for them, and re-layouts, send_rows(): jnp.take(rows, pick_rows, axis=0, mode='clip')  32.6 us
    pallas_call x5, Pallas kernels, combine_call(): pl.pallas_call(combine_kernel, grid=(groups,), in_specs=[pl.BlockSpec(mem...  29.8 us
    all_to_all x5, starting transfers between devices, on_device(): lax.all_to_all(sends[c], 'stream', split_axis=0, concat_axis=0, tiled=True)  29.3 us
    pallas_call x5, Pallas kernels, carried_call(): pl.pallas_call(carried_kernel, grid=(groups,), in_specs=[pl.BlockSpec(bt....  24.3 us
    ppermute x7, starting transfers between devices, earlier_blocks(): lax.ppermute(carried, 'pos', [(i, i + shift) for i in range(peers - shift)])  16 us
  transfers between devices with their start and end apart: 17, of which 7 were waited for; matrix products, arithmetic and copies ran while one was open for 25% of the time, Pallas kernels for 23%

profile of v4, /device:TPU:1, one launch (start us, length us, event | category | flops | bytes accessed | tf_op | source)
XLA Modules:
  0.0 348.9 jit_solution(13790560653725997877)
XLA Ops:
  9.4 3.3 gather_fusion.2
  12.7 8.4 %all-to-all-start.2 = ((bf16[16,48,384]{2,1,0:T(8,128)(2,1)}), bf16[16,48,384]{2,1,0:T(8,128)(2,1)S(1)}, u32[]{:S(2)}, u32[]{:S(2)}) async-start(bf16[16,48,384]{2,1,0:T(8,128)(2,1)} %bitcast.8), calls=%async_computation.2 | async-start | bytes 1179648 | tf_op jit(solution)/shard_map/all_to_all | solution.py:180
  21.1 5.9 %fusion.12 = (bf16[512,2048]{1,0:T(8,128)(2,1)S(1)}, bf16[512,2048]{1,0:T(8,128)(2,1)}, bf16[512,2048]{1,0:T(8,128)(2,1)}) fusion(bf16[512,8192]{1,0:T(8,128)(2,1)} %bitcast.120), kind=kLoop, calls=%fused_computation.70 | loop fusion | bytes 12582912 | tf_op jit(solution)/shard_map/slice | solution.py:249
  27.0 8.9 %gather_fusion = bf16[768,2048]{1,0:T(8,128)(2,1)} fusion(bf16[512,2048]{1,0:T(8,128)(2,1)} %get-tuple-element.42, s32[1024]{0:T(1024)S(1)} %pad_clamp_fusion.1), kind=kCustom, calls=%fused_computation | custom fusion | bytes 6294528 | tf_op jit(solution)/shard_map/jit(_take)/gather | solution.py:170
  36.0 9.0 %gather_fusion.1 = bf16[768,2048]{1,0:T(8,128)(2,1)} fusion(bf16[512,2048]{1,0:T(8,128)(2,1)} %get-tuple-element.41, s32[1024]{0:T(1024)S(1)} %pad_clamp_fusion.1), kind=kCustom, calls=%fused_computation.1 | custom fusion | bytes 6294528 | tf_op jit(solution)/shard_map/jit(_take)/gather | solution.py:170
  46.1 6.7 %all-to-all-start = ((bf16[16,48,2048]{2,1,0:T(8,128)(2,1)}), bf16[16,48,2048]{2,1,0:T(8,128)(2,1)}, u32[]{:S(2)}, u32[]{:S(2)}) async-start(bf16[16,48,2048]{2,1,0:T(8,128)(2,1)} %bitcast.118), calls=%async_computation | async-start | bytes 6291456 | tf_op jit(solution)/shard_map/all_to_all | solution.py:257
  54.1 4.2 %compare_select_fusion.2 = (s32[512,1]{0,1:T(1,128)S(1)}, s32[512,1]{0,1:T(1,128)S(1)}) fusion(s32[]{:T(128)} %bitcast.21, s32[]{:T(128)} %bitcast.22, s32[]{:T(128)} %bitcast.23, s32[]{:T(128)} %bitcast.24, s32[]{:T(128)} %bitcast.25, s32[]{:T(128)} %bitcast.27, s32[]{:T(128)} %bitcast.26, s32[512,1]{0,1:T(1,128)S(1)} %bitcast.138), kind=kLoop, calls=%fused_computation.46 | loop fusion | flops 7680 | bytes 6172 | tf_op jit(solution)/shard_map/jit(_take)/gather | solution.py:215
  58.4 5.6 %select_select_fusion = s32[512]{0:T(512)S(1)} fusion(pred[512]{0:T(512)(128)(4,1)S(1)} %get-tuple-element.36, pred[512]{0:T(512)(128)(4,1)S(1)} %get-tuple-element.35, pred[512]{0:T(512)(128)(4,1)S(1)} %get-tuple-element.37, pred[512]{0:T(512)(128)(4,1)S(1)} %get-tuple-element.34, pred[512]{0:T(512)(128)(4,1)S(1)} %get-tuple-element.33, ...), kind=kLoop, calls=%fused_computation.59 | loop fusion | flops 4608 | bytes 8740 | tf_op jit(solution)/shard_map/jit(_take)/gather | solution.py:215
  64.0 1.9 gather_fusion.3
  70.5 2.6 copy.40
  73.8 24.1 %all-to-all-done = bf16[16,48,2048]{2,1,0:T(8,128)(2,1)} async-done(((bf16[16,48,2048]{2,1,0:T(8,128)(2,1)}), bf16[16,48,2048]{2,1,0:T(8,128)(2,1)}, u32[]{:S(2)}, u32[]{:S(2)}) %all-to-all-start) | async-done | bytes 3145760 | tf_op jit(solution)/shard_map/all_to_all | solution.py:257
  97.9 7.5 %gather_fusion.4 = bf16[512,2048]{1,0:T(8,128)(2,1)} fusion(bf16[768,2048]{1,0:T(8,128)(2,1)} %bitcast.37, s32[1024]{0:T(1024)S(1)} %pad_clamp_fusion), kind=kCustom, calls=%fused_computation.4 | custom fusion | bytes 4196352 | tf_op jit(solution)/shard_map/jit(_take)/gather | solution.py:175
  105.4 5.6 %shard_map.66 = bf16[16,144,128]{2,1,0:T(8,128)(2,1)} custom-call(bf16[128,512]{1,0:T(8,128)(2,1)} %bitcast.123, f32[16,512,8]{2,1,0:T(8,128)} %bitcast.103, f32[1,8192]{1,0:T(1,128)} %reshape_reshape.7.decay_ref, bf16[512,2048]{1,0:T(8,128)(2,1)} %gather_fusion.4), custom_call_target="tpu_custom_call" | custom-call | tf_op jit(solution)/shard_map/pallas_call | solution.py:106
  111.1 4.5 %all-to-all-start.1 = ((bf16[16,48,2048]{2,1,0:T(8,128)(2,1)}), bf16[16,48,2048]{2,1,0:T(8,128)(2,1)}, u32[]{:S(2)}, u32[]{:S(2)}) async-start(bf16[16,48,2048]{2,1,0:T(8,128)(2,1)} %bitcast.117), calls=%async_computation.1 | async-start | bytes 6291456 | tf_op jit(solution)/shard_map/all_to_all | solution.py:257
  116.6 4.2 %gather_fusion.5 = bf16[768,2048]{1,0:T(8,128)(2,1)} fusion(bf16[512,2048]{1,0:T(8,128)(2,1)S(1)} %get-tuple-element.40, s32[1024]{0:T(1024)S(1)} %pad_clamp_fusion.1), kind=kCustom, calls=%fused_computation.5 | custom fusion | bytes 6294528 | tf_op jit(solution)/shard_map/jit(_take)/gather | solution.py:170
  120.8 2.7 copy.39
  124.9 9.4 %shard_map.64.refs_0_ = f32[512,2048]{1,0:T(8,128)} custom-call(f32[512,512]{1,0:T(8,128)} %fusion.7.scores_ref, f32[16,512,8]{2,1,0:T(8,128)} %bitcast.93, f32[128,512]{1,0:T(8,128)} %bitcast.112, f32[128,512]{1,0:T(8,128)} %get-tuple-element.50.stept_ref, bf16[512,2048]{1,0:T(8,128)(2,1)} %gather_fusion.4, f32[1,8192]{1,0:T(1,128)} %reshape_reshape.6.skip_ref), custom_call_target="tpu_custom_call" | custom-call | tf_op jit(solution)/shard_map/pallas_call | solution.py:124
  134.3 23.2 %all-to-all-done.1 = bf16[16,48,2048]{2,1,0:T(8,128)(2,1)} async-done(((bf16[16,48,2048]{2,1,0:T(8,128)(2,1)}), bf16[16,48,2048]{2,1,0:T(8,128)(2,1)}, u32[]{:S(2)}, u32[]{:S(2)}) %all-to-all-start.1) | async-done | bytes 3145760 | tf_op jit(solution)/shard_map/all_to_all | solution.py:257
  157.5 7.5 %gather_fusion.6 = bf16[512,2048]{1,0:T(8,128)(2,1)} fusion(bf16[768,2048]{1,0:T(8,128)(2,1)} %bitcast.39, s32[1024]{0:T(1024)S(1)} %pad_clamp_fusion), kind=kCustom, calls=%fused_computation.6 | custom fusion | bytes 4196352 | tf_op jit(solution)/shard_map/jit(_take)/gather | solution.py:175
  165.0 5.6 %shard_map.69 = bf16[16,144,128]{2,1,0:T(8,128)(2,1)} custom-call(bf16[128,512]{1,0:T(8,128)(2,1)} %bitcast.124, f32[16,512,8]{2,1,0:T(8,128)} %bitcast.104, f32[1,8192]{1,0:T(1,128)} %reshape_reshape.7.decay_ref, bf16[512,2048]{1,0:T(8,128)(2,1)} %gather_fusion.6), custom_call_target="tpu_custom_call" | custom-call | tf_op jit(solution)/shard_map/pallas_call | solution.py:106
  170.6 5.6 %all-to-all-start.3 = ((bf16[16,48,2048]{2,1,0:T(8,128)(2,1)}), bf16[16,48,2048]{2,1,0:T(8,128)(2,1)}, u32[]{:S(2)}, u32[]{:S(2)}) async-start(bf16[16,48,2048]{2,1,0:T(8,128)(2,1)} %bitcast.119), calls=%async_computation.3 | async-start | bytes 6291456 | tf_op jit(solution)/shard_map/all_to_all | solution.py:257
  178.0 3.9 %gather_fusion.7 = bf16[768,1536]{1,0:T(8,128)(2,1)} fusion(bf16[512,1536]{1,0:T(8,128)(2,1)S(1)} %slice.96, s32[1024]{0:T(1024)S(1)} %pad_clamp_fusion.1), kind=kCustom, calls=%fused_computation.7 | custom fusion | bytes 4721664 | tf_op jit(solution)/shard_map/jit(_take)/gather | solution.py:170
  181.9 9.8 %shard_map.65.refs_1_ = f32[512,2048]{1,0:T(8,128)} custom-call(f32[512,512]{1,0:T(8,128)} %fusion.7.scores_ref, f32[16,512,8]{2,1,0:T(8,128)} %bitcast.94, f32[128,512]{1,0:T(8,128)} %bitcast.113, f32[128,512]{1,0:T(8,128)} %get-tuple-element.50.stept_ref, bf16[512,2048]{1,0:T(8,128)(2,1)} %gather_fusion.6, f32[1,8192]{1,0:T(1,128)} %reshape_reshape.6.skip_ref), custom_call_target="tpu_custom_call" | custom-call | tf_op jit(solution)/shard_map/pallas_call | solution.py:124
  191.7 6.8 %shard_map.67.refs_0_ = bf16[512,8192]{1,0:T(8,128)(2,1)} custom-call(s32[1]{0:T(128)} %bitcast.place_ref, f32[512,2048]{1,0:T(8,128)} %shard_map.64.refs_0_, bf16[8,16,144,128]{3,2,1,0:T(8,128)(2,1)} %bitcast.129, f32[16,512,8]{2,1,0:T(8,128)} %bitcast.95, bf16[512,128]{1,0:T(8,128)(2,1)} %get-tuple-element.43.refs_3_.refs_4_), custom_call_target="tpu_custom_call" | custom-call | tf_op jit(solution)/shard_map/pallas_call | solution.py:157
  198.5 19.7 %all-to-all-done.3 = bf16[16,48,2048]{2,1,0:T(8,128)(2,1)} async-done(((bf16[16,48,2048]{2,1,0:T(8,128)(2,1)}), bf16[16,48,2048]{2,1,0:T(8,128)(2,1)}, u32[]{:S(2)}, u32[]{:S(2)}) %all-to-all-start.3) | async-done | bytes 3145760 | tf_op jit(solution)/shard_map/all_to_all | solution.py:257
  218.2 7.5 %gather_fusion.8 = bf16[512,2048]{1,0:T(8,128)(2,1)} fusion(bf16[768,2048]{1,0:T(8,128)(2,1)} %bitcast.45, s32[1024]{0:T(1024)S(1)} %pad_clamp_fusion), kind=kCustom, calls=%fused_computation.8 | custom fusion | bytes 4196352 | tf_op jit(solution)/shard_map/jit(_take)/gather | solution.py:175
  225.7 5.7 %shard_map.72 = bf16[16,144,128]{2,1,0:T(8,128)(2,1)} custom-call(bf16[128,512]{1,0:T(8,128)(2,1)} %bitcast.125, f32[16,512,8]{2,1,0:T(8,128)} %bitcast.105, f32[1,8192]{1,0:T(1,128)} %reshape_reshape.7.decay_ref, bf16[512,2048]{1,0:T(8,128)(2,1)} %gather_fusion.8), custom_call_target="tpu_custom_call" | custom-call | tf_op jit(solution)/shard_map/pallas_call | solution.py:106
  231.4 5.7 %all-to-all-start.4 = ((bf16[16,48,1536]{2,1,0:T(8,128)(2,1)}), bf16[16,48,1536]{2,1,0:T(8,128)(2,1)}, u32[]{:S(2)}, u32[]{:S(2)}) async-start(bf16[16,48,1536]{2,1,0:T(8,128)(2,1)} %bitcast.44), calls=%async_computation.4 | async-start | bytes 4718592 | tf_op jit(solution)/shard_map/all_to_all | solution.py:257
  238.5 3.3 gather_fusion.9
  241.8 9.7 %shard_map.68.refs_1_ = f32[512,2048]{1,0:T(8,128)} custom-call(f32[512,512]{1,0:T(8,128)} %fusion.7.scores_ref, f32[16,512,8]{2,1,0:T(8,128)} %bitcast.96, f32[128,512]{1,0:T(8,128)} %bitcast.114, f32[128,512]{1,0:T(8,128)} %get-tuple-element.50.stept_ref, bf16[512,2048]{1,0:T(8,128)(2,1)} %gather_fusion.8, f32[1,8192]{1,0:T(1,128)} %reshape_reshape.6.skip_ref), custom_call_target="tpu_custom_call" | custom-call | tf_op jit(solution)/shard_map/pallas_call | solution.py:124
  251.5 6.8 %shard_map.70.refs_0_ = bf16[512,8192]{1,0:T(8,128)(2,1)} custom-call(s32[1]{0:T(128)} %bitcast.place_ref, bf16[512,8192]{1,0:T(8,128)(2,1)} %shard_map.67.refs_0_, f32[512,2048]{1,0:T(8,128)} %shard_map.65.refs_1_, bf16[8,16,144,128]{3,2,1,0:T(8,128)(2,1)} %bitcast.128, f32[16,512,8]{2,1,0:T(8,128)} %bitcast.97, ...), custom_call_target="tpu_custom_call", output_to_operand_aliasing={{}: (1, {})} | custom-call | tf_op jit(solution)/shard_map/pallas_call | solution.py:157
  258.3 9.0 %all-to-all-done.4 = bf16[16,48,1536]{2,1,0:T(8,128)(2,1)} async-done(((bf16[16,48,1536]{2,1,0:T(8,128)(2,1)}), bf16[16,48,1536]{2,1,0:T(8,128)(2,1)}, u32[]{:S(2)}, u32[]{:S(2)}) %all-to-all-start.4) | async-done | bytes 2359328 | tf_op jit(solution)/shard_map/all_to_all | solution.py:257
  267.3 6.4 %gather_fusion.10 = bf16[512,1536]{1,0:T(8,128)(2,1)} fusion(bf16[768,1536]{1,0:T(8,128)(2,1)} %bitcast.48, s32[1024]{0:T(1024)S(1)} %pad_clamp_fusion), kind=kCustom, calls=%fused_computation.10 | custom fusion | bytes 3147776 | tf_op jit(solution)/shard_map/jit(_take)/gather | solution.py:175
  273.6 4.7 %shard_map.74 = bf16[12,144,128]{2,1,0:T(8,128)(2,1)} custom-call(bf16[128,512]{1,0:T(8,128)(2,1)} %bitcast.126, f32[16,512,8]{2,1,0:T(8,128)} %bitcast.106, f32[1,8192]{1,0:T(1,128)} %reshape_reshape.7.decay_ref, bf16[512,1536]{1,0:T(8,128)(2,1)} %gather_fusion.10), custom_call_target="tpu_custom_call" | custom-call | tf_op jit(solution)/shard_map/pallas_call | solution.py:106
  278.4 6.8 %all-to-all-start.5 = ((bf16[16,48,512]{2,1,0:T(8,128)(2,1)}), bf16[16,48,512]{2,1,0:T(8,128)(2,1)S(1)}, u32[]{:S(2)}, u32[]{:S(2)}) async-start(bf16[16,48,512]{2,1,0:T(8,128)(2,1)} %bitcast.47), calls=%async_computation.5 | async-start | bytes 1572864 | tf_op jit(solution)/shard_map/all_to_all | solution.py:257
  285.1 7.7 %shard_map.71.refs_1_ = f32[512,1536]{1,0:T(8,128)} custom-call(f32[512,512]{1,0:T(8,128)} %fusion.7.scores_ref, f32[16,512,8]{2,1,0:T(8,128)} %bitcast.98, f32[128,512]{1,0:T(8,128)} %bitcast.115, f32[128,512]{1,0:T(8,128)} %get-tuple-element.50.stept_ref, bf16[512,1536]{1,0:T(8,128)(2,1)} %gather_fusion.10, f32[1,8192]{1,0:T(1,128)} %reshape_reshape.6.skip_ref), custom_call_target="tpu_custom_call" | custom-call | tf_op jit(solution)/shard_map/pallas_call | solution.py:124
  292.9 6.8 %shard_map.73.refs_0_ = bf16[512,8192]{1,0:T(8,128)(2,1)} custom-call(s32[1]{0:T(128)} %bitcast.place_ref, bf16[512,8192]{1,0:T(8,128)(2,1)} %shard_map.70.refs_0_, f32[512,2048]{1,0:T(8,128)} %shard_map.68.refs_1_, bf16[8,16,144,128]{3,2,1,0:T(8,128)(2,1)} %bitcast.130, f32[16,512,8]{2,1,0:T(8,128)} %bitcast.99, ...), custom_call_target="tpu_custom_call", output_to_operand_aliasing={{}: (1, {})} | custom-call | tf_op jit(solution)/shard_map/pallas_call | solution.py:157
  299.7 2.6 gather_fusion.11
  302.3 2.7 shard_map.77
  305.0 4.7 %collective-permute-start = (bf16[4,144,128]{2,1,0:T(8,128)(2,1)}, bf16[4,144,128]{2,1,0:T(8,128)(2,1)S(1)}, u32[]{:S(2)}, u32[]{:S(2)}) collective-permute-start(bf16[4,144,128]{2,1,0:T(8,128)(2,1)} %shard_map.77), channel_id=1, source_target_pairs={{0,16},{16,32},{32,48},{48,64},{64,80},{80,96},{96,112},{1,17},{17... | collective-permute-start | bytes 442376 | tf_op jit(solution)/shard_map/ppermute | solution.py:187
  309.7 4.1 %shard_map.76.refs_1_ = f32[512,512]{1,0:T(8,128)} custom-call(f32[512,512]{1,0:T(8,128)} %fusion.7.scores_ref, f32[16,512,8]{2,1,0:T(8,128)} %bitcast.100, f32[128,512]{1,0:T(8,128)} %bitcast.116, f32[128,512]{1,0:T(8,128)} %get-tuple-element.50.stept_ref, bf16[512,512]{1,0:T(8,128)(2,1)} %gather_fusion.11, f32[1,8192]{1,0:T(1,128)} %reshape_reshape.6.skip_ref), custom_call_target="tpu_custom_call" | custom-call | tf_op jit(solution)/shard_map/pallas_call | solution.py:124
  313.8 3.3 collective-permute-start.1
  317.1 3.5 collective-permute-start.2
  325.3 2.1 collective-permute-done.3
  327.4 2.2 collective-permute-done.4
  329.6 3.1 collective-permute-done.5
  332.8 6.2 %shard_map.75.refs_0_ = bf16[512,8192]{1,0:T(8,128)(2,1)} custom-call(s32[1]{0:T(128)} %bitcast.place_ref, bf16[512,8192]{1,0:T(8,128)(2,1)} %shard_map.73.refs_0_, f32[512,1536]{1,0:T(8,128)} %shard_map.71.refs_1_, bf16[8,12,144,128]{3,2,1,0:T(8,128)(2,1)} %bitcast.131, f32[16,512,8]{2,1,0:T(8,128)} %bitcast.101, ...), custom_call_target="tpu_custom_call", output_to_operand_aliasing={{}: (1, {})} | custom-call | tf_op jit(solution)/shard_map/pallas_call | solution.py:157
  339.0 3.1 shard_map.78
  (83 shorter events, 20.9 us)
Async XLA Ops:
  12.7 33.4 %all-to-all-start.2 = ((bf16[16,48,384]{2,1,0:T(8,128)(2,1)}), bf16[16,48,384]{2,1,0:T(8,128)(2,1)S(1)}, u32[]{:S(2)}, u32[]{:S(2)}) async-start(bf16[16,48,384]{2,1,0:T(8,128)(2,1)} %bitcast.8), calls=%async_computation.2 | async-start | bytes 1179648 | tf_op jit(solution)/shard_map/all_to_all | solution.py:180
  46.1 17.9 %copy-start.4 = (f32[128]{0:T(128)S(1)}, f32[128]{0:T(128)}, u32[]{:S(2)}) copy-start(f32[128]{0:T(128)} %param.9) | copy-start | bytes 1540
  46.1 51.8 %all-to-all-start = ((bf16[16,48,2048]{2,1,0:T(8,128)(2,1)}), bf16[16,48,2048]{2,1,0:T(8,128)(2,1)}, u32[]{:S(2)}, u32[]{:S(2)}) async-start(bf16[16,48,2048]{2,1,0:T(8,128)(2,1)} %bitcast.118), calls=%async_computation | async-start | bytes 6291456 | tf_op jit(solution)/shard_map/all_to_all | solution.py:257
  52.8 138.9 %all-gather.9.cloned.1.call-start = ((), (), s32[]{:S(2)}) async-start(), calls=%async_computation.6 | async-start | bytes 5308416 | tf_op jit(solution)/shard_map/all_gather | solution.py:279
  67.6 53.2 %copy-start = (f32[16,8,4,128]{3,1,2,0:T(8,128)}, f32[16,8,4,128]{3,1,2,0:T(8,128)S(1)}, u32[]{:S(2)}) copy-start(f32[16,8,4,128]{3,1,2,0:T(8,128)S(1)} %copy.51) | copy-start | bytes 786436
  111.1 4.7 %copy-start.3 = (f32[128]{0:T(128)S(1)}, f32[128]{0:T(128)}, u32[]{:S(2)}) copy-start(f32[128]{0:T(128)} %param.10) | copy-start | bytes 1540
  111.1 46.4 %all-to-all-start.1 = ((bf16[16,48,2048]{2,1,0:T(8,128)(2,1)}), bf16[16,48,2048]{2,1,0:T(8,128)(2,1)}, u32[]{:S(2)}, u32[]{:S(2)}) async-start(bf16[16,48,2048]{2,1,0:T(8,128)(2,1)} %bitcast.117), calls=%async_computation.1 | async-start | bytes 6291456 | tf_op jit(solution)/shard_map/all_to_all | solution.py:257
  115.6 135.9 %all-gather.11.cloned.1.call-start = ((), (), s32[]{:S(2)}) async-start(), calls=%async_computation.7 | async-start | bytes 5308416 | tf_op jit(solution)/shard_map/all_gather | solution.py:279
  170.6 47.5 %all-to-all-start.3 = ((bf16[16,48,2048]{2,1,0:T(8,128)(2,1)}), bf16[16,48,2048]{2,1,0:T(8,128)(2,1)}, u32[]{:S(2)}, u32[]{:S(2)}) async-start(bf16[16,48,2048]{2,1,0:T(8,128)(2,1)} %bitcast.119), calls=%async_computation.3 | async-start | bytes 6291456 | tf_op jit(solution)/shard_map/all_to_all | solution.py:257
  176.3 116.6 %all-gather.13.cloned.1.call-start = ((), (), s32[]{:S(2)}) async-start(), calls=%async_computation.8 | async-start | bytes 5308416 | tf_op jit(solution)/shard_map/all_gather | solution.py:279
  231.4 35.9 %all-to-all-start.4 = ((bf16[16,48,1536]{2,1,0:T(8,128)(2,1)}), bf16[16,48,1536]{2,1,0:T(8,128)(2,1)}, u32[]{:S(2)}, u32[]{:S(2)}) async-start(bf16[16,48,1536]{2,1,0:T(8,128)(2,1)} %bitcast.44), calls=%async_computation.4 | async-start | bytes 4718592 | tf_op jit(solution)/shard_map/all_to_all | solution.py:257
  237.1 95.7 %all-gather.15.cloned.1.call-start = ((), (), s32[]{:S(2)}) async-start(), calls=%async_computation.9 | async-start | bytes 3981312 | tf_op jit(solution)/shard_map/all_gather | solution.py:279
  278.4 21.3 %all-to-all-start.5 = ((bf16[16,48,512]{2,1,0:T(8,128)(2,1)}), bf16[16,48,512]{2,1,0:T(8,128)(2,1)S(1)}, u32[]{:S(2)}, u32[]{:S(2)}) async-start(bf16[16,48,512]{2,1,0:T(8,128)(2,1)} %bitcast.47), calls=%async_computation.5 | async-start | bytes 1572864 | tf_op jit(solution)/shard_map/all_to_all | solution.py:257
  305.0 8.8 %copy-start.2 = (bf16[4,144,128]{2,1,0:T(8,128)(2,1)S(1)}, bf16[4,144,128]{2,1,0:T(8,128)(2,1)}, u32[]{:S(2)}) copy-start(bf16[4,144,128]{2,1,0:T(8,128)(2,1)} %shard_map.77) | copy-start | bytes 442372
  305.0 18.2 %collective-permute-start = (bf16[4,144,128]{2,1,0:T(8,128)(2,1)}, bf16[4,144,128]{2,1,0:T(8,128)(2,1)S(1)}, u32[]{:S(2)}, u32[]{:S(2)}) collective-permute-start(bf16[4,144,128]{2,1,0:T(8,128)(2,1)} %shard_map.77), channel_id=1, source_target_pairs={{0,16},{16,32},{32,48},{48,64},{64,80},{80,96},{96,112},{1,17},{17... | collective-permute-start | bytes 442376 | tf_op jit(solution)/shard_map/ppermute | solution.py:187
  313.8 10.7 %collective-permute-start.1 = (bf16[4,144,128]{2,1,0:T(8,128)(2,1)S(1)}, bf16[4,144,128]{2,1,0:T(8,128)(2,1)S(1)}, u32[]{:S(2)}, u32[]{:S(2)}) collective-permute-start(bf16[4,144,128]{2,1,0:T(8,128)(2,1)S(1)} %copy-done.2), channel_id=1, source_target_pairs={{0,32},{16,48},{32,64},{48,80},{64,96},{80,112},{1,33},{17,49},{33... | collective-permute-start | bytes 442376 | tf_op jit(solution)/shard_map/ppermute | solution.py:187
  317.1 8.1 %collective-permute-start.2 = (bf16[4,144,128]{2,1,0:T(8,128)(2,1)S(1)}, bf16[4,144,128]{2,1,0:T(8,128)(2,1)S(1)}, u32[]{:S(2)}, u32[]{:S(2)}) collective-permute-start(bf16[4,144,128]{2,1,0:T(8,128)(2,1)S(1)} %copy-done.2), channel_id=1, source_target_pairs={{0,48},{16,64},{32,80},{48,96},{64,112},{1,49},{17,65},{33,81},{49... | collective-permute-start | bytes 442376 | tf_op jit(solution)/shard_map/ppermute | solution.py:187
  320.6 6.8 %collective-permute-start.3 = (bf16[4,144,128]{2,1,0:T(8,128)(2,1)S(1)}, bf16[4,144,128]{2,1,0:T(8,128)(2,1)S(1)}, u32[]{:S(2)}, u32[]{:S(2)}) collective-permute-start(bf16[4,144,128]{2,1,0:T(8,128)(2,1)S(1)} %copy-done.2), channel_id=1, source_target_pairs={{0,64},{16,80},{32,96},{48,112},{1,65},{17,81},{33,97},{49,113},{2... | collective-permute-start | bytes 442376 | tf_op jit(solution)/shard_map/ppermute | solution.py:187
  321.9 7.7 %collective-permute-start.4 = (bf16[4,144,128]{2,1,0:T(8,128)(2,1)S(1)}, bf16[4,144,128]{2,1,0:T(8,128)(2,1)S(1)}, u32[]{:S(2)}, u32[]{:S(2)}) collective-permute-start(bf16[4,144,128]{2,1,0:T(8,128)(2,1)S(1)} %copy-done.2), channel_id=1, source_target_pairs={{0,80},{16,96},{32,112},{1,81},{17,97},{33,113},{2,82},{18,98},{34... | collective-permute-start | bytes 442376 | tf_op jit(solution)/shard_map/ppermute | solution.py:187
  323.2 9.5 %collective-permute-start.5 = (bf16[4,144,128]{2,1,0:T(8,128)(2,1)S(1)}, bf16[4,144,128]{2,1,0:T(8,128)(2,1)S(1)}, u32[]{:S(2)}, u32[]{:S(2)}) collective-permute-start(bf16[4,144,128]{2,1,0:T(8,128)(2,1)S(1)} %copy-done.2), channel_id=1, source_target_pairs={{0,96},{16,112},{1,97},{17,113},{2,98},{18,114},{3,99},{19,115},{4... | collective-permute-start | bytes 442376 | tf_op jit(solution)/shard_map/ppermute | solution.py:187
  324.5 8.2 %collective-permute-start.6 = (bf16[4,144,128]{2,1,0:T(8,128)(2,1)S(1)}, bf16[4,144,128]{2,1,0:T(8,128)(2,1)S(1)}, u32[]{:S(2)}, u32[]{:S(2)}) collective-permute-start(bf16[4,144,128]{2,1,0:T(8,128)(2,1)S(1)} %copy-done.2), channel_id=1, source_target_pairs={{0,112},{1,113},{2,114},{3,115},{4,116},{5,117},{6,118},{7,119},{8... | collective-permute-start | bytes 442376 | tf_op jit(solution)/shard_map/ppermute | solution.py:187
  332.8 6.2 %copy-start.1 = (bf16[7,4,144,128]{3,2,1,0:T(8,128)(2,1)}, bf16[7,4,144,128]{3,2,1,0:T(8,128)(2,1)S(1)}, u32[]{:S(2)}) copy-start(bf16[7,4,144,128]{3,2,1,0:T(8,128)(2,1)S(1)} %bitcast_dynamic-update-slice_fusion.refs_2_) | copy-start | bytes 3096580
Sparse Core Ops, SparseCore 0:
  111.2 34.2 all-gather.8
  170.8 35.9 all-gather.10
  231.5 36.0 all-gather.12
  278.5 31.2 all-gather.14

commit v5 on v3

--- a/solution.py
+++ b/solution.py
@@ -16,12 +16,21 @@
     return jnp.where(lane_low, low, high)
 
 
-def carried_kernel(bt_ref, facg_ref, decay_ref, tok_ref, out_ref):
+def carried_kernel(bt_ref, facg_ref, decay_ref, onehot_ref, arr_ref, out_ref, tok_ref):
     pairs = out_ref.shape[0]
     state_size = bt_ref.shape[0]
+    ordered = jnp.dot(onehot_ref[...], arr_ref[...], preferred_element_type=jnp.float32)
+    tok_ref[...] = ordered.astype(tok_ref.dtype)
+    factors = facg_ref[0]
+    heads = factors.shape[1]
+    head_row = lax.broadcasted_iota(jnp.int32, (heads, 128), 0)
+    lane_high = (lax.broadcasted_iota(jnp.int32, (heads, 128), 1) >= 64).astype(jnp.int32)
     for q in range(pairs):
-        x = tok_ref[:, 128 * q : 128 * (q + 1)].astype(jnp.float32)
-        factor = lane_pick(facg_ref[0, :, 2 * q : 2 * q + 1], facg_ref[0, :, 2 * q + 1 : 2 * q + 2])
+        x = ordered[:, 128 * q : 128 * (q + 1)]
+        spread = (head_row == 2 * q + lane_high).astype(jnp.float32)
+        factor = jnp.dot(
+            factors, spread, precision=lax.Precision.HIGHEST, preferred_element_type=jnp.float32
+        )
         scaled = (factor * x).astype(jnp.bfloat16)
         out_ref[q, 0:state_size, :] = jnp.dot(
             bt_ref[...], scaled, preferred_element_type=jnp.float32
@@ -92,8 +101,9 @@
     return pltpu.CompilerParams(dimension_semantics=("arbitrary",))
 
 
-def carried_call(bt, fac_grouped, decay_lanes, tokens, first):
-    length, width = tokens.shape
+def carried_call(bt, fac_grouped, decay_lanes, onehot, arrived, first):
+    rows, width = arrived.shape
+    length = onehot.shape[0]
     groups = width // (GROUP * 64)
     state_size = bt.shape[0]
     return pl.pallas_call(
@@ -103,12 +113,19 @@
             pl.BlockSpec(bt.shape, lambda g: (0, 0)),
             pl.BlockSpec((1, length, GROUP), lambda g: (g + first, 0, 0)),
             pl.BlockSpec((1, GROUP * 64), lambda g: (0, g + first)),
+            pl.BlockSpec(onehot.shape, lambda g: (0, 0)),
+            pl.BlockSpec((rows, GROUP * 64), lambda g: (0, g)),
+        ],
+        out_specs=[
+            pl.BlockSpec((GROUP // 2, state_size + EXTRA, 128), lambda g: (g, 0, 0)),
             pl.BlockSpec((length, GROUP * 64), lambda g: (0, g)),
         ],
-        out_specs=pl.BlockSpec((GROUP // 2, state_size + EXTRA, 128), lambda g: (g, 0, 0)),
-        out_shape=jax.ShapeDtypeStruct((width // 128, state_size + EXTRA, 128), jnp.bfloat16),
+        out_shape=[
+            jax.ShapeDtypeStruct((width // 128, state_size + EXTRA, 128), jnp.bfloat16),
+            jax.ShapeDtypeStruct((length, width), jnp.bfloat16),
+        ],
         compiler_params=arbitrary(),
-    )(bt, fac_grouped, decay_lanes, tokens)
+    )(bt, fac_grouped, decay_lanes, onehot, arrived)
 
 
 def local_call(scores, cum_grouped, cum_t, step_t, tokens, skip_lanes, first):
@@ -225,6 +242,8 @@
     scores = jnp.dot(readout, inputs.T, preferred_element_type=jnp.float32)
     bt = inputs.T
     place = place_index.astype(jnp.int32).reshape(1)
+    slots = jnp.arange(stream_count * capacity, dtype=jnp.int32)
+    onehot = (flat_rows[:, None] == slots[None, :]).astype(jnp.bfloat16)
 
     sizes = CHUNK_GROUPS
     firsts = [sum(sizes[:c]) for c in range(len(sizes))]
@@ -257,8 +276,9 @@
             sends[c + 1] = tied["send"]
         if c >= 2:
             result = tied["result"]
-        chunk_tokens = receive_rows(arrived, flat_rows)
-        carried = carried_call(bt, fac_grouped, decay_lanes, chunk_tokens, firsts[c])
+        carried, chunk_tokens = carried_call(
+            bt, fac_grouped, decay_lanes, onehot, arrived.reshape(-1, arrived.shape[2]), firsts[c]
+        )
         gathers.append(lax.all_gather(carried, "pos"))
         partials.append(
             local_call(scores, cum_grouped, cum_t, step_t, chunk_tokens, skip_lanes, firsts[c])

time: 348 us -> 338 us (0.971); the launches traced: 341 us -> 336 us
  Pallas kernels: 94.5 us -> 126 us
  local copies, waits for them, and re-layouts: 83.6 us -> 56.5 us
  waiting for transfers between devices: 97.1 us -> 85.7 us
    pallas_call x5, Pallas kernels: 24.3 us -> 56.1 us  [carried_call(): pl.pallas_call(carried_kernel, grid=(groups,), in_specs=[pl.BlockSpec(bt....]
    gather x6 -> x1, local copies, waits for them, and re-layouts: 30.1 us -> 1.93 us  [receive_rows(): return jnp.take(arrived.reshape(-1, width), flat_rows, axis=0, mode='clip')]
    all_to_all x5, waiting for transfers between devices: 77.5 us -> 66.4 us  [on_device(): lax.all_to_all(sends[c], 'stream', split_axis=0, concat_axis=0, tiled=True)]
    sub x1 -> x2, other arithmetic: 0.01 us -> 5.65 us  [on_device(): flat_rows = source * capacity + positions - source_start]
    gather x3 -> x2, other arithmetic: 9.83 us -> 4.48 us  [on_device(): source_start = jnp.take(recv_start, source)]
  transfers between devices with their start and end apart: 11 -> 11, of which waited for: 6 -> 5; matrix products, arithmetic and copies ran while one was open for 25% -> 19% of each run, Pallas kernels for 25% -> 33%
where the time goes in v5:
time: 338 us; the launch traced here: 336 us
  Pallas kernels  126 us (37%)
  waiting for transfers between devices  85.7 us (25%)
  local copies, waits for them, and re-layouts  56.5 us (17%)
  starting transfers between devices  38.3 us (11%)
  other arithmetic  14.7 us (4%)
  between operations  13.4 us (4%)
    all_to_all x5, waiting for transfers between devices, on_device(): lax.all_to_all(sends[c], 'stream', split_axis=0, concat_axis=0, tiled=True)  66.4 us
    pallas_call x5, Pallas kernels, carried_call(): pl.pallas_call(carried_kernel, grid=(groups,), in_specs=[pl.BlockSpec(bt....  56.1 us
    pallas_call x5, Pallas kernels, local_call(): pl.pallas_call(local_kernel, grid=(groups,), in_specs=[pl.BlockSpec((leng...  40.6 us
    gather x6, local copies, waits for them, and re-layouts, send_rows(): jnp.take(rows, pick_rows, axis=0, mode='clip')  32.6 us
    pallas_call x5, Pallas kernels, combine_call(): pl.pallas_call(combine_kernel, grid=(groups,), in_specs=[pl.BlockSpec(mem...  29.5 us
    all_to_all x5, starting transfers between devices, on_device(): lax.all_to_all(sends[c], 'stream', split_axis=0, concat_axis=0, tiled=True)  29.3 us
    all_gather x5, waiting for transfers between devices, on_device(): gathers.append(lax.all_gather(carried, 'pos'))  19.2 us
    slice x3, local copies, waits for them, and re-layouts, on_device(): tokens[:, f * group_width:(f + n) * group_width]  8.57 us
  transfers between devices with their start and end apart: 11, of which 5 were waited for; matrix products, arithmetic and copies ran while one was open for 19% of the time, Pallas kernels for 33%

profile of v5, /device:TPU:1, one launch (start us, length us, event | category | flops | bytes accessed | tf_op | source)
XLA Modules:
  0.0 336.2 jit_solution(17065001742212687971)
XLA Ops:
  8.3 1.1 pad_maximum_fusion
  9.4 3.2 gather_fusion.2
  12.6 8.4 %all-to-all-start.2 = ((bf16[16,48,384]{2,1,0:T(8,128)(2,1)}), bf16[16,48,384]{2,1,0:T(8,128)(2,1)S(1)}, u32[]{:S(2)}, u32[]{:S(2)}) async-start(bf16[16,48,384]{2,1,0:T(8,128)(2,1)} %bitcast.8), calls=%async_computation.2 | async-start | bytes 1179648 | tf_op jit(solution)/shard_map/all_to_all | solution.py:190
  21.1 6.0 %fusion.13 = (bf16[512,2048]{1,0:T(8,128)(2,1)S(1)}, bf16[512,2048]{1,0:T(8,128)(2,1)}, bf16[512,2048]{1,0:T(8,128)(2,1)}) fusion(bf16[512,8192]{1,0:T(8,128)(2,1)} %bitcast.106), kind=kLoop, calls=%fused_computation.62 | loop fusion | bytes 12582912 | tf_op jit(solution)/shard_map/slice | solution.py:252
  27.1 0.9 dynamic-slice_reduce_fusion
  28.1 9.0 %gather_fusion = bf16[768,2048]{1,0:T(8,128)(2,1)} fusion(bf16[512,2048]{1,0:T(8,128)(2,1)} %get-tuple-element.64, s32[1024]{0:T(1024)S(1)} %pad_clamp_fusion.1), kind=kCustom, calls=%fused_computation | custom fusion | bytes 6294528 | tf_op jit(solution)/shard_map/jit(_take)/gather | solution.py:180
  37.1 6.7 %all-to-all-start = ((bf16[16,48,2048]{2,1,0:T(8,128)(2,1)}), bf16[16,48,2048]{2,1,0:T(8,128)(2,1)}, u32[]{:S(2)}, u32[]{:S(2)}) async-start(bf16[16,48,2048]{2,1,0:T(8,128)(2,1)} %bitcast.103), calls=%async_computation | async-start | bytes 6291456 | tf_op jit(solution)/shard_map/all_to_all | solution.py:260
  44.6 9.0 %gather_fusion.1 = bf16[768,2048]{1,0:T(8,128)(2,1)} fusion(bf16[512,2048]{1,0:T(8,128)(2,1)} %get-tuple-element.63, s32[1024]{0:T(1024)S(1)} %pad_clamp_fusion.1), kind=kCustom, calls=%fused_computation.1 | custom fusion | bytes 6294528 | tf_op jit(solution)/shard_map/jit(_take)/gather | solution.py:180
  53.6 4.4 %compare_select_fusion.2 = (s32[512,1]{0,1:T(1,128)S(1)}, s32[512,1]{0,1:T(1,128)S(1)}) fusion(s32[]{:T(128)} %bitcast.21, s32[]{:T(128)} %bitcast.22, s32[]{:T(128)} %bitcast.23, s32[]{:T(128)} %bitcast.24, s32[]{:T(128)} %bitcast.25, s32[]{:T(128)} %bitcast.27, s32[]{:T(128)} %bitcast.26, s32[512,1]{0,1:T(1,128)S(1)} %bitcast.126), kind=kLoop, calls=%fused_computation.36 | loop fusion | flops 7680 | bytes 6172 | tf_op jit(solution)/shard_map/jit(_take)/gather | solution.py:216
  58.1 5.6 %select_subtract_fusion = (s32[512]{0:T(512)S(1)}, s32[512]{0:T(512)S(1)}) fusion(s32[512]{0:T(512)S(1)} %convert_reduce_fusion, pred[512]{0:T(512)(128)(4,1)S(1)} %get-tuple-element.56, pred[512]{0:T(512)(128)(4,1)S(1)} %get-tuple-element.55, pred[512]{0:T(512)(128)(4,1)S(1)} %get-tuple-element.57, pred[512]{0:T(512)(128)(4,1)S(1)} %get-tuple-element.54, ...), kind=kLoop, calls=%fused_computation.51 | loop fusion | flops 10240 | bytes 12836 | tf_op jit(solution)/shard_map/sub | solution.py:217
  63.8 1.1 fusion.onehot_ref
  64.9 1.9 gather_fusion.3
  66.8 0.8 fusion.14
  68.7 0.9 multiply_bitcast_fusion
  69.6 2.6 copy.41
  73.0 1.7 copy.42
  74.7 14.3 %all-to-all-done = bf16[16,48,2048]{2,1,0:T(8,128)(2,1)} async-done(((bf16[16,48,2048]{2,1,0:T(8,128)(2,1)}), bf16[16,48,2048]{2,1,0:T(8,128)(2,1)}, u32[]{:S(2)}, u32[]{:S(2)}) %all-to-all-start) | async-done | bytes 3145760 | tf_op jit(solution)/shard_map/all_to_all | solution.py:260
  89.0 13.5 %shard_map.64 = (bf16[16,144,128]{2,1,0:T(8,128)(2,1)}, bf16[512,2048]{1,0:T(8,128)(2,1)}) custom-call(bf16[128,512]{1,0:T(8,128)(2,1)} %bitcast.109, f32[16,512,8]{2,1,0:T(8,128)} %bitcast.90, f32[1,8192]{1,0:T(1,128)} %reshape_reshape.6.decay_ref, bf16[512,768]{1,0:T(8,128)(2,1)} %fusion.onehot_ref, bf16[768,2048]{1,0:T(8,128)(2,1)} %bitcast.40.arr_ref), custom_call_target="tpu_custom_call" | custom-call | tf_op jit(solution)/shard_map/pallas_call | solution.py:109
  102.5 4.5 %all-to-all-start.1 = ((bf16[16,48,2048]{2,1,0:T(8,128)(2,1)}), bf16[16,48,2048]{2,1,0:T(8,128)(2,1)}, u32[]{:S(2)}, u32[]{:S(2)}) async-start(bf16[16,48,2048]{2,1,0:T(8,128)(2,1)} %bitcast.104), calls=%async_computation.1 | async-start | bytes 6291456 | tf_op jit(solution)/shard_map/all_to_all | solution.py:260
  108.0 4.2 %gather_fusion.4 = bf16[768,2048]{1,0:T(8,128)(2,1)} fusion(bf16[512,2048]{1,0:T(8,128)(2,1)S(1)} %get-tuple-element.62, s32[1024]{0:T(1024)S(1)} %pad_clamp_fusion.1), kind=kCustom, calls=%fused_computation.4 | custom fusion | bytes 6294528 | tf_op jit(solution)/shard_map/jit(_take)/gather | solution.py:180
  112.3 2.7 copy.40
  115.0 1.3 fusion.8.scores_ref
  116.3 9.4 %shard_map.65.refs_0_ = f32[512,2048]{1,0:T(8,128)} custom-call(f32[512,512]{1,0:T(8,128)} %fusion.8.scores_ref, f32[16,512,8]{2,1,0:T(8,128)} %bitcast.80, f32[128,512]{1,0:T(8,128)} %bitcast.98, f32[128,512]{1,0:T(8,128)} %get-tuple-element.72.stept_ref, bf16[512,2048]{1,0:T(8,128)(2,1)} %get-tuple-element.29.tok_ref, f32[1,8192]{1,0:T(1,128)} %reshape_reshape.7.skip_ref), custom_call_target="tpu_custom_call" | custom-call | tf_op jit(solution)/shard_map/pallas_call | solution.py:134
  125.7 23.1 %all-to-all-done.1 = bf16[16,48,2048]{2,1,0:T(8,128)(2,1)} async-done(((bf16[16,48,2048]{2,1,0:T(8,128)(2,1)}), bf16[16,48,2048]{2,1,0:T(8,128)(2,1)}, u32[]{:S(2)}, u32[]{:S(2)}) %all-to-all-start.1) | async-done | bytes 3145760 | tf_op jit(solution)/shard_map/all_to_all | solution.py:260
  148.9 13.5 %shard_map.66 = (bf16[16,144,128]{2,1,0:T(8,128)(2,1)}, bf16[512,2048]{1,0:T(8,128)(2,1)}) custom-call(bf16[128,512]{1,0:T(8,128)(2,1)} %bitcast.110, f32[16,512,8]{2,1,0:T(8,128)} %bitcast.91, f32[1,8192]{1,0:T(1,128)} %reshape_reshape.6.decay_ref, bf16[512,768]{1,0:T(8,128)(2,1)} %fusion.onehot_ref, bf16[768,2048]{1,0:T(8,128)(2,1)} %bitcast.42.arr_ref), custom_call_target="tpu_custom_call" | custom-call | tf_op jit(solution)/shard_map/pallas_call | solution.py:109
  162.4 5.6 %all-to-all-start.3 = ((bf16[16,48,2048]{2,1,0:T(8,128)(2,1)}), bf16[16,48,2048]{2,1,0:T(8,128)(2,1)}, u32[]{:S(2)}, u32[]{:S(2)}) async-start(bf16[16,48,2048]{2,1,0:T(8,128)(2,1)} %bitcast.105), calls=%async_computation.3 | async-start | bytes 6291456 | tf_op jit(solution)/shard_map/all_to_all | solution.py:260
  168.1 1.5 slice.86
  169.6 3.9 %gather_fusion.5 = bf16[768,1536]{1,0:T(8,128)(2,1)} fusion(bf16[512,1536]{1,0:T(8,128)(2,1)S(1)} %slice.86, s32[1024]{0:T(1024)S(1)} %pad_clamp_fusion.1), kind=kCustom, calls=%fused_computation.5 | custom fusion | bytes 4721664 | tf_op jit(solution)/shard_map/jit(_take)/gather | solution.py:180
  173.5 9.6 %shard_map.67.refs_1_ = f32[512,2048]{1,0:T(8,128)} custom-call(f32[512,512]{1,0:T(8,128)} %fusion.8.scores_ref, f32[16,512,8]{2,1,0:T(8,128)} %bitcast.81, f32[128,512]{1,0:T(8,128)} %bitcast.99, f32[128,512]{1,0:T(8,128)} %get-tuple-element.72.stept_ref, bf16[512,2048]{1,0:T(8,128)(2,1)} %get-tuple-element.32.tok_ref, f32[1,8192]{1,0:T(1,128)} %reshape_reshape.7.skip_ref), custom_call_target="tpu_custom_call" | custom-call | tf_op jit(solution)/shard_map/pallas_call | solution.py:134
  183.1 6.8 %shard_map.68.refs_0_ = bf16[512,8192]{1,0:T(8,128)(2,1)} custom-call(s32[1]{0:T(128)} %bitcast.place_ref, f32[512,2048]{1,0:T(8,128)} %shard_map.65.refs_0_, bf16[8,16,144,128]{3,2,1,0:T(8,128)(2,1)} %bitcast.115, f32[16,512,8]{2,1,0:T(8,128)} %bitcast.82, bf16[512,128]{1,0:T(8,128)(2,1)} %get-tuple-element.65.refs_3_.refs_4_), custom_call_target="tpu_custom_call" | custom-call | tf_op jit(solution)/shard_map/pallas_call | solution.py:167
  190.0 20.0 %all-to-all-done.3 = bf16[16,48,2048]{2,1,0:T(8,128)(2,1)} async-done(((bf16[16,48,2048]{2,1,0:T(8,128)(2,1)}), bf16[16,48,2048]{2,1,0:T(8,128)(2,1)}, u32[]{:S(2)}, u32[]{:S(2)}) %all-to-all-start.3) | async-done | bytes 3145760 | tf_op jit(solution)/shard_map/all_to_all | solution.py:260
  210.0 13.5 %shard_map.69 = (bf16[16,144,128]{2,1,0:T(8,128)(2,1)}, bf16[512,2048]{1,0:T(8,128)(2,1)}) custom-call(bf16[128,512]{1,0:T(8,128)(2,1)} %bitcast.111, f32[16,512,8]{2,1,0:T(8,128)} %bitcast.92, f32[1,8192]{1,0:T(1,128)} %reshape_reshape.6.decay_ref, bf16[512,768]{1,0:T(8,128)(2,1)} %fusion.onehot_ref, bf16[768,2048]{1,0:T(8,128)(2,1)} %bitcast.45.arr_ref), custom_call_target="tpu_custom_call" | custom-call | tf_op jit(solution)/shard_map/pallas_call | solution.py:109
  223.5 5.7 %all-to-all-start.4 = ((bf16[16,48,1536]{2,1,0:T(8,128)(2,1)}), bf16[16,48,1536]{2,1,0:T(8,128)(2,1)}, u32[]{:S(2)}, u32[]{:S(2)}) async-start(bf16[16,48,1536]{2,1,0:T(8,128)(2,1)} %bitcast.44), calls=%async_computation.4 | async-start | bytes 4718592 | tf_op jit(solution)/shard_map/all_to_all | solution.py:260
  229.5 1.1 slice.87
  230.5 3.3 gather_fusion.6
  233.9 9.7 %shard_map.70.refs_1_ = f32[512,2048]{1,0:T(8,128)} custom-call(f32[512,512]{1,0:T(8,128)} %fusion.8.scores_ref, f32[16,512,8]{2,1,0:T(8,128)} %bitcast.83, f32[128,512]{1,0:T(8,128)} %bitcast.100, f32[128,512]{1,0:T(8,128)} %get-tuple-element.72.stept_ref, bf16[512,2048]{1,0:T(8,128)(2,1)} %get-tuple-element.36.tok_ref, f32[1,8192]{1,0:T(1,128)} %reshape_reshape.7.skip_ref), custom_call_target="tpu_custom_call" | custom-call | tf_op jit(solution)/shard_map/pallas_call | solution.py:134
  243.5 6.9 %shard_map.71.refs_0_ = bf16[512,8192]{1,0:T(8,128)(2,1)} custom-call(s32[1]{0:T(128)} %bitcast.place_ref, bf16[512,8192]{1,0:T(8,128)(2,1)} %shard_map.68.refs_0_, f32[512,2048]{1,0:T(8,128)} %shard_map.67.refs_1_, bf16[8,16,144,128]{3,2,1,0:T(8,128)(2,1)} %bitcast.114, f32[16,512,8]{2,1,0:T(8,128)} %bitcast.84, ...), custom_call_target="tpu_custom_call", output_to_operand_aliasing={{}: (1, {})} | custom-call | tf_op jit(solution)/shard_map/pallas_call | solution.py:167
  250.4 9.0 %all-to-all-done.4 = bf16[16,48,1536]{2,1,0:T(8,128)(2,1)} async-done(((bf16[16,48,1536]{2,1,0:T(8,128)(2,1)}), bf16[16,48,1536]{2,1,0:T(8,128)(2,1)}, u32[]{:S(2)}, u32[]{:S(2)}) %all-to-all-start.4) | async-done | bytes 2359328 | tf_op jit(solution)/shard_map/all_to_all | solution.py:260
  259.4 10.7 %shard_map.72 = (bf16[12,144,128]{2,1,0:T(8,128)(2,1)}, bf16[512,1536]{1,0:T(8,128)(2,1)}) custom-call(bf16[128,512]{1,0:T(8,128)(2,1)} %bitcast.112, f32[16,512,8]{2,1,0:T(8,128)} %bitcast.93, f32[1,8192]{1,0:T(1,128)} %reshape_reshape.6.decay_ref, bf16[512,768]{1,0:T(8,128)(2,1)} %fusion.onehot_ref, bf16[768,1536]{1,0:T(8,128)(2,1)} %bitcast.48.arr_ref), custom_call_target="tpu_custom_call" | custom-call | tf_op jit(solution)/shard_map/pallas_call | solution.py:109
  270.0 6.8 %all-to-all-start.5 = ((bf16[16,48,512]{2,1,0:T(8,128)(2,1)}), bf16[16,48,512]{2,1,0:T(8,128)(2,1)S(1)}, u32[]{:S(2)}, u32[]{:S(2)}) async-start(bf16[16,48,512]{2,1,0:T(8,128)(2,1)} %bitcast.47), calls=%async_computation.5 | async-start | bytes 1572864 | tf_op jit(solution)/shard_map/all_to_all | solution.py:260
  276.9 7.7 %shard_map.73.refs_1_ = f32[512,1536]{1,0:T(8,128)} custom-call(f32[512,512]{1,0:T(8,128)} %fusion.8.scores_ref, f32[16,512,8]{2,1,0:T(8,128)} %bitcast.85, f32[128,512]{1,0:T(8,128)} %bitcast.101, f32[128,512]{1,0:T(8,128)} %get-tuple-element.72.stept_ref, bf16[512,1536]{1,0:T(8,128)(2,1)} %get-tuple-element.41.tok_ref, f32[1,8192]{1,0:T(1,128)} %reshape_reshape.7.skip_ref), custom_call_target="tpu_custom_call" | custom-call | tf_op jit(solution)/shard_map/pallas_call | solution.py:134
  284.6 6.8 %shard_map.74.refs_0_ = bf16[512,8192]{1,0:T(8,128)(2,1)} custom-call(s32[1]{0:T(128)} %bitcast.place_ref, bf16[512,8192]{1,0:T(8,128)(2,1)} %shard_map.71.refs_0_, f32[512,2048]{1,0:T(8,128)} %shard_map.70.refs_1_, bf16[8,16,144,128]{3,2,1,0:T(8,128)(2,1)} %bitcast.116, f32[16,512,8]{2,1,0:T(8,128)} %bitcast.86, ...), custom_call_target="tpu_custom_call", output_to_operand_aliasing={{}: (1, {})} | custom-call | tf_op jit(solution)/shard_map/pallas_call | solution.py:167
  291.4 0.9 copy-done.1
  292.3 5.0 %shard_map.76 = (bf16[4,144,128]{2,1,0:T(8,128)(2,1)}, bf16[512,512]{1,0:T(8,128)(2,1)}) custom-call(bf16[128,512]{1,0:T(8,128)(2,1)} %bitcast.113, f32[16,512,8]{2,1,0:T(8,128)} %bitcast.94, f32[1,8192]{1,0:T(1,128)} %reshape_reshape.6.decay_ref, bf16[512,768]{1,0:T(8,128)(2,1)} %fusion.onehot_ref, bf16[768,512]{1,0:T(8,128)(2,1)} %bitcast.118), custom_call_target="tpu_custom_call" | custom-call | tf_op jit(solution)/shard_map/pallas_call | solution.py:109
  297.3 4.2 %shard_map.77.refs_1_ = f32[512,512]{1,0:T(8,128)} custom-call(f32[512,512]{1,0:T(8,128)} %fusion.8.scores_ref, f32[16,512,8]{2,1,0:T(8,128)} %bitcast.87, f32[128,512]{1,0:T(8,128)} %bitcast.102, f32[128,512]{1,0:T(8,128)} %get-tuple-element.72.stept_ref, bf16[512,512]{1,0:T(8,128)(2,1)} %get-tuple-element.47.tok_ref, f32[1,8192]{1,0:T(1,128)} %reshape_reshape.7.skip_ref), custom_call_target="tpu_custom_call" | custom-call | tf_op jit(solution)/shard_map/pallas_call | solution.py:134
  301.5 5.9 %shard_map.75.refs_0_ = bf16[512,8192]{1,0:T(8,128)(2,1)} custom-call(s32[1]{0:T(128)} %bitcast.place_ref, bf16[512,8192]{1,0:T(8,128)(2,1)} %shard_map.74.refs_0_, f32[512,1536]{1,0:T(8,128)} %shard_map.73.refs_1_, bf16[8,12,144,128]{3,2,1,0:T(8,128)(2,1)} %bitcast.117, f32[16,512,8]{2,1,0:T(8,128)} %bitcast.88, ...), custom_call_target="tpu_custom_call", output_to_operand_aliasing={{}: (1, {})} | custom-call | tf_op jit(solution)/shard_map/pallas_call | solution.py:167
  307.4 19.2 %all-gather.19.cloned.1.call-done = bf16[32,144,128]{2,1,0:T(8,128)(2,1)} async-done(((bf16[4,144,128]{2,1,0:T(8,128)(2,1)}), bf16[32,144,128]{2,1,0:T(8,128)(2,1)}) %all-gather.19.cloned.1.call-update) | async-done | bytes 1179664 | tf_op jit(solution)/shard_map/all_gather | solution.py:282
  326.5 3.1 shard_map.78
  (59 shorter events, 6.2 us)
Async XLA Ops:
  12.6 24.5 %all-to-all-start.2 = ((bf16[16,48,384]{2,1,0:T(8,128)(2,1)}), bf16[16,48,384]{2,1,0:T(8,128)(2,1)S(1)}, u32[]{:S(2)}, u32[]{:S(2)}) async-start(bf16[16,48,384]{2,1,0:T(8,128)(2,1)} %bitcast.8), calls=%async_computation.2 | async-start | bytes 1179648 | tf_op jit(solution)/shard_map/all_to_all | solution.py:190
  37.1 51.8 %all-to-all-start = ((bf16[16,48,2048]{2,1,0:T(8,128)(2,1)}), bf16[16,48,2048]{2,1,0:T(8,128)(2,1)}, u32[]{:S(2)}, u32[]{:S(2)}) async-start(bf16[16,48,2048]{2,1,0:T(8,128)(2,1)} %bitcast.103), calls=%async_computation | async-start | bytes 6291456 | tf_op jit(solution)/shard_map/all_to_all | solution.py:260
  43.9 139.3 %all-gather.11.cloned.1.call-start = ((), (), s32[]{:S(2)}) async-start(), calls=%async_computation.6 | async-start | bytes 5308416 | tf_op jit(solution)/shard_map/all_gather | solution.py:282
  44.6 19.2 %copy-start.3 = (f32[128]{0:T(128)S(1)}, f32[128]{0:T(128)}, u32[]{:S(2)}) copy-start(f32[128]{0:T(128)} %param.9) | copy-start | bytes 1540
  68.5 43.7 %copy-start = (f32[16,8,4,128]{3,1,2,0:T(8,128)}, f32[16,8,4,128]{3,1,2,0:T(8,128)S(1)}, u32[]{:S(2)}) copy-start(f32[16,8,4,128]{3,1,2,0:T(8,128)S(1)} %copy.52) | copy-start | bytes 786436
  102.5 4.7 %copy-start.2 = (f32[128]{0:T(128)S(1)}, f32[128]{0:T(128)}, u32[]{:S(2)}) copy-start(f32[128]{0:T(128)} %param.10) | copy-start | bytes 1540
  102.5 46.4 %all-to-all-start.1 = ((bf16[16,48,2048]{2,1,0:T(8,128)(2,1)}), bf16[16,48,2048]{2,1,0:T(8,128)(2,1)}, u32[]{:S(2)}, u32[]{:S(2)}) async-start(bf16[16,48,2048]{2,1,0:T(8,128)(2,1)} %bitcast.104), calls=%async_computation.1 | async-start | bytes 6291456 | tf_op jit(solution)/shard_map/all_to_all | solution.py:260
  107.0 136.5 %all-gather.13.cloned.1.call-start = ((), (), s32[]{:S(2)}) async-start(), calls=%async_computation.7 | async-start | bytes 5308416 | tf_op jit(solution)/shard_map/all_gather | solution.py:282
  162.4 47.6 %all-to-all-start.3 = ((bf16[16,48,2048]{2,1,0:T(8,128)(2,1)}), bf16[16,48,2048]{2,1,0:T(8,128)(2,1)}, u32[]{:S(2)}, u32[]{:S(2)}) async-start(bf16[16,48,2048]{2,1,0:T(8,128)(2,1)} %bitcast.105), calls=%async_computation.3 | async-start | bytes 6291456 | tf_op jit(solution)/shard_map/all_to_all | solution.py:260
  168.0 116.6 %all-gather.15.cloned.1.call-start = ((), (), s32[]{:S(2)}) async-start(), calls=%async_computation.8 | async-start | bytes 5308416 | tf_op jit(solution)/shard_map/all_gather | solution.py:282
  223.5 35.9 %all-to-all-start.4 = ((bf16[16,48,1536]{2,1,0:T(8,128)(2,1)}), bf16[16,48,1536]{2,1,0:T(8,128)(2,1)}, u32[]{:S(2)}, u32[]{:S(2)}) async-start(bf16[16,48,1536]{2,1,0:T(8,128)(2,1)} %bitcast.44), calls=%async_computation.4 | async-start | bytes 4718592 | tf_op jit(solution)/shard_map/all_to_all | solution.py:260
  229.2 72.3 %all-gather.17.cloned.1.call-start = ((), (), s32[]{:S(2)}) async-start(), calls=%async_computation.9 | async-start | bytes 3981312 | tf_op jit(solution)/shard_map/all_gather | solution.py:282
  270.0 21.3 %all-to-all-start.5 = ((bf16[16,48,512]{2,1,0:T(8,128)(2,1)}), bf16[16,48,512]{2,1,0:T(8,128)(2,1)S(1)}, u32[]{:S(2)}, u32[]{:S(2)}) async-start(bf16[16,48,512]{2,1,0:T(8,128)(2,1)} %bitcast.47), calls=%async_computation.5 | async-start | bytes 1572864 | tf_op jit(solution)/shard_map/all_to_all | solution.py:260
  276.8 49.7 %all-gather.19.cloned.1.call-start = ((), (), s32[]{:S(2)}) async-start(), calls=%async_computation.10 | async-start | bytes 1327104 | tf_op jit(solution)/shard_map/all_gather | solution.py:282
  291.4 0.9 copy-start.1
Sparse Core Ops, SparseCore 0:
  102.6 34.2 all-gather.10
  162.5 35.9 all-gather.12
  223.6 36.0 all-gather.14
  270.2 31.2 all-gather.16
  303.0 23.5 all-gather.18

commit v6 on v5

--- a/solution.py
+++ b/solution.py
@@ -21,16 +21,9 @@
     state_size = bt_ref.shape[0]
     ordered = jnp.dot(onehot_ref[...], arr_ref[...], preferred_element_type=jnp.float32)
     tok_ref[...] = ordered.astype(tok_ref.dtype)
-    factors = facg_ref[0]
-    heads = factors.shape[1]
-    head_row = lax.broadcasted_iota(jnp.int32, (heads, 128), 0)
-    lane_high = (lax.broadcasted_iota(jnp.int32, (heads, 128), 1) >= 64).astype(jnp.int32)
     for q in range(pairs):
         x = ordered[:, 128 * q : 128 * (q + 1)]
-        spread = (head_row == 2 * q + lane_high).astype(jnp.float32)
-        factor = jnp.dot(
-            factors, spread, precision=lax.Precision.HIGHEST, preferred_element_type=jnp.float32
-        )
+        factor = lane_pick(facg_ref[0, :, 2 * q : 2 * q + 1], facg_ref[0, :, 2 * q + 1 : 2 * q + 2])
         scaled = (factor * x).astype(jnp.bfloat16)
         out_ref[q, 0:state_size, :] = jnp.dot(
             bt_ref[...], scaled, preferred_element_type=jnp.float32

time: 338 us -> 310 us (0.917)
  Pallas kernels: 126 us -> 96.8 us
    pallas_call x5, Pallas kernels: 56.1 us -> 26.7 us  [carried_call(): pl.pallas_call(carried_kernel, grid=(groups,), in_specs=[pl.BlockSpec(bt....]
  transfers between devices with their start and end apart: 11 -> 11, of which waited for: 5 -> 6; matrix products, arithmetic and copies ran while one was open for 19% -> 21% of each run, Pallas kernels for 33% -> 28%
where the time goes in v6:
time: 310 us; the launch traced here: 309 us
  Pallas kernels  96.8 us (31%)
  waiting for transfers between devices  87.7 us (28%)
  local copies, waits for them, and re-layouts  56.5 us (18%)
  starting transfers between devices  38.3 us (12%)
  other arithmetic  14.7 us (5%)
  between operations  13.4 us (4%)
    all_to_all x5, waiting for transfers between devices, on_device(): lax.all_to_all(sends[c], 'stream', split_axis=0, concat_axis=0, tiled=True)  66.4 us
    pallas_call x5, Pallas kernels, local_call(): pl.pallas_call(local_kernel, grid=(groups,), in_specs=[pl.BlockSpec((leng...  40.6 us
    gather x6, local copies, waits for them, and re-layouts, send_rows(): jnp.take(rows, pick_rows, axis=0, mode='clip')  32.6 us
    pallas_call x5, Pallas kernels, combine_call(): pl.pallas_call(combine_kernel, grid=(groups,), in_specs=[pl.BlockSpec(mem...  29.4 us
    all_to_all x5, starting transfers between devices, on_device(): lax.all_to_all(sends[c], 'stream', split_axis=0, concat_axis=0, tiled=True)  29.3 us
    pallas_call x5, Pallas kernels, carried_call(): pl.pallas_call(carried_kernel, grid=(groups,), in_specs=[pl.BlockSpec(bt....  26.7 us
    all_gather x5, waiting for transfers between devices, on_device(): gathers.append(lax.all_gather(carried, 'pos'))  21.2 us
    slice x3, local copies, waits for them, and re-layouts, on_device(): tokens[:, f * group_width:(f + n) * group_width]  8.57 us
  transfers between devices with their start and end apart: 11, of which 6 were waited for; matrix products, arithmetic and copies ran while one was open for 21% of the time, Pallas kernels for 28%

profile of v6, /device:TPU:1, one launch (start us, length us, event | category | flops | bytes accessed | tf_op | source)
XLA Modules:
  0.0 308.7 jit_solution(10417379717427161855)
XLA Ops:
  8.3 1.1 pad_maximum_fusion
  9.4 3.2 %gather_fusion.2 = bf16[768,384]{1,0:T(8,128)(2,1)} fusion(bf16[512,384]{1,0:T(8,128)(2,1)S(1)} %pad_maximum_fusion, s32[1024]{0:T(1024)S(1)} %pad_clamp_fusion.1), kind=kCustom, calls=%fused_computation.2 | custom fusion | bytes 1182720 | tf_op jit(solution)/shard_map/jit(_take)/gather | solution.py:173
  12.6 8.4 %all-to-all-start.2 = ((bf16[16,48,384]{2,1,0:T(8,128)(2,1)}), bf16[16,48,384]{2,1,0:T(8,128)(2,1)S(1)}, u32[]{:S(2)}, u32[]{:S(2)}) async-start(bf16[16,48,384]{2,1,0:T(8,128)(2,1)} %bitcast.8), calls=%async_computation.2 | async-start | bytes 1179648 | tf_op jit(solution)/shard_map/all_to_all | solution.py:183
  21.1 6.0 %fusion.13 = (bf16[512,2048]{1,0:T(8,128)(2,1)S(1)}, bf16[512,2048]{1,0:T(8,128)(2,1)}, bf16[512,2048]{1,0:T(8,128)(2,1)}) fusion(bf16[512,8192]{1,0:T(8,128)(2,1)} %bitcast.106), kind=kLoop, calls=%fused_computation.62 | loop fusion | bytes 12582912 | tf_op jit(solution)/shard_map/slice | solution.py:245
  27.1 0.9 dynamic-slice_reduce_fusion
  28.1 9.0 %gather_fusion = bf16[768,2048]{1,0:T(8,128)(2,1)} fusion(bf16[512,2048]{1,0:T(8,128)(2,1)} %get-tuple-element.64, s32[1024]{0:T(1024)S(1)} %pad_clamp_fusion.1), kind=kCustom, calls=%fused_computation | custom fusion | bytes 6294528 | tf_op jit(solution)/shard_map/jit(_take)/gather | solution.py:173
  37.1 6.7 %all-to-all-start = ((bf16[16,48,2048]{2,1,0:T(8,128)(2,1)}), bf16[16,48,2048]{2,1,0:T(8,128)(2,1)}, u32[]{:S(2)}, u32[]{:S(2)}) async-start(bf16[16,48,2048]{2,1,0:T(8,128)(2,1)} %bitcast.103), calls=%async_computation | async-start | bytes 6291456 | tf_op jit(solution)/shard_map/all_to_all | solution.py:253
  44.6 9.0 %gather_fusion.1 = bf16[768,2048]{1,0:T(8,128)(2,1)} fusion(bf16[512,2048]{1,0:T(8,128)(2,1)} %get-tuple-element.63, s32[1024]{0:T(1024)S(1)} %pad_clamp_fusion.1), kind=kCustom, calls=%fused_computation.1 | custom fusion | bytes 6294528 | tf_op jit(solution)/shard_map/jit(_take)/gather | solution.py:173
  53.6 4.4 %compare_select_fusion.2 = (s32[512,1]{0,1:T(1,128)S(1)}, s32[512,1]{0,1:T(1,128)S(1)}) fusion(s32[]{:T(128)} %bitcast.21, s32[]{:T(128)} %bitcast.22, s32[]{:T(128)} %bitcast.23, s32[]{:T(128)} %bitcast.24, s32[]{:T(128)} %bitcast.25, s32[]{:T(128)} %bitcast.27, s32[]{:T(128)} %bitcast.26, s32[512,1]{0,1:T(1,128)S(1)} %bitcast.126), kind=kLoop, calls=%fused_computation.36 | loop fusion | flops 7680 | bytes 6172 | tf_op jit(solution)/shard_map/jit(_take)/gather | solution.py:209
  58.1 5.6 %select_subtract_fusion = (s32[512]{0:T(512)S(1)}, s32[512]{0:T(512)S(1)}) fusion(s32[512]{0:T(512)S(1)} %convert_reduce_fusion, pred[512]{0:T(512)(128)(4,1)S(1)} %get-tuple-element.56, pred[512]{0:T(512)(128)(4,1)S(1)} %get-tuple-element.55, pred[512]{0:T(512)(128)(4,1)S(1)} %get-tuple-element.57, pred[512]{0:T(512)(128)(4,1)S(1)} %get-tuple-element.54, ...), kind=kLoop, calls=%fused_computation.51 | loop fusion | flops 10240 | bytes 12836 | tf_op jit(solution)/shard_map/sub | solution.py:210
  63.8 1.1 fusion.onehot_ref
  64.9 1.9 gather_fusion.3
  68.7 0.9 multiply_bitcast_fusion
  69.6 2.6 copy.41
  73.0 1.7 copy.42
  74.7 14.3 %all-to-all-done = bf16[16,48,2048]{2,1,0:T(8,128)(2,1)} async-done(((bf16[16,48,2048]{2,1,0:T(8,128)(2,1)}), bf16[16,48,2048]{2,1,0:T(8,128)(2,1)}, u32[]{:S(2)}, u32[]{:S(2)}) %all-to-all-start) | async-done | bytes 3145760 | tf_op jit(solution)/shard_map/all_to_all | solution.py:253
  89.0 6.2 %shard_map.64 = (bf16[16,144,128]{2,1,0:T(8,128)(2,1)}, bf16[512,2048]{1,0:T(8,128)(2,1)}) custom-call(bf16[128,512]{1,0:T(8,128)(2,1)} %bitcast.109, f32[16,512,8]{2,1,0:T(8,128)} %bitcast.90, f32[1,8192]{1,0:T(1,128)} %reshape_reshape.6.decay_ref, bf16[512,768]{1,0:T(8,128)(2,1)} %fusion.onehot_ref, bf16[768,2048]{1,0:T(8,128)(2,1)} %bitcast.40.arr_ref), custom_call_target="tpu_custom_call" | custom-call | tf_op jit(solution)/shard_map/pallas_call | solution.py:102
  95.2 4.5 %all-to-all-start.1 = ((bf16[16,48,2048]{2,1,0:T(8,128)(2,1)}), bf16[16,48,2048]{2,1,0:T(8,128)(2,1)}, u32[]{:S(2)}, u32[]{:S(2)}) async-start(bf16[16,48,2048]{2,1,0:T(8,128)(2,1)} %bitcast.104), calls=%async_computation.1 | async-start | bytes 6291456 | tf_op jit(solution)/shard_map/all_to_all | solution.py:253
  100.7 4.2 %gather_fusion.4 = bf16[768,2048]{1,0:T(8,128)(2,1)} fusion(bf16[512,2048]{1,0:T(8,128)(2,1)S(1)} %get-tuple-element.62, s32[1024]{0:T(1024)S(1)} %pad_clamp_fusion.1), kind=kCustom, calls=%fused_computation.4 | custom fusion | bytes 6294528 | tf_op jit(solution)/shard_map/jit(_take)/gather | solution.py:173
  104.9 2.7 copy.40
  107.7 1.3 fusion.8.scores_ref
  109.0 9.4 %shard_map.65.refs_0_ = f32[512,2048]{1,0:T(8,128)} custom-call(f32[512,512]{1,0:T(8,128)} %fusion.8.scores_ref, f32[16,512,8]{2,1,0:T(8,128)} %bitcast.80, f32[128,512]{1,0:T(8,128)} %bitcast.98, f32[128,512]{1,0:T(8,128)} %get-tuple-element.72.stept_ref, bf16[512,2048]{1,0:T(8,128)(2,1)} %get-tuple-element.29.tok_ref, f32[1,8192]{1,0:T(1,128)} %reshape_reshape.7.skip_ref), custom_call_target="tpu_custom_call" | custom-call | tf_op jit(solution)/shard_map/pallas_call | solution.py:127
  118.4 23.2 %all-to-all-done.1 = bf16[16,48,2048]{2,1,0:T(8,128)(2,1)} async-done(((bf16[16,48,2048]{2,1,0:T(8,128)(2,1)}), bf16[16,48,2048]{2,1,0:T(8,128)(2,1)}, u32[]{:S(2)}, u32[]{:S(2)}) %all-to-all-start.1) | async-done | bytes 3145760 | tf_op jit(solution)/shard_map/all_to_all | solution.py:253
  141.6 6.2 %shard_map.66 = (bf16[16,144,128]{2,1,0:T(8,128)(2,1)}, bf16[512,2048]{1,0:T(8,128)(2,1)}) custom-call(bf16[128,512]{1,0:T(8,128)(2,1)} %bitcast.110, f32[16,512,8]{2,1,0:T(8,128)} %bitcast.91, f32[1,8192]{1,0:T(1,128)} %reshape_reshape.6.decay_ref, bf16[512,768]{1,0:T(8,128)(2,1)} %fusion.onehot_ref, bf16[768,2048]{1,0:T(8,128)(2,1)} %bitcast.42.arr_ref), custom_call_target="tpu_custom_call" | custom-call | tf_op jit(solution)/shard_map/pallas_call | solution.py:102
  147.8 5.6 %all-to-all-start.3 = ((bf16[16,48,2048]{2,1,0:T(8,128)(2,1)}), bf16[16,48,2048]{2,1,0:T(8,128)(2,1)}, u32[]{:S(2)}, u32[]{:S(2)}) async-start(bf16[16,48,2048]{2,1,0:T(8,128)(2,1)} %bitcast.105), calls=%async_computation.3 | async-start | bytes 6291456 | tf_op jit(solution)/shard_map/all_to_all | solution.py:253
  153.5 1.5 slice.86
  155.0 3.9 %gather_fusion.5 = bf16[768,1536]{1,0:T(8,128)(2,1)} fusion(bf16[512,1536]{1,0:T(8,128)(2,1)S(1)} %slice.86, s32[1024]{0:T(1024)S(1)} %pad_clamp_fusion.1), kind=kCustom, calls=%fused_computation.5 | custom fusion | bytes 4721664 | tf_op jit(solution)/shard_map/jit(_take)/gather | solution.py:173
  158.8 9.7 %shard_map.67.refs_1_ = f32[512,2048]{1,0:T(8,128)} custom-call(f32[512,512]{1,0:T(8,128)} %fusion.8.scores_ref, f32[16,512,8]{2,1,0:T(8,128)} %bitcast.81, f32[128,512]{1,0:T(8,128)} %bitcast.99, f32[128,512]{1,0:T(8,128)} %get-tuple-element.72.stept_ref, bf16[512,2048]{1,0:T(8,128)(2,1)} %get-tuple-element.32.tok_ref, f32[1,8192]{1,0:T(1,128)} %reshape_reshape.7.skip_ref), custom_call_target="tpu_custom_call" | custom-call | tf_op jit(solution)/shard_map/pallas_call | solution.py:127
  168.5 6.8 %shard_map.68.refs_0_ = bf16[512,8192]{1,0:T(8,128)(2,1)} custom-call(s32[1]{0:T(128)} %bitcast.place_ref, f32[512,2048]{1,0:T(8,128)} %shard_map.65.refs_0_, bf16[8,16,144,128]{3,2,1,0:T(8,128)(2,1)} %bitcast.115, f32[16,512,8]{2,1,0:T(8,128)} %bitcast.82, bf16[512,128]{1,0:T(8,128)(2,1)} %get-tuple-element.65.refs_3_.refs_4_), custom_call_target="tpu_custom_call" | custom-call | tf_op jit(solution)/shard_map/pallas_call | solution.py:160
  175.3 20.0 %all-to-all-done.3 = bf16[16,48,2048]{2,1,0:T(8,128)(2,1)} async-done(((bf16[16,48,2048]{2,1,0:T(8,128)(2,1)}), bf16[16,48,2048]{2,1,0:T(8,128)(2,1)}, u32[]{:S(2)}, u32[]{:S(2)}) %all-to-all-start.3) | async-done | bytes 3145760 | tf_op jit(solution)/shard_map/all_to_all | solution.py:253
  195.3 6.2 %shard_map.69 = (bf16[16,144,128]{2,1,0:T(8,128)(2,1)}, bf16[512,2048]{1,0:T(8,128)(2,1)}) custom-call(bf16[128,512]{1,0:T(8,128)(2,1)} %bitcast.111, f32[16,512,8]{2,1,0:T(8,128)} %bitcast.92, f32[1,8192]{1,0:T(1,128)} %reshape_reshape.6.decay_ref, bf16[512,768]{1,0:T(8,128)(2,1)} %fusion.onehot_ref, bf16[768,2048]{1,0:T(8,128)(2,1)} %bitcast.45.arr_ref), custom_call_target="tpu_custom_call" | custom-call | tf_op jit(solution)/shard_map/pallas_call | solution.py:102
  201.5 5.7 %all-to-all-start.4 = ((bf16[16,48,1536]{2,1,0:T(8,128)(2,1)}), bf16[16,48,1536]{2,1,0:T(8,128)(2,1)}, u32[]{:S(2)}, u32[]{:S(2)}) async-start(bf16[16,48,1536]{2,1,0:T(8,128)(2,1)} %bitcast.44), calls=%async_computation.4 | async-start | bytes 4718592 | tf_op jit(solution)/shard_map/all_to_all | solution.py:253
  207.5 1.1 slice.87
  208.6 3.3 %gather_fusion.6 = bf16[768,512]{1,0:T(8,128)(2,1)} fusion(bf16[512,512]{1,0:T(8,128)(2,1)S(1)} %slice.87, s32[1024]{0:T(1024)S(1)} %pad_clamp_fusion.1), kind=kCustom, calls=%fused_computation.6 | custom fusion | bytes 1575936 | tf_op jit(solution)/shard_map/jit(_take)/gather | solution.py:173
  211.9 9.7 %shard_map.70.refs_1_ = f32[512,2048]{1,0:T(8,128)} custom-call(f32[512,512]{1,0:T(8,128)} %fusion.8.scores_ref, f32[16,512,8]{2,1,0:T(8,128)} %bitcast.83, f32[128,512]{1,0:T(8,128)} %bitcast.100, f32[128,512]{1,0:T(8,128)} %get-tuple-element.72.stept_ref, bf16[512,2048]{1,0:T(8,128)(2,1)} %get-tuple-element.36.tok_ref, f32[1,8192]{1,0:T(1,128)} %reshape_reshape.7.skip_ref), custom_call_target="tpu_custom_call" | custom-call | tf_op jit(solution)/shard_map/pallas_call | solution.py:127
  221.6 6.9 %shard_map.71.refs_0_ = bf16[512,8192]{1,0:T(8,128)(2,1)} custom-call(s32[1]{0:T(128)} %bitcast.place_ref, bf16[512,8192]{1,0:T(8,128)(2,1)} %shard_map.68.refs_0_, f32[512,2048]{1,0:T(8,128)} %shard_map.67.refs_1_, bf16[8,16,144,128]{3,2,1,0:T(8,128)(2,1)} %bitcast.114, f32[16,512,8]{2,1,0:T(8,128)} %bitcast.84, ...), custom_call_target="tpu_custom_call", output_to_operand_aliasing={{}: (1, {})} | custom-call | tf_op jit(solution)/shard_map/pallas_call | solution.py:160
  228.4 9.0 %all-to-all-done.4 = bf16[16,48,1536]{2,1,0:T(8,128)(2,1)} async-done(((bf16[16,48,1536]{2,1,0:T(8,128)(2,1)}), bf16[16,48,1536]{2,1,0:T(8,128)(2,1)}, u32[]{:S(2)}, u32[]{:S(2)}) %all-to-all-start.4) | async-done | bytes 2359328 | tf_op jit(solution)/shard_map/all_to_all | solution.py:253
  237.4 5.2 %shard_map.72 = (bf16[12,144,128]{2,1,0:T(8,128)(2,1)}, bf16[512,1536]{1,0:T(8,128)(2,1)}) custom-call(bf16[128,512]{1,0:T(8,128)(2,1)} %bitcast.112, f32[16,512,8]{2,1,0:T(8,128)} %bitcast.93, f32[1,8192]{1,0:T(1,128)} %reshape_reshape.6.decay_ref, bf16[512,768]{1,0:T(8,128)(2,1)} %fusion.onehot_ref, bf16[768,1536]{1,0:T(8,128)(2,1)} %bitcast.48.arr_ref), custom_call_target="tpu_custom_call" | custom-call | tf_op jit(solution)/shard_map/pallas_call | solution.py:102
  242.6 6.8 %all-to-all-start.5 = ((bf16[16,48,512]{2,1,0:T(8,128)(2,1)}), bf16[16,48,512]{2,1,0:T(8,128)(2,1)S(1)}, u32[]{:S(2)}, u32[]{:S(2)}) async-start(bf16[16,48,512]{2,1,0:T(8,128)(2,1)} %bitcast.47), calls=%async_computation.5 | async-start | bytes 1572864 | tf_op jit(solution)/shard_map/all_to_all | solution.py:253
  249.4 7.7 %shard_map.73.refs_1_ = f32[512,1536]{1,0:T(8,128)} custom-call(f32[512,512]{1,0:T(8,128)} %fusion.8.scores_ref, f32[16,512,8]{2,1,0:T(8,128)} %bitcast.85, f32[128,512]{1,0:T(8,128)} %bitcast.101, f32[128,512]{1,0:T(8,128)} %get-tuple-element.72.stept_ref, bf16[512,1536]{1,0:T(8,128)(2,1)} %get-tuple-element.41.tok_ref, f32[1,8192]{1,0:T(1,128)} %reshape_reshape.7.skip_ref), custom_call_target="tpu_custom_call" | custom-call | tf_op jit(solution)/shard_map/pallas_call | solution.py:127
  257.2 6.8 %shard_map.74.refs_0_ = bf16[512,8192]{1,0:T(8,128)(2,1)} custom-call(s32[1]{0:T(128)} %bitcast.place_ref, bf16[512,8192]{1,0:T(8,128)(2,1)} %shard_map.71.refs_0_, f32[512,2048]{1,0:T(8,128)} %shard_map.70.refs_1_, bf16[8,16,144,128]{3,2,1,0:T(8,128)(2,1)} %bitcast.116, f32[16,512,8]{2,1,0:T(8,128)} %bitcast.86, ...), custom_call_target="tpu_custom_call", output_to_operand_aliasing={{}: (1, {})} | custom-call | tf_op jit(solution)/shard_map/pallas_call | solution.py:160
  263.9 0.9 copy-done.1
  264.8 3.1 shard_map.76
  267.9 4.1 %shard_map.77.refs_1_ = f32[512,512]{1,0:T(8,128)} custom-call(f32[512,512]{1,0:T(8,128)} %fusion.8.scores_ref, f32[16,512,8]{2,1,0:T(8,128)} %bitcast.87, f32[128,512]{1,0:T(8,128)} %bitcast.102, f32[128,512]{1,0:T(8,128)} %get-tuple-element.72.stept_ref, bf16[512,512]{1,0:T(8,128)(2,1)} %get-tuple-element.47.tok_ref, f32[1,8192]{1,0:T(1,128)} %reshape_reshape.7.skip_ref), custom_call_target="tpu_custom_call" | custom-call | tf_op jit(solution)/shard_map/pallas_call | solution.py:127
  272.1 1.9 all-gather.17.cloned.1.call-done
  274.0 5.9 %shard_map.75.refs_0_ = bf16[512,8192]{1,0:T(8,128)(2,1)} custom-call(s32[1]{0:T(128)} %bitcast.place_ref, bf16[512,8192]{1,0:T(8,128)(2,1)} %shard_map.74.refs_0_, f32[512,1536]{1,0:T(8,128)} %shard_map.73.refs_1_, bf16[8,12,144,128]{3,2,1,0:T(8,128)(2,1)} %bitcast.117, f32[16,512,8]{2,1,0:T(8,128)} %bitcast.88, ...), custom_call_target="tpu_custom_call", output_to_operand_aliasing={{}: (1, {})} | custom-call | tf_op jit(solution)/shard_map/pallas_call | solution.py:160
  279.8 19.2 %all-gather.19.cloned.1.call-done = bf16[32,144,128]{2,1,0:T(8,128)(2,1)} async-done(((bf16[4,144,128]{2,1,0:T(8,128)(2,1)}), bf16[32,144,128]{2,1,0:T(8,128)(2,1)}) %all-gather.19.cloned.1.call-update) | async-done | bytes 1179664 | tf_op jit(solution)/shard_map/all_gather | solution.py:275
  299.1 3.1 %shard_map.78 = bf16[512,8192]{1,0:T(8,128)(2,1)} custom-call(s32[1]{0:T(128)} %bitcast.place_ref, bf16[512,8192]{1,0:T(8,128)(2,1)} %shard_map.75.refs_0_, f32[512,512]{1,0:T(8,128)} %shard_map.77.refs_1_, bf16[8,4,144,128]{3,2,1,0:T(8,128)(2,1)} %bitcast.121, f32[16,512,8]{2,1,0:T(8,128)} %bitcast.89, ...), custom_call_target="tpu_custom_call", output_to_operand_aliasing={{}: (1, {})} | custom-call | tf_op jit(solution)/shard_map/pallas_call | solution.py:160
  (59 shorter events, 7.0 us)
Async XLA Ops:
  12.6 24.5 %all-to-all-start.2 = ((bf16[16,48,384]{2,1,0:T(8,128)(2,1)}), bf16[16,48,384]{2,1,0:T(8,128)(2,1)S(1)}, u32[]{:S(2)}, u32[]{:S(2)}) async-start(bf16[16,48,384]{2,1,0:T(8,128)(2,1)} %bitcast.8), calls=%async_computation.2 | async-start | bytes 1179648 | tf_op jit(solution)/shard_map/all_to_all | solution.py:183
  37.1 51.8 %all-to-all-start = ((bf16[16,48,2048]{2,1,0:T(8,128)(2,1)}), bf16[16,48,2048]{2,1,0:T(8,128)(2,1)}, u32[]{:S(2)}, u32[]{:S(2)}) async-start(bf16[16,48,2048]{2,1,0:T(8,128)(2,1)} %bitcast.103), calls=%async_computation | async-start | bytes 6291456 | tf_op jit(solution)/shard_map/all_to_all | solution.py:253
  43.9 124.6 %all-gather.11.cloned.1.call-start = ((), (), s32[]{:S(2)}) async-start(), calls=%async_computation.6 | async-start | bytes 5308416 | tf_op jit(solution)/shard_map/all_gather | solution.py:275
  44.6 19.2 %copy-start.3 = (f32[128]{0:T(128)S(1)}, f32[128]{0:T(128)}, u32[]{:S(2)}) copy-start(f32[128]{0:T(128)} %param.9) | copy-start | bytes 1540
  68.5 36.4 %copy-start = (f32[16,8,4,128]{3,1,2,0:T(8,128)}, f32[16,8,4,128]{3,1,2,0:T(8,128)S(1)}, u32[]{:S(2)}) copy-start(f32[16,8,4,128]{3,1,2,0:T(8,128)S(1)} %copy.52) | copy-start | bytes 786436
  95.2 4.7 %copy-start.2 = (f32[128]{0:T(128)S(1)}, f32[128]{0:T(128)}, u32[]{:S(2)}) copy-start(f32[128]{0:T(128)} %param.10) | copy-start | bytes 1540
  95.2 46.4 %all-to-all-start.1 = ((bf16[16,48,2048]{2,1,0:T(8,128)(2,1)}), bf16[16,48,2048]{2,1,0:T(8,128)(2,1)}, u32[]{:S(2)}, u32[]{:S(2)}) async-start(bf16[16,48,2048]{2,1,0:T(8,128)(2,1)} %bitcast.104), calls=%async_computation.1 | async-start | bytes 6291456 | tf_op jit(solution)/shard_map/all_to_all | solution.py:253
  99.7 121.9 %all-gather.13.cloned.1.call-start = ((), (), s32[]{:S(2)}) async-start(), calls=%async_computation.7 | async-start | bytes 5308416 | tf_op jit(solution)/shard_map/all_gather | solution.py:275
  147.8 47.5 %all-to-all-start.3 = ((bf16[16,48,2048]{2,1,0:T(8,128)(2,1)}), bf16[16,48,2048]{2,1,0:T(8,128)(2,1)}, u32[]{:S(2)}, u32[]{:S(2)}) async-start(bf16[16,48,2048]{2,1,0:T(8,128)(2,1)} %bitcast.105), calls=%async_computation.3 | async-start | bytes 6291456 | tf_op jit(solution)/shard_map/all_to_all | solution.py:253
  153.4 103.8 %all-gather.15.cloned.1.call-start = ((), (), s32[]{:S(2)}) async-start(), calls=%async_computation.8 | async-start | bytes 5308416 | tf_op jit(solution)/shard_map/all_gather | solution.py:275
  201.5 35.9 %all-to-all-start.4 = ((bf16[16,48,1536]{2,1,0:T(8,128)(2,1)}), bf16[16,48,1536]{2,1,0:T(8,128)(2,1)}, u32[]{:S(2)}, u32[]{:S(2)}) async-start(bf16[16,48,1536]{2,1,0:T(8,128)(2,1)} %bitcast.44), calls=%async_computation.4 | async-start | bytes 4718592 | tf_op jit(solution)/shard_map/all_to_all | solution.py:253
  207.2 66.8 %all-gather.17.cloned.1.call-start = ((), (), s32[]{:S(2)}) async-start(), calls=%async_computation.9 | async-start | bytes 3981312 | tf_op jit(solution)/shard_map/all_gather | solution.py:275
  242.6 21.4 %all-to-all-start.5 = ((bf16[16,48,512]{2,1,0:T(8,128)(2,1)}), bf16[16,48,512]{2,1,0:T(8,128)(2,1)S(1)}, u32[]{:S(2)}, u32[]{:S(2)}) async-start(bf16[16,48,512]{2,1,0:T(8,128)(2,1)} %bitcast.47), calls=%async_computation.5 | async-start | bytes 1572864 | tf_op jit(solution)/shard_map/all_to_all | solution.py:253
  249.4 49.7 %all-gather.19.cloned.1.call-start = ((), (), s32[]{:S(2)}) async-start(), calls=%async_computation.10 | async-start | bytes 1327104 | tf_op jit(solution)/shard_map/all_gather | solution.py:275
  263.9 0.9 copy-start.1
Sparse Core Ops, SparseCore 0:
  95.3 34.2 all-gather.10
  147.9 35.8 all-gather.12
  201.6 36.0 all-gather.14
  242.7 31.2 all-gather.16
  275.5 23.5 all-gather.18

commit v7 on v6

--- a/solution.py
+++ b/solution.py
@@ -34,6 +34,29 @@
         low = (decay - high.astype(jnp.float32)).astype(out_ref.dtype)
         extra = jnp.where(rows == 0, high, jnp.where(rows == 1, low, jnp.zeros_like(high)))
         out_ref[q, state_size : state_size + EXTRA, :] = extra
+
+
+def send_kernel(onehot_ref, tok_ref, out_ref):
+    out_ref[...] = jnp.dot(
+        onehot_ref[...], tok_ref[...], preferred_element_type=jnp.float32
+    ).astype(out_ref.dtype)
+
+
+def send_call(onehot, tokens, first, groups, stream_count):
+    rows, length = onehot.shape
+    width = GROUP * 64
+    picked = pl.pallas_call(
+        send_kernel,
+        grid=(groups,),
+        in_specs=[
+            pl.BlockSpec(onehot.shape, lambda g: (0, 0)),
+            pl.BlockSpec((length, width), lambda g: (0, g + first)),
+        ],
+        out_specs=pl.BlockSpec((rows, width), lambda g: (0, g)),
+        out_shape=jax.ShapeDtypeStruct((rows, groups * width), tokens.dtype),
+        compiler_params=arbitrary(),
+    )(onehot, tokens)
+    return picked.reshape(stream_count, rows // stream_count, groups * width)
 
 
 def local_kernel(scores_ref, cumg_ref, cumt_ref, stept_ref, tok_ref, skip_ref, out_ref):
@@ -241,10 +264,8 @@
     sizes = CHUNK_GROUPS
     firsts = [sum(sizes[:c]) for c in range(len(sizes))]
     group_width = GROUP * head_size
-    sends = [
-        send_rows(tokens[:, f * group_width : (f + n) * group_width], pick_rows, stream_count, capacity)
-        for f, n in zip(firsts, sizes)
-    ]
+    send_onehot = (pick_rows[:, None] == positions[None, :]).astype(jnp.bfloat16)
+    sends = [send_call(send_onehot, tokens, f, n, stream_count) for f, n in zip(firsts, sizes)]
     partials = []
     gathers = []
     result = None

time: 310 us -> 303 us (0.977)
  local copies, waits for them, and re-layouts: 56.5 us -> 19 us
  Pallas kernels: 96.8 us -> 120 us
  waiting for transfers between devices: 87.7 us -> 96.3 us
    gather x6 -> x1, local copies, waits for them, and re-layouts: 32.6 us -> 3.25 us  [send_rows(): jnp.take(rows, pick_rows, axis=0, mode='clip')]
    pallas_call x0 -> x5, Pallas kernels: none -> 23.5 us  [send_call(): pl.pallas_call(send_kernel, grid=(groups,), in_specs=[pl.BlockSpec(onehot...]
    slice x3 -> x0, local copies, waits for them, and re-layouts: 8.57 us -> none  [on_device(): tokens[:, f * group_width:(f + n) * group_width]]
    all_to_all x5, waiting for transfers between devices: 66.4 us -> 71.8 us  [on_device(): lax.all_to_all(sends[c], 'stream', split_axis=0, concat_axis=0, tiled=True)]
    all_to_all x1, waiting for transfers between devices: 0.01 us -> 3.56 us  [deliver(): lax.all_to_all(send, 'stream', split_axis=0, concat_axis=0, tiled=True)]
  transfers between devices with their start and end apart: 11 -> 11, of which waited for: 6 -> 7; matrix products, arithmetic and copies ran while one was open for 21% -> 9% of each run, Pallas kernels for 28% -> 37%
where the time goes in v7:
time: 303 us; the launch traced here: 301 us
  Pallas kernels  120 us (40%)
  waiting for transfers between devices  96.3 us (32%)
  starting transfers between devices  35.7 us (12%)
  local copies, waits for them, and re-layouts  19 us (6%)
  other arithmetic  15.6 us (5%)
  between operations  13.4 us (4%)
    all_to_all x5, waiting for transfers between devices, on_device(): lax.all_to_all(sends[c], 'stream', split_axis=0, concat_axis=0, tiled=True)  71.8 us
    pallas_call x5, Pallas kernels, local_call(): pl.pallas_call(local_kernel, grid=(groups,), in_specs=[pl.BlockSpec((leng...  40.3 us
    pallas_call x5, Pallas kernels, combine_call(): pl.pallas_call(combine_kernel, grid=(groups,), in_specs=[pl.BlockSpec(mem...  29.4 us
    pallas_call x5, Pallas kernels, carried_call(): pl.pallas_call(carried_kernel, grid=(groups,), in_specs=[pl.BlockSpec(bt....  26.8 us
    all_to_all x5, starting transfers between devices, on_device(): lax.all_to_all(sends[c], 'stream', split_axis=0, concat_axis=0, tiled=True)  26.7 us
    pallas_call x5, Pallas kernels, send_call(): pl.pallas_call(send_kernel, grid=(groups,), in_specs=[pl.BlockSpec(onehot...  23.5 us
    all_gather x5, waiting for transfers between devices, on_device(): gathers.append(lax.all_gather(carried, 'pos'))  20.9 us
    all_to_all x1, starting transfers between devices, deliver(): lax.all_to_all(send, 'stream', split_axis=0, concat_axis=0, tiled=True)  8.43 us
  transfers between devices with their start and end apart: 11, of which 7 were waited for; matrix products, arithmetic and copies ran while one was open for 9% of the time, Pallas kernels for 37%

profile of v7, /device:TPU:1, one launch (start us, length us, event | category | flops | bytes accessed | tf_op | source)
XLA Modules:
  0.0 301.4 jit_solution(15604488966588558136)
XLA Ops:
  8.3 1.1 pad_maximum_fusion
  9.4 3.2 %gather_fusion = bf16[768,384]{1,0:T(8,128)(2,1)} fusion(bf16[512,384]{1,0:T(8,128)(2,1)S(1)} %pad_maximum_fusion, s32[1024]{0:T(1024)S(1)} %pad_clamp_fusion.1), kind=kCustom, calls=%fused_computation | custom fusion | bytes 1182720 | tf_op jit(solution)/shard_map/jit(_take)/gather | solution.py:196
  12.6 8.4 %all-to-all-start.2 = ((bf16[16,48,384]{2,1,0:T(8,128)(2,1)}), bf16[16,48,384]{2,1,0:T(8,128)(2,1)S(1)}, u32[]{:S(2)}, u32[]{:S(2)}) async-start(bf16[16,48,384]{2,1,0:T(8,128)(2,1)} %bitcast.8), calls=%async_computation.2 | async-start | bytes 1179648 | tf_op jit(solution)/shard_map/all_to_all | solution.py:206
  21.1 0.9 dynamic-slice_reduce_fusion
  22.1 1.1 fusion.onehot_ref
  23.2 5.3 %shard_map.64 = bf16[768,2048]{1,0:T(8,128)(2,1)} custom-call(bf16[768,512]{1,0:T(8,128)(2,1)} %fusion.onehot_ref, bf16[512,8192]{1,0:T(8,128)(2,1)} %bitcast.90), custom_call_target="tpu_custom_call" | custom-call | tf_op jit(solution)/shard_map/pallas_call | solution.py:48
  28.6 3.6 %all-to-all-done.2 = bf16[16,48,384]{2,1,0:T(8,128)(2,1)S(1)} async-done(((bf16[16,48,384]{2,1,0:T(8,128)(2,1)}), bf16[16,48,384]{2,1,0:T(8,128)(2,1)S(1)}, u32[]{:S(2)}, u32[]{:S(2)}) %all-to-all-start.2) | async-done | bytes 589856 | tf_op jit(solution)/shard_map/all_to_all | solution.py:206
  32.1 4.5 %all-to-all-start = ((bf16[16,48,2048]{2,1,0:T(8,128)(2,1)}), bf16[16,48,2048]{2,1,0:T(8,128)(2,1)}, u32[]{:S(2)}, u32[]{:S(2)}) async-start(bf16[16,48,2048]{2,1,0:T(8,128)(2,1)} %bitcast.108), calls=%async_computation | async-start | bytes 6291456 | tf_op jit(solution)/shard_map/all_to_all | solution.py:274
  37.4 5.4 %shard_map.65 = bf16[768,2048]{1,0:T(8,128)(2,1)} custom-call(bf16[768,512]{1,0:T(8,128)(2,1)} %fusion.onehot_ref, bf16[512,8192]{1,0:T(8,128)(2,1)} %bitcast.91), custom_call_target="tpu_custom_call" | custom-call | tf_op jit(solution)/shard_map/pallas_call | solution.py:48
  42.8 4.2 %compare_select_fusion.2 = (s32[512,1]{0,1:T(1,128)S(1)}, s32[512,1]{0,1:T(1,128)S(1)}) fusion(s32[]{:T(128)} %bitcast.21, s32[]{:T(128)} %bitcast.22, s32[]{:T(128)} %bitcast.23, s32[]{:T(128)} %bitcast.24, s32[]{:T(128)} %bitcast.25, s32[]{:T(128)} %bitcast.27, s32[]{:T(128)} %bitcast.26, s32[512,1]{0,1:T(1,128)S(1)} %bitcast.130), kind=kLoop, calls=%fused_computation.33 | loop fusion | flops 7680 | bytes 6172 | tf_op jit(solution)/shard_map/jit(_take)/gather | solution.py:232
  47.1 5.6 %select_subtract_fusion = (s32[512]{0:T(512)S(1)}, s32[512]{0:T(512)S(1)}) fusion(s32[512]{0:T(512)S(1)} %convert_reduce_fusion, pred[512]{0:T(512)(128)(4,1)S(1)} %get-tuple-element.56, pred[512]{0:T(512)(128)(4,1)S(1)} %get-tuple-element.55, pred[512]{0:T(512)(128)(4,1)S(1)} %get-tuple-element.57, pred[512]{0:T(512)(128)(4,1)S(1)} %get-tuple-element.54, ...), kind=kLoop, calls=%fused_computation.48 | loop fusion | flops 10240 | bytes 12836 | tf_op jit(solution)/shard_map/sub | solution.py:233
  52.8 1.1 fusion.1.onehot_ref
  53.9 1.9 gather_fusion.1
  57.7 0.9 multiply_bitcast_fusion
  58.6 2.6 copy.41
  62.0 0.8 copy.42
  62.7 16.7 %all-to-all-done = bf16[16,48,2048]{2,1,0:T(8,128)(2,1)} async-done(((bf16[16,48,2048]{2,1,0:T(8,128)(2,1)}), bf16[16,48,2048]{2,1,0:T(8,128)(2,1)}, u32[]{:S(2)}, u32[]{:S(2)}) %all-to-all-start) | async-done | bytes 3145760 | tf_op jit(solution)/shard_map/all_to_all | solution.py:274
  79.4 6.2 %shard_map.66 = (bf16[16,144,128]{2,1,0:T(8,128)(2,1)}, bf16[512,2048]{1,0:T(8,128)(2,1)}) custom-call(bf16[128,512]{1,0:T(8,128)(2,1)} %bitcast.112, f32[16,512,8]{2,1,0:T(8,128)} %bitcast.95, f32[1,8192]{1,0:T(1,128)} %reshape_reshape.6.decay_ref, bf16[512,768]{1,0:T(8,128)(2,1)} %fusion.1.onehot_ref, bf16[768,2048]{1,0:T(8,128)(2,1)} %bitcast.40.arr_ref), custom_call_target="tpu_custom_call" | custom-call | tf_op jit(solution)/shard_map/pallas_call | solution.py:125
  85.6 5.0 %all-to-all-start.1 = ((bf16[16,48,2048]{2,1,0:T(8,128)(2,1)}), bf16[16,48,2048]{2,1,0:T(8,128)(2,1)}, u32[]{:S(2)}, u32[]{:S(2)}) async-start(bf16[16,48,2048]{2,1,0:T(8,128)(2,1)} %bitcast.5), calls=%async_computation.1 | async-start | bytes 6291456 | tf_op jit(solution)/shard_map/all_to_all | solution.py:274
  90.7 5.4 %shard_map.68 = bf16[768,2048]{1,0:T(8,128)(2,1)} custom-call(bf16[768,512]{1,0:T(8,128)(2,1)} %fusion.onehot_ref, bf16[512,8192]{1,0:T(8,128)(2,1)} %bitcast.92), custom_call_target="tpu_custom_call" | custom-call | tf_op jit(solution)/shard_map/pallas_call | solution.py:48
  96.9 2.7 copy.40
  99.6 1.3 fusion.9.scores_ref
  100.9 9.4 %shard_map.67.refs_0_ = f32[512,2048]{1,0:T(8,128)} custom-call(f32[512,512]{1,0:T(8,128)} %fusion.9.scores_ref, f32[16,512,8]{2,1,0:T(8,128)} %bitcast.80, f32[128,512]{1,0:T(8,128)} %bitcast.103, f32[128,512]{1,0:T(8,128)} %get-tuple-element.69.stept_ref, bf16[512,2048]{1,0:T(8,128)(2,1)} %get-tuple-element.29.tok_ref, f32[1,8192]{1,0:T(1,128)} %reshape_reshape.7.skip_ref), custom_call_target="tpu_custom_call" | custom-call | tf_op jit(solution)/shard_map/pallas_call | solution.py:150
  110.4 21.3 %all-to-all-done.1 = bf16[16,48,2048]{2,1,0:T(8,128)(2,1)} async-done(((bf16[16,48,2048]{2,1,0:T(8,128)(2,1)}), bf16[16,48,2048]{2,1,0:T(8,128)(2,1)}, u32[]{:S(2)}, u32[]{:S(2)}) %all-to-all-start.1) | async-done | bytes 3145760 | tf_op jit(solution)/shard_map/all_to_all | solution.py:274
  131.6 6.2 %shard_map.69 = (bf16[16,144,128]{2,1,0:T(8,128)(2,1)}, bf16[512,2048]{1,0:T(8,128)(2,1)}) custom-call(bf16[128,512]{1,0:T(8,128)(2,1)} %bitcast.113, f32[16,512,8]{2,1,0:T(8,128)} %bitcast.96, f32[1,8192]{1,0:T(1,128)} %reshape_reshape.6.decay_ref, bf16[512,768]{1,0:T(8,128)(2,1)} %fusion.1.onehot_ref, bf16[768,2048]{1,0:T(8,128)(2,1)} %bitcast.42.arr_ref), custom_call_target="tpu_custom_call" | custom-call | tf_op jit(solution)/shard_map/pallas_call | solution.py:125
  137.8 6.2 %all-to-all-start.3 = ((bf16[16,48,2048]{2,1,0:T(8,128)(2,1)}), bf16[16,48,2048]{2,1,0:T(8,128)(2,1)}, u32[]{:S(2)}, u32[]{:S(2)}) async-start(bf16[16,48,2048]{2,1,0:T(8,128)(2,1)} %bitcast.109), calls=%async_computation.3 | async-start | bytes 6291456 | tf_op jit(solution)/shard_map/all_to_all | solution.py:274
  144.3 4.7 %shard_map.72 = bf16[768,1536]{1,0:T(8,128)(2,1)} custom-call(bf16[768,512]{1,0:T(8,128)(2,1)} %fusion.onehot_ref, bf16[512,8192]{1,0:T(8,128)(2,1)} %bitcast.93), custom_call_target="tpu_custom_call" | custom-call | tf_op jit(solution)/shard_map/pallas_call | solution.py:48
  149.0 9.5 %shard_map.70.refs_1_ = f32[512,2048]{1,0:T(8,128)} custom-call(f32[512,512]{1,0:T(8,128)} %fusion.9.scores_ref, f32[16,512,8]{2,1,0:T(8,128)} %bitcast.81, f32[128,512]{1,0:T(8,128)} %bitcast.104, f32[128,512]{1,0:T(8,128)} %get-tuple-element.69.stept_ref, bf16[512,2048]{1,0:T(8,128)(2,1)} %get-tuple-element.32.tok_ref, f32[1,8192]{1,0:T(1,128)} %reshape_reshape.7.skip_ref), custom_call_target="tpu_custom_call" | custom-call | tf_op jit(solution)/shard_map/pallas_call | solution.py:150
  158.5 6.8 %shard_map.71.refs_0_ = bf16[512,8192]{1,0:T(8,128)(2,1)} custom-call(s32[1]{0:T(128)} %bitcast.place_ref, f32[512,2048]{1,0:T(8,128)} %shard_map.67.refs_0_, bf16[8,16,144,128]{3,2,1,0:T(8,128)(2,1)} %bitcast.118, f32[16,512,8]{2,1,0:T(8,128)} %bitcast.82, bf16[512,128]{1,0:T(8,128)(2,1)} %get-tuple-element.62.refs_3_.refs_4_), custom_call_target="tpu_custom_call" | custom-call | tf_op jit(solution)/shard_map/pallas_call | solution.py:183
  165.3 21.6 %all-to-all-done.3 = bf16[16,48,2048]{2,1,0:T(8,128)(2,1)} async-done(((bf16[16,48,2048]{2,1,0:T(8,128)(2,1)}), bf16[16,48,2048]{2,1,0:T(8,128)(2,1)}, u32[]{:S(2)}, u32[]{:S(2)}) %all-to-all-start.3) | async-done | bytes 3145760 | tf_op jit(solution)/shard_map/all_to_all | solution.py:274
  186.9 6.2 %shard_map.73 = (bf16[16,144,128]{2,1,0:T(8,128)(2,1)}, bf16[512,2048]{1,0:T(8,128)(2,1)}) custom-call(bf16[128,512]{1,0:T(8,128)(2,1)} %bitcast.114, f32[16,512,8]{2,1,0:T(8,128)} %bitcast.97, f32[1,8192]{1,0:T(1,128)} %reshape_reshape.6.decay_ref, bf16[512,768]{1,0:T(8,128)(2,1)} %fusion.1.onehot_ref, bf16[768,2048]{1,0:T(8,128)(2,1)} %bitcast.45.arr_ref), custom_call_target="tpu_custom_call" | custom-call | tf_op jit(solution)/shard_map/pallas_call | solution.py:125
  193.1 5.0 %all-to-all-start.4 = ((bf16[16,48,1536]{2,1,0:T(8,128)(2,1)}), bf16[16,48,1536]{2,1,0:T(8,128)(2,1)S(1)}, u32[]{:S(2)}, u32[]{:S(2)}) async-start(bf16[16,48,1536]{2,1,0:T(8,128)(2,1)} %bitcast.111), calls=%async_computation.4 | async-start | bytes 4718592 | tf_op jit(solution)/shard_map/all_to_all | solution.py:274
  198.2 2.7 shard_map.76
  201.0 9.5 %shard_map.74.refs_1_ = f32[512,2048]{1,0:T(8,128)} custom-call(f32[512,512]{1,0:T(8,128)} %fusion.9.scores_ref, f32[16,512,8]{2,1,0:T(8,128)} %bitcast.83, f32[128,512]{1,0:T(8,128)} %bitcast.105, f32[128,512]{1,0:T(8,128)} %get-tuple-element.69.stept_ref, bf16[512,2048]{1,0:T(8,128)(2,1)} %get-tuple-element.36.tok_ref, f32[1,8192]{1,0:T(1,128)} %reshape_reshape.7.skip_ref), custom_call_target="tpu_custom_call" | custom-call | tf_op jit(solution)/shard_map/pallas_call | solution.py:150
  210.4 6.8 %shard_map.75.refs_0_ = bf16[512,8192]{1,0:T(8,128)(2,1)} custom-call(s32[1]{0:T(128)} %bitcast.place_ref, bf16[512,8192]{1,0:T(8,128)(2,1)} %shard_map.71.refs_0_, f32[512,2048]{1,0:T(8,128)} %shard_map.70.refs_1_, bf16[8,16,144,128]{3,2,1,0:T(8,128)(2,1)} %bitcast.117, f32[16,512,8]{2,1,0:T(8,128)} %bitcast.84, ...), custom_call_target="tpu_custom_call", output_to_operand_aliasing={{}: (1, {})} | custom-call | tf_op jit(solution)/shard_map/pallas_call | solution.py:183
  217.3 12.2 %all-to-all-done.4 = bf16[16,48,1536]{2,1,0:T(8,128)(2,1)S(1)} async-done(((bf16[16,48,1536]{2,1,0:T(8,128)(2,1)}), bf16[16,48,1536]{2,1,0:T(8,128)(2,1)S(1)}, u32[]{:S(2)}, u32[]{:S(2)}) %all-to-all-start.4) | async-done | bytes 2359328 | tf_op jit(solution)/shard_map/all_to_all | solution.py:274
  229.5 1.4 copy-done.1
  230.9 5.2 %shard_map.77 = (bf16[12,144,128]{2,1,0:T(8,128)(2,1)}, bf16[512,1536]{1,0:T(8,128)(2,1)}) custom-call(bf16[128,512]{1,0:T(8,128)(2,1)} %bitcast.115, f32[16,512,8]{2,1,0:T(8,128)} %bitcast.98, f32[1,8192]{1,0:T(1,128)} %reshape_reshape.6.decay_ref, bf16[512,768]{1,0:T(8,128)(2,1)} %fusion.1.onehot_ref, bf16[768,1536]{1,0:T(8,128)(2,1)} %bitcast.110), custom_call_target="tpu_custom_call" | custom-call | tf_op jit(solution)/shard_map/pallas_call | solution.py:125
  236.1 5.9 %all-to-all-start.5 = ((bf16[16,48,512]{2,1,0:T(8,128)(2,1)}), bf16[16,48,512]{2,1,0:T(8,128)(2,1)S(1)}, u32[]{:S(2)}, u32[]{:S(2)}) async-start(bf16[16,48,512]{2,1,0:T(8,128)(2,1)} %bitcast.121), calls=%async_computation.5 | async-start | bytes 1572864 | tf_op jit(solution)/shard_map/all_to_all | solution.py:274
  242.3 7.7 %shard_map.78.refs_1_ = f32[512,1536]{1,0:T(8,128)} custom-call(f32[512,512]{1,0:T(8,128)} %fusion.9.scores_ref, f32[16,512,8]{2,1,0:T(8,128)} %bitcast.85, f32[128,512]{1,0:T(8,128)} %bitcast.106, f32[128,512]{1,0:T(8,128)} %get-tuple-element.69.stept_ref, bf16[512,1536]{1,0:T(8,128)(2,1)} %get-tuple-element.41.tok_ref, f32[1,8192]{1,0:T(1,128)} %reshape_reshape.7.skip_ref), custom_call_target="tpu_custom_call" | custom-call | tf_op jit(solution)/shard_map/pallas_call | solution.py:150
  250.0 6.7 %shard_map.79.refs_0_ = bf16[512,8192]{1,0:T(8,128)(2,1)} custom-call(s32[1]{0:T(128)} %bitcast.place_ref, bf16[512,8192]{1,0:T(8,128)(2,1)} %shard_map.75.refs_0_, f32[512,2048]{1,0:T(8,128)} %shard_map.74.refs_1_, bf16[8,16,144,128]{3,2,1,0:T(8,128)(2,1)} %bitcast.119, f32[16,512,8]{2,1,0:T(8,128)} %bitcast.86, ...), custom_call_target="tpu_custom_call", output_to_operand_aliasing={{}: (1, {})} | custom-call | tf_op jit(solution)/shard_map/pallas_call | solution.py:183
  256.8 0.9 copy-done.2
  257.7 3.1 %shard_map.81 = (bf16[4,144,128]{2,1,0:T(8,128)(2,1)}, bf16[512,512]{1,0:T(8,128)(2,1)}) custom-call(bf16[128,512]{1,0:T(8,128)(2,1)} %bitcast.116, f32[16,512,8]{2,1,0:T(8,128)} %bitcast.99, f32[1,8192]{1,0:T(1,128)} %reshape_reshape.6.decay_ref, bf16[512,768]{1,0:T(8,128)(2,1)} %fusion.1.onehot_ref, bf16[768,512]{1,0:T(8,128)(2,1)} %bitcast.122), custom_call_target="tpu_custom_call" | custom-call | tf_op jit(solution)/shard_map/pallas_call | solution.py:125
  260.8 4.1 %shard_map.82.refs_1_ = f32[512,512]{1,0:T(8,128)} custom-call(f32[512,512]{1,0:T(8,128)} %fusion.9.scores_ref, f32[16,512,8]{2,1,0:T(8,128)} %bitcast.87, f32[128,512]{1,0:T(8,128)} %bitcast.107, f32[128,512]{1,0:T(8,128)} %get-tuple-element.69.stept_ref, bf16[512,512]{1,0:T(8,128)(2,1)} %get-tuple-element.47.tok_ref, f32[1,8192]{1,0:T(1,128)} %reshape_reshape.7.skip_ref), custom_call_target="tpu_custom_call" | custom-call | tf_op jit(solution)/shard_map/pallas_call | solution.py:150
  264.9 1.7 all-gather.17.cloned.1.call-done
  266.6 5.9 %shard_map.80.refs_0_ = bf16[512,8192]{1,0:T(8,128)(2,1)} custom-call(s32[1]{0:T(128)} %bitcast.place_ref, bf16[512,8192]{1,0:T(8,128)(2,1)} %shard_map.79.refs_0_, f32[512,1536]{1,0:T(8,128)} %shard_map.78.refs_1_, bf16[8,12,144,128]{3,2,1,0:T(8,128)(2,1)} %bitcast.120, f32[16,512,8]{2,1,0:T(8,128)} %bitcast.88, ...), custom_call_target="tpu_custom_call", output_to_operand_aliasing={{}: (1, {})} | custom-call | tf_op jit(solution)/shard_map/pallas_call | solution.py:183
  272.5 19.2 %all-gather.19.cloned.1.call-done = bf16[32,144,128]{2,1,0:T(8,128)(2,1)} async-done(((bf16[4,144,128]{2,1,0:T(8,128)(2,1)}), bf16[32,144,128]{2,1,0:T(8,128)(2,1)}) %all-gather.19.cloned.1.call-update) | async-done | bytes 1179664 | tf_op jit(solution)/shard_map/all_gather | solution.py:296
  291.7 3.1 %shard_map.83 = bf16[512,8192]{1,0:T(8,128)(2,1)} custom-call(s32[1]{0:T(128)} %bitcast.place_ref, bf16[512,8192]{1,0:T(8,128)(2,1)} %shard_map.80.refs_0_, f32[512,512]{1,0:T(8,128)} %shard_map.82.refs_1_, bf16[8,4,144,128]{3,2,1,0:T(8,128)(2,1)} %bitcast.125, f32[16,512,8]{2,1,0:T(8,128)} %bitcast.89, ...), custom_call_target="tpu_custom_call", output_to_operand_aliasing={{}: (1, {})} | custom-call | tf_op jit(solution)/shard_map/pallas_call | solution.py:183
  (59 shorter events, 6.9 us)
Async XLA Ops:
  12.6 19.5 %all-to-all-start.2 = ((bf16[16,48,384]{2,1,0:T(8,128)(2,1)}), bf16[16,48,384]{2,1,0:T(8,128)(2,1)S(1)}, u32[]{:S(2)}, u32[]{:S(2)}) async-start(bf16[16,48,384]{2,1,0:T(8,128)(2,1)} %bitcast.8), calls=%async_computation.2 | async-start | bytes 1179648 | tf_op jit(solution)/shard_map/all_to_all | solution.py:206
  32.1 47.3 %all-to-all-start = ((bf16[16,48,2048]{2,1,0:T(8,128)(2,1)}), bf16[16,48,2048]{2,1,0:T(8,128)(2,1)}, u32[]{:S(2)}, u32[]{:S(2)}) async-start(bf16[16,48,2048]{2,1,0:T(8,128)(2,1)} %bitcast.108), calls=%async_computation | async-start | bytes 6291456 | tf_op jit(solution)/shard_map/all_to_all | solution.py:274
  36.6 121.9 %all-gather.11.cloned.1.call-start = ((), (), s32[]{:S(2)}) async-start(), calls=%async_computation.6 | async-start | bytes 5308416 | tf_op jit(solution)/shard_map/all_gather | solution.py:296
  37.4 15.4 %copy-start.4 = (f32[128]{0:T(128)S(1)}, f32[128]{0:T(128)}, u32[]{:S(2)}) copy-start(f32[128]{0:T(128)} %param.9) | copy-start | bytes 1540
  57.5 39.4 %copy-start = (f32[16,8,4,128]{3,1,2,0:T(8,128)}, f32[16,8,4,128]{3,1,2,0:T(8,128)S(1)}, u32[]{:S(2)}) copy-start(f32[16,8,4,128]{3,1,2,0:T(8,128)S(1)} %copy.52) | copy-start | bytes 786436
  85.6 46.0 %all-to-all-start.1 = ((bf16[16,48,2048]{2,1,0:T(8,128)(2,1)}), bf16[16,48,2048]{2,1,0:T(8,128)(2,1)}, u32[]{:S(2)}, u32[]{:S(2)}) async-start(bf16[16,48,2048]{2,1,0:T(8,128)(2,1)} %bitcast.5), calls=%async_computation.1 | async-start | bytes 6291456 | tf_op jit(solution)/shard_map/all_to_all | solution.py:274
  90.7 5.5 %copy-start.3 = (f32[128]{0:T(128)S(1)}, f32[128]{0:T(128)}, u32[]{:S(2)}) copy-start(f32[128]{0:T(128)} %param.10) | copy-start | bytes 1540
  90.7 119.8 %all-gather.13.cloned.1.call-start = ((), (), s32[]{:S(2)}) async-start(), calls=%async_computation.7 | async-start | bytes 5308416 | tf_op jit(solution)/shard_map/all_gather | solution.py:296
  137.8 49.1 %all-to-all-start.3 = ((bf16[16,48,2048]{2,1,0:T(8,128)(2,1)}), bf16[16,48,2048]{2,1,0:T(8,128)(2,1)}, u32[]{:S(2)}, u32[]{:S(2)}) async-start(bf16[16,48,2048]{2,1,0:T(8,128)(2,1)} %bitcast.109), calls=%async_computation.3 | async-start | bytes 6291456 | tf_op jit(solution)/shard_map/all_to_all | solution.py:274
  144.1 106.0 %all-gather.15.cloned.1.call-start = ((), (), s32[]{:S(2)}) async-start(), calls=%async_computation.8 | async-start | bytes 5308416 | tf_op jit(solution)/shard_map/all_gather | solution.py:296
  193.1 36.3 %all-to-all-start.4 = ((bf16[16,48,1536]{2,1,0:T(8,128)(2,1)}), bf16[16,48,1536]{2,1,0:T(8,128)(2,1)S(1)}, u32[]{:S(2)}, u32[]{:S(2)}) async-start(bf16[16,48,1536]{2,1,0:T(8,128)(2,1)} %bitcast.111), calls=%async_computation.4 | async-start | bytes 4718592 | tf_op jit(solution)/shard_map/all_to_all | solution.py:274
  198.2 68.4 %all-gather.17.cloned.1.call-start = ((), (), s32[]{:S(2)}) async-start(), calls=%async_computation.9 | async-start | bytes 3981312 | tf_op jit(solution)/shard_map/all_gather | solution.py:296
  229.5 1.4 copy-start.1
  236.1 20.7 %all-to-all-start.5 = ((bf16[16,48,512]{2,1,0:T(8,128)(2,1)}), bf16[16,48,512]{2,1,0:T(8,128)(2,1)S(1)}, u32[]{:S(2)}, u32[]{:S(2)}) async-start(bf16[16,48,512]{2,1,0:T(8,128)(2,1)} %bitcast.121), calls=%async_computation.5 | async-start | bytes 1572864 | tf_op jit(solution)/shard_map/all_to_all | solution.py:274
  242.0 49.7 %all-gather.19.cloned.1.call-start = ((), (), s32[]{:S(2)}) async-start(), calls=%async_computation.10 | async-start | bytes 1327104 | tf_op jit(solution)/shard_map/all_gather | solution.py:296
  256.8 0.9 copy-start.2
Sparse Core Ops, SparseCore 0:
  85.8 35.3 all-gather.10
  137.9 36.2 all-gather.12
  193.3 35.4 all-gather.14
  236.2 30.3 all-gather.16
  268.1 23.5 all-gather.18

commit v8 on v7

--- a/solution.py
+++ b/solution.py
@@ -233,7 +233,17 @@
     flat_rows = source * capacity + positions - source_start
 
     small = jnp.concatenate([proj_in[0], step_raw[0]], axis=1)
-    ordered_small = deliver(small, pick_rows, flat_rows, stream_count, capacity)
+    small_send = send_rows(small, pick_rows, stream_count, capacity)
+    sizes = CHUNK_GROUPS
+    firsts = [sum(sizes[:c]) for c in range(len(sizes))]
+    positions = jnp.arange(local_rows, dtype=jnp.int32)
+    send_onehot = (pick_rows[:, None] == positions[None, :]).astype(jnp.bfloat16)
+    first_send = send_call(send_onehot, tokens, firsts[0], sizes[0], stream_count)
+    first_width = first_send.shape[2]
+    first_arrived = lax.all_to_all(
+        jnp.concatenate([first_send, small_send], axis=2), "stream", 0, 0, tiled=True
+    )
+    ordered_small = receive_rows(first_arrived[:, :, first_width:], flat_rows)
     ordered_proj = ordered_small[:, : 2 * state_size]
     ordered_steps = ordered_small[:, 2 * state_size :]
 
@@ -261,17 +271,18 @@
     slots = jnp.arange(stream_count * capacity, dtype=jnp.int32)
     onehot = (flat_rows[:, None] == slots[None, :]).astype(jnp.bfloat16)
 
-    sizes = CHUNK_GROUPS
-    firsts = [sum(sizes[:c]) for c in range(len(sizes))]
-    group_width = GROUP * head_size
-    send_onehot = (pick_rows[:, None] == positions[None, :]).astype(jnp.bfloat16)
-    sends = [send_call(send_onehot, tokens, f, n, stream_count) for f, n in zip(firsts, sizes)]
+    sends = [None] + [
+        send_call(send_onehot, tokens, f, n, stream_count) for f, n in zip(firsts[1:], sizes[1:])
+    ]
     partials = []
     gathers = []
     result = None
     done = 0
     for c in range(len(sizes)):
-        arrived = lax.all_to_all(sends[c], "stream", split_axis=0, concat_axis=0, tiled=True)
+        if c == 0:
+            arrived = first_arrived
+        else:
+            arrived = lax.all_to_all(sends[c], "stream", split_axis=0, concat_axis=0, tiled=True)
         tied = {"arrived": arrived}
         if c + 1 < len(sizes):
             tied["send"] = sends[c + 1]

time: 303 us -> 324 us (1.069)
  waiting for transfers between devices: 96.3 us -> 114 us
  starting transfers between devices: 35.7 us -> 29.4 us
  local copies, waits for them, and re-layouts: 19 us -> 23.6 us
  other arithmetic: 15.6 us -> 19 us
    all_to_all x1, waiting for transfers between devices: 3.56 us -> 37 us  [on_device(): lax.all_to_all(jnp.concatenate([first_send, small_send], axis=2), 'stream...]
    all_to_all x5 -> x4, waiting for transfers between devices: 71.8 us -> 55.8 us  [on_device(): lax.all_to_all(sends[c], 'stream', split_axis=0, concat_axis=0, tiled=True)]
    all_to_all x5 -> x4, starting transfers between devices: 26.7 us -> 20.3 us  [on_device(): lax.all_to_all(sends[c], 'stream', split_axis=0, concat_axis=0, tiled=True)]
    unnamed x14 -> x22, local copies, waits for them, and re-layouts: 3.2 us -> 6.6 us
  transfers between devices with their start and end apart: 11 -> 10, of which waited for: 7 -> 6; matrix products, arithmetic and copies ran while one was open for 9% -> 6% of each run, Pallas kernels for 37% -> 33%
where the time goes in v8:
time: 324 us; the launch traced here: 322 us
  Pallas kernels  120 us (37%)
  waiting for transfers between devices  114 us (35%)
  starting transfers between devices  29.4 us (9%)
  local copies, waits for them, and re-layouts  23.6 us (7%)
  other arithmetic  19 us (6%)
  between operations  13.4 us (4%)
    all_to_all x4, waiting for transfers between devices, on_device(): lax.all_to_all(sends[c], 'stream', split_axis=0, concat_axis=0, tiled=True)  55.8 us
    pallas_call x5, Pallas kernels, local_call(): pl.pallas_call(local_kernel, grid=(groups,), in_specs=[pl.BlockSpec((leng...  40.2 us
    all_to_all x1, waiting for transfers between devices, on_device(): lax.all_to_all(jnp.concatenate([first_send, small_send], axis=2), 'stream...  37 us
    pallas_call x5, Pallas kernels, combine_call(): pl.pallas_call(combine_kernel, grid=(groups,), in_specs=[pl.BlockSpec(mem...  29.5 us
    pallas_call x5, Pallas kernels, carried_call(): pl.pallas_call(carried_kernel, grid=(groups,), in_specs=[pl.BlockSpec(bt....  27.2 us
    pallas_call x5, Pallas kernels, send_call(): pl.pallas_call(send_kernel, grid=(groups,), in_specs=[pl.BlockSpec(onehot...  23.6 us
    all_gather x5, waiting for transfers between devices, on_device(): gathers.append(lax.all_gather(carried, 'pos'))  21 us
    all_to_all x4, starting transfers between devices, on_device(): lax.all_to_all(sends[c], 'stream', split_axis=0, concat_axis=0, tiled=True)  20.3 us
  transfers between devices with their start and end apart: 10, of which 6 were waited for; matrix products, arithmetic and copies ran while one was open for 6% of the time, Pallas kernels for 33%

profile of v8, /device:TPU:1, one launch (start us, length us, event | category | flops | bytes accessed | tf_op | source)
XLA Modules:
  0.0 322.0 jit_solution(8844600919035570681)
XLA Ops:
  8.3 1.1 fusion.onehot_ref
  9.4 5.3 %shard_map.64 = bf16[768,2048]{1,0:T(8,128)(2,1)} custom-call(bf16[768,512]{1,0:T(8,128)(2,1)} %fusion.onehot_ref, bf16[512,8192]{1,0:T(8,128)(2,1)} %bitcast.90), custom_call_target="tpu_custom_call" | custom-call | tf_op jit(solution)/shard_map/pallas_call | solution.py:48
  14.7 1.2 pad_maximum_fusion.1
  15.9 3.2 %gather_fusion = bf16[768,384]{1,0:T(8,128)(2,1)} fusion(bf16[512,384]{1,0:T(8,128)(2,1)S(1)} %pad_maximum_fusion.1, s32[1024]{0:T(1024)S(1)} %pad_clamp_fusion.1), kind=kCustom, calls=%fused_computation | custom fusion | bytes 1182720 | tf_op jit(solution)/shard_map/jit(_take)/gather | solution.py:196
  19.2 3.2 %pad_maximum_fusion = bf16[16,48,2432]{2,1,0:T(8,128)(2,1)} fusion(bf16[16,48,384]{2,1,0:T(8,128)(2,1)} %bitcast.123, bf16[16,48,2048]{2,1,0:T(8,128)(2,1)S(1)} %bitcast.108), kind=kLoop, calls=%fused_computation.2 | loop fusion | flops 7471104 | bytes 7471104 | tf_op jit(solution)/shard_map/concatenate | solution.py:244
  22.4 8.5 %all-to-all-start = ((bf16[16,48,2432]{2,1,0:T(8,128)(2,1)}), bf16[16,48,2432]{2,1,0:T(8,128)(2,1)}, u32[]{:S(2)}, u32[]{:S(2)}) async-start(bf16[16,48,2432]{2,1,0:T(8,128)(2,1)} %pad_maximum_fusion), calls=%async_computation | async-start | bytes 7471104 | tf_op jit(solution)/shard_map/all_to_all | solution.py:243
  30.9 5.4 %shard_map.65 = bf16[768,2048]{1,0:T(8,128)(2,1)} custom-call(bf16[768,512]{1,0:T(8,128)(2,1)} %fusion.onehot_ref, bf16[512,8192]{1,0:T(8,128)(2,1)} %bitcast.91), custom_call_target="tpu_custom_call" | custom-call | tf_op jit(solution)/shard_map/pallas_call | solution.py:48
  38.2 4.4 %compare_select_fusion.2 = (s32[512,1]{0,1:T(1,128)S(1)}, s32[512,1]{0,1:T(1,128)S(1)}) fusion(s32[]{:T(128)} %bitcast.21, s32[]{:T(128)} %bitcast.22, s32[]{:T(128)} %bitcast.23, s32[]{:T(128)} %bitcast.24, s32[]{:T(128)} %bitcast.25, s32[]{:T(128)} %bitcast.27, s32[]{:T(128)} %bitcast.26, s32[512,1]{0,1:T(1,128)S(1)} %bitcast.131), kind=kLoop, calls=%fused_computation.34 | loop fusion | flops 7680 | bytes 6172 | tf_op jit(solution)/shard_map/jit(_take)/gather | solution.py:232
  42.6 5.5 %select_subtract_fusion = (s32[512]{0:T(512)S(1)}, s32[512]{0:T(512)S(1)}) fusion(s32[512]{0:T(512)S(1)} %convert_reduce_fusion, pred[512]{0:T(512)(128)(4,1)S(1)} %get-tuple-element.56, pred[512]{0:T(512)(128)(4,1)S(1)} %get-tuple-element.55, pred[512]{0:T(512)(128)(4,1)S(1)} %get-tuple-element.57, pred[512]{0:T(512)(128)(4,1)S(1)} %get-tuple-element.54, ...), kind=kLoop, calls=%fused_computation.49 | loop fusion | flops 10240 | bytes 12836 | tf_op jit(solution)/shard_map/sub | solution.py:233
  48.2 1.1 fusion.1.onehot_ref
  49.2 37.0 %all-to-all-done = bf16[16,48,2432]{2,1,0:T(8,128)(2,1)} async-done(((bf16[16,48,2432]{2,1,0:T(8,128)(2,1)}), bf16[16,48,2432]{2,1,0:T(8,128)(2,1)}, u32[]{:S(2)}, u32[]{:S(2)}) %all-to-all-start) | async-done | bytes 3735584 | tf_op jit(solution)/shard_map/all_to_all | solution.py:243
  86.3 1.1 slice.52
  87.4 1.9 gather_fusion.1
  91.3 0.9 multiply_bitcast_fusion
  92.2 2.7 copy.41
  96.4 6.6 %shard_map.66 = (bf16[19,144,128]{2,1,0:T(8,128)(2,1)}, bf16[512,2432]{1,0:T(8,128)(2,1)}) custom-call(bf16[128,512]{1,0:T(8,128)(2,1)} %bitcast.114, f32[16,512,8]{2,1,0:T(8,128)} %bitcast.95, f32[1,8192]{1,0:T(1,128)} %reshape_reshape.6.decay_ref, bf16[512,768]{1,0:T(8,128)(2,1)} %fusion.1.onehot_ref, bf16[768,2432]{1,0:T(8,128)(2,1)} %bitcast.40.arr_ref), custom_call_target="tpu_custom_call" | custom-call | tf_op jit(solution)/shard_map/pallas_call | solution.py:125
  103.0 4.3 %all-to-all-start.1 = ((bf16[16,48,2048]{2,1,0:T(8,128)(2,1)}), bf16[16,48,2048]{2,1,0:T(8,128)(2,1)S(1)}, u32[]{:S(2)}, u32[]{:S(2)}) async-start(bf16[16,48,2048]{2,1,0:T(8,128)(2,1)} %bitcast.8), calls=%async_computation.1 | async-start | bytes 6291456 | tf_op jit(solution)/shard_map/all_to_all | solution.py:285
  107.4 5.4 %shard_map.68 = bf16[768,2048]{1,0:T(8,128)(2,1)} custom-call(bf16[768,512]{1,0:T(8,128)(2,1)} %fusion.onehot_ref, bf16[512,8192]{1,0:T(8,128)(2,1)} %bitcast.92), custom_call_target="tpu_custom_call" | custom-call | tf_op jit(solution)/shard_map/pallas_call | solution.py:48
  113.6 2.6 copy.40
  116.3 2.2 fusion.9.scores_ref
  118.5 9.2 %shard_map.67.refs_0_ = f32[512,2432]{1,0:T(8,128)} custom-call(f32[512,512]{1,0:T(8,128)} %fusion.9.scores_ref, f32[16,512,8]{2,1,0:T(8,128)} %bitcast.80, f32[128,512]{1,0:T(8,128)} %bitcast.103, f32[128,512]{1,0:T(8,128)} %get-tuple-element.69.stept_ref, bf16[512,2432]{1,0:T(8,128)(2,1)} %get-tuple-element.29.tok_ref, f32[1,8192]{1,0:T(1,128)} %reshape_reshape.7.skip_ref), custom_call_target="tpu_custom_call" | custom-call | tf_op jit(solution)/shard_map/pallas_call | solution.py:150
  127.7 22.5 %all-to-all-done.1 = bf16[16,48,2048]{2,1,0:T(8,128)(2,1)S(1)} async-done(((bf16[16,48,2048]{2,1,0:T(8,128)(2,1)}), bf16[16,48,2048]{2,1,0:T(8,128)(2,1)S(1)}, u32[]{:S(2)}, u32[]{:S(2)}) %all-to-all-start.1) | async-done | bytes 3145760 | tf_op jit(solution)/shard_map/all_to_all | solution.py:285
  150.2 1.7 copy-done.3
  151.9 6.2 %shard_map.69 = (bf16[16,144,128]{2,1,0:T(8,128)(2,1)}, bf16[512,2048]{1,0:T(8,128)(2,1)}) custom-call(bf16[128,512]{1,0:T(8,128)(2,1)} %bitcast.115, f32[16,512,8]{2,1,0:T(8,128)} %bitcast.96, f32[1,8192]{1,0:T(1,128)} %reshape_reshape.6.decay_ref, bf16[512,768]{1,0:T(8,128)(2,1)} %fusion.1.onehot_ref, bf16[768,2048]{1,0:T(8,128)(2,1)} %bitcast.110), custom_call_target="tpu_custom_call" | custom-call | tf_op jit(solution)/shard_map/pallas_call | solution.py:125
  158.1 5.0 %all-to-all-start.2 = ((bf16[16,48,2048]{2,1,0:T(8,128)(2,1)}), bf16[16,48,2048]{2,1,0:T(8,128)(2,1)S(1)}, u32[]{:S(2)}, u32[]{:S(2)}) async-start(bf16[16,48,2048]{2,1,0:T(8,128)(2,1)} %bitcast.41), calls=%async_computation.2 | async-start | bytes 6291456 | tf_op jit(solution)/shard_map/all_to_all | solution.py:285
  163.3 4.7 %shard_map.72 = bf16[768,1536]{1,0:T(8,128)(2,1)} custom-call(bf16[768,512]{1,0:T(8,128)(2,1)} %fusion.onehot_ref, bf16[512,8192]{1,0:T(8,128)(2,1)} %bitcast.93), custom_call_target="tpu_custom_call" | custom-call | tf_op jit(solution)/shard_map/pallas_call | solution.py:48
  168.0 9.6 %shard_map.70.refs_1_ = f32[512,2048]{1,0:T(8,128)} custom-call(f32[512,512]{1,0:T(8,128)} %fusion.9.scores_ref, f32[16,512,8]{2,1,0:T(8,128)} %bitcast.81, f32[128,512]{1,0:T(8,128)} %bitcast.104, f32[128,512]{1,0:T(8,128)} %get-tuple-element.69.stept_ref, bf16[512,2048]{1,0:T(8,128)(2,1)} %get-tuple-element.32.tok_ref, f32[1,8192]{1,0:T(1,128)} %reshape_reshape.7.skip_ref), custom_call_target="tpu_custom_call" | custom-call | tf_op jit(solution)/shard_map/pallas_call | solution.py:150
  177.6 6.8 %shard_map.71.refs_0_ = bf16[512,8192]{1,0:T(8,128)(2,1)} custom-call(s32[1]{0:T(128)} %bitcast.place_ref, f32[512,2432]{1,0:T(8,128)} %shard_map.67.refs_0_, bf16[8,19,144,128]{3,2,1,0:T(8,128)(2,1)} %bitcast.113, f32[16,512,8]{2,1,0:T(8,128)} %bitcast.82, bf16[512,128]{1,0:T(8,128)(2,1)} %get-tuple-element.62.refs_3_.refs_4_), custom_call_target="tpu_custom_call" | custom-call | tf_op jit(solution)/shard_map/pallas_call | solution.py:183
  184.4 21.7 %all-to-all-done.2 = bf16[16,48,2048]{2,1,0:T(8,128)(2,1)S(1)} async-done(((bf16[16,48,2048]{2,1,0:T(8,128)(2,1)}), bf16[16,48,2048]{2,1,0:T(8,128)(2,1)S(1)}, u32[]{:S(2)}, u32[]{:S(2)}) %all-to-all-start.2) | async-done | bytes 3145760 | tf_op jit(solution)/shard_map/all_to_all | solution.py:285
  206.1 1.7 copy-done.2
  207.8 6.2 %shard_map.73 = (bf16[16,144,128]{2,1,0:T(8,128)(2,1)}, bf16[512,2048]{1,0:T(8,128)(2,1)}) custom-call(bf16[128,512]{1,0:T(8,128)(2,1)} %bitcast.116, f32[16,512,8]{2,1,0:T(8,128)} %bitcast.97, f32[1,8192]{1,0:T(1,128)} %reshape_reshape.6.decay_ref, bf16[512,768]{1,0:T(8,128)(2,1)} %fusion.1.onehot_ref, bf16[768,2048]{1,0:T(8,128)(2,1)} %bitcast.109), custom_call_target="tpu_custom_call" | custom-call | tf_op jit(solution)/shard_map/pallas_call | solution.py:125
  214.0 4.8 %all-to-all-start.3 = ((bf16[16,48,1536]{2,1,0:T(8,128)(2,1)}), bf16[16,48,1536]{2,1,0:T(8,128)(2,1)S(1)}, u32[]{:S(2)}, u32[]{:S(2)}) async-start(bf16[16,48,1536]{2,1,0:T(8,128)(2,1)} %bitcast.112), calls=%async_computation.3 | async-start | bytes 4718592 | tf_op jit(solution)/shard_map/all_to_all | solution.py:285
  218.9 2.8 shard_map.76
  221.7 9.5 %shard_map.74.refs_1_ = f32[512,2048]{1,0:T(8,128)} custom-call(f32[512,512]{1,0:T(8,128)} %fusion.9.scores_ref, f32[16,512,8]{2,1,0:T(8,128)} %bitcast.83, f32[128,512]{1,0:T(8,128)} %bitcast.105, f32[128,512]{1,0:T(8,128)} %get-tuple-element.69.stept_ref, bf16[512,2048]{1,0:T(8,128)(2,1)} %get-tuple-element.36.tok_ref, f32[1,8192]{1,0:T(1,128)} %reshape_reshape.7.skip_ref), custom_call_target="tpu_custom_call" | custom-call | tf_op jit(solution)/shard_map/pallas_call | solution.py:150
  231.2 6.8 %shard_map.75.refs_0_ = bf16[512,8192]{1,0:T(8,128)(2,1)} custom-call(s32[1]{0:T(128)} %bitcast.place_ref, bf16[512,8192]{1,0:T(8,128)(2,1)} %shard_map.71.refs_0_, f32[512,2048]{1,0:T(8,128)} %shard_map.70.refs_1_, bf16[8,16,144,128]{3,2,1,0:T(8,128)(2,1)} %bitcast.119, f32[16,512,8]{2,1,0:T(8,128)} %bitcast.84, ...), custom_call_target="tpu_custom_call", output_to_operand_aliasing={{}: (1, {})} | custom-call | tf_op jit(solution)/shard_map/pallas_call | solution.py:183
  238.0 11.7 %all-to-all-done.3 = bf16[16,48,1536]{2,1,0:T(8,128)(2,1)S(1)} async-done(((bf16[16,48,1536]{2,1,0:T(8,128)(2,1)}), bf16[16,48,1536]{2,1,0:T(8,128)(2,1)S(1)}, u32[]{:S(2)}, u32[]{:S(2)}) %all-to-all-start.3) | async-done | bytes 2359328 | tf_op jit(solution)/shard_map/all_to_all | solution.py:285
  249.7 1.4 copy-done.4
  251.1 5.2 %shard_map.77 = (bf16[12,144,128]{2,1,0:T(8,128)(2,1)}, bf16[512,1536]{1,0:T(8,128)(2,1)}) custom-call(bf16[128,512]{1,0:T(8,128)(2,1)} %bitcast.117, f32[16,512,8]{2,1,0:T(8,128)} %bitcast.98, f32[1,8192]{1,0:T(1,128)} %reshape_reshape.6.decay_ref, bf16[512,768]{1,0:T(8,128)(2,1)} %fusion.1.onehot_ref, bf16[768,1536]{1,0:T(8,128)(2,1)} %bitcast.111), custom_call_target="tpu_custom_call" | custom-call | tf_op jit(solution)/shard_map/pallas_call | solution.py:125
  256.3 6.2 %all-to-all-start.4 = ((bf16[16,48,512]{2,1,0:T(8,128)(2,1)}), bf16[16,48,512]{2,1,0:T(8,128)(2,1)S(1)}, u32[]{:S(2)}, u32[]{:S(2)}) async-start(bf16[16,48,512]{2,1,0:T(8,128)(2,1)} %bitcast.47), calls=%async_computation.4 | async-start | bytes 1572864 | tf_op jit(solution)/shard_map/all_to_all | solution.py:285
  262.8 7.8 %shard_map.78.refs_1_ = f32[512,1536]{1,0:T(8,128)} custom-call(f32[512,512]{1,0:T(8,128)} %fusion.9.scores_ref, f32[16,512,8]{2,1,0:T(8,128)} %bitcast.85, f32[128,512]{1,0:T(8,128)} %bitcast.106, f32[128,512]{1,0:T(8,128)} %get-tuple-element.69.stept_ref, bf16[512,1536]{1,0:T(8,128)(2,1)} %get-tuple-element.41.tok_ref, f32[1,8192]{1,0:T(1,128)} %reshape_reshape.7.skip_ref), custom_call_target="tpu_custom_call" | custom-call | tf_op jit(solution)/shard_map/pallas_call | solution.py:150
  270.6 6.8 %shard_map.79.refs_0_ = bf16[512,8192]{1,0:T(8,128)(2,1)} custom-call(s32[1]{0:T(128)} %bitcast.place_ref, bf16[512,8192]{1,0:T(8,128)(2,1)} %shard_map.75.refs_0_, f32[512,2048]{1,0:T(8,128)} %shard_map.74.refs_1_, bf16[8,16,144,128]{3,2,1,0:T(8,128)(2,1)} %bitcast.120, f32[16,512,8]{2,1,0:T(8,128)} %bitcast.86, ...), custom_call_target="tpu_custom_call", output_to_operand_aliasing={{}: (1, {})} | custom-call | tf_op jit(solution)/shard_map/pallas_call | solution.py:183
  277.4 0.9 copy-done.5
  278.2 3.1 shard_map.81
  281.4 4.1 %shard_map.82.refs_1_ = f32[512,512]{1,0:T(8,128)} custom-call(f32[512,512]{1,0:T(8,128)} %fusion.9.scores_ref, f32[16,512,8]{2,1,0:T(8,128)} %bitcast.87, f32[128,512]{1,0:T(8,128)} %bitcast.107, f32[128,512]{1,0:T(8,128)} %get-tuple-element.69.stept_ref, bf16[512,512]{1,0:T(8,128)(2,1)} %get-tuple-element.47.tok_ref, f32[1,8192]{1,0:T(1,128)} %reshape_reshape.7.skip_ref), custom_call_target="tpu_custom_call" | custom-call | tf_op jit(solution)/shard_map/pallas_call | solution.py:150
  285.5 1.8 all-gather.17.cloned.1.call-done
  287.2 5.9 %shard_map.80.refs_0_ = bf16[512,8192]{1,0:T(8,128)(2,1)} custom-call(s32[1]{0:T(128)} %bitcast.place_ref, bf16[512,8192]{1,0:T(8,128)(2,1)} %shard_map.79.refs_0_, f32[512,1536]{1,0:T(8,128)} %shard_map.78.refs_1_, bf16[8,12,144,128]{3,2,1,0:T(8,128)(2,1)} %bitcast.121, f32[16,512,8]{2,1,0:T(8,128)} %bitcast.88, ...), custom_call_target="tpu_custom_call", output_to_operand_aliasing={{}: (1, {})} | custom-call | tf_op jit(solution)/shard_map/pallas_call | solution.py:183
  293.1 19.2 %all-gather.19.cloned.1.call-done = bf16[32,144,128]{2,1,0:T(8,128)(2,1)} async-done(((bf16[4,144,128]{2,1,0:T(8,128)(2,1)}), bf16[32,144,128]{2,1,0:T(8,128)(2,1)}) %all-gather.19.cloned.1.call-update) | async-done | bytes 1179664 | tf_op jit(solution)/shard_map/all_gather | solution.py:307
  312.3 3.1 shard_map.83
  (67 shorter events, 8.7 us)
Async XLA Ops:
  14.7 4.5 %copy-start.1 = (bf16[768,2048]{1,0:T(8,128)(2,1)S(1)}, bf16[768,2048]{1,0:T(8,128)(2,1)}, u32[]{:S(2)}) copy-start(bf16[768,2048]{1,0:T(8,128)(2,1)} %shard_map.64) | copy-start | bytes 9437188
  22.4 63.9 %all-to-all-start = ((bf16[16,48,2432]{2,1,0:T(8,128)(2,1)}), bf16[16,48,2432]{2,1,0:T(8,128)(2,1)}, u32[]{:S(2)}, u32[]{:S(2)}) async-start(bf16[16,48,2432]{2,1,0:T(8,128)(2,1)} %pad_maximum_fusion), calls=%async_computation | async-start | bytes 7471104 | tf_op jit(solution)/shard_map/all_to_all | solution.py:243
  30.9 17.3 %copy-start.8 = (f32[128]{0:T(128)S(1)}, f32[128]{0:T(128)}, u32[]{:S(2)}) copy-start(f32[128]{0:T(128)} %param.9) | copy-start | bytes 1540
  30.9 146.7 %all-gather.11.cloned.1.call-start = ((), (), s32[]{:S(2)}) async-start(), calls=%async_computation.5 | async-start | bytes 6303744 | tf_op jit(solution)/shard_map/all_gather | solution.py:307
  89.4 5.5 %copy-start.6 = (bf16[512,384]{1,0:T(8,128)(2,1)}, bf16[512,384]{1,0:T(8,128)(2,1)S(1)}, u32[]{:S(2)}) copy-start(bf16[512,384]{1,0:T(8,128)(2,1)S(1)} %gather_fusion.1) | copy-start | bytes 1179652
  91.1 22.5 %copy-start = (f32[16,8,4,128]{3,1,2,0:T(8,128)}, f32[16,8,4,128]{3,1,2,0:T(8,128)S(1)}, u32[]{:S(2)}) copy-start(f32[16,8,4,128]{3,1,2,0:T(8,128)S(1)} %copy.52) | copy-start | bytes 786436
  103.0 47.2 %all-to-all-start.1 = ((bf16[16,48,2048]{2,1,0:T(8,128)(2,1)}), bf16[16,48,2048]{2,1,0:T(8,128)(2,1)S(1)}, u32[]{:S(2)}, u32[]{:S(2)}) async-start(bf16[16,48,2048]{2,1,0:T(8,128)(2,1)} %bitcast.8), calls=%async_computation.1 | async-start | bytes 6291456 | tf_op jit(solution)/shard_map/all_to_all | solution.py:285
  107.4 5.5 %copy-start.7 = (f32[128]{0:T(128)S(1)}, f32[128]{0:T(128)}, u32[]{:S(2)}) copy-start(f32[128]{0:T(128)} %param.10) | copy-start | bytes 1540
  107.4 123.8 %all-gather.13.cloned.1.call-start = ((), (), s32[]{:S(2)}) async-start(), calls=%async_computation.6 | async-start | bytes 5308416 | tf_op jit(solution)/shard_map/all_gather | solution.py:307
  150.2 1.7 copy-start.3
  158.1 48.1 %all-to-all-start.2 = ((bf16[16,48,2048]{2,1,0:T(8,128)(2,1)}), bf16[16,48,2048]{2,1,0:T(8,128)(2,1)S(1)}, u32[]{:S(2)}, u32[]{:S(2)}) async-start(bf16[16,48,2048]{2,1,0:T(8,128)(2,1)} %bitcast.41), calls=%async_computation.2 | async-start | bytes 6291456 | tf_op jit(solution)/shard_map/all_to_all | solution.py:285
  163.1 107.5 %all-gather.15.cloned.1.call-start = ((), (), s32[]{:S(2)}) async-start(), calls=%async_computation.7 | async-start | bytes 5308416 | tf_op jit(solution)/shard_map/all_gather | solution.py:307
  206.1 1.7 copy-start.2
  214.0 35.6 %all-to-all-start.3 = ((bf16[16,48,1536]{2,1,0:T(8,128)(2,1)}), bf16[16,48,1536]{2,1,0:T(8,128)(2,1)S(1)}, u32[]{:S(2)}, u32[]{:S(2)}) async-start(bf16[16,48,1536]{2,1,0:T(8,128)(2,1)} %bitcast.112), calls=%async_computation.3 | async-start | bytes 4718592 | tf_op jit(solution)/shard_map/all_to_all | solution.py:285
  218.8 68.4 %all-gather.17.cloned.1.call-start = ((), (), s32[]{:S(2)}) async-start(), calls=%async_computation.8 | async-start | bytes 3981312 | tf_op jit(solution)/shard_map/all_gather | solution.py:307
  249.7 1.4 copy-start.4
  256.3 21.1 %all-to-all-start.4 = ((bf16[16,48,512]{2,1,0:T(8,128)(2,1)}), bf16[16,48,512]{2,1,0:T(8,128)(2,1)S(1)}, u32[]{:S(2)}, u32[]{:S(2)}) async-start(bf16[16,48,512]{2,1,0:T(8,128)(2,1)} %bitcast.47), calls=%async_computation.4 | async-start | bytes 1572864 | tf_op jit(solution)/shard_map/all_to_all | solution.py:285
  262.5 49.8 %all-gather.19.cloned.1.call-start = ((), (), s32[]{:S(2)}) async-start(), calls=%async_computation.9 | async-start | bytes 1327104 | tf_op jit(solution)/shard_map/all_gather | solution.py:307
  277.4 0.9 copy-start.5
Sparse Core Ops, SparseCore 0:
  103.2 38.6 all-gather.10
  158.2 35.3 all-gather.12
  214.2 35.2 all-gather.14
  256.4 30.7 all-gather.16
  288.8 23.5 all-gather.18

commit v9 on v7

--- a/solution.py
+++ b/solution.py
@@ -23,7 +23,7 @@
     tok_ref[...] = ordered.astype(tok_ref.dtype)
     for q in range(pairs):
         x = ordered[:, 128 * q : 128 * (q + 1)]
-        factor = lane_pick(facg_ref[0, :, 2 * q : 2 * q + 1], facg_ref[0, :, 2 * q + 1 : 2 * q + 2])
+        factor = facg_ref[:, 128 * q : 128 * (q + 1)]
         scaled = (factor * x).astype(jnp.bfloat16)
         out_ref[q, 0:state_size, :] = jnp.dot(
             bt_ref[...], scaled, preferred_element_type=jnp.float32
@@ -127,7 +127,7 @@
         grid=(groups,),
         in_specs=[
             pl.BlockSpec(bt.shape, lambda g: (0, 0)),
-            pl.BlockSpec((1, length, GROUP), lambda g: (g + first, 0, 0)),
+            pl.BlockSpec((length, GROUP * 64), lambda g: (0, g + first)),
             pl.BlockSpec((1, GROUP * 64), lambda g: (0, g + first)),
             pl.BlockSpec(onehot.shape, lambda g: (0, 0)),
             pl.BlockSpec((rows, GROUP * 64), lambda g: (0, g)),
@@ -250,7 +250,7 @@
         return a.reshape(local_rows, groups, GROUP).transpose(1, 0, 2)
 
     cum_grouped = grouped(cum)
-    fac_grouped = grouped(factor)
+    fac_grouped = jnp.repeat(factor, head_size, axis=1)
     cum_t = cum.T
     step_t = steps.T
     decay_lanes = jnp.repeat(jnp.exp(ending), head_size).reshape(1, -1)

time: 303 us -> 317 us (1.046)
  local copies, waits for them, and re-layouts: 19 us -> 45.2 us
  waiting for transfers between devices: 96.3 us -> 78.8 us
    reshape x0 -> x1, local copies, waits for them, and re-layouts: none -> 17.4 us  [on_device(): fac_grouped = jnp.repeat(factor, head_size, axis=1)]
    all_to_all x5, waiting for transfers between devices: 71.8 us -> 54.5 us  [on_device(): lax.all_to_all(sends[c], 'stream', split_axis=0, concat_axis=0, tiled=True)]
    broadcast_in_dim x0 -> x1, local copies, waits for them, and re-layouts: none -> 7.95 us  [on_device(): fac_grouped = jnp.repeat(factor, head_size, axis=1)]
    unnamed x14 -> x20, local copies, waits for them, and re-layouts: 3.2 us -> 6.53 us
  transfers between devices with their start and end apart: 11 -> 11, of which waited for: 7 -> 6; matrix products, arithmetic and copies ran while one was open for 9% -> 16% of each run, Pallas kernels for 37% -> 36%
where the time goes in v9:
time: 317 us; the launch traced here: 315 us
  Pallas kernels  122 us (38%)
  waiting for transfers between devices  78.8 us (25%)
  local copies, waits for them, and re-layouts  45.2 us (14%)
  starting transfers between devices  37 us (12%)
  other arithmetic  15.8 us (5%)
  between operations  13.4 us (4%)
    all_to_all x5, waiting for transfers between devices, on_device(): lax.all_to_all(sends[c], 'stream', split_axis=0, concat_axis=0, tiled=True)  54.5 us
    pallas_call x5, Pallas kernels, local_call(): pl.pallas_call(local_kernel, grid=(groups,), in_specs=[pl.BlockSpec((leng...  40.6 us
    pallas_call x5, Pallas kernels, combine_call(): pl.pallas_call(combine_kernel, grid=(groups,), in_specs=[pl.BlockSpec(mem...  29.4 us
    pallas_call x5, Pallas kernels, carried_call(): pl.pallas_call(carried_kernel, grid=(groups,), in_specs=[pl.BlockSpec(bt....  28.7 us
    all_to_all x5, starting transfers between devices, on_device(): lax.all_to_all(sends[c], 'stream', split_axis=0, concat_axis=0, tiled=True)  27.9 us
    pallas_call x5, Pallas kernels, send_call(): pl.pallas_call(send_kernel, grid=(groups,), in_specs=[pl.BlockSpec(onehot...  23.7 us
    all_gather x5, waiting for transfers between devices, on_device(): gathers.append(lax.all_gather(carried, 'pos'))  20.6 us
    reshape x1, local copies, waits for them, and re-layouts, on_device(): fac_grouped = jnp.repeat(factor, head_size, axis=1)  17.4 us
  transfers between devices with their start and end apart: 11, of which 6 were waited for; matrix products, arithmetic and copies ran while one was open for 16% of the time, Pallas kernels for 36%

profile of v9, /device:TPU:1, one launch (start us, length us, event | category | flops | bytes accessed | tf_op | source)
XLA Modules:
  0.0 314.7 jit_solution(15255421712590752465)
XLA Ops:
  8.3 1.1 pad_maximum_fusion
  9.4 3.3 %gather_fusion = bf16[768,384]{1,0:T(8,128)(2,1)} fusion(bf16[512,384]{1,0:T(8,128)(2,1)S(1)} %pad_maximum_fusion, s32[1024]{0:T(1024)S(1)} %pad_clamp_fusion.1), kind=kCustom, calls=%fused_computation | custom fusion | bytes 1182720 | tf_op jit(solution)/shard_map/jit(_take)/gather | solution.py:196
  12.7 8.4 %all-to-all-start.2 = ((bf16[16,48,384]{2,1,0:T(8,128)(2,1)}), bf16[16,48,384]{2,1,0:T(8,128)(2,1)S(1)}, u32[]{:S(2)}, u32[]{:S(2)}) async-start(bf16[16,48,384]{2,1,0:T(8,128)(2,1)} %bitcast.8), calls=%async_computation.2 | async-start | bytes 1179648 | tf_op jit(solution)/shard_map/all_to_all | solution.py:206
  21.1 0.9 dynamic-slice_reduce_fusion
  22.1 1.1 fusion.onehot_ref
  23.2 5.3 %shard_map.64 = bf16[768,2048]{1,0:T(8,128)(2,1)} custom-call(bf16[768,512]{1,0:T(8,128)(2,1)} %fusion.onehot_ref, bf16[512,8192]{1,0:T(8,128)(2,1)} %bitcast.88), custom_call_target="tpu_custom_call" | custom-call | tf_op jit(solution)/shard_map/pallas_call | solution.py:48
  28.6 3.6 %all-to-all-done.2 = bf16[16,48,384]{2,1,0:T(8,128)(2,1)S(1)} async-done(((bf16[16,48,384]{2,1,0:T(8,128)(2,1)}), bf16[16,48,384]{2,1,0:T(8,128)(2,1)S(1)}, u32[]{:S(2)}, u32[]{:S(2)}) %all-to-all-start.2) | async-done | bytes 589856 | tf_op jit(solution)/shard_map/all_to_all | solution.py:206
  32.2 4.5 %all-to-all-start = ((bf16[16,48,2048]{2,1,0:T(8,128)(2,1)}), bf16[16,48,2048]{2,1,0:T(8,128)(2,1)}, u32[]{:S(2)}, u32[]{:S(2)}) async-start(bf16[16,48,2048]{2,1,0:T(8,128)(2,1)} %bitcast.105), calls=%async_computation | async-start | bytes 6291456 | tf_op jit(solution)/shard_map/all_to_all | solution.py:274
  37.4 5.4 %shard_map.65 = bf16[768,2048]{1,0:T(8,128)(2,1)} custom-call(bf16[768,512]{1,0:T(8,128)(2,1)} %fusion.onehot_ref, bf16[512,8192]{1,0:T(8,128)(2,1)} %bitcast.89), custom_call_target="tpu_custom_call" | custom-call | tf_op jit(solution)/shard_map/pallas_call | solution.py:48
  42.9 4.4 %compare_select_fusion.2 = (s32[512,1]{0,1:T(1,128)S(1)}, s32[512,1]{0,1:T(1,128)S(1)}) fusion(s32[]{:T(128)} %bitcast.21, s32[]{:T(128)} %bitcast.22, s32[]{:T(128)} %bitcast.23, s32[]{:T(128)} %bitcast.24, s32[]{:T(128)} %bitcast.25, s32[]{:T(128)} %bitcast.27, s32[]{:T(128)} %bitcast.26, s32[512,1]{0,1:T(1,128)S(1)} %bitcast.126), kind=kLoop, calls=%fused_computation.33 | loop fusion | flops 7680 | bytes 6172 | tf_op jit(solution)/shard_map/jit(_take)/gather | solution.py:232
  47.4 5.6 %select_subtract_fusion = (s32[512]{0:T(512)S(1)}, s32[512]{0:T(512)S(1)}) fusion(s32[512]{0:T(512)S(1)} %convert_reduce_fusion, pred[512]{0:T(512)(128)(4,1)S(1)} %get-tuple-element.56, pred[512]{0:T(512)(128)(4,1)S(1)} %get-tuple-element.55, pred[512]{0:T(512)(128)(4,1)S(1)} %get-tuple-element.57, pred[512]{0:T(512)(128)(4,1)S(1)} %get-tuple-element.54, ...), kind=kLoop, calls=%fused_computation.48 | loop fusion | flops 10240 | bytes 12836 | tf_op jit(solution)/shard_map/sub | solution.py:233
  53.0 1.1 fusion.1.onehot_ref
  54.1 1.9 gather_fusion.1
  58.0 0.9 exponential_multiply_fusion
  58.9 8.0 %broadcast_in_dim.33 = f32[512,128,64]{0,2,1:T(8,128)} broadcast(f32[512,128]{0,1:T(8,128)S(1)} %get-tuple-element.68), dimensions={0,1} | broadcast | bytes 17039360 | tf_op jit(solution)/shard_map/broadcast_in_dim | solution.py:253
  66.9 17.4 %copy.49.facg_ref = f32[512,8192]{1,0:T(8,128)} copy(f32[512,8192]{0,1:T(8,128)} %bitcast.93) | data formatting | bytes 33554432 | tf_op jit(solution)/shard_map/reshape | solution.py:253
  85.8 6.6 %shard_map.66 = (bf16[16,144,128]{2,1,0:T(8,128)(2,1)}, bf16[512,2048]{1,0:T(8,128)(2,1)}) custom-call(bf16[128,512]{1,0:T(8,128)(2,1)} %bitcast.109, f32[512,8192]{1,0:T(8,128)} %copy.49.facg_ref, f32[1,8192]{1,0:T(1,128)} %reshape_reshape.6.decay_ref, bf16[512,768]{1,0:T(8,128)(2,1)} %fusion.1.onehot_ref, bf16[768,2048]{1,0:T(8,128)(2,1)} %bitcast.39.arr_ref), custom_call_target="tpu_custom_call" | custom-call | tf_op jit(solution)/shard_map/pallas_call | solution.py:125
  92.5 6.6 %all-to-all-start.1 = ((bf16[16,48,2048]{2,1,0:T(8,128)(2,1)}), bf16[16,48,2048]{2,1,0:T(8,128)(2,1)S(1)}, u32[]{:S(2)}, u32[]{:S(2)}) async-start(bf16[16,48,2048]{2,1,0:T(8,128)(2,1)} %bitcast.104), calls=%async_computation.1 | async-start | bytes 6291456 | tf_op jit(solution)/shard_map/all_to_all | solution.py:274
  99.1 5.5 %shard_map.68 = bf16[768,2048]{1,0:T(8,128)(2,1)} custom-call(bf16[768,512]{1,0:T(8,128)(2,1)} %fusion.onehot_ref, bf16[512,8192]{1,0:T(8,128)(2,1)} %bitcast.90), custom_call_target="tpu_custom_call" | custom-call | tf_op jit(solution)/shard_map/pallas_call | solution.py:48
  105.3 2.7 copy.48
  108.1 2.3 fusion.9.scores_ref
  110.3 9.5 %shard_map.67.refs_0_ = f32[512,2048]{1,0:T(8,128)} custom-call(f32[512,512]{1,0:T(8,128)} %fusion.9.scores_ref, f32[16,512,8]{2,1,0:T(8,128)} %bitcast.78, f32[128,512]{1,0:T(8,128)} %bitcast.97, f32[128,512]{1,0:T(8,128)} %get-tuple-element.69.stept_ref, bf16[512,2048]{1,0:T(8,128)(2,1)} %get-tuple-element.29.tok_ref, f32[1,8192]{1,0:T(1,128)} %reshape_reshape.7.skip_ref), custom_call_target="tpu_custom_call" | custom-call | tf_op jit(solution)/shard_map/pallas_call | solution.py:150
  119.8 20.2 %all-to-all-done.1 = bf16[16,48,2048]{2,1,0:T(8,128)(2,1)S(1)} async-done(((bf16[16,48,2048]{2,1,0:T(8,128)(2,1)}), bf16[16,48,2048]{2,1,0:T(8,128)(2,1)S(1)}, u32[]{:S(2)}, u32[]{:S(2)}) %all-to-all-start.1) | async-done | bytes 3145760 | tf_op jit(solution)/shard_map/all_to_all | solution.py:274
  140.0 1.7 copy-done.2
  141.7 6.6 %shard_map.69 = (bf16[16,144,128]{2,1,0:T(8,128)(2,1)}, bf16[512,2048]{1,0:T(8,128)(2,1)}) custom-call(bf16[128,512]{1,0:T(8,128)(2,1)} %bitcast.110, f32[512,8192]{1,0:T(8,128)} %copy.49.facg_ref, f32[1,8192]{1,0:T(1,128)} %reshape_reshape.6.decay_ref, bf16[512,768]{1,0:T(8,128)(2,1)} %fusion.1.onehot_ref, bf16[768,2048]{1,0:T(8,128)(2,1)} %bitcast.103), custom_call_target="tpu_custom_call" | custom-call | tf_op jit(solution)/shard_map/pallas_call | solution.py:125
  148.3 6.1 %all-to-all-start.3 = ((bf16[16,48,2048]{2,1,0:T(8,128)(2,1)}), bf16[16,48,2048]{2,1,0:T(8,128)(2,1)S(1)}, u32[]{:S(2)}, u32[]{:S(2)}) async-start(bf16[16,48,2048]{2,1,0:T(8,128)(2,1)} %bitcast.106), calls=%async_computation.3 | async-start | bytes 6291456 | tf_op jit(solution)/shard_map/all_to_all | solution.py:274
  154.6 4.8 %shard_map.72 = bf16[768,1536]{1,0:T(8,128)(2,1)} custom-call(bf16[768,512]{1,0:T(8,128)(2,1)} %fusion.onehot_ref, bf16[512,8192]{1,0:T(8,128)(2,1)} %bitcast.91), custom_call_target="tpu_custom_call" | custom-call | tf_op jit(solution)/shard_map/pallas_call | solution.py:48
  159.4 9.7 %shard_map.70.refs_1_ = f32[512,2048]{1,0:T(8,128)} custom-call(f32[512,512]{1,0:T(8,128)} %fusion.9.scores_ref, f32[16,512,8]{2,1,0:T(8,128)} %bitcast.79, f32[128,512]{1,0:T(8,128)} %bitcast.98, f32[128,512]{1,0:T(8,128)} %get-tuple-element.69.stept_ref, bf16[512,2048]{1,0:T(8,128)(2,1)} %get-tuple-element.32.tok_ref, f32[1,8192]{1,0:T(1,128)} %reshape_reshape.7.skip_ref), custom_call_target="tpu_custom_call" | custom-call | tf_op jit(solution)/shard_map/pallas_call | solution.py:150
  169.1 6.8 %shard_map.71.refs_0_ = bf16[512,8192]{1,0:T(8,128)(2,1)} custom-call(s32[1]{0:T(128)} %bitcast.place_ref, f32[512,2048]{1,0:T(8,128)} %shard_map.67.refs_0_, bf16[8,16,144,128]{3,2,1,0:T(8,128)(2,1)} %bitcast.115, f32[16,512,8]{2,1,0:T(8,128)} %bitcast.80, bf16[512,128]{1,0:T(8,128)(2,1)} %get-tuple-element.62.refs_3_.refs_4_), custom_call_target="tpu_custom_call" | custom-call | tf_op jit(solution)/shard_map/pallas_call | solution.py:183
  175.9 23.6 %all-to-all-done.3 = bf16[16,48,2048]{2,1,0:T(8,128)(2,1)S(1)} async-done(((bf16[16,48,2048]{2,1,0:T(8,128)(2,1)}), bf16[16,48,2048]{2,1,0:T(8,128)(2,1)S(1)}, u32[]{:S(2)}, u32[]{:S(2)}) %all-to-all-start.3) | async-done | bytes 3145760 | tf_op jit(solution)/shard_map/all_to_all | solution.py:274
  199.5 1.6 copy-done.1
  201.1 6.6 %shard_map.73 = (bf16[16,144,128]{2,1,0:T(8,128)(2,1)}, bf16[512,2048]{1,0:T(8,128)(2,1)}) custom-call(bf16[128,512]{1,0:T(8,128)(2,1)} %bitcast.111, f32[512,8192]{1,0:T(8,128)} %copy.49.facg_ref, f32[1,8192]{1,0:T(1,128)} %reshape_reshape.6.decay_ref, bf16[512,768]{1,0:T(8,128)(2,1)} %fusion.1.onehot_ref, bf16[768,2048]{1,0:T(8,128)(2,1)} %bitcast.102), custom_call_target="tpu_custom_call" | custom-call | tf_op jit(solution)/shard_map/pallas_call | solution.py:125
  207.7 3.7 %all-to-all-start.4 = ((bf16[16,48,1536]{2,1,0:T(8,128)(2,1)}), bf16[16,48,1536]{2,1,0:T(8,128)(2,1)S(1)}, u32[]{:S(2)}, u32[]{:S(2)}) async-start(bf16[16,48,1536]{2,1,0:T(8,128)(2,1)} %bitcast.108), calls=%async_computation.4 | async-start | bytes 4718592 | tf_op jit(solution)/shard_map/all_to_all | solution.py:274
  211.5 2.7 shard_map.76
  214.3 9.5 %shard_map.74.refs_1_ = f32[512,2048]{1,0:T(8,128)} custom-call(f32[512,512]{1,0:T(8,128)} %fusion.9.scores_ref, f32[16,512,8]{2,1,0:T(8,128)} %bitcast.81, f32[128,512]{1,0:T(8,128)} %bitcast.99, f32[128,512]{1,0:T(8,128)} %get-tuple-element.69.stept_ref, bf16[512,2048]{1,0:T(8,128)(2,1)} %get-tuple-element.36.tok_ref, f32[1,8192]{1,0:T(1,128)} %reshape_reshape.7.skip_ref), custom_call_target="tpu_custom_call" | custom-call | tf_op jit(solution)/shard_map/pallas_call | solution.py:150
  223.7 6.8 %shard_map.75.refs_0_ = bf16[512,8192]{1,0:T(8,128)(2,1)} custom-call(s32[1]{0:T(128)} %bitcast.place_ref, bf16[512,8192]{1,0:T(8,128)(2,1)} %shard_map.71.refs_0_, f32[512,2048]{1,0:T(8,128)} %shard_map.70.refs_1_, bf16[8,16,144,128]{3,2,1,0:T(8,128)(2,1)} %bitcast.114, f32[16,512,8]{2,1,0:T(8,128)} %bitcast.82, ...), custom_call_target="tpu_custom_call", output_to_operand_aliasing={{}: (1, {})} | custom-call | tf_op jit(solution)/shard_map/pallas_call | solution.py:183
  230.6 10.7 %all-to-all-done.4 = bf16[16,48,1536]{2,1,0:T(8,128)(2,1)S(1)} async-done(((bf16[16,48,1536]{2,1,0:T(8,128)(2,1)}), bf16[16,48,1536]{2,1,0:T(8,128)(2,1)S(1)}, u32[]{:S(2)}, u32[]{:S(2)}) %all-to-all-start.4) | async-done | bytes 2359328 | tf_op jit(solution)/shard_map/all_to_all | solution.py:274
  241.2 1.4 copy-done.3
  242.7 5.6 %shard_map.77 = (bf16[12,144,128]{2,1,0:T(8,128)(2,1)}, bf16[512,1536]{1,0:T(8,128)(2,1)}) custom-call(bf16[128,512]{1,0:T(8,128)(2,1)} %bitcast.112, f32[512,8192]{1,0:T(8,128)} %copy.49.facg_ref, f32[1,8192]{1,0:T(1,128)} %reshape_reshape.6.decay_ref, bf16[512,768]{1,0:T(8,128)(2,1)} %fusion.1.onehot_ref, bf16[768,1536]{1,0:T(8,128)(2,1)} %bitcast.107), custom_call_target="tpu_custom_call" | custom-call | tf_op jit(solution)/shard_map/pallas_call | solution.py:125
  248.3 7.1 %all-to-all-start.5 = ((bf16[16,48,512]{2,1,0:T(8,128)(2,1)}), bf16[16,48,512]{2,1,0:T(8,128)(2,1)S(1)}, u32[]{:S(2)}, u32[]{:S(2)}) async-start(bf16[16,48,512]{2,1,0:T(8,128)(2,1)} %bitcast.46), calls=%async_computation.5 | async-start | bytes 1572864 | tf_op jit(solution)/shard_map/all_to_all | solution.py:274
  255.6 7.8 %shard_map.78.refs_1_ = f32[512,1536]{1,0:T(8,128)} custom-call(f32[512,512]{1,0:T(8,128)} %fusion.9.scores_ref, f32[16,512,8]{2,1,0:T(8,128)} %bitcast.83, f32[128,512]{1,0:T(8,128)} %bitcast.100, f32[128,512]{1,0:T(8,128)} %get-tuple-element.69.stept_ref, bf16[512,1536]{1,0:T(8,128)(2,1)} %get-tuple-element.41.tok_ref, f32[1,8192]{1,0:T(1,128)} %reshape_reshape.7.skip_ref), custom_call_target="tpu_custom_call" | custom-call | tf_op jit(solution)/shard_map/pallas_call | solution.py:150
  263.4 6.8 %shard_map.79.refs_0_ = bf16[512,8192]{1,0:T(8,128)(2,1)} custom-call(s32[1]{0:T(128)} %bitcast.place_ref, bf16[512,8192]{1,0:T(8,128)(2,1)} %shard_map.75.refs_0_, f32[512,2048]{1,0:T(8,128)} %shard_map.74.refs_1_, bf16[8,16,144,128]{3,2,1,0:T(8,128)(2,1)} %bitcast.116, f32[16,512,8]{2,1,0:T(8,128)} %bitcast.84, ...), custom_call_target="tpu_custom_call", output_to_operand_aliasing={{}: (1, {})} | custom-call | tf_op jit(solution)/shard_map/pallas_call | solution.py:183
  271.1 3.3 %shard_map.81 = (bf16[4,144,128]{2,1,0:T(8,128)(2,1)}, bf16[512,512]{1,0:T(8,128)(2,1)}) custom-call(bf16[128,512]{1,0:T(8,128)(2,1)} %bitcast.113, f32[512,8192]{1,0:T(8,128)} %copy.49.facg_ref, f32[1,8192]{1,0:T(1,128)} %reshape_reshape.6.decay_ref, bf16[512,768]{1,0:T(8,128)(2,1)} %fusion.1.onehot_ref, bf16[768,512]{1,0:T(8,128)(2,1)} %bitcast.118), custom_call_target="tpu_custom_call" | custom-call | tf_op jit(solution)/shard_map/pallas_call | solution.py:125
  274.5 4.1 %shard_map.82.refs_1_ = f32[512,512]{1,0:T(8,128)} custom-call(f32[512,512]{1,0:T(8,128)} %fusion.9.scores_ref, f32[16,512,8]{2,1,0:T(8,128)} %bitcast.85, f32[128,512]{1,0:T(8,128)} %bitcast.101, f32[128,512]{1,0:T(8,128)} %get-tuple-element.69.stept_ref, bf16[512,512]{1,0:T(8,128)(2,1)} %get-tuple-element.47.tok_ref, f32[1,8192]{1,0:T(1,128)} %reshape_reshape.7.skip_ref), custom_call_target="tpu_custom_call" | custom-call | tf_op jit(solution)/shard_map/pallas_call | solution.py:150
  278.6 1.4 all-gather.17.cloned.1.call-done
  280.0 5.9 %shard_map.80.refs_0_ = bf16[512,8192]{1,0:T(8,128)(2,1)} custom-call(s32[1]{0:T(128)} %bitcast.place_ref, bf16[512,8192]{1,0:T(8,128)(2,1)} %shard_map.79.refs_0_, f32[512,1536]{1,0:T(8,128)} %shard_map.78.refs_1_, bf16[8,12,144,128]{3,2,1,0:T(8,128)(2,1)} %bitcast.117, f32[16,512,8]{2,1,0:T(8,128)} %bitcast.86, ...), custom_call_target="tpu_custom_call", output_to_operand_aliasing={{}: (1, {})} | custom-call | tf_op jit(solution)/shard_map/pallas_call | solution.py:183
  285.8 19.2 %all-gather.19.cloned.1.call-done = bf16[32,144,128]{2,1,0:T(8,128)(2,1)} async-done(((bf16[4,144,128]{2,1,0:T(8,128)(2,1)}), bf16[32,144,128]{2,1,0:T(8,128)(2,1)}) %all-gather.19.cloned.1.call-update) | async-done | bytes 1179664 | tf_op jit(solution)/shard_map/all_gather | solution.py:296
  305.1 3.1 shard_map.83
  (66 shorter events, 8.7 us)
Async XLA Ops:
  12.7 19.5 %all-to-all-start.2 = ((bf16[16,48,384]{2,1,0:T(8,128)(2,1)}), bf16[16,48,384]{2,1,0:T(8,128)(2,1)S(1)}, u32[]{:S(2)}, u32[]{:S(2)}) async-start(bf16[16,48,384]{2,1,0:T(8,128)(2,1)} %bitcast.8), calls=%async_computation.2 | async-start | bytes 1179648 | tf_op jit(solution)/shard_map/all_to_all | solution.py:206
  32.2 53.7 %all-to-all-start = ((bf16[16,48,2048]{2,1,0:T(8,128)(2,1)}), bf16[16,48,2048]{2,1,0:T(8,128)(2,1)}, u32[]{:S(2)}, u32[]{:S(2)}) async-start(bf16[16,48,2048]{2,1,0:T(8,128)(2,1)} %bitcast.105), calls=%async_computation | async-start | bytes 6291456 | tf_op jit(solution)/shard_map/all_to_all | solution.py:274
  36.7 132.4 %all-gather.11.cloned.1.call-start = ((), (), s32[]{:S(2)}) async-start(), calls=%async_computation.6 | async-start | bytes 5308416 | tf_op jit(solution)/shard_map/all_gather | solution.py:296
  37.4 15.6 %copy-start.7 = (f32[128]{0:T(128)S(1)}, f32[128]{0:T(128)}, u32[]{:S(2)}) copy-start(f32[128]{0:T(128)} %param.9) | copy-start | bytes 1540
  56.0 10.8 %copy-start.5 = (bf16[512,384]{1,0:T(8,128)(2,1)}, bf16[512,384]{1,0:T(8,128)(2,1)S(1)}, u32[]{:S(2)}) copy-start(bf16[512,384]{1,0:T(8,128)(2,1)S(1)} %gather_fusion.1) | copy-start | bytes 1179652
  57.8 47.5 %copy-start = (f32[16,8,4,128]{3,1,2,0:T(8,128)}, f32[16,8,4,128]{3,1,2,0:T(8,128)S(1)}, u32[]{:S(2)}) copy-start(f32[16,8,4,128]{3,1,2,0:T(8,128)S(1)} %copy.64) | copy-start | bytes 786436
  92.5 47.6 %all-to-all-start.1 = ((bf16[16,48,2048]{2,1,0:T(8,128)(2,1)}), bf16[16,48,2048]{2,1,0:T(8,128)(2,1)S(1)}, u32[]{:S(2)}, u32[]{:S(2)}) async-start(bf16[16,48,2048]{2,1,0:T(8,128)(2,1)} %bitcast.104), calls=%async_computation.1 | async-start | bytes 6291456 | tf_op jit(solution)/shard_map/all_to_all | solution.py:274
  99.0 5.5 %copy-start.6 = (f32[128]{0:T(128)S(1)}, f32[128]{0:T(128)}, u32[]{:S(2)}) copy-start(f32[128]{0:T(128)} %param.10) | copy-start | bytes 1540
  99.0 124.7 %all-gather.13.cloned.1.call-start = ((), (), s32[]{:S(2)}) async-start(), calls=%async_computation.7 | async-start | bytes 5308416 | tf_op jit(solution)/shard_map/all_gather | solution.py:296
  140.0 1.7 copy-start.2
  148.3 51.2 %all-to-all-start.3 = ((bf16[16,48,2048]{2,1,0:T(8,128)(2,1)}), bf16[16,48,2048]{2,1,0:T(8,128)(2,1)S(1)}, u32[]{:S(2)}, u32[]{:S(2)}) async-start(bf16[16,48,2048]{2,1,0:T(8,128)(2,1)} %bitcast.106), calls=%async_computation.3 | async-start | bytes 6291456 | tf_op jit(solution)/shard_map/all_to_all | solution.py:274
  154.4 109.0 %all-gather.15.cloned.1.call-start = ((), (), s32[]{:S(2)}) async-start(), calls=%async_computation.8 | async-start | bytes 5308416 | tf_op jit(solution)/shard_map/all_gather | solution.py:296
  199.5 1.6 copy-start.1
  207.7 33.5 %all-to-all-start.4 = ((bf16[16,48,1536]{2,1,0:T(8,128)(2,1)}), bf16[16,48,1536]{2,1,0:T(8,128)(2,1)S(1)}, u32[]{:S(2)}, u32[]{:S(2)}) async-start(bf16[16,48,1536]{2,1,0:T(8,128)(2,1)} %bitcast.108), calls=%async_computation.4 | async-start | bytes 4718592 | tf_op jit(solution)/shard_map/all_to_all | solution.py:274
  211.5 68.5 %all-gather.17.cloned.1.call-start = ((), (), s32[]{:S(2)}) async-start(), calls=%async_computation.9 | async-start | bytes 3981312 | tf_op jit(solution)/shard_map/all_gather | solution.py:296
  241.2 1.4 copy-start.3
  248.3 22.0 %all-to-all-start.5 = ((bf16[16,48,512]{2,1,0:T(8,128)(2,1)}), bf16[16,48,512]{2,1,0:T(8,128)(2,1)S(1)}, u32[]{:S(2)}, u32[]{:S(2)}) async-start(bf16[16,48,512]{2,1,0:T(8,128)(2,1)} %bitcast.46), calls=%async_computation.5 | async-start | bytes 1572864 | tf_op jit(solution)/shard_map/all_to_all | solution.py:274
  255.4 49.7 %all-gather.19.cloned.1.call-start = ((), (), s32[]{:S(2)}) async-start(), calls=%async_computation.10 | async-start | bytes 1327104 | tf_op jit(solution)/shard_map/all_gather | solution.py:296
  270.2 0.9 copy-start.4
Sparse Core Ops, SparseCore 0:
  92.6 37.7 all-gather.10
  148.4 36.1 all-gather.12
  207.8 34.2 all-gather.14
  248.4 31.5 all-gather.16
  281.5 23.5 all-gather.18

commit v10 on v7

--- a/solution.py
+++ b/solution.py
@@ -293,7 +293,16 @@
         carried, chunk_tokens = carried_call(
             bt, fac_grouped, decay_lanes, onehot, arrived.reshape(-1, arrived.shape[2]), firsts[c]
         )
-        gathers.append(lax.all_gather(carried, "pos"))
+        if c + 1 < len(sizes):
+            gathers.append(lax.all_gather(carried, "pos"))
+        else:
+            half = carried.shape[0] // 2
+            gathers.append(
+                jnp.concatenate(
+                    [lax.all_gather(carried[:half], "pos"), lax.all_gather(carried[half:], "pos")],
+                    axis=1,
+                )
+            )
         partials.append(
             local_call(scores, cum_grouped, cum_t, step_t, chunk_tokens, skip_lanes, firsts[c])
         )

time: 303 us -> 316 us (1.043)
  blocking collectives: 0 us -> 28.3 us
  waiting for transfers between devices: 96.3 us -> 75.8 us
  local copies, waits for them, and re-layouts: 19 us -> 22.4 us
    all_gather x0 -> x2, blocking collectives: none -> 28.3 us  [the longest x1 15.2 us: on_device(): lax.all_gather(carried[:half], 'pos')]
    all_gather x5 -> x4, waiting for transfers between devices: 20.9 us -> 0.01 us  [on_device(): gathers.append(lax.all_gather(carried, 'pos'))]
    unnamed x14 -> x22, local copies, waits for them, and re-layouts: 3.2 us -> 6.57 us
  transfers between devices with their start and end apart: 11 -> 10, of which waited for: 7 -> 5; matrix products, arithmetic and copies ran while one was open for 9% -> 10% of each run, Pallas kernels for 37% -> 34%
where the time goes in v10:
time: 316 us; the launch traced here: 314 us
  Pallas kernels  120 us (38%)
  waiting for transfers between devices  75.8 us (24%)
  starting transfers between devices  34 us (11%)
  blocking collectives  28.3 us (9%)
  local copies, waits for them, and re-layouts  22.4 us (7%)
  other arithmetic  17.1 us (5%)
  between operations  13.4 us (4%)
    all_to_all x5, waiting for transfers between devices, on_device(): lax.all_to_all(sends[c], 'stream', split_axis=0, concat_axis=0, tiled=True)  72.2 us
    pallas_call x5, Pallas kernels, local_call(): pl.pallas_call(local_kernel, grid=(groups,), in_specs=[pl.BlockSpec((leng...  40.5 us
    pallas_call x5, Pallas kernels, combine_call(): pl.pallas_call(combine_kernel, grid=(groups,), in_specs=[pl.BlockSpec(mem...  29.5 us
    pallas_call x5, Pallas kernels, carried_call(): pl.pallas_call(carried_kernel, grid=(groups,), in_specs=[pl.BlockSpec(bt....  26.8 us
    all_to_all x5, starting transfers between devices, on_device(): lax.all_to_all(sends[c], 'stream', split_axis=0, concat_axis=0, tiled=True)  25.2 us
    pallas_call x5, Pallas kernels, send_call(): pl.pallas_call(send_kernel, grid=(groups,), in_specs=[pl.BlockSpec(onehot...  23.5 us
    all_gather x1, blocking collectives, on_device(): lax.all_gather(carried[:half], 'pos')  15.2 us
    all_gather x1, blocking collectives, on_device(): lax.all_gather(carried[half:], 'pos')  13.2 us
  transfers between devices with their start and end apart: 10, of which 5 were waited for; matrix products, arithmetic and copies ran while one was open for 10% of the time, Pallas kernels for 34%

profile of v10, /device:TPU:1, one launch (start us, length us, event | category | flops | bytes accessed | tf_op | source)
XLA Modules:
  0.0 313.6 jit_solution(15875677901705646020)
XLA Ops:
  8.3 1.1 pad_maximum_fusion.1
  9.4 3.2 %gather_fusion = bf16[768,384]{1,0:T(8,128)(2,1)} fusion(bf16[512,384]{1,0:T(8,128)(2,1)S(1)} %pad_maximum_fusion.1, s32[1024]{0:T(1024)S(1)} %pad_clamp_fusion.1), kind=kCustom, calls=%fused_computation | custom fusion | bytes 1182720 | tf_op jit(solution)/shard_map/jit(_take)/gather | solution.py:196
  12.6 8.4 %all-to-all-start.2 = ((bf16[16,48,384]{2,1,0:T(8,128)(2,1)}), bf16[16,48,384]{2,1,0:T(8,128)(2,1)S(1)}, u32[]{:S(2)}, u32[]{:S(2)}) async-start(bf16[16,48,384]{2,1,0:T(8,128)(2,1)} %bitcast.8), calls=%async_computation.2 | async-start | bytes 1179648 | tf_op jit(solution)/shard_map/all_to_all | solution.py:206
  22.1 1.1 fusion.onehot_ref
  23.3 5.3 %shard_map.64 = bf16[768,2048]{1,0:T(8,128)(2,1)} custom-call(bf16[768,512]{1,0:T(8,128)(2,1)} %fusion.onehot_ref, bf16[512,8192]{1,0:T(8,128)(2,1)} %bitcast.91), custom_call_target="tpu_custom_call" | custom-call | tf_op jit(solution)/shard_map/pallas_call | solution.py:48
  28.6 3.5 %all-to-all-done.2 = bf16[16,48,384]{2,1,0:T(8,128)(2,1)S(1)} async-done(((bf16[16,48,384]{2,1,0:T(8,128)(2,1)}), bf16[16,48,384]{2,1,0:T(8,128)(2,1)S(1)}, u32[]{:S(2)}, u32[]{:S(2)}) %all-to-all-start.2) | async-done | bytes 589856 | tf_op jit(solution)/shard_map/all_to_all | solution.py:206
  32.1 4.5 %all-to-all-start = ((bf16[16,48,2048]{2,1,0:T(8,128)(2,1)}), bf16[16,48,2048]{2,1,0:T(8,128)(2,1)}, u32[]{:S(2)}, u32[]{:S(2)}) async-start(bf16[16,48,2048]{2,1,0:T(8,128)(2,1)} %bitcast.109), calls=%async_computation | async-start | bytes 6291456 | tf_op jit(solution)/shard_map/all_to_all | solution.py:274
  37.4 5.4 %shard_map.65 = bf16[768,2048]{1,0:T(8,128)(2,1)} custom-call(bf16[768,512]{1,0:T(8,128)(2,1)} %fusion.onehot_ref, bf16[512,8192]{1,0:T(8,128)(2,1)} %bitcast.92), custom_call_target="tpu_custom_call" | custom-call | tf_op jit(solution)/shard_map/pallas_call | solution.py:48
  42.8 4.5 %compare_select_fusion.2 = (s32[512,1]{0,1:T(1,128)S(1)}, s32[512,1]{0,1:T(1,128)S(1)}) fusion(s32[]{:T(128)} %bitcast.21, s32[]{:T(128)} %bitcast.22, s32[]{:T(128)} %bitcast.23, s32[]{:T(128)} %bitcast.24, s32[]{:T(128)} %bitcast.25, s32[]{:T(128)} %bitcast.27, s32[]{:T(128)} %bitcast.26, s32[512,1]{0,1:T(1,128)S(1)} %bitcast.132), kind=kLoop, calls=%fused_computation.34 | loop fusion | flops 7680 | bytes 6172 | tf_op jit(solution)/shard_map/jit(_take)/gather | solution.py:232
  47.4 5.7 %select_subtract_fusion = (s32[512]{0:T(512)S(1)}, s32[512]{0:T(512)S(1)}) fusion(s32[512]{0:T(512)S(1)} %convert_reduce_fusion, pred[512]{0:T(512)(128)(4,1)S(1)} %get-tuple-element.56, pred[512]{0:T(512)(128)(4,1)S(1)} %get-tuple-element.55, pred[512]{0:T(512)(128)(4,1)S(1)} %get-tuple-element.57, pred[512]{0:T(512)(128)(4,1)S(1)} %get-tuple-element.54, ...), kind=kLoop, calls=%fused_computation.49 | loop fusion | flops 10240 | bytes 12836 | tf_op jit(solution)/shard_map/sub | solution.py:233
  53.2 1.1 fusion.1.onehot_ref
  54.2 1.9 gather_fusion.1
  59.0 2.6 copy.41
  63.1 16.3 %all-to-all-done = bf16[16,48,2048]{2,1,0:T(8,128)(2,1)} async-done(((bf16[16,48,2048]{2,1,0:T(8,128)(2,1)}), bf16[16,48,2048]{2,1,0:T(8,128)(2,1)}, u32[]{:S(2)}, u32[]{:S(2)}) %all-to-all-start) | async-done | bytes 3145760 | tf_op jit(solution)/shard_map/all_to_all | solution.py:274
  79.4 6.2 %shard_map.66 = (bf16[16,144,128]{2,1,0:T(8,128)(2,1)}, bf16[512,2048]{1,0:T(8,128)(2,1)}) custom-call(bf16[128,512]{1,0:T(8,128)(2,1)} %bitcast.114, f32[16,512,8]{2,1,0:T(8,128)} %bitcast.96, f32[1,8192]{1,0:T(1,128)} %reshape_reshape.6.decay_ref, bf16[512,768]{1,0:T(8,128)(2,1)} %fusion.1.onehot_ref, bf16[768,2048]{1,0:T(8,128)(2,1)} %bitcast.40.arr_ref), custom_call_target="tpu_custom_call" | custom-call | tf_op jit(solution)/shard_map/pallas_call | solution.py:125
  85.6 5.0 %all-to-all-start.1 = ((bf16[16,48,2048]{2,1,0:T(8,128)(2,1)}), bf16[16,48,2048]{2,1,0:T(8,128)(2,1)S(1)}, u32[]{:S(2)}, u32[]{:S(2)}) async-start(bf16[16,48,2048]{2,1,0:T(8,128)(2,1)} %bitcast.5), calls=%async_computation.1 | async-start | bytes 6291456 | tf_op jit(solution)/shard_map/all_to_all | solution.py:274
  90.7 5.4 %shard_map.68 = bf16[768,2048]{1,0:T(8,128)(2,1)} custom-call(bf16[768,512]{1,0:T(8,128)(2,1)} %fusion.onehot_ref, bf16[512,8192]{1,0:T(8,128)(2,1)} %bitcast.93), custom_call_target="tpu_custom_call" | custom-call | tf_op jit(solution)/shard_map/pallas_call | solution.py:48
  96.9 2.7 copy.40
  99.6 2.2 fusion.9.scores_ref
  101.8 9.5 %shard_map.67.refs_0_ = f32[512,2048]{1,0:T(8,128)} custom-call(f32[512,512]{1,0:T(8,128)} %fusion.9.scores_ref, f32[16,512,8]{2,1,0:T(8,128)} %bitcast.81, f32[128,512]{1,0:T(8,128)} %bitcast.104, f32[128,512]{1,0:T(8,128)} %get-tuple-element.71.stept_ref, bf16[512,2048]{1,0:T(8,128)(2,1)} %get-tuple-element.29.tok_ref, f32[1,8192]{1,0:T(1,128)} %reshape_reshape.7.skip_ref), custom_call_target="tpu_custom_call" | custom-call | tf_op jit(solution)/shard_map/pallas_call | solution.py:150
  111.4 22.3 %all-to-all-done.1 = bf16[16,48,2048]{2,1,0:T(8,128)(2,1)S(1)} async-done(((bf16[16,48,2048]{2,1,0:T(8,128)(2,1)}), bf16[16,48,2048]{2,1,0:T(8,128)(2,1)S(1)}, u32[]{:S(2)}, u32[]{:S(2)}) %all-to-all-start.1) | async-done | bytes 3145760 | tf_op jit(solution)/shard_map/all_to_all | solution.py:274
  133.7 1.7 copy-done.2
  135.3 6.2 %shard_map.69 = (bf16[16,144,128]{2,1,0:T(8,128)(2,1)}, bf16[512,2048]{1,0:T(8,128)(2,1)}) custom-call(bf16[128,512]{1,0:T(8,128)(2,1)} %bitcast.115, f32[16,512,8]{2,1,0:T(8,128)} %bitcast.97, f32[1,8192]{1,0:T(1,128)} %reshape_reshape.6.decay_ref, bf16[512,768]{1,0:T(8,128)(2,1)} %fusion.1.onehot_ref, bf16[768,2048]{1,0:T(8,128)(2,1)} %bitcast.111), custom_call_target="tpu_custom_call" | custom-call | tf_op jit(solution)/shard_map/pallas_call | solution.py:125
  141.6 4.8 %all-to-all-start.3 = ((bf16[16,48,2048]{2,1,0:T(8,128)(2,1)}), bf16[16,48,2048]{2,1,0:T(8,128)(2,1)S(1)}, u32[]{:S(2)}, u32[]{:S(2)}) async-start(bf16[16,48,2048]{2,1,0:T(8,128)(2,1)} %bitcast.41), calls=%async_computation.3 | async-start | bytes 6291456 | tf_op jit(solution)/shard_map/all_to_all | solution.py:274
  146.7 4.7 %shard_map.72 = bf16[768,1536]{1,0:T(8,128)(2,1)} custom-call(bf16[768,512]{1,0:T(8,128)(2,1)} %fusion.onehot_ref, bf16[512,8192]{1,0:T(8,128)(2,1)} %bitcast.94), custom_call_target="tpu_custom_call" | custom-call | tf_op jit(solution)/shard_map/pallas_call | solution.py:48
  151.4 9.6 %shard_map.70.refs_1_ = f32[512,2048]{1,0:T(8,128)} custom-call(f32[512,512]{1,0:T(8,128)} %fusion.9.scores_ref, f32[16,512,8]{2,1,0:T(8,128)} %bitcast.82, f32[128,512]{1,0:T(8,128)} %bitcast.105, f32[128,512]{1,0:T(8,128)} %get-tuple-element.71.stept_ref, bf16[512,2048]{1,0:T(8,128)(2,1)} %get-tuple-element.32.tok_ref, f32[1,8192]{1,0:T(1,128)} %reshape_reshape.7.skip_ref), custom_call_target="tpu_custom_call" | custom-call | tf_op jit(solution)/shard_map/pallas_call | solution.py:150
  160.9 6.8 %shard_map.71.refs_0_ = bf16[512,8192]{1,0:T(8,128)(2,1)} custom-call(s32[1]{0:T(128)} %bitcast.place_ref, f32[512,2048]{1,0:T(8,128)} %shard_map.67.refs_0_, bf16[8,16,144,128]{3,2,1,0:T(8,128)(2,1)} %bitcast.120, f32[16,512,8]{2,1,0:T(8,128)} %bitcast.83, bf16[512,128]{1,0:T(8,128)(2,1)} %get-tuple-element.62.refs_3_.refs_4_), custom_call_target="tpu_custom_call" | custom-call | tf_op jit(solution)/shard_map/pallas_call | solution.py:183
  167.8 21.6 %all-to-all-done.3 = bf16[16,48,2048]{2,1,0:T(8,128)(2,1)S(1)} async-done(((bf16[16,48,2048]{2,1,0:T(8,128)(2,1)}), bf16[16,48,2048]{2,1,0:T(8,128)(2,1)S(1)}, u32[]{:S(2)}, u32[]{:S(2)}) %all-to-all-start.3) | async-done | bytes 3145760 | tf_op jit(solution)/shard_map/all_to_all | solution.py:274
  189.4 1.7 copy-done.1
  191.0 6.2 %shard_map.73 = (bf16[16,144,128]{2,1,0:T(8,128)(2,1)}, bf16[512,2048]{1,0:T(8,128)(2,1)}) custom-call(bf16[128,512]{1,0:T(8,128)(2,1)} %bitcast.116, f32[16,512,8]{2,1,0:T(8,128)} %bitcast.98, f32[1,8192]{1,0:T(1,128)} %reshape_reshape.6.decay_ref, bf16[512,768]{1,0:T(8,128)(2,1)} %fusion.1.onehot_ref, bf16[768,2048]{1,0:T(8,128)(2,1)} %bitcast.110), custom_call_target="tpu_custom_call" | custom-call | tf_op jit(solution)/shard_map/pallas_call | solution.py:125
  197.2 4.9 %all-to-all-start.4 = ((bf16[16,48,1536]{2,1,0:T(8,128)(2,1)}), bf16[16,48,1536]{2,1,0:T(8,128)(2,1)S(1)}, u32[]{:S(2)}, u32[]{:S(2)}) async-start(bf16[16,48,1536]{2,1,0:T(8,128)(2,1)} %bitcast.113), calls=%async_computation.4 | async-start | bytes 4718592 | tf_op jit(solution)/shard_map/all_to_all | solution.py:274
  202.2 2.7 shard_map.76
  204.9 9.5 %shard_map.74.refs_1_ = f32[512,2048]{1,0:T(8,128)} custom-call(f32[512,512]{1,0:T(8,128)} %fusion.9.scores_ref, f32[16,512,8]{2,1,0:T(8,128)} %bitcast.84, f32[128,512]{1,0:T(8,128)} %bitcast.106, f32[128,512]{1,0:T(8,128)} %get-tuple-element.71.stept_ref, bf16[512,2048]{1,0:T(8,128)(2,1)} %get-tuple-element.36.tok_ref, f32[1,8192]{1,0:T(1,128)} %reshape_reshape.7.skip_ref), custom_call_target="tpu_custom_call" | custom-call | tf_op jit(solution)/shard_map/pallas_call | solution.py:150
  214.4 6.9 %shard_map.75.refs_0_ = bf16[512,8192]{1,0:T(8,128)(2,1)} custom-call(s32[1]{0:T(128)} %bitcast.place_ref, bf16[512,8192]{1,0:T(8,128)(2,1)} %shard_map.71.refs_0_, f32[512,2048]{1,0:T(8,128)} %shard_map.70.refs_1_, bf16[8,16,144,128]{3,2,1,0:T(8,128)(2,1)} %bitcast.119, f32[16,512,8]{2,1,0:T(8,128)} %bitcast.85, ...), custom_call_target="tpu_custom_call", output_to_operand_aliasing={{}: (1, {})} | custom-call | tf_op jit(solution)/shard_map/pallas_call | solution.py:183
  221.3 12.0 %all-to-all-done.4 = bf16[16,48,1536]{2,1,0:T(8,128)(2,1)S(1)} async-done(((bf16[16,48,1536]{2,1,0:T(8,128)(2,1)}), bf16[16,48,1536]{2,1,0:T(8,128)(2,1)S(1)}, u32[]{:S(2)}, u32[]{:S(2)}) %all-to-all-start.4) | async-done | bytes 2359328 | tf_op jit(solution)/shard_map/all_to_all | solution.py:274
  233.3 1.4 copy-done.3
  234.7 5.2 %shard_map.77 = (bf16[12,144,128]{2,1,0:T(8,128)(2,1)}, bf16[512,1536]{1,0:T(8,128)(2,1)}) custom-call(bf16[128,512]{1,0:T(8,128)(2,1)} %bitcast.117, f32[16,512,8]{2,1,0:T(8,128)} %bitcast.99, f32[1,8192]{1,0:T(1,128)} %reshape_reshape.6.decay_ref, bf16[512,768]{1,0:T(8,128)(2,1)} %fusion.1.onehot_ref, bf16[768,1536]{1,0:T(8,128)(2,1)} %bitcast.112), custom_call_target="tpu_custom_call" | custom-call | tf_op jit(solution)/shard_map/pallas_call | solution.py:125
  239.9 6.0 %all-to-all-start.5 = ((bf16[16,48,512]{2,1,0:T(8,128)(2,1)}), bf16[16,48,512]{2,1,0:T(8,128)(2,1)S(1)}, u32[]{:S(2)}, u32[]{:S(2)}) async-start(bf16[16,48,512]{2,1,0:T(8,128)(2,1)} %bitcast.47), calls=%async_computation.5 | async-start | bytes 1572864 | tf_op jit(solution)/shard_map/all_to_all | solution.py:274
  245.9 7.7 %shard_map.78.refs_1_ = f32[512,1536]{1,0:T(8,128)} custom-call(f32[512,512]{1,0:T(8,128)} %fusion.9.scores_ref, f32[16,512,8]{2,1,0:T(8,128)} %bitcast.86, f32[128,512]{1,0:T(8,128)} %bitcast.107, f32[128,512]{1,0:T(8,128)} %get-tuple-element.71.stept_ref, bf16[512,1536]{1,0:T(8,128)(2,1)} %get-tuple-element.41.tok_ref, f32[1,8192]{1,0:T(1,128)} %reshape_reshape.7.skip_ref), custom_call_target="tpu_custom_call" | custom-call | tf_op jit(solution)/shard_map/pallas_call | solution.py:150
  253.6 6.8 %shard_map.79.refs_0_ = bf16[512,8192]{1,0:T(8,128)(2,1)} custom-call(s32[1]{0:T(128)} %bitcast.place_ref, bf16[512,8192]{1,0:T(8,128)(2,1)} %shard_map.75.refs_0_, f32[512,2048]{1,0:T(8,128)} %shard_map.74.refs_1_, bf16[8,16,144,128]{3,2,1,0:T(8,128)(2,1)} %bitcast.121, f32[16,512,8]{2,1,0:T(8,128)} %bitcast.87, ...), custom_call_target="tpu_custom_call", output_to_operand_aliasing={{}: (1, {})} | custom-call | tf_op jit(solution)/shard_map/pallas_call | solution.py:183
  260.4 0.9 copy-done.4
  261.3 3.1 shard_map.81
  264.4 4.2 %shard_map.82.refs_1_ = f32[512,512]{1,0:T(8,128)} custom-call(f32[512,512]{1,0:T(8,128)} %fusion.9.scores_ref, f32[16,512,8]{2,1,0:T(8,128)} %bitcast.88, f32[128,512]{1,0:T(8,128)} %bitcast.108, f32[128,512]{1,0:T(8,128)} %get-tuple-element.71.stept_ref, bf16[512,512]{1,0:T(8,128)(2,1)} %get-tuple-element.47.tok_ref, f32[1,8192]{1,0:T(1,128)} %reshape_reshape.7.skip_ref), custom_call_target="tpu_custom_call" | custom-call | tf_op jit(solution)/shard_map/pallas_call | solution.py:150
  268.6 15.2 %all-gather.4 = bf16[16,144,128]{2,1,0:T(8,128)(2,1)S(1)} all-gather(bf16[2,144,128]{2,1,0:T(8,128)(2,1)S(1)} %get-tuple-element.68), channel_id=6, replica_groups=mesh['pos'=8,'stream'=16] {'pos'}, dimensions={0}, use_global_device_ids=true | all-gather | bytes 663552 | tf_op jit(solution)/shard_map/all_gather | solution.py:302
  283.8 13.2 %all-gather.5 = bf16[16,144,128]{2,1,0:T(8,128)(2,1)S(1)} all-gather(bf16[2,144,128]{2,1,0:T(8,128)(2,1)S(1)} %get-tuple-element.69), channel_id=7, replica_groups=mesh['pos'=8,'stream'=16] {'pos'}, dimensions={0}, use_global_device_ids=true | all-gather | bytes 663552 | tf_op jit(solution)/shard_map/all_gather | solution.py:302
  297.0 1.1 pad_maximum_fusion.refs_2_
  298.1 5.9 %shard_map.80.refs_0_ = bf16[512,8192]{1,0:T(8,128)(2,1)} custom-call(s32[1]{0:T(128)} %bitcast.place_ref, bf16[512,8192]{1,0:T(8,128)(2,1)} %shard_map.79.refs_0_, f32[512,1536]{1,0:T(8,128)} %shard_map.78.refs_1_, bf16[8,12,144,128]{3,2,1,0:T(8,128)(2,1)} %bitcast.122, f32[16,512,8]{2,1,0:T(8,128)} %bitcast.89, ...), custom_call_target="tpu_custom_call", output_to_operand_aliasing={{}: (1, {})} | custom-call | tf_op jit(solution)/shard_map/pallas_call | solution.py:183
  304.0 3.1 shard_map.83
  (68 shorter events, 9.3 us)
Async XLA Ops:
  12.6 19.5 %all-to-all-start.2 = ((bf16[16,48,384]{2,1,0:T(8,128)(2,1)}), bf16[16,48,384]{2,1,0:T(8,128)(2,1)S(1)}, u32[]{:S(2)}, u32[]{:S(2)}) async-start(bf16[16,48,384]{2,1,0:T(8,128)(2,1)} %bitcast.8), calls=%async_computation.2 | async-start | bytes 1179648 | tf_op jit(solution)/shard_map/all_to_all | solution.py:206
  32.1 47.3 %all-to-all-start = ((bf16[16,48,2048]{2,1,0:T(8,128)(2,1)}), bf16[16,48,2048]{2,1,0:T(8,128)(2,1)}, u32[]{:S(2)}, u32[]{:S(2)}) async-start(bf16[16,48,2048]{2,1,0:T(8,128)(2,1)} %bitcast.109), calls=%async_computation | async-start | bytes 6291456 | tf_op jit(solution)/shard_map/all_to_all | solution.py:274
  36.6 124.3 %all-gather.11.cloned.1.call-start = ((), (), s32[]{:S(2)}) async-start(), calls=%async_computation.6 | async-start | bytes 5308416 | tf_op jit(solution)/shard_map/all_gather | solution.py:297
  37.4 15.7 %copy-start.8 = (f32[128]{0:T(128)S(1)}, f32[128]{0:T(128)}, u32[]{:S(2)}) copy-start(f32[128]{0:T(128)} %param.9) | copy-start | bytes 1540
  56.2 5.4 %copy-start.5 = (bf16[512,384]{1,0:T(8,128)(2,1)}, bf16[512,384]{1,0:T(8,128)(2,1)S(1)}, u32[]{:S(2)}) copy-start(bf16[512,384]{1,0:T(8,128)(2,1)S(1)} %gather_fusion.1) | copy-start | bytes 1179652
  57.9 38.9 %copy-start = (f32[16,8,4,128]{3,1,2,0:T(8,128)}, f32[16,8,4,128]{3,1,2,0:T(8,128)S(1)}, u32[]{:S(2)}) copy-start(f32[16,8,4,128]{3,1,2,0:T(8,128)S(1)} %copy.52) | copy-start | bytes 786436
  85.6 48.0 %all-to-all-start.1 = ((bf16[16,48,2048]{2,1,0:T(8,128)(2,1)}), bf16[16,48,2048]{2,1,0:T(8,128)(2,1)S(1)}, u32[]{:S(2)}, u32[]{:S(2)}) async-start(bf16[16,48,2048]{2,1,0:T(8,128)(2,1)} %bitcast.5), calls=%async_computation.1 | async-start | bytes 6291456 | tf_op jit(solution)/shard_map/all_to_all | solution.py:274
  90.6 5.5 %copy-start.7 = (f32[128]{0:T(128)S(1)}, f32[128]{0:T(128)}, u32[]{:S(2)}) copy-start(f32[128]{0:T(128)} %param.10) | copy-start | bytes 1540
  90.6 123.8 %all-gather.13.cloned.1.call-start = ((), (), s32[]{:S(2)}) async-start(), calls=%async_computation.7 | async-start | bytes 5308416 | tf_op jit(solution)/shard_map/all_gather | solution.py:297
  133.7 1.7 copy-start.2
  141.6 47.8 %all-to-all-start.3 = ((bf16[16,48,2048]{2,1,0:T(8,128)(2,1)}), bf16[16,48,2048]{2,1,0:T(8,128)(2,1)S(1)}, u32[]{:S(2)}, u32[]{:S(2)}) async-start(bf16[16,48,2048]{2,1,0:T(8,128)(2,1)} %bitcast.41), calls=%async_computation.3 | async-start | bytes 6291456 | tf_op jit(solution)/shard_map/all_to_all | solution.py:274
  146.4 107.2 %all-gather.15.cloned.1.call-start = ((), (), s32[]{:S(2)}) async-start(), calls=%async_computation.8 | async-start | bytes 5308416 | tf_op jit(solution)/shard_map/all_gather | solution.py:297
  189.4 1.7 copy-start.1
  197.2 36.1 %all-to-all-start.4 = ((bf16[16,48,1536]{2,1,0:T(8,128)(2,1)}), bf16[16,48,1536]{2,1,0:T(8,128)(2,1)S(1)}, u32[]{:S(2)}, u32[]{:S(2)}) async-start(bf16[16,48,1536]{2,1,0:T(8,128)(2,1)} %bitcast.113), calls=%async_computation.4 | async-start | bytes 4718592 | tf_op jit(solution)/shard_map/all_to_all | solution.py:274
  202.1 96.0 %all-gather.17.cloned.1.call-start = ((), (), s32[]{:S(2)}) async-start(), calls=%async_computation.9 | async-start | bytes 3981312 | tf_op jit(solution)/shard_map/all_gather | solution.py:297
  233.3 1.4 copy-start.3
  239.9 20.5 %all-to-all-start.5 = ((bf16[16,48,512]{2,1,0:T(8,128)(2,1)}), bf16[16,48,512]{2,1,0:T(8,128)(2,1)S(1)}, u32[]{:S(2)}, u32[]{:S(2)}) async-start(bf16[16,48,512]{2,1,0:T(8,128)(2,1)} %bitcast.47), calls=%async_computation.5 | async-start | bytes 1572864 | tf_op jit(solution)/shard_map/all_to_all | solution.py:274
  260.4 0.9 copy-start.4
  264.4 4.2 %copy-start.6 = (bf16[4,144,128]{2,1,0:T(8,128)(2,1)S(1)}, bf16[4,144,128]{2,1,0:T(8,128)(2,1)}, u32[]{:S(2)}) copy-start(bf16[4,144,128]{2,1,0:T(8,128)(2,1)} %get-tuple-element.48) | copy-start | bytes 442372
Sparse Core Ops, SparseCore 0:
  85.7 35.3 all-gather.10
  141.7 35.2 all-gather.12
  197.3 35.2 all-gather.14
  240.0 30.4 all-gather.16

commit v11 on v7

--- a/solution.py
+++ b/solution.py
@@ -7,7 +7,7 @@
 
 GROUP = 8
 TILE = 128
-CHUNK_GROUPS = (4, 4, 4, 3, 1)
+CHUNK_GROUPS = (4, 4, 4, 4)
 EXTRA = 16
 
 

time: 303 us -> 303 us (level)
  waiting for transfers between devices: 96.3 us -> 109 us
  Pallas kernels: 120 us -> 112 us
  starting transfers between devices: 35.7 us -> 28 us
    all_to_all x5 -> x4, waiting for transfers between devices: 71.8 us -> 86.6 us  [on_device(): lax.all_to_all(sends[c], 'stream', split_axis=0, concat_axis=0, tiled=True)]
    all_to_all x5 -> x4, starting transfers between devices: 26.7 us -> 19.3 us  [on_device(): lax.all_to_all(sends[c], 'stream', split_axis=0, concat_axis=0, tiled=True)]
    pallas_call x5 -> x4, Pallas kernels: 40.3 us -> 38.1 us  [local_call(): pl.pallas_call(local_kernel, grid=(groups,), in_specs=[pl.BlockSpec((leng...]
    all_gather x5 -> x4, waiting for transfers between devices: 20.9 us -> 18.8 us  [on_device(): gathers.append(lax.all_gather(carried, 'pos'))]
    pallas_call x5 -> x4, Pallas kernels: 26.8 us -> 24.7 us  [carried_call(): pl.pallas_call(carried_kernel, grid=(groups,), in_specs=[pl.BlockSpec(bt....]
    pallas_call x5 -> x4, Pallas kernels: 23.5 us -> 21.5 us  [send_call(): pl.pallas_call(send_kernel, grid=(groups,), in_specs=[pl.BlockSpec(onehot...]
    pallas_call x5 -> x4, Pallas kernels: 29.4 us -> 27.5 us  [combine_call(): pl.pallas_call(combine_kernel, grid=(groups,), in_specs=[pl.BlockSpec(mem...]
  transfers between devices with their start and end apart: 11 -> 9, of which waited for: 7 -> 6; matrix products, arithmetic and copies ran while one was open for 9% -> 9% of each run, Pallas kernels for 37% -> 33%
where the time goes in v11:
time: 303 us; the launch traced here: 302 us
  Pallas kernels  112 us (37%)
  waiting for transfers between devices  109 us (36%)
  starting transfers between devices  28 us (9%)
  local copies, waits for them, and re-layouts  21.7 us (7%)
  other arithmetic  15.6 us (5%)
  between operations  13.4 us (4%)
    all_to_all x4, waiting for transfers between devices, on_device(): lax.all_to_all(sends[c], 'stream', split_axis=0, concat_axis=0, tiled=True)  86.6 us
    pallas_call x4, Pallas kernels, local_call(): pl.pallas_call(local_kernel, grid=(groups,), in_specs=[pl.BlockSpec((leng...  38.1 us
    pallas_call x4, Pallas kernels, combine_call(): pl.pallas_call(combine_kernel, grid=(groups,), in_specs=[pl.BlockSpec(mem...  27.5 us
    pallas_call x4, Pallas kernels, carried_call(): pl.pallas_call(carried_kernel, grid=(groups,), in_specs=[pl.BlockSpec(bt....  24.7 us
    pallas_call x4, Pallas kernels, send_call(): pl.pallas_call(send_kernel, grid=(groups,), in_specs=[pl.BlockSpec(onehot...  21.5 us
    all_to_all x4, starting transfers between devices, on_device(): lax.all_to_all(sends[c], 'stream', split_axis=0, concat_axis=0, tiled=True)  19.3 us
    all_gather x4, waiting for transfers between devices, on_device(): gathers.append(lax.all_gather(carried, 'pos'))  18.8 us
    all_to_all x1, starting transfers between devices, deliver(): lax.all_to_all(send, 'stream', split_axis=0, concat_axis=0, tiled=True)  8.43 us
  transfers between devices with their start and end apart: 9, of which 6 were waited for; matrix products, arithmetic and copies ran while one was open for 9% of the time, Pallas kernels for 33%

profile of v11, /device:TPU:1, one launch (start us, length us, event | category | flops | bytes accessed | tf_op | source)
XLA Modules:
  0.0 301.6 jit_solution(12137862600298115809)
XLA Ops:
  7.5 0.7 bitcast_subtract_fusion
  8.3 1.1 pad_maximum_fusion
  9.4 3.2 %gather_fusion = bf16[768,384]{1,0:T(8,128)(2,1)} fusion(bf16[512,384]{1,0:T(8,128)(2,1)S(1)} %pad_maximum_fusion, s32[1024]{0:T(1024)S(1)} %pad_clamp_fusion.1), kind=kCustom, calls=%fused_computation | custom fusion | bytes 1182720 | tf_op jit(solution)/shard_map/jit(_take)/gather | solution.py:196
  12.6 8.4 %all-to-all-start.2 = ((bf16[16,48,384]{2,1,0:T(8,128)(2,1)}), bf16[16,48,384]{2,1,0:T(8,128)(2,1)S(1)}, u32[]{:S(2)}, u32[]{:S(2)}) async-start(bf16[16,48,384]{2,1,0:T(8,128)(2,1)} %bitcast.8), calls=%async_computation.2 | async-start | bytes 1179648 | tf_op jit(solution)/shard_map/all_to_all | solution.py:206
  21.1 0.9 dynamic-slice_reduce_fusion
  22.1 1.1 fusion.onehot_ref
  23.2 5.3 %shard_map.64 = bf16[768,2048]{1,0:T(8,128)(2,1)} custom-call(bf16[768,512]{1,0:T(8,128)(2,1)} %fusion.onehot_ref, bf16[512,8192]{1,0:T(8,128)(2,1)} %bitcast.85), custom_call_target="tpu_custom_call" | custom-call | tf_op jit(solution)/shard_map/pallas_call | solution.py:48
  28.6 3.5 %all-to-all-done.2 = bf16[16,48,384]{2,1,0:T(8,128)(2,1)S(1)} async-done(((bf16[16,48,384]{2,1,0:T(8,128)(2,1)}), bf16[16,48,384]{2,1,0:T(8,128)(2,1)S(1)}, u32[]{:S(2)}, u32[]{:S(2)}) %all-to-all-start.2) | async-done | bytes 589856 | tf_op jit(solution)/shard_map/all_to_all | solution.py:206
  32.1 4.5 %all-to-all-start = ((bf16[16,48,2048]{2,1,0:T(8,128)(2,1)}), bf16[16,48,2048]{2,1,0:T(8,128)(2,1)}, u32[]{:S(2)}, u32[]{:S(2)}) async-start(bf16[16,48,2048]{2,1,0:T(8,128)(2,1)} %bitcast.94), calls=%async_computation | async-start | bytes 6291456 | tf_op jit(solution)/shard_map/all_to_all | solution.py:274
  36.7 0.7 fusion.15
  37.4 5.4 %shard_map.65 = bf16[768,2048]{1,0:T(8,128)(2,1)} custom-call(bf16[768,512]{1,0:T(8,128)(2,1)} %fusion.onehot_ref, bf16[512,8192]{1,0:T(8,128)(2,1)} %bitcast.86), custom_call_target="tpu_custom_call" | custom-call | tf_op jit(solution)/shard_map/pallas_call | solution.py:48
  42.8 4.3 %compare_select_fusion.2 = (s32[512,1]{0,1:T(1,128)S(1)}, s32[512,1]{0,1:T(1,128)S(1)}) fusion(s32[]{:T(128)} %bitcast.21, s32[]{:T(128)} %bitcast.22, s32[]{:T(128)} %bitcast.23, s32[]{:T(128)} %bitcast.24, s32[]{:T(128)} %bitcast.25, s32[]{:T(128)} %bitcast.27, s32[]{:T(128)} %bitcast.26, s32[512,1]{0,1:T(1,128)S(1)} %bitcast.118), kind=kLoop, calls=%fused_computation.33 | loop fusion | flops 7680 | bytes 6172 | tf_op jit(solution)/shard_map/jit(_take)/gather | solution.py:232
  47.2 5.5 %select_subtract_fusion = (s32[512]{0:T(512)S(1)}, s32[512]{0:T(512)S(1)}) fusion(s32[512]{0:T(512)S(1)} %convert_reduce_fusion, pred[512]{0:T(512)(128)(4,1)S(1)} %get-tuple-element.46, pred[512]{0:T(512)(128)(4,1)S(1)} %get-tuple-element.45, pred[512]{0:T(512)(128)(4,1)S(1)} %get-tuple-element.47, pred[512]{0:T(512)(128)(4,1)S(1)} %get-tuple-element.44, ...), kind=kLoop, calls=%fused_computation.48 | loop fusion | flops 10240 | bytes 12836 | tf_op jit(solution)/shard_map/sub | solution.py:233
  52.7 1.1 fusion.1.onehot_ref
  53.8 1.9 gather_fusion.1
  55.8 0.8 fusion.14
  57.7 0.9 multiply_bitcast_fusion
  58.6 2.6 copy.40
  61.3 0.7 reshape_reshape.6.decay_ref
  62.0 0.8 copy.41
  62.7 16.7 %all-to-all-done = bf16[16,48,2048]{2,1,0:T(8,128)(2,1)} async-done(((bf16[16,48,2048]{2,1,0:T(8,128)(2,1)}), bf16[16,48,2048]{2,1,0:T(8,128)(2,1)}, u32[]{:S(2)}, u32[]{:S(2)}) %all-to-all-start) | async-done | bytes 3145760 | tf_op jit(solution)/shard_map/all_to_all | solution.py:274
  79.4 6.2 %shard_map.66 = (bf16[16,144,128]{2,1,0:T(8,128)(2,1)}, bf16[512,2048]{1,0:T(8,128)(2,1)}) custom-call(bf16[128,512]{1,0:T(8,128)(2,1)} %bitcast.108, f32[16,512,8]{2,1,0:T(8,128)} %bitcast.89, f32[1,8192]{1,0:T(1,128)} %reshape_reshape.6.decay_ref, bf16[512,768]{1,0:T(8,128)(2,1)} %fusion.1.onehot_ref, bf16[768,2048]{1,0:T(8,128)(2,1)} %bitcast.40.arr_ref), custom_call_target="tpu_custom_call" | custom-call | tf_op jit(solution)/shard_map/pallas_call | solution.py:125
  85.6 5.0 %all-to-all-start.1 = ((bf16[16,48,2048]{2,1,0:T(8,128)(2,1)}), bf16[16,48,2048]{2,1,0:T(8,128)(2,1)S(1)}, u32[]{:S(2)}, u32[]{:S(2)}) async-start(bf16[16,48,2048]{2,1,0:T(8,128)(2,1)} %bitcast.5), calls=%async_computation.1 | async-start | bytes 6291456 | tf_op jit(solution)/shard_map/all_to_all | solution.py:274
  90.7 5.4 %shard_map.68 = bf16[768,2048]{1,0:T(8,128)(2,1)} custom-call(bf16[768,512]{1,0:T(8,128)(2,1)} %fusion.onehot_ref, bf16[512,8192]{1,0:T(8,128)(2,1)} %bitcast.87), custom_call_target="tpu_custom_call" | custom-call | tf_op jit(solution)/shard_map/pallas_call | solution.py:48
  96.1 0.7 reshape_reshape.7.skip_ref
  96.8 2.7 copy.39
  99.6 2.3 fusion.9.scores_ref
  101.8 9.4 %shard_map.67.refs_0_ = f32[512,2048]{1,0:T(8,128)} custom-call(f32[512,512]{1,0:T(8,128)} %fusion.9.scores_ref, f32[16,512,8]{2,1,0:T(8,128)} %bitcast.77, f32[128,512]{1,0:T(8,128)} %bitcast.100, f32[128,512]{1,0:T(8,128)} %get-tuple-element.59.stept_ref, bf16[512,2048]{1,0:T(8,128)(2,1)} %get-tuple-element.24.tok_ref, f32[1,8192]{1,0:T(1,128)} %reshape_reshape.7.skip_ref), custom_call_target="tpu_custom_call" | custom-call | tf_op jit(solution)/shard_map/pallas_call | solution.py:150
  111.3 22.4 %all-to-all-done.1 = bf16[16,48,2048]{2,1,0:T(8,128)(2,1)S(1)} async-done(((bf16[16,48,2048]{2,1,0:T(8,128)(2,1)}), bf16[16,48,2048]{2,1,0:T(8,128)(2,1)S(1)}, u32[]{:S(2)}, u32[]{:S(2)}) %all-to-all-start.1) | async-done | bytes 3145760 | tf_op jit(solution)/shard_map/all_to_all | solution.py:274
  133.7 1.7 copy-done.2
  135.3 6.2 %shard_map.69 = (bf16[16,144,128]{2,1,0:T(8,128)(2,1)}, bf16[512,2048]{1,0:T(8,128)(2,1)}) custom-call(bf16[128,512]{1,0:T(8,128)(2,1)} %bitcast.109, f32[16,512,8]{2,1,0:T(8,128)} %bitcast.90, f32[1,8192]{1,0:T(1,128)} %reshape_reshape.6.decay_ref, bf16[512,768]{1,0:T(8,128)(2,1)} %fusion.1.onehot_ref, bf16[768,2048]{1,0:T(8,128)(2,1)} %bitcast.97), custom_call_target="tpu_custom_call" | custom-call | tf_op jit(solution)/shard_map/pallas_call | solution.py:125
  141.5 4.8 %all-to-all-start.3 = ((bf16[16,48,2048]{2,1,0:T(8,128)(2,1)}), bf16[16,48,2048]{2,1,0:T(8,128)(2,1)S(1)}, u32[]{:S(2)}, u32[]{:S(2)}) async-start(bf16[16,48,2048]{2,1,0:T(8,128)(2,1)} %bitcast.41), calls=%async_computation.3 | async-start | bytes 6291456 | tf_op jit(solution)/shard_map/all_to_all | solution.py:274
  146.6 5.4 %shard_map.72 = bf16[768,2048]{1,0:T(8,128)(2,1)} custom-call(bf16[768,512]{1,0:T(8,128)(2,1)} %fusion.onehot_ref, bf16[512,8192]{1,0:T(8,128)(2,1)} %bitcast.88), custom_call_target="tpu_custom_call" | custom-call | tf_op jit(solution)/shard_map/pallas_call | solution.py:48
  152.0 9.8 %shard_map.70.refs_1_ = f32[512,2048]{1,0:T(8,128)} custom-call(f32[512,512]{1,0:T(8,128)} %fusion.9.scores_ref, f32[16,512,8]{2,1,0:T(8,128)} %bitcast.78, f32[128,512]{1,0:T(8,128)} %bitcast.101, f32[128,512]{1,0:T(8,128)} %get-tuple-element.59.stept_ref, bf16[512,2048]{1,0:T(8,128)(2,1)} %get-tuple-element.27.tok_ref, f32[1,8192]{1,0:T(1,128)} %reshape_reshape.7.skip_ref), custom_call_target="tpu_custom_call" | custom-call | tf_op jit(solution)/shard_map/pallas_call | solution.py:150
  161.8 6.8 %shard_map.71.refs_0_ = bf16[512,8192]{1,0:T(8,128)(2,1)} custom-call(s32[1]{0:T(128)} %bitcast.place_ref, f32[512,2048]{1,0:T(8,128)} %shard_map.67.refs_0_, bf16[8,16,144,128]{3,2,1,0:T(8,128)(2,1)} %bitcast.104, f32[16,512,8]{2,1,0:T(8,128)} %bitcast.79, bf16[512,128]{1,0:T(8,128)(2,1)} %get-tuple-element.52.refs_3_.refs_4_), custom_call_target="tpu_custom_call" | custom-call | tf_op jit(solution)/shard_map/pallas_call | solution.py:183
  168.6 20.6 %all-to-all-done.3 = bf16[16,48,2048]{2,1,0:T(8,128)(2,1)S(1)} async-done(((bf16[16,48,2048]{2,1,0:T(8,128)(2,1)}), bf16[16,48,2048]{2,1,0:T(8,128)(2,1)S(1)}, u32[]{:S(2)}, u32[]{:S(2)}) %all-to-all-start.3) | async-done | bytes 3145760 | tf_op jit(solution)/shard_map/all_to_all | solution.py:274
  189.3 1.6 copy-done.1
  190.9 6.2 %shard_map.73 = (bf16[16,144,128]{2,1,0:T(8,128)(2,1)}, bf16[512,2048]{1,0:T(8,128)(2,1)}) custom-call(bf16[128,512]{1,0:T(8,128)(2,1)} %bitcast.110, f32[16,512,8]{2,1,0:T(8,128)} %bitcast.91, f32[1,8192]{1,0:T(1,128)} %reshape_reshape.6.decay_ref, bf16[512,768]{1,0:T(8,128)(2,1)} %fusion.1.onehot_ref, bf16[768,2048]{1,0:T(8,128)(2,1)} %bitcast.96), custom_call_target="tpu_custom_call" | custom-call | tf_op jit(solution)/shard_map/pallas_call | solution.py:125
  197.1 5.0 %all-to-all-start.4 = ((bf16[16,48,2048]{2,1,0:T(8,128)(2,1)}), bf16[16,48,2048]{2,1,0:T(8,128)(2,1)S(1)}, u32[]{:S(2)}, u32[]{:S(2)}) async-start(bf16[16,48,2048]{2,1,0:T(8,128)(2,1)} %bitcast.44), calls=%async_computation.4 | async-start | bytes 6291456 | tf_op jit(solution)/shard_map/all_to_all | solution.py:274
  202.1 9.4 %shard_map.74.refs_1_ = f32[512,2048]{1,0:T(8,128)} custom-call(f32[512,512]{1,0:T(8,128)} %fusion.9.scores_ref, f32[16,512,8]{2,1,0:T(8,128)} %bitcast.80, f32[128,512]{1,0:T(8,128)} %bitcast.102, f32[128,512]{1,0:T(8,128)} %get-tuple-element.59.stept_ref, bf16[512,2048]{1,0:T(8,128)(2,1)} %get-tuple-element.31.tok_ref, f32[1,8192]{1,0:T(1,128)} %reshape_reshape.7.skip_ref), custom_call_target="tpu_custom_call" | custom-call | tf_op jit(solution)/shard_map/pallas_call | solution.py:150
  211.5 6.8 %shard_map.75.refs_0_ = bf16[512,8192]{1,0:T(8,128)(2,1)} custom-call(s32[1]{0:T(128)} %bitcast.place_ref, bf16[512,8192]{1,0:T(8,128)(2,1)} %shard_map.71.refs_0_, f32[512,2048]{1,0:T(8,128)} %shard_map.70.refs_1_, bf16[8,16,144,128]{3,2,1,0:T(8,128)(2,1)} %bitcast.105, f32[16,512,8]{2,1,0:T(8,128)} %bitcast.81, ...), custom_call_target="tpu_custom_call", output_to_operand_aliasing={{}: (1, {})} | custom-call | tf_op jit(solution)/shard_map/pallas_call | solution.py:183
  218.3 26.9 %all-to-all-done.4 = bf16[16,48,2048]{2,1,0:T(8,128)(2,1)S(1)} async-done(((bf16[16,48,2048]{2,1,0:T(8,128)(2,1)}), bf16[16,48,2048]{2,1,0:T(8,128)(2,1)S(1)}, u32[]{:S(2)}, u32[]{:S(2)}) %all-to-all-start.4) | async-done | bytes 3145760 | tf_op jit(solution)/shard_map/all_to_all | solution.py:274
  245.2 1.7 copy-done
  246.8 6.2 %shard_map.77 = (bf16[16,144,128]{2,1,0:T(8,128)(2,1)}, bf16[512,2048]{1,0:T(8,128)(2,1)}) custom-call(bf16[128,512]{1,0:T(8,128)(2,1)} %bitcast.111, f32[16,512,8]{2,1,0:T(8,128)} %bitcast.92, f32[1,8192]{1,0:T(1,128)} %reshape_reshape.6.decay_ref, bf16[512,768]{1,0:T(8,128)(2,1)} %fusion.1.onehot_ref, bf16[768,2048]{1,0:T(8,128)(2,1)} %bitcast.95), custom_call_target="tpu_custom_call" | custom-call | tf_op jit(solution)/shard_map/pallas_call | solution.py:125
  253.0 9.4 %shard_map.78.refs_1_ = f32[512,2048]{1,0:T(8,128)} custom-call(f32[512,512]{1,0:T(8,128)} %fusion.9.scores_ref, f32[16,512,8]{2,1,0:T(8,128)} %bitcast.82, f32[128,512]{1,0:T(8,128)} %bitcast.103, f32[128,512]{1,0:T(8,128)} %get-tuple-element.59.stept_ref, bf16[512,2048]{1,0:T(8,128)(2,1)} %get-tuple-element.37.tok_ref, f32[1,8192]{1,0:T(1,128)} %reshape_reshape.7.skip_ref), custom_call_target="tpu_custom_call" | custom-call | tf_op jit(solution)/shard_map/pallas_call | solution.py:150
  262.5 7.2 %shard_map.76.refs_0_ = bf16[512,8192]{1,0:T(8,128)(2,1)} custom-call(s32[1]{0:T(128)} %bitcast.place_ref, bf16[512,8192]{1,0:T(8,128)(2,1)} %shard_map.75.refs_0_, f32[512,2048]{1,0:T(8,128)} %shard_map.74.refs_1_, bf16[8,16,144,128]{3,2,1,0:T(8,128)(2,1)} %bitcast.106, f32[16,512,8]{2,1,0:T(8,128)} %bitcast.83, ...), custom_call_target="tpu_custom_call", output_to_operand_aliasing={{}: (1, {})} | custom-call | tf_op jit(solution)/shard_map/pallas_call | solution.py:183
  269.6 18.8 %all-gather.15.cloned.1.call-done = bf16[128,144,128]{2,1,0:T(8,128)(2,1)} async-done(((bf16[16,144,128]{2,1,0:T(8,128)(2,1)}), bf16[128,144,128]{2,1,0:T(8,128)(2,1)}) %all-gather.15.cloned.1.call-update) | async-done | bytes 4718608 | tf_op jit(solution)/shard_map/all_gather | solution.py:296
  288.4 6.7 %shard_map.79 = bf16[512,8192]{1,0:T(8,128)(2,1)} custom-call(s32[1]{0:T(128)} %bitcast.place_ref, bf16[512,8192]{1,0:T(8,128)(2,1)} %shard_map.76.refs_0_, f32[512,2048]{1,0:T(8,128)} %shard_map.78.refs_1_, bf16[8,16,144,128]{3,2,1,0:T(8,128)(2,1)} %bitcast.107, f32[16,512,8]{2,1,0:T(8,128)} %bitcast.84, ...), custom_call_target="tpu_custom_call", output_to_operand_aliasing={{}: (1, {})} | custom-call | tf_op jit(solution)/shard_map/pallas_call | solution.py:183
  (54 shorter events, 3.1 us)
Async XLA Ops:
  12.6 19.5 %all-to-all-start.2 = ((bf16[16,48,384]{2,1,0:T(8,128)(2,1)}), bf16[16,48,384]{2,1,0:T(8,128)(2,1)S(1)}, u32[]{:S(2)}, u32[]{:S(2)}) async-start(bf16[16,48,384]{2,1,0:T(8,128)(2,1)} %bitcast.8), calls=%async_computation.2 | async-start | bytes 1179648 | tf_op jit(solution)/shard_map/all_to_all | solution.py:206
  32.1 47.3 %all-to-all-start = ((bf16[16,48,2048]{2,1,0:T(8,128)(2,1)}), bf16[16,48,2048]{2,1,0:T(8,128)(2,1)}, u32[]{:S(2)}, u32[]{:S(2)}) async-start(bf16[16,48,2048]{2,1,0:T(8,128)(2,1)} %bitcast.94), calls=%async_computation | async-start | bytes 6291456 | tf_op jit(solution)/shard_map/all_to_all | solution.py:274
  36.6 125.1 %all-gather.9.cloned.1.call-start = ((), (), s32[]{:S(2)}) async-start(), calls=%async_computation.5 | async-start | bytes 5308416 | tf_op jit(solution)/shard_map/all_gather | solution.py:296
  37.4 15.3 %copy-start.6 = (f32[128]{0:T(128)S(1)}, f32[128]{0:T(128)}, u32[]{:S(2)}) copy-start(f32[128]{0:T(128)} %param.9) | copy-start | bytes 1540
  55.8 5.4 %copy-start.4 = (bf16[512,384]{1,0:T(8,128)(2,1)}, bf16[512,384]{1,0:T(8,128)(2,1)S(1)}, u32[]{:S(2)}) copy-start(bf16[512,384]{1,0:T(8,128)(2,1)S(1)} %gather_fusion.1) | copy-start | bytes 1179652
  57.5 39.3 %copy-start.3 = (f32[16,8,4,128]{3,1,2,0:T(8,128)}, f32[16,8,4,128]{3,1,2,0:T(8,128)S(1)}, u32[]{:S(2)}) copy-start(f32[16,8,4,128]{3,1,2,0:T(8,128)S(1)} %copy.51) | copy-start | bytes 786436
  85.6 48.0 %all-to-all-start.1 = ((bf16[16,48,2048]{2,1,0:T(8,128)(2,1)}), bf16[16,48,2048]{2,1,0:T(8,128)(2,1)S(1)}, u32[]{:S(2)}, u32[]{:S(2)}) async-start(bf16[16,48,2048]{2,1,0:T(8,128)(2,1)} %bitcast.5), calls=%async_computation.1 | async-start | bytes 6291456 | tf_op jit(solution)/shard_map/all_to_all | solution.py:274
  90.6 5.4 %copy-start.5 = (f32[128]{0:T(128)S(1)}, f32[128]{0:T(128)}, u32[]{:S(2)}) copy-start(f32[128]{0:T(128)} %param.10) | copy-start | bytes 1540
  90.6 120.9 %all-gather.11.cloned.1.call-start = ((), (), s32[]{:S(2)}) async-start(), calls=%async_computation.6 | async-start | bytes 5308416 | tf_op jit(solution)/shard_map/all_gather | solution.py:296
  133.7 1.7 copy-start.2
  141.5 47.7 %all-to-all-start.3 = ((bf16[16,48,2048]{2,1,0:T(8,128)(2,1)}), bf16[16,48,2048]{2,1,0:T(8,128)(2,1)S(1)}, u32[]{:S(2)}, u32[]{:S(2)}) async-start(bf16[16,48,2048]{2,1,0:T(8,128)(2,1)} %bitcast.41), calls=%async_computation.3 | async-start | bytes 6291456 | tf_op jit(solution)/shard_map/all_to_all | solution.py:274
  146.4 116.1 %all-gather.13.cloned.1.call-start = ((), (), s32[]{:S(2)}) async-start(), calls=%async_computation.7 | async-start | bytes 5308416 | tf_op jit(solution)/shard_map/all_gather | solution.py:296
  189.3 1.6 copy-start.1
  197.1 48.1 %all-to-all-start.4 = ((bf16[16,48,2048]{2,1,0:T(8,128)(2,1)}), bf16[16,48,2048]{2,1,0:T(8,128)(2,1)S(1)}, u32[]{:S(2)}, u32[]{:S(2)}) async-start(bf16[16,48,2048]{2,1,0:T(8,128)(2,1)} %bitcast.44), calls=%async_computation.4 | async-start | bytes 6291456 | tf_op jit(solution)/shard_map/all_to_all | solution.py:274
  202.0 86.4 %all-gather.15.cloned.1.call-start = ((), (), s32[]{:S(2)}) async-start(), calls=%async_computation.8 | async-start | bytes 5308416 | tf_op jit(solution)/shard_map/all_gather | solution.py:296
  245.2 1.7 copy-start
Sparse Core Ops, SparseCore 0:
  85.7 35.3 all-gather.8
  141.6 35.2 all-gather.10
  197.2 35.2 all-gather.12
  253.2 35.2 all-gather.14

commit v12 on v11

--- a/solution.py
+++ b/solution.py
@@ -7,7 +7,7 @@
 
 GROUP = 8
 TILE = 128
-CHUNK_GROUPS = (4, 4, 4, 4)
+CHUNK_GROUPS = (2, 4, 4, 4, 2)
 EXTRA = 16
 
 

time: 303 us -> 322 us (1.063)
  starting transfers between devices: 28 us -> 35.2 us
  Pallas kernels: 112 us -> 118 us
    all_to_all x4 -> x5, starting transfers between devices: 19.3 us -> 26.1 us  [on_device(): lax.all_to_all(sends[c], 'stream', split_axis=0, concat_axis=0, tiled=True)]
    all_to_all x4 -> x5, waiting for transfers between devices: 86.6 us -> 90.7 us  [on_device(): lax.all_to_all(sends[c], 'stream', split_axis=0, concat_axis=0, tiled=True)]
    all_to_all x1, waiting for transfers between devices: 3.55 us -> 0.01 us  [deliver(): lax.all_to_all(send, 'stream', split_axis=0, concat_axis=0, tiled=True)]
    pallas_call x4 -> x5, Pallas kernels: 38.1 us -> 40.7 us  [local_call(): pl.pallas_call(local_kernel, grid=(groups,), in_specs=[pl.BlockSpec((leng...]
    unnamed x18 -> x22, local copies, waits for them, and re-layouts: 5.85 us -> 8.16 us
    pallas_call x4 -> x5, Pallas kernels: 24.7 us -> 26.5 us  [carried_call(): pl.pallas_call(carried_kernel, grid=(groups,), in_specs=[pl.BlockSpec(bt....]
    pallas_call x4 -> x5, Pallas kernels: 21.5 us -> 22.9 us  [send_call(): pl.pallas_call(send_kernel, grid=(groups,), in_specs=[pl.BlockSpec(onehot...]
    all_gather x4 -> x5, waiting for transfers between devices: 18.8 us -> 20.1 us  [on_device(): gathers.append(lax.all_gather(carried, 'pos'))]
  transfers between devices with their start and end apart: 9 -> 11, of which waited for: 6 -> 6; matrix products, arithmetic and copies ran while one was open for 9% -> 9% of each run, Pallas kernels for 33% -> 35%
where the time goes in v12:
time: 322 us; the launch traced here: 320 us
  Pallas kernels  118 us (37%)
  waiting for transfers between devices  111 us (34%)
  starting transfers between devices  35.2 us (11%)
  local copies, waits for them, and re-layouts  24 us (7%)
  other arithmetic  15.7 us (5%)
  between operations  13.4 us (4%)
    all_to_all x5, waiting for transfers between devices, on_device(): lax.all_to_all(sends[c], 'stream', split_axis=0, concat_axis=0, tiled=True)  90.7 us
    pallas_call x5, Pallas kernels, local_call(): pl.pallas_call(local_kernel, grid=(groups,), in_specs=[pl.BlockSpec((leng...  40.7 us
    pallas_call x5, Pallas kernels, combine_call(): pl.pallas_call(combine_kernel, grid=(groups,), in_specs=[pl.BlockSpec(mem...  28.2 us
    pallas_call x5, Pallas kernels, carried_call(): pl.pallas_call(carried_kernel, grid=(groups,), in_specs=[pl.BlockSpec(bt....  26.5 us
    all_to_all x5, starting transfers between devices, on_device(): lax.all_to_all(sends[c], 'stream', split_axis=0, concat_axis=0, tiled=True)  26.1 us
    pallas_call x5, Pallas kernels, send_call(): pl.pallas_call(send_kernel, grid=(groups,), in_specs=[pl.BlockSpec(onehot...  22.9 us
    all_gather x5, waiting for transfers between devices, on_device(): gathers.append(lax.all_gather(carried, 'pos'))  20.1 us
    all_to_all x1, starting transfers between devices, deliver(): lax.all_to_all(send, 'stream', split_axis=0, concat_axis=0, tiled=True)  8.43 us
  transfers between devices with their start and end apart: 11, of which 6 were waited for; matrix products, arithmetic and copies ran while one was open for 9% of the time, Pallas kernels for 35%

profile of v12, /device:TPU:1, one launch (start us, length us, event | category | flops | bytes accessed | tf_op | source)
XLA Modules:
  0.0 319.9 jit_solution(888308914609870329)
XLA Ops:
  8.3 1.1 pad_maximum_fusion
  9.4 3.2 %gather_fusion = bf16[768,384]{1,0:T(8,128)(2,1)} fusion(bf16[512,384]{1,0:T(8,128)(2,1)S(1)} %pad_maximum_fusion, s32[1024]{0:T(1024)S(1)} %pad_clamp_fusion.1), kind=kCustom, calls=%fused_computation | custom fusion | bytes 1182720 | tf_op jit(solution)/shard_map/jit(_take)/gather | solution.py:196
  12.6 8.4 %all-to-all-start.2 = ((bf16[16,48,384]{2,1,0:T(8,128)(2,1)}), bf16[16,48,384]{2,1,0:T(8,128)(2,1)S(1)}, u32[]{:S(2)}, u32[]{:S(2)}) async-start(bf16[16,48,384]{2,1,0:T(8,128)(2,1)} %bitcast.8), calls=%async_computation.2 | async-start | bytes 1179648 | tf_op jit(solution)/shard_map/all_to_all | solution.py:206
  22.0 1.1 fusion.onehot_ref
  23.1 5.3 %shard_map.65 = bf16[768,2048]{1,0:T(8,128)(2,1)} custom-call(bf16[768,512]{1,0:T(8,128)(2,1)} %fusion.onehot_ref, bf16[512,8192]{1,0:T(8,128)(2,1)} %bitcast.90), custom_call_target="tpu_custom_call" | custom-call | tf_op jit(solution)/shard_map/pallas_call | solution.py:48
  28.4 3.4 %shard_map.64 = bf16[768,1024]{1,0:T(8,128)(2,1)} custom-call(bf16[768,512]{1,0:T(8,128)(2,1)} %fusion.onehot_ref, bf16[512,8192]{1,0:T(8,128)(2,1)} %bitcast.91), custom_call_target="tpu_custom_call" | custom-call | tf_op jit(solution)/shard_map/pallas_call | solution.py:48
  32.8 4.2 %compare_select_fusion.2 = (s32[512,1]{0,1:T(1,128)S(1)}, s32[512,1]{0,1:T(1,128)S(1)}) fusion(s32[]{:T(128)} %bitcast.21, s32[]{:T(128)} %bitcast.22, s32[]{:T(128)} %bitcast.23, s32[]{:T(128)} %bitcast.24, s32[]{:T(128)} %bitcast.25, s32[]{:T(128)} %bitcast.27, s32[]{:T(128)} %bitcast.26, s32[512,1]{0,1:T(1,128)S(1)} %bitcast.131), kind=kLoop, calls=%fused_computation.33 | loop fusion | flops 7680 | bytes 6172 | tf_op jit(solution)/shard_map/jit(_take)/gather | solution.py:232
  37.0 5.7 %select_subtract_fusion = (s32[512]{0:T(512)S(1)}, s32[512]{0:T(512)S(1)}) fusion(s32[512]{0:T(512)S(1)} %convert_reduce_fusion, pred[512]{0:T(512)(128)(4,1)S(1)} %get-tuple-element.56, pred[512]{0:T(512)(128)(4,1)S(1)} %get-tuple-element.55, pred[512]{0:T(512)(128)(4,1)S(1)} %get-tuple-element.57, pred[512]{0:T(512)(128)(4,1)S(1)} %get-tuple-element.54, ...), kind=kLoop, calls=%fused_computation.48 | loop fusion | flops 10240 | bytes 12836 | tf_op jit(solution)/shard_map/sub | solution.py:233
  42.8 1.1 fusion.1.onehot_ref
  43.9 6.7 %all-to-all-start = ((bf16[16,48,1024]{2,1,0:T(8,128)(2,1)}), bf16[16,48,1024]{2,1,0:T(8,128)(2,1)S(1)}, u32[]{:S(2)}, u32[]{:S(2)}) async-start(bf16[16,48,1024]{2,1,0:T(8,128)(2,1)} %bitcast.113), calls=%async_computation | async-start | bytes 3145728 | tf_op jit(solution)/shard_map/all_to_all | solution.py:274
  50.6 1.9 gather_fusion.1
  54.5 0.9 multiply_bitcast_fusion
  55.4 2.6 copy.41
  59.5 12.1 %all-to-all-done = bf16[16,48,1024]{2,1,0:T(8,128)(2,1)S(1)} async-done(((bf16[16,48,1024]{2,1,0:T(8,128)(2,1)}), bf16[16,48,1024]{2,1,0:T(8,128)(2,1)S(1)}, u32[]{:S(2)}, u32[]{:S(2)}) %all-to-all-start) | async-done | bytes 1572896 | tf_op jit(solution)/shard_map/all_to_all | solution.py:274
  71.6 1.2 copy-done.4
  72.7 3.9 %shard_map.66 = (bf16[8,144,128]{2,1,0:T(8,128)(2,1)}, bf16[512,1024]{1,0:T(8,128)(2,1)}) custom-call(bf16[128,512]{1,0:T(8,128)(2,1)} %bitcast.115, f32[16,512,8]{2,1,0:T(8,128)} %bitcast.95, f32[1,8192]{1,0:T(1,128)} %reshape_reshape.6.decay_ref, bf16[512,768]{1,0:T(8,128)(2,1)} %fusion.1.onehot_ref, bf16[768,1024]{1,0:T(8,128)(2,1)} %bitcast.111), custom_call_target="tpu_custom_call" | custom-call | tf_op jit(solution)/shard_map/pallas_call | solution.py:125
  76.7 6.3 %all-to-all-start.1 = ((bf16[16,48,2048]{2,1,0:T(8,128)(2,1)}), bf16[16,48,2048]{2,1,0:T(8,128)(2,1)S(1)}, u32[]{:S(2)}, u32[]{:S(2)}) async-start(bf16[16,48,2048]{2,1,0:T(8,128)(2,1)} %bitcast.5), calls=%async_computation.1 | async-start | bytes 6291456 | tf_op jit(solution)/shard_map/all_to_all | solution.py:274
  83.0 5.4 %shard_map.68 = bf16[768,2048]{1,0:T(8,128)(2,1)} custom-call(bf16[768,512]{1,0:T(8,128)(2,1)} %fusion.onehot_ref, bf16[512,8192]{1,0:T(8,128)(2,1)} %bitcast.92), custom_call_target="tpu_custom_call" | custom-call | tf_op jit(solution)/shard_map/pallas_call | solution.py:48
  89.3 2.7 copy.40
  92.0 2.3 fusion.9.scores_ref
  94.3 6.1 %shard_map.67.refs_0_ = f32[512,1024]{1,0:T(8,128)} custom-call(f32[512,512]{1,0:T(8,128)} %fusion.9.scores_ref, f32[16,512,8]{2,1,0:T(8,128)} %bitcast.80, f32[128,512]{1,0:T(8,128)} %bitcast.103, f32[128,512]{1,0:T(8,128)} %get-tuple-element.69.stept_ref, bf16[512,1024]{1,0:T(8,128)(2,1)} %get-tuple-element.29.tok_ref, f32[1,8192]{1,0:T(1,128)} %reshape_reshape.7.skip_ref), custom_call_target="tpu_custom_call" | custom-call | tf_op jit(solution)/shard_map/pallas_call | solution.py:150
  100.4 28.3 %all-to-all-done.1 = bf16[16,48,2048]{2,1,0:T(8,128)(2,1)S(1)} async-done(((bf16[16,48,2048]{2,1,0:T(8,128)(2,1)}), bf16[16,48,2048]{2,1,0:T(8,128)(2,1)S(1)}, u32[]{:S(2)}, u32[]{:S(2)}) %all-to-all-start.1) | async-done | bytes 3145760 | tf_op jit(solution)/shard_map/all_to_all | solution.py:274
  128.7 1.7 copy-done.3
  130.4 6.2 %shard_map.69 = (bf16[16,144,128]{2,1,0:T(8,128)(2,1)}, bf16[512,2048]{1,0:T(8,128)(2,1)}) custom-call(bf16[128,512]{1,0:T(8,128)(2,1)} %bitcast.116, f32[16,512,8]{2,1,0:T(8,128)} %bitcast.96, f32[1,8192]{1,0:T(1,128)} %reshape_reshape.6.decay_ref, bf16[512,768]{1,0:T(8,128)(2,1)} %fusion.1.onehot_ref, bf16[768,2048]{1,0:T(8,128)(2,1)} %bitcast.110), custom_call_target="tpu_custom_call" | custom-call | tf_op jit(solution)/shard_map/pallas_call | solution.py:125
  136.6 3.8 %all-to-all-start.3 = ((bf16[16,48,2048]{2,1,0:T(8,128)(2,1)}), bf16[16,48,2048]{2,1,0:T(8,128)(2,1)S(1)}, u32[]{:S(2)}, u32[]{:S(2)}) async-start(bf16[16,48,2048]{2,1,0:T(8,128)(2,1)} %bitcast.41), calls=%async_computation.3 | async-start | bytes 6291456 | tf_op jit(solution)/shard_map/all_to_all | solution.py:274
  140.6 5.4 %shard_map.72 = bf16[768,2048]{1,0:T(8,128)(2,1)} custom-call(bf16[768,512]{1,0:T(8,128)(2,1)} %fusion.onehot_ref, bf16[512,8192]{1,0:T(8,128)(2,1)} %bitcast.93), custom_call_target="tpu_custom_call" | custom-call | tf_op jit(solution)/shard_map/pallas_call | solution.py:48
  146.0 9.5 %shard_map.70.refs_1_ = f32[512,2048]{1,0:T(8,128)} custom-call(f32[512,512]{1,0:T(8,128)} %fusion.9.scores_ref, f32[16,512,8]{2,1,0:T(8,128)} %bitcast.81, f32[128,512]{1,0:T(8,128)} %bitcast.104, f32[128,512]{1,0:T(8,128)} %get-tuple-element.69.stept_ref, bf16[512,2048]{1,0:T(8,128)(2,1)} %get-tuple-element.32.tok_ref, f32[1,8192]{1,0:T(1,128)} %reshape_reshape.7.skip_ref), custom_call_target="tpu_custom_call" | custom-call | tf_op jit(solution)/shard_map/pallas_call | solution.py:150
  155.5 4.0 %shard_map.71.refs_0_ = bf16[512,8192]{1,0:T(8,128)(2,1)} custom-call(s32[1]{0:T(128)} %bitcast.place_ref, f32[512,1024]{1,0:T(8,128)} %shard_map.67.refs_0_, bf16[8,8,144,128]{3,2,1,0:T(8,128)(2,1)} %bitcast.123, f32[16,512,8]{2,1,0:T(8,128)} %bitcast.82, bf16[512,128]{1,0:T(8,128)(2,1)} %get-tuple-element.62.refs_3_.refs_4_), custom_call_target="tpu_custom_call" | custom-call | tf_op jit(solution)/shard_map/pallas_call | solution.py:183
  159.5 23.1 %all-to-all-done.3 = bf16[16,48,2048]{2,1,0:T(8,128)(2,1)S(1)} async-done(((bf16[16,48,2048]{2,1,0:T(8,128)(2,1)}), bf16[16,48,2048]{2,1,0:T(8,128)(2,1)S(1)}, u32[]{:S(2)}, u32[]{:S(2)}) %all-to-all-start.3) | async-done | bytes 3145760 | tf_op jit(solution)/shard_map/all_to_all | solution.py:274
  182.6 1.7 copy-done.2
  184.3 6.2 %shard_map.73 = (bf16[16,144,128]{2,1,0:T(8,128)(2,1)}, bf16[512,2048]{1,0:T(8,128)(2,1)}) custom-call(bf16[128,512]{1,0:T(8,128)(2,1)} %bitcast.117, f32[16,512,8]{2,1,0:T(8,128)} %bitcast.97, f32[1,8192]{1,0:T(1,128)} %reshape_reshape.6.decay_ref, bf16[512,768]{1,0:T(8,128)(2,1)} %fusion.1.onehot_ref, bf16[768,2048]{1,0:T(8,128)(2,1)} %bitcast.109), custom_call_target="tpu_custom_call" | custom-call | tf_op jit(solution)/shard_map/pallas_call | solution.py:125
  190.5 5.3 %all-to-all-start.4 = ((bf16[16,48,2048]{2,1,0:T(8,128)(2,1)}), bf16[16,48,2048]{2,1,0:T(8,128)(2,1)S(1)}, u32[]{:S(2)}, u32[]{:S(2)}) async-start(bf16[16,48,2048]{2,1,0:T(8,128)(2,1)} %bitcast.44), calls=%async_computation.4 | async-start | bytes 6291456 | tf_op jit(solution)/shard_map/all_to_all | solution.py:274
  195.8 3.4 %shard_map.76 = bf16[768,1024]{1,0:T(8,128)(2,1)} custom-call(bf16[768,512]{1,0:T(8,128)(2,1)} %fusion.onehot_ref, bf16[512,8192]{1,0:T(8,128)(2,1)} %bitcast.94), custom_call_target="tpu_custom_call" | custom-call | tf_op jit(solution)/shard_map/pallas_call | solution.py:48
  199.3 9.6 %shard_map.74.refs_1_ = f32[512,2048]{1,0:T(8,128)} custom-call(f32[512,512]{1,0:T(8,128)} %fusion.9.scores_ref, f32[16,512,8]{2,1,0:T(8,128)} %bitcast.83, f32[128,512]{1,0:T(8,128)} %bitcast.105, f32[128,512]{1,0:T(8,128)} %get-tuple-element.69.stept_ref, bf16[512,2048]{1,0:T(8,128)(2,1)} %get-tuple-element.36.tok_ref, f32[1,8192]{1,0:T(1,128)} %reshape_reshape.7.skip_ref), custom_call_target="tpu_custom_call" | custom-call | tf_op jit(solution)/shard_map/pallas_call | solution.py:150
  208.9 6.8 %shard_map.75.refs_0_ = bf16[512,8192]{1,0:T(8,128)(2,1)} custom-call(s32[1]{0:T(128)} %bitcast.place_ref, bf16[512,8192]{1,0:T(8,128)(2,1)} %shard_map.71.refs_0_, f32[512,2048]{1,0:T(8,128)} %shard_map.70.refs_1_, bf16[8,16,144,128]{3,2,1,0:T(8,128)(2,1)} %bitcast.120, f32[16,512,8]{2,1,0:T(8,128)} %bitcast.84, ...), custom_call_target="tpu_custom_call", output_to_operand_aliasing={{}: (1, {})} | custom-call | tf_op jit(solution)/shard_map/pallas_call | solution.py:183
  215.7 23.7 %all-to-all-done.4 = bf16[16,48,2048]{2,1,0:T(8,128)(2,1)S(1)} async-done(((bf16[16,48,2048]{2,1,0:T(8,128)(2,1)}), bf16[16,48,2048]{2,1,0:T(8,128)(2,1)S(1)}, u32[]{:S(2)}, u32[]{:S(2)}) %all-to-all-start.4) | async-done | bytes 3145760 | tf_op jit(solution)/shard_map/all_to_all | solution.py:274
  239.4 1.6 copy-done.1
  241.1 6.2 %shard_map.77 = (bf16[16,144,128]{2,1,0:T(8,128)(2,1)}, bf16[512,2048]{1,0:T(8,128)(2,1)}) custom-call(bf16[128,512]{1,0:T(8,128)(2,1)} %bitcast.118, f32[16,512,8]{2,1,0:T(8,128)} %bitcast.98, f32[1,8192]{1,0:T(1,128)} %reshape_reshape.6.decay_ref, bf16[512,768]{1,0:T(8,128)(2,1)} %fusion.1.onehot_ref, bf16[768,2048]{1,0:T(8,128)(2,1)} %bitcast.108), custom_call_target="tpu_custom_call" | custom-call | tf_op jit(solution)/shard_map/pallas_call | solution.py:125
  247.2 4.1 %all-to-all-start.5 = ((bf16[16,48,1024]{2,1,0:T(8,128)(2,1)}), bf16[16,48,1024]{2,1,0:T(8,128)(2,1)S(1)}, u32[]{:S(2)}, u32[]{:S(2)}) async-start(bf16[16,48,1024]{2,1,0:T(8,128)(2,1)} %bitcast.114), calls=%async_computation.5 | async-start | bytes 3145728 | tf_op jit(solution)/shard_map/all_to_all | solution.py:274
  251.7 9.4 %shard_map.78.refs_1_ = f32[512,2048]{1,0:T(8,128)} custom-call(f32[512,512]{1,0:T(8,128)} %fusion.9.scores_ref, f32[16,512,8]{2,1,0:T(8,128)} %bitcast.85, f32[128,512]{1,0:T(8,128)} %bitcast.106, f32[128,512]{1,0:T(8,128)} %get-tuple-element.69.stept_ref, bf16[512,2048]{1,0:T(8,128)(2,1)} %get-tuple-element.41.tok_ref, f32[1,8192]{1,0:T(1,128)} %reshape_reshape.7.skip_ref), custom_call_target="tpu_custom_call" | custom-call | tf_op jit(solution)/shard_map/pallas_call | solution.py:150
  261.1 6.8 %shard_map.79.refs_0_ = bf16[512,8192]{1,0:T(8,128)(2,1)} custom-call(s32[1]{0:T(128)} %bitcast.place_ref, bf16[512,8192]{1,0:T(8,128)(2,1)} %shard_map.75.refs_0_, f32[512,2048]{1,0:T(8,128)} %shard_map.74.refs_1_, bf16[8,16,144,128]{3,2,1,0:T(8,128)(2,1)} %bitcast.121, f32[16,512,8]{2,1,0:T(8,128)} %bitcast.86, ...), custom_call_target="tpu_custom_call", output_to_operand_aliasing={{}: (1, {})} | custom-call | tf_op jit(solution)/shard_map/pallas_call | solution.py:183
  267.9 3.5 %all-to-all-done.5 = bf16[16,48,1024]{2,1,0:T(8,128)(2,1)S(1)} async-done(((bf16[16,48,1024]{2,1,0:T(8,128)(2,1)}), bf16[16,48,1024]{2,1,0:T(8,128)(2,1)S(1)}, u32[]{:S(2)}, u32[]{:S(2)}) %all-to-all-start.5) | async-done | bytes 1572896 | tf_op jit(solution)/shard_map/all_to_all | solution.py:274
  271.4 1.2 copy-done.5
  272.6 4.0 %shard_map.81 = (bf16[8,144,128]{2,1,0:T(8,128)(2,1)}, bf16[512,1024]{1,0:T(8,128)(2,1)}) custom-call(bf16[128,512]{1,0:T(8,128)(2,1)} %bitcast.119, f32[16,512,8]{2,1,0:T(8,128)} %bitcast.99, f32[1,8192]{1,0:T(1,128)} %reshape_reshape.6.decay_ref, bf16[512,768]{1,0:T(8,128)(2,1)} %fusion.1.onehot_ref, bf16[768,1024]{1,0:T(8,128)(2,1)} %bitcast.112), custom_call_target="tpu_custom_call" | custom-call | tf_op jit(solution)/shard_map/pallas_call | solution.py:125
  276.6 6.1 %shard_map.82.refs_1_ = f32[512,1024]{1,0:T(8,128)} custom-call(f32[512,512]{1,0:T(8,128)} %fusion.9.scores_ref, f32[16,512,8]{2,1,0:T(8,128)} %bitcast.87, f32[128,512]{1,0:T(8,128)} %bitcast.107, f32[128,512]{1,0:T(8,128)} %get-tuple-element.69.stept_ref, bf16[512,1024]{1,0:T(8,128)(2,1)} %get-tuple-element.47.tok_ref, f32[1,8192]{1,0:T(1,128)} %reshape_reshape.7.skip_ref), custom_call_target="tpu_custom_call" | custom-call | tf_op jit(solution)/shard_map/pallas_call | solution.py:150
  282.7 6.7 %shard_map.80.refs_0_ = bf16[512,8192]{1,0:T(8,128)(2,1)} custom-call(s32[1]{0:T(128)} %bitcast.place_ref, bf16[512,8192]{1,0:T(8,128)(2,1)} %shard_map.79.refs_0_, f32[512,2048]{1,0:T(8,128)} %shard_map.78.refs_1_, bf16[8,16,144,128]{3,2,1,0:T(8,128)(2,1)} %bitcast.122, f32[16,512,8]{2,1,0:T(8,128)} %bitcast.88, ...), custom_call_target="tpu_custom_call", output_to_operand_aliasing={{}: (1, {})} | custom-call | tf_op jit(solution)/shard_map/pallas_call | solution.py:183
  289.4 20.1 %all-gather.19.cloned.1.call-done = bf16[64,144,128]{2,1,0:T(8,128)(2,1)} async-done(((bf16[8,144,128]{2,1,0:T(8,128)(2,1)}), bf16[64,144,128]{2,1,0:T(8,128)(2,1)}) %all-gather.19.cloned.1.call-update) | async-done | bytes 2359312 | tf_op jit(solution)/shard_map/all_gather | solution.py:296
  309.4 3.9 %shard_map.83 = bf16[512,8192]{1,0:T(8,128)(2,1)} custom-call(s32[1]{0:T(128)} %bitcast.place_ref, bf16[512,8192]{1,0:T(8,128)(2,1)} %shard_map.80.refs_0_, f32[512,1024]{1,0:T(8,128)} %shard_map.82.refs_1_, bf16[8,8,144,128]{3,2,1,0:T(8,128)(2,1)} %bitcast.126, f32[16,512,8]{2,1,0:T(8,128)} %bitcast.89, ...), custom_call_target="tpu_custom_call", output_to_operand_aliasing={{}: (1, {})} | custom-call | tf_op jit(solution)/shard_map/pallas_call | solution.py:183
  (67 shorter events, 8.6 us)
Async XLA Ops:
  12.6 31.2 %all-to-all-start.2 = ((bf16[16,48,384]{2,1,0:T(8,128)(2,1)}), bf16[16,48,384]{2,1,0:T(8,128)(2,1)S(1)}, u32[]{:S(2)}, u32[]{:S(2)}) async-start(bf16[16,48,384]{2,1,0:T(8,128)(2,1)} %bitcast.8), calls=%async_computation.2 | async-start | bytes 1179648 | tf_op jit(solution)/shard_map/all_to_all | solution.py:206
  28.4 14.4 %copy-start.8 = (f32[128]{0:T(128)S(1)}, f32[128]{0:T(128)}, u32[]{:S(2)}) copy-start(f32[128]{0:T(128)} %param.9) | copy-start | bytes 1540
  43.9 27.7 %all-to-all-start = ((bf16[16,48,1024]{2,1,0:T(8,128)(2,1)}), bf16[16,48,1024]{2,1,0:T(8,128)(2,1)S(1)}, u32[]{:S(2)}, u32[]{:S(2)}) async-start(bf16[16,48,1024]{2,1,0:T(8,128)(2,1)} %bitcast.113), calls=%async_computation | async-start | bytes 3145728 | tf_op jit(solution)/shard_map/all_to_all | solution.py:274
  50.6 104.9 %all-gather.11.cloned.1.call-start = ((), (), s32[]{:S(2)}) async-start(), calls=%async_computation.6 | async-start | bytes 2654208 | tf_op jit(solution)/shard_map/all_gather | solution.py:296
  52.5 24.2 %copy-start.6 = (bf16[512,384]{1,0:T(8,128)(2,1)}, bf16[512,384]{1,0:T(8,128)(2,1)S(1)}, u32[]{:S(2)}) copy-start(bf16[512,384]{1,0:T(8,128)(2,1)S(1)} %gather_fusion.1) | copy-start | bytes 1179652
  54.3 35.0 %copy-start = (f32[16,8,4,128]{3,1,2,0:T(8,128)}, f32[16,8,4,128]{3,1,2,0:T(8,128)S(1)}, u32[]{:S(2)}) copy-start(f32[16,8,4,128]{3,1,2,0:T(8,128)S(1)} %copy.52) | copy-start | bytes 786436
  71.6 1.2 copy-start.4
  76.7 52.0 %all-to-all-start.1 = ((bf16[16,48,2048]{2,1,0:T(8,128)(2,1)}), bf16[16,48,2048]{2,1,0:T(8,128)(2,1)S(1)}, u32[]{:S(2)}, u32[]{:S(2)}) async-start(bf16[16,48,2048]{2,1,0:T(8,128)(2,1)} %bitcast.5), calls=%async_computation.1 | async-start | bytes 6291456 | tf_op jit(solution)/shard_map/all_to_all | solution.py:274
  83.0 5.5 %copy-start.7 = (f32[128]{0:T(128)S(1)}, f32[128]{0:T(128)}, u32[]{:S(2)}) copy-start(f32[128]{0:T(128)} %param.10) | copy-start | bytes 1540
  83.0 125.9 %all-gather.13.cloned.1.call-start = ((), (), s32[]{:S(2)}) async-start(), calls=%async_computation.7 | async-start | bytes 5308416 | tf_op jit(solution)/shard_map/all_gather | solution.py:296
  128.7 1.7 copy-start.3
  136.6 46.0 %all-to-all-start.3 = ((bf16[16,48,2048]{2,1,0:T(8,128)(2,1)}), bf16[16,48,2048]{2,1,0:T(8,128)(2,1)S(1)}, u32[]{:S(2)}, u32[]{:S(2)}) async-start(bf16[16,48,2048]{2,1,0:T(8,128)(2,1)} %bitcast.41), calls=%async_computation.3 | async-start | bytes 6291456 | tf_op jit(solution)/shard_map/all_to_all | solution.py:274
  140.3 120.7 %all-gather.15.cloned.1.call-start = ((), (), s32[]{:S(2)}) async-start(), calls=%async_computation.8 | async-start | bytes 5308416 | tf_op jit(solution)/shard_map/all_gather | solution.py:296
  182.6 1.7 copy-start.2
  190.5 49.0 %all-to-all-start.4 = ((bf16[16,48,2048]{2,1,0:T(8,128)(2,1)}), bf16[16,48,2048]{2,1,0:T(8,128)(2,1)S(1)}, u32[]{:S(2)}, u32[]{:S(2)}) async-start(bf16[16,48,2048]{2,1,0:T(8,128)(2,1)} %bitcast.44), calls=%async_computation.4 | async-start | bytes 6291456 | tf_op jit(solution)/shard_map/all_to_all | solution.py:274
  195.8 86.9 %all-gather.17.cloned.1.call-start = ((), (), s32[]{:S(2)}) async-start(), calls=%async_computation.9 | async-start | bytes 5308416 | tf_op jit(solution)/shard_map/all_gather | solution.py:296
  239.4 1.6 copy-start.1
  247.2 24.1 %all-to-all-start.5 = ((bf16[16,48,1024]{2,1,0:T(8,128)(2,1)}), bf16[16,48,1024]{2,1,0:T(8,128)(2,1)S(1)}, u32[]{:S(2)}, u32[]{:S(2)}) async-start(bf16[16,48,1024]{2,1,0:T(8,128)(2,1)} %bitcast.114), calls=%async_computation.5 | async-start | bytes 3145728 | tf_op jit(solution)/shard_map/all_to_all | solution.py:274
  251.4 58.0 %all-gather.19.cloned.1.call-start = ((), (), s32[]{:S(2)}) async-start(), calls=%async_computation.10 | async-start | bytes 2654208 | tf_op jit(solution)/shard_map/all_gather | solution.py:296
  271.4 1.2 copy-start.5
Sparse Core Ops, SparseCore 0:
  76.8 26.8 all-gather.10
  136.7 34.5 all-gather.12
  190.6 35.5 all-gather.14
  247.4 34.8 all-gather.16
  283.8 25.5 all-gather.18

commit v13 on v11

--- a/solution.py
+++ b/solution.py
@@ -8,7 +8,7 @@
 GROUP = 8
 TILE = 128
 CHUNK_GROUPS = (4, 4, 4, 4)
-EXTRA = 16
+EXTRA = 8
 
 
 def lane_pick(low, high):

time: 303 us -> 302 us (level)
  no operation moved by 1% of the time
where the time goes in v13:
time: 302 us; the launch traced here: 301 us
  Pallas kernels  112 us (37%)
  waiting for transfers between devices  108 us (36%)
  starting transfers between devices  28 us (9%)
  local copies, waits for them, and re-layouts  21.7 us (7%)
  other arithmetic  15.5 us (5%)
  between operations  13.4 us (4%)
    all_to_all x4, waiting for transfers between devices, on_device(): lax.all_to_all(sends[c], 'stream', split_axis=0, concat_axis=0, tiled=True)  86.7 us
    pallas_call x4, Pallas kernels, local_call(): pl.pallas_call(local_kernel, grid=(groups,), in_specs=[pl.BlockSpec((leng...  38.1 us
    pallas_call x4, Pallas kernels, combine_call(): pl.pallas_call(combine_kernel, grid=(groups,), in_specs=[pl.BlockSpec(mem...  27.3 us
    pallas_call x4, Pallas kernels, carried_call(): pl.pallas_call(carried_kernel, grid=(groups,), in_specs=[pl.BlockSpec(bt....  24.8 us
    pallas_call x4, Pallas kernels, send_call(): pl.pallas_call(send_kernel, grid=(groups,), in_specs=[pl.BlockSpec(onehot...  21.5 us
    all_to_all x4, starting transfers between devices, on_device(): lax.all_to_all(sends[c], 'stream', split_axis=0, concat_axis=0, tiled=True)  19.2 us
    all_gather x4, waiting for transfers between devices, on_device(): gathers.append(lax.all_gather(carried, 'pos'))  17.8 us
    all_to_all x1, starting transfers between devices, deliver(): lax.all_to_all(send, 'stream', split_axis=0, concat_axis=0, tiled=True)  8.43 us
  transfers between devices with their start and end apart: 9, of which 6 were waited for; matrix products, arithmetic and copies ran while one was open for 9% of the time, Pallas kernels for 33%

profile of v13, /device:TPU:1, one launch (start us, length us, event | category | flops | bytes accessed | tf_op | source)
XLA Modules:
  0.0 300.6 jit_solution(4001270293265977119)
XLA Ops:
  7.5 0.7 bitcast_subtract_fusion
  8.3 1.1 pad_maximum_fusion
  9.4 3.2 %gather_fusion = bf16[768,384]{1,0:T(8,128)(2,1)} fusion(bf16[512,384]{1,0:T(8,128)(2,1)S(1)} %pad_maximum_fusion, s32[1024]{0:T(1024)S(1)} %pad_clamp_fusion.1), kind=kCustom, calls=%fused_computation | custom fusion | bytes 1182720 | tf_op jit(solution)/shard_map/jit(_take)/gather | solution.py:196
  12.6 8.4 %all-to-all-start.2 = ((bf16[16,48,384]{2,1,0:T(8,128)(2,1)}), bf16[16,48,384]{2,1,0:T(8,128)(2,1)S(1)}, u32[]{:S(2)}, u32[]{:S(2)}) async-start(bf16[16,48,384]{2,1,0:T(8,128)(2,1)} %bitcast.8), calls=%async_computation.2 | async-start | bytes 1179648 | tf_op jit(solution)/shard_map/all_to_all | solution.py:206
  21.1 0.9 dynamic-slice_reduce_fusion
  22.1 1.1 fusion.onehot_ref
  23.2 5.3 %shard_map.64 = bf16[768,2048]{1,0:T(8,128)(2,1)} custom-call(bf16[768,512]{1,0:T(8,128)(2,1)} %fusion.onehot_ref, bf16[512,8192]{1,0:T(8,128)(2,1)} %bitcast.85), custom_call_target="tpu_custom_call" | custom-call | tf_op jit(solution)/shard_map/pallas_call | solution.py:48
  28.6 3.6 %all-to-all-done.2 = bf16[16,48,384]{2,1,0:T(8,128)(2,1)S(1)} async-done(((bf16[16,48,384]{2,1,0:T(8,128)(2,1)}), bf16[16,48,384]{2,1,0:T(8,128)(2,1)S(1)}, u32[]{:S(2)}, u32[]{:S(2)}) %all-to-all-start.2) | async-done | bytes 589856 | tf_op jit(solution)/shard_map/all_to_all | solution.py:206
  32.1 4.5 %all-to-all-start = ((bf16[16,48,2048]{2,1,0:T(8,128)(2,1)}), bf16[16,48,2048]{2,1,0:T(8,128)(2,1)}, u32[]{:S(2)}, u32[]{:S(2)}) async-start(bf16[16,48,2048]{2,1,0:T(8,128)(2,1)} %bitcast.94), calls=%async_computation | async-start | bytes 6291456 | tf_op jit(solution)/shard_map/all_to_all | solution.py:274
  36.7 0.7 fusion.15
  37.4 5.4 %shard_map.65 = bf16[768,2048]{1,0:T(8,128)(2,1)} custom-call(bf16[768,512]{1,0:T(8,128)(2,1)} %fusion.onehot_ref, bf16[512,8192]{1,0:T(8,128)(2,1)} %bitcast.86), custom_call_target="tpu_custom_call" | custom-call | tf_op jit(solution)/shard_map/pallas_call | solution.py:48
  42.9 4.3 %compare_select_fusion.2 = (s32[512,1]{0,1:T(1,128)S(1)}, s32[512,1]{0,1:T(1,128)S(1)}) fusion(s32[]{:T(128)} %bitcast.21, s32[]{:T(128)} %bitcast.22, s32[]{:T(128)} %bitcast.23, s32[]{:T(128)} %bitcast.24, s32[]{:T(128)} %bitcast.25, s32[]{:T(128)} %bitcast.27, s32[]{:T(128)} %bitcast.26, s32[512,1]{0,1:T(1,128)S(1)} %bitcast.118), kind=kLoop, calls=%fused_computation.33 | loop fusion | flops 7680 | bytes 6172 | tf_op jit(solution)/shard_map/jit(_take)/gather | solution.py:232
  47.2 5.5 %select_subtract_fusion = (s32[512]{0:T(512)S(1)}, s32[512]{0:T(512)S(1)}) fusion(s32[512]{0:T(512)S(1)} %convert_reduce_fusion, pred[512]{0:T(512)(128)(4,1)S(1)} %get-tuple-element.46, pred[512]{0:T(512)(128)(4,1)S(1)} %get-tuple-element.45, pred[512]{0:T(512)(128)(4,1)S(1)} %get-tuple-element.47, pred[512]{0:T(512)(128)(4,1)S(1)} %get-tuple-element.44, ...), kind=kLoop, calls=%fused_computation.48 | loop fusion | flops 10240 | bytes 12836 | tf_op jit(solution)/shard_map/sub | solution.py:233
  52.8 1.1 fusion.1.onehot_ref
  53.8 1.9 gather_fusion.1
  55.8 0.8 fusion.14
  57.7 0.9 multiply_bitcast_fusion
  58.6 2.6 copy.40
  61.3 0.7 reshape_reshape.6.decay_ref
  62.0 0.8 copy.41
  62.8 16.7 %all-to-all-done = bf16[16,48,2048]{2,1,0:T(8,128)(2,1)} async-done(((bf16[16,48,2048]{2,1,0:T(8,128)(2,1)}), bf16[16,48,2048]{2,1,0:T(8,128)(2,1)}, u32[]{:S(2)}, u32[]{:S(2)}) %all-to-all-start) | async-done | bytes 3145760 | tf_op jit(solution)/shard_map/all_to_all | solution.py:274
  79.4 6.2 %shard_map.66 = (bf16[16,136,128]{2,1,0:T(8,128)(2,1)}, bf16[512,2048]{1,0:T(8,128)(2,1)}) custom-call(bf16[128,512]{1,0:T(8,128)(2,1)} %bitcast.108, f32[16,512,8]{2,1,0:T(8,128)} %bitcast.89, f32[1,8192]{1,0:T(1,128)} %reshape_reshape.6.decay_ref, bf16[512,768]{1,0:T(8,128)(2,1)} %fusion.1.onehot_ref, bf16[768,2048]{1,0:T(8,128)(2,1)} %bitcast.40.arr_ref), custom_call_target="tpu_custom_call" | custom-call | tf_op jit(solution)/shard_map/pallas_call | solution.py:125
  85.6 5.0 %all-to-all-start.1 = ((bf16[16,48,2048]{2,1,0:T(8,128)(2,1)}), bf16[16,48,2048]{2,1,0:T(8,128)(2,1)S(1)}, u32[]{:S(2)}, u32[]{:S(2)}) async-start(bf16[16,48,2048]{2,1,0:T(8,128)(2,1)} %bitcast.5), calls=%async_computation.1 | async-start | bytes 6291456 | tf_op jit(solution)/shard_map/all_to_all | solution.py:274
  90.7 5.4 %shard_map.68 = bf16[768,2048]{1,0:T(8,128)(2,1)} custom-call(bf16[768,512]{1,0:T(8,128)(2,1)} %fusion.onehot_ref, bf16[512,8192]{1,0:T(8,128)(2,1)} %bitcast.87), custom_call_target="tpu_custom_call" | custom-call | tf_op jit(solution)/shard_map/pallas_call | solution.py:48
  96.2 0.7 reshape_reshape.7.skip_ref
  96.9 2.6 copy.39
  99.5 2.2 fusion.9.scores_ref
  101.7 9.5 %shard_map.67.refs_0_ = f32[512,2048]{1,0:T(8,128)} custom-call(f32[512,512]{1,0:T(8,128)} %fusion.9.scores_ref, f32[16,512,8]{2,1,0:T(8,128)} %bitcast.77, f32[128,512]{1,0:T(8,128)} %bitcast.100, f32[128,512]{1,0:T(8,128)} %get-tuple-element.59.stept_ref, bf16[512,2048]{1,0:T(8,128)(2,1)} %get-tuple-element.24.tok_ref, f32[1,8192]{1,0:T(1,128)} %reshape_reshape.7.skip_ref), custom_call_target="tpu_custom_call" | custom-call | tf_op jit(solution)/shard_map/pallas_call | solution.py:150
  111.2 22.5 %all-to-all-done.1 = bf16[16,48,2048]{2,1,0:T(8,128)(2,1)S(1)} async-done(((bf16[16,48,2048]{2,1,0:T(8,128)(2,1)}), bf16[16,48,2048]{2,1,0:T(8,128)(2,1)S(1)}, u32[]{:S(2)}, u32[]{:S(2)}) %all-to-all-start.1) | async-done | bytes 3145760 | tf_op jit(solution)/shard_map/all_to_all | solution.py:274
  133.7 1.7 copy-done.2
  135.3 6.2 %shard_map.69 = (bf16[16,136,128]{2,1,0:T(8,128)(2,1)}, bf16[512,2048]{1,0:T(8,128)(2,1)}) custom-call(bf16[128,512]{1,0:T(8,128)(2,1)} %bitcast.109, f32[16,512,8]{2,1,0:T(8,128)} %bitcast.90, f32[1,8192]{1,0:T(1,128)} %reshape_reshape.6.decay_ref, bf16[512,768]{1,0:T(8,128)(2,1)} %fusion.1.onehot_ref, bf16[768,2048]{1,0:T(8,128)(2,1)} %bitcast.97), custom_call_target="tpu_custom_call" | custom-call | tf_op jit(solution)/shard_map/pallas_call | solution.py:125
  141.6 4.9 %all-to-all-start.3 = ((bf16[16,48,2048]{2,1,0:T(8,128)(2,1)}), bf16[16,48,2048]{2,1,0:T(8,128)(2,1)S(1)}, u32[]{:S(2)}, u32[]{:S(2)}) async-start(bf16[16,48,2048]{2,1,0:T(8,128)(2,1)} %bitcast.41), calls=%async_computation.3 | async-start | bytes 6291456 | tf_op jit(solution)/shard_map/all_to_all | solution.py:274
  146.7 5.4 %shard_map.72 = bf16[768,2048]{1,0:T(8,128)(2,1)} custom-call(bf16[768,512]{1,0:T(8,128)(2,1)} %fusion.onehot_ref, bf16[512,8192]{1,0:T(8,128)(2,1)} %bitcast.88), custom_call_target="tpu_custom_call" | custom-call | tf_op jit(solution)/shard_map/pallas_call | solution.py:48
  152.0 9.8 %shard_map.70.refs_1_ = f32[512,2048]{1,0:T(8,128)} custom-call(f32[512,512]{1,0:T(8,128)} %fusion.9.scores_ref, f32[16,512,8]{2,1,0:T(8,128)} %bitcast.78, f32[128,512]{1,0:T(8,128)} %bitcast.101, f32[128,512]{1,0:T(8,128)} %get-tuple-element.59.stept_ref, bf16[512,2048]{1,0:T(8,128)(2,1)} %get-tuple-element.27.tok_ref, f32[1,8192]{1,0:T(1,128)} %reshape_reshape.7.skip_ref), custom_call_target="tpu_custom_call" | custom-call | tf_op jit(solution)/shard_map/pallas_call | solution.py:150
  161.9 6.8 %shard_map.71.refs_0_ = bf16[512,8192]{1,0:T(8,128)(2,1)} custom-call(s32[1]{0:T(128)} %bitcast.place_ref, f32[512,2048]{1,0:T(8,128)} %shard_map.67.refs_0_, bf16[8,16,136,128]{3,2,1,0:T(8,128)(2,1)} %bitcast.104, f32[16,512,8]{2,1,0:T(8,128)} %bitcast.79, bf16[512,128]{1,0:T(8,128)(2,1)} %get-tuple-element.52.refs_3_.refs_4_), custom_call_target="tpu_custom_call" | custom-call | tf_op jit(solution)/shard_map/pallas_call | solution.py:183
  168.7 20.8 %all-to-all-done.3 = bf16[16,48,2048]{2,1,0:T(8,128)(2,1)S(1)} async-done(((bf16[16,48,2048]{2,1,0:T(8,128)(2,1)}), bf16[16,48,2048]{2,1,0:T(8,128)(2,1)S(1)}, u32[]{:S(2)}, u32[]{:S(2)}) %all-to-all-start.3) | async-done | bytes 3145760 | tf_op jit(solution)/shard_map/all_to_all | solution.py:274
  189.4 1.6 copy-done.1
  191.1 6.2 %shard_map.73 = (bf16[16,136,128]{2,1,0:T(8,128)(2,1)}, bf16[512,2048]{1,0:T(8,128)(2,1)}) custom-call(bf16[128,512]{1,0:T(8,128)(2,1)} %bitcast.110, f32[16,512,8]{2,1,0:T(8,128)} %bitcast.91, f32[1,8192]{1,0:T(1,128)} %reshape_reshape.6.decay_ref, bf16[512,768]{1,0:T(8,128)(2,1)} %fusion.1.onehot_ref, bf16[768,2048]{1,0:T(8,128)(2,1)} %bitcast.96), custom_call_target="tpu_custom_call" | custom-call | tf_op jit(solution)/shard_map/pallas_call | solution.py:125
  197.3 4.9 %all-to-all-start.4 = ((bf16[16,48,2048]{2,1,0:T(8,128)(2,1)}), bf16[16,48,2048]{2,1,0:T(8,128)(2,1)S(1)}, u32[]{:S(2)}, u32[]{:S(2)}) async-start(bf16[16,48,2048]{2,1,0:T(8,128)(2,1)} %bitcast.44), calls=%async_computation.4 | async-start | bytes 6291456 | tf_op jit(solution)/shard_map/all_to_all | solution.py:274
  202.2 9.4 %shard_map.74.refs_1_ = f32[512,2048]{1,0:T(8,128)} custom-call(f32[512,512]{1,0:T(8,128)} %fusion.9.scores_ref, f32[16,512,8]{2,1,0:T(8,128)} %bitcast.80, f32[128,512]{1,0:T(8,128)} %bitcast.102, f32[128,512]{1,0:T(8,128)} %get-tuple-element.59.stept_ref, bf16[512,2048]{1,0:T(8,128)(2,1)} %get-tuple-element.31.tok_ref, f32[1,8192]{1,0:T(1,128)} %reshape_reshape.7.skip_ref), custom_call_target="tpu_custom_call" | custom-call | tf_op jit(solution)/shard_map/pallas_call | solution.py:150
  211.7 6.7 %shard_map.75.refs_0_ = bf16[512,8192]{1,0:T(8,128)(2,1)} custom-call(s32[1]{0:T(128)} %bitcast.place_ref, bf16[512,8192]{1,0:T(8,128)(2,1)} %shard_map.71.refs_0_, f32[512,2048]{1,0:T(8,128)} %shard_map.70.refs_1_, bf16[8,16,136,128]{3,2,1,0:T(8,128)(2,1)} %bitcast.105, f32[16,512,8]{2,1,0:T(8,128)} %bitcast.81, ...), custom_call_target="tpu_custom_call", output_to_operand_aliasing={{}: (1, {})} | custom-call | tf_op jit(solution)/shard_map/pallas_call | solution.py:183
  218.4 26.8 %all-to-all-done.4 = bf16[16,48,2048]{2,1,0:T(8,128)(2,1)S(1)} async-done(((bf16[16,48,2048]{2,1,0:T(8,128)(2,1)}), bf16[16,48,2048]{2,1,0:T(8,128)(2,1)S(1)}, u32[]{:S(2)}, u32[]{:S(2)}) %all-to-all-start.4) | async-done | bytes 3145760 | tf_op jit(solution)/shard_map/all_to_all | solution.py:274
  245.2 1.7 copy-done
  246.9 6.2 %shard_map.77 = (bf16[16,136,128]{2,1,0:T(8,128)(2,1)}, bf16[512,2048]{1,0:T(8,128)(2,1)}) custom-call(bf16[128,512]{1,0:T(8,128)(2,1)} %bitcast.111, f32[16,512,8]{2,1,0:T(8,128)} %bitcast.92, f32[1,8192]{1,0:T(1,128)} %reshape_reshape.6.decay_ref, bf16[512,768]{1,0:T(8,128)(2,1)} %fusion.1.onehot_ref, bf16[768,2048]{1,0:T(8,128)(2,1)} %bitcast.95), custom_call_target="tpu_custom_call" | custom-call | tf_op jit(solution)/shard_map/pallas_call | solution.py:125
  253.1 9.4 %shard_map.78.refs_1_ = f32[512,2048]{1,0:T(8,128)} custom-call(f32[512,512]{1,0:T(8,128)} %fusion.9.scores_ref, f32[16,512,8]{2,1,0:T(8,128)} %bitcast.82, f32[128,512]{1,0:T(8,128)} %bitcast.103, f32[128,512]{1,0:T(8,128)} %get-tuple-element.59.stept_ref, bf16[512,2048]{1,0:T(8,128)(2,1)} %get-tuple-element.37.tok_ref, f32[1,8192]{1,0:T(1,128)} %reshape_reshape.7.skip_ref), custom_call_target="tpu_custom_call" | custom-call | tf_op jit(solution)/shard_map/pallas_call | solution.py:150
  262.6 7.1 %shard_map.76.refs_0_ = bf16[512,8192]{1,0:T(8,128)(2,1)} custom-call(s32[1]{0:T(128)} %bitcast.place_ref, bf16[512,8192]{1,0:T(8,128)(2,1)} %shard_map.75.refs_0_, f32[512,2048]{1,0:T(8,128)} %shard_map.74.refs_1_, bf16[8,16,136,128]{3,2,1,0:T(8,128)(2,1)} %bitcast.106, f32[16,512,8]{2,1,0:T(8,128)} %bitcast.83, ...), custom_call_target="tpu_custom_call", output_to_operand_aliasing={{}: (1, {})} | custom-call | tf_op jit(solution)/shard_map/pallas_call | solution.py:183
  269.6 17.8 %all-gather.15.cloned.1.call-done = bf16[128,136,128]{2,1,0:T(8,128)(2,1)} async-done(((bf16[16,136,128]{2,1,0:T(8,128)(2,1)}), bf16[128,136,128]{2,1,0:T(8,128)(2,1)}) %all-gather.15.cloned.1.call-update) | async-done | bytes 4456464 | tf_op jit(solution)/shard_map/all_gather | solution.py:296
  287.4 6.7 %shard_map.79 = bf16[512,8192]{1,0:T(8,128)(2,1)} custom-call(s32[1]{0:T(128)} %bitcast.place_ref, bf16[512,8192]{1,0:T(8,128)(2,1)} %shard_map.76.refs_0_, f32[512,2048]{1,0:T(8,128)} %shard_map.78.refs_1_, bf16[8,16,136,128]{3,2,1,0:T(8,128)(2,1)} %bitcast.107, f32[16,512,8]{2,1,0:T(8,128)} %bitcast.84, ...), custom_call_target="tpu_custom_call", output_to_operand_aliasing={{}: (1, {})} | custom-call | tf_op jit(solution)/shard_map/pallas_call | solution.py:183
  (54 shorter events, 3.1 us)
Async XLA Ops:
  12.6 19.5 %all-to-all-start.2 = ((bf16[16,48,384]{2,1,0:T(8,128)(2,1)}), bf16[16,48,384]{2,1,0:T(8,128)(2,1)S(1)}, u32[]{:S(2)}, u32[]{:S(2)}) async-start(bf16[16,48,384]{2,1,0:T(8,128)(2,1)} %bitcast.8), calls=%async_computation.2 | async-start | bytes 1179648 | tf_op jit(solution)/shard_map/all_to_all | solution.py:206
  32.1 47.3 %all-to-all-start = ((bf16[16,48,2048]{2,1,0:T(8,128)(2,1)}), bf16[16,48,2048]{2,1,0:T(8,128)(2,1)}, u32[]{:S(2)}, u32[]{:S(2)}) async-start(bf16[16,48,2048]{2,1,0:T(8,128)(2,1)} %bitcast.94), calls=%async_computation | async-start | bytes 6291456 | tf_op jit(solution)/shard_map/all_to_all | solution.py:274
  36.6 125.2 %all-gather.9.cloned.1.call-start = ((), (), s32[]{:S(2)}) async-start(), calls=%async_computation.5 | async-start | bytes 5013504 | tf_op jit(solution)/shard_map/all_gather | solution.py:296
  37.4 15.3 %copy-start.6 = (f32[128]{0:T(128)S(1)}, f32[128]{0:T(128)}, u32[]{:S(2)}) copy-start(f32[128]{0:T(128)} %param.9) | copy-start | bytes 1540
  55.8 5.4 %copy-start.4 = (bf16[512,384]{1,0:T(8,128)(2,1)}, bf16[512,384]{1,0:T(8,128)(2,1)S(1)}, u32[]{:S(2)}) copy-start(bf16[512,384]{1,0:T(8,128)(2,1)S(1)} %gather_fusion.1) | copy-start | bytes 1179652
  57.5 39.4 %copy-start.3 = (f32[16,8,4,128]{3,1,2,0:T(8,128)}, f32[16,8,4,128]{3,1,2,0:T(8,128)S(1)}, u32[]{:S(2)}) copy-start(f32[16,8,4,128]{3,1,2,0:T(8,128)S(1)} %copy.51) | copy-start | bytes 786436
  85.6 48.0 %all-to-all-start.1 = ((bf16[16,48,2048]{2,1,0:T(8,128)(2,1)}), bf16[16,48,2048]{2,1,0:T(8,128)(2,1)S(1)}, u32[]{:S(2)}, u32[]{:S(2)}) async-start(bf16[16,48,2048]{2,1,0:T(8,128)(2,1)} %bitcast.5), calls=%async_computation.1 | async-start | bytes 6291456 | tf_op jit(solution)/shard_map/all_to_all | solution.py:274
  90.6 5.4 %copy-start.5 = (f32[128]{0:T(128)S(1)}, f32[128]{0:T(128)}, u32[]{:S(2)}) copy-start(f32[128]{0:T(128)} %param.10) | copy-start | bytes 1540
  90.6 121.0 %all-gather.11.cloned.1.call-start = ((), (), s32[]{:S(2)}) async-start(), calls=%async_computation.6 | async-start | bytes 5013504 | tf_op jit(solution)/shard_map/all_gather | solution.py:296
  133.7 1.7 copy-start.2
  141.6 47.9 %all-to-all-start.3 = ((bf16[16,48,2048]{2,1,0:T(8,128)(2,1)}), bf16[16,48,2048]{2,1,0:T(8,128)(2,1)S(1)}, u32[]{:S(2)}, u32[]{:S(2)}) async-start(bf16[16,48,2048]{2,1,0:T(8,128)(2,1)} %bitcast.41), calls=%async_computation.3 | async-start | bytes 6291456 | tf_op jit(solution)/shard_map/all_to_all | solution.py:274
  146.4 116.1 %all-gather.13.cloned.1.call-start = ((), (), s32[]{:S(2)}) async-start(), calls=%async_computation.7 | async-start | bytes 5013504 | tf_op jit(solution)/shard_map/all_gather | solution.py:296
  189.4 1.6 copy-start.1
  197.3 47.9 %all-to-all-start.4 = ((bf16[16,48,2048]{2,1,0:T(8,128)(2,1)}), bf16[16,48,2048]{2,1,0:T(8,128)(2,1)S(1)}, u32[]{:S(2)}, u32[]{:S(2)}) async-start(bf16[16,48,2048]{2,1,0:T(8,128)(2,1)} %bitcast.44), calls=%async_computation.4 | async-start | bytes 6291456 | tf_op jit(solution)/shard_map/all_to_all | solution.py:274
  202.2 85.2 %all-gather.15.cloned.1.call-start = ((), (), s32[]{:S(2)}) async-start(), calls=%async_computation.8 | async-start | bytes 5013504 | tf_op jit(solution)/shard_map/all_gather | solution.py:296
  245.2 1.7 copy-start
Sparse Core Ops, SparseCore 0:
  85.7 34.2 all-gather.8
  141.7 34.1 all-gather.10
  197.4 34.1 all-gather.12
  253.2 34.1 all-gather.14
